TPU v7x, 32 devices: a whole 2x2x4 slice. The times are simulated.
32 devices in a mesh: seq: 16 (over z, y, x), head: 2 (over core).
Axes of the slice: x: 2, y: 2, z: 4, core: 2. Of those that a mesh axis runs over, the one named last changes fastest.
Arguments:
- ingest: bfloat16 [256, 128, 1024], P('seq', None, 'head'), may hold values from -6 to 6
- dest_tile: int32 [256], P('seq'), may hold values from 0 to 255, as said below
- doc_start: int32 [256], P('seq'), may hold values from 0 to 128, as said below
- w_zx: bfloat16 [1024, 2, 2048], P(None, None, 'head'), may hold values from -0.1875 to 0.1875
- w_bc: bfloat16 [1024, 256], replicated, may hold values from -0.1875 to 0.1875
- w_dt: bfloat16 [1024, 32], P(None, 'head'), may hold values from -0.1875 to 0.1875
- dt_bias: float32 [32], P('head'), may hold values from -7.5 to -5.5
- a_log: float32 [32], P('head'), may hold values from -10 to 3
- conv_x: float32 [4, 2048], P(None, 'head'), may hold values from -3 to 3
- conv_bc: float32 [4, 256], replicated, may hold values from -3 to 3
- cbias_x: float32 [2048], P('head'), may hold values from -3 to 3
- cbias_bc: float32 [256], replicated, may hold values from -3 to 3
- d_skip: float32 [32], P('head'), may hold values from 0.5 to 1.5
- norm_gain: float32 [2048], P('head'), may hold values from 0.1 to 1.9
Outputs:
- embedded: bfloat16 [32768, 2048], P('seq', 'head')
Inputs may be any that keep to these rules, and one draw needn't show every extreme that they name: dest_tile is a permutation of the sequence tiles; the owner of sequence tile p is p // 16; the 16 tiles of one ingest device go to 16 different owners, and every owner receives exactly 16 tiles. `doc_start`: 128 means that no document starts in the tile.
All inputs are finite; a program needn't handle non-finite values.
Results may differ from a plain program's by a relative error of at most 0.0056.
Values may be sent and summed in bfloat16 or wider, within the bound.
No kernel may reach another device: no remote copies, remote signals or barrier semaphores. Data moves between devices by JAX's collectives and lax.ppermute only.
A program may use at most 128 MiB of HBM per device.

v0:
```python
import jax
import jax.numpy as jnp
from jax import lax
from jax.sharding import PartitionSpec as P

INNER = 2048


EPSILON = 1e-05


def shifted(x, axis, by):
    devices = lax.axis_size(axis)
    pairs = [(i, i + by) for i in range(devices) if 0 <= i + by < devices]
    return lax.ppermute(x, axis, pairs)


def advance(carry, item):
    passing, contrib = item
    return (passing[:, None, None] * carry + contrib, carry)


def shards(
    ingest,
    dest_tile,
    doc_start,
    w_zx,
    w_bc,
    w_dt,
    dt_bias,
    a_log,
    conv_x,
    conv_bc,
    cbias_x,
    cbias_bc,
    d_skip,
    norm_gain,
):
    seq_count = lax.axis_size("seq")
    tiles_dev = ingest.shape[0]
    tile_len = ingest.shape[1]
    columns = ingest.shape[2]
    row_count = tiles_dev * tile_len
    heads_here = a_log.shape[0]
    inner_here = conv_x.shape[1]
    head_dim = inner_here // heads_here
    state_dim = conv_bc.shape[1] // 2
    taps = conv_x.shape[0]
    keep_rows = taps - 1
    owner = dest_tile // tiles_dev
    offset = dest_tile % tiles_dev
    slots = jnp.arange(seq_count, dtype=jnp.int32)
    pick = (owner[None, :] == slots[:, None]).astype(jnp.float32)
    outgoing = jnp.einsum(
        "sj,jrc->src", pick.astype(jnp.bfloat16), ingest, preferred_element_type=jnp.float32
    ).astype(jnp.bfloat16)
    marks = (
        jnp.dot(pick, (offset + 1).astype(jnp.float32), precision=lax.Precision.HIGHEST) - 1.0
    ).astype(jnp.bfloat16)
    incoming, got_marks = (
        lax.all_to_all(outgoing, "seq", split_axis=0, concat_axis=0, tiled=True),
        lax.all_to_all(marks, "seq", split_axis=0, concat_axis=0, tiled=True),
    )
    local_slots = jnp.arange(tiles_dev, dtype=jnp.float32)
    place = (got_marks.astype(jnp.float32)[None, :] == local_slots[:, None]).astype(jnp.bfloat16)
    arrived = jnp.einsum("js,src->jrc", place, incoming, preferred_element_type=jnp.float32).astype(
        jnp.bfloat16
    )
    own_rows = arrived.reshape(row_count, columns)
    zx_cols = w_zx.reshape(w_zx.shape[0], -1)
    weight_set = (zx_cols, w_bc, w_dt)
    piece = lax.all_gather(own_rows, "head", axis=1, tiled=True)
    acc_zx, acc_bc, acc_dt = tuple(
        (jnp.dot(piece, weight, preferred_element_type=jnp.float32) for weight in weight_set)
    )
    gate = acc_zx[:, :inner_here].astype(jnp.bfloat16)
    x_in = acc_zx[:, inner_here:].astype(jnp.bfloat16)
    bc_all = acc_bc.astype(jnp.bfloat16)
    step_dt = jax.nn.softplus(acc_dt + dt_bias[None, :])
    within = jnp.arange(tile_len, dtype=jnp.int32)
    has_bound = (doc_start < tile_len).astype(jnp.float32)
    before_count = jnp.cumsum(has_bound) - has_bound
    later = (within[None, :] >= doc_start[:, None]).astype(jnp.float32)
    segment = (before_count[:, None] + later).reshape(row_count)
    conv_in = jnp.concatenate([x_in, bc_all], 1)
    tail = conv_in[row_count - keep_rows :]
    tail_seg = (segment[row_count - keep_rows :] - segment[row_count - 1]).astype(jnp.bfloat16)
    got_tail, got_seg = shifted((tail, tail_seg), "seq", 1)
    extended = jnp.concatenate([got_tail, conv_in], 0)
    ext_seg = jnp.concatenate([got_seg.astype(jnp.float32), segment], 0)
    conv_weight = jnp.concatenate([conv_x, conv_bc], 1)
    conv_bias = jnp.concatenate([cbias_x, cbias_bc], 0)
    total = conv_bias[None, :] + conv_weight[taps - 1][None, :] * conv_in.astype(jnp.float32)
    for back_step in range(keep_rows):
        same = ext_seg[back_step : back_step + row_count] == segment
        total = total + jnp.where(
            same[:, None],
            conv_weight[back_step][None, :]
            * extended[back_step : back_step + row_count].astype(jnp.float32),
            0.0,
        )
    conv_out = jax.nn.silu(total).astype(jnp.bfloat16)
    x_heads = conv_out[:, :inner_here].reshape(tiles_dev, tile_len, heads_here, head_dim)
    b_part = conv_out[:, inner_here : inner_here + state_dim].reshape(
        tiles_dev, tile_len, state_dim
    )
    c_part = conv_out[:, inner_here + state_dim :].reshape(tiles_dev, tile_len, state_dim)
    rate = -jnp.exp(a_log)
    tile_dt = step_dt.reshape(tiles_dev, tile_len, heads_here)
    cumul = jnp.cumsum(tile_dt * rate[None, None, :], 1)
    cumul_t = cumul.transpose(0, 2, 1)
    dt_t = tile_dt.transpose(0, 2, 1)
    causal = within[:, None] >= within[None, :]
    keep = causal[None, :, :] & (later[:, :, None] == later[:, None, :])
    mask_four = keep[:, None, :, :]
    diff = cumul_t[:, :, :, None] - cumul_t[:, :, None, :]
    decay = jnp.where(mask_four, jnp.exp(jnp.where(mask_four, diff, 0.0)), 0.0)
    scores = jnp.einsum("jin,jsn->jis", c_part, b_part, preferred_element_type=jnp.float32)
    weights = (scores[:, None, :, :] * decay * dt_t[:, :, None, :]).astype(jnp.bfloat16)
    intra = jnp.einsum("jhis,jshp->jihp", weights, x_heads, preferred_element_type=jnp.float32)
    last_part = later[:, tile_len - 1]
    tail_keep = (later == last_part[:, None]).astype(jnp.float32)
    to_end = jnp.exp(cumul[:, tile_len - 1 :, :] - cumul) * tile_dt * tail_keep[:, :, None]
    scaled = (x_heads.astype(jnp.float32) * to_end[:, :, :, None]).astype(jnp.bfloat16)
    contrib = jnp.einsum("jshp,jsn->jhpn", scaled, b_part, preferred_element_type=jnp.float32)
    passing = jnp.exp(cumul[:, tile_len - 1, :]) * (1.0 - has_bound)[:, None]
    final, before_tile = lax.scan(
        advance, jnp.zeros((heads_here, head_dim, state_dim), jnp.float32), (passing, contrib)
    )
    through = jnp.cumprod(passing, 0)
    prefix = jnp.concatenate([jnp.ones((1, heads_here), jnp.float32), through[:-1]], 0)
    all_decay, all_state = (
        lax.all_gather(through[tiles_dev - 1 :], "seq", axis=0, tiled=True),
        lax.all_gather(final[None], "seq", axis=0, tiled=True),
    )
    position = lax.axis_index("seq")
    index = jnp.arange(seq_count, dtype=jnp.int32)
    between = (index[None, :] > index[:, None]) & (index[None, :] < position)
    factors = jnp.where(between[:, :, None], all_decay[None, :, :], 1.0)
    reach = jnp.prod(factors, 1) * (index < position).astype(jnp.float32)[:, None]
    entering = jnp.einsum(
        "jh,jhq->hq",
        reach,
        all_state.reshape(seq_count, heads_here, head_dim * state_dim),
        precision=lax.Precision.HIGHEST,
    ).reshape(heads_here, head_dim, state_dim)
    tile_state = before_tile + prefix[:, :, None, None] * entering[None]
    carried = tile_state.astype(jnp.bfloat16)
    inter = (
        jnp.exp(cumul)[:, :, :, None]
        * (1.0 - later)[:, :, None, None]
        * jnp.einsum("jin,jhpn->jihp", c_part, carried, preferred_element_type=jnp.float32)
    )
    mixed = intra + inter + d_skip[None, None, :, None] * x_heads.astype(jnp.float32)
    gated = mixed.reshape(row_count, inner_here) * jax.nn.silu(gate.astype(jnp.float32))
    sums = lax.psum(jnp.sum(gated * gated, 1), "head")
    return (gated * lax.rsqrt(sums / INNER + EPSILON)[:, None] * norm_gain[None, :]).astype(
        jnp.bfloat16
    )


def solution(mesh):
    return jax.shard_map(
        shards,
        mesh=mesh,
        in_specs=(
            P("seq", None, "head"),
            P("seq"),
            P("seq"),
            P(None, None, "head"),
            P(),
            P(None, "head"),
            P("head"),
            P("head"),
            P(None, "head"),
            P(),
            P("head"),
            P(),
            P("head"),
            P("head"),
        ),
        out_specs=P("seq", "head"),
        check_vma=False,
    )
```

profile of v0, /device:TPU:0, one launch (start us, length us, event | category | flops | bytes accessed | tf_op | source)
XLA Modules:
  0.0 385.2 jit_solution(12651790448696187915)
XLA Ops:
  8.8 8.3 %all-to-all-start = ((bf16[16,1,1]{2,1,0:T(2,128)(2,1)}), bf16[16,1,1]{2,1,0:T(2,128)(2,1)S(1)}, u32[]{:S(2)}, u32[]{:S(2)}) async-start(bf16[16,1,1]{2,1,0:T(2,128)(2,1)} %copy.114), calls=%async_computation | async-start | bytes 16384 | tf_op jit(solution)/shard_map/all_to_all | solution.py:62
  21.0 3.4 all-to-all-done
  24.4 3.7 all-to-all-start.1
  28.4 42.4 %all-to-all-done.1 = bf16[16,128,512]{2,1,0:T(8,128)(2,1)S(1)} async-done(((bf16[16,128,512]{2,1,0:T(8,128)(2,1)}), bf16[16,128,512]{2,1,0:T(8,128)(2,1)S(1)}, u32[]{:S(2)}, u32[]{:S(2)}) %all-to-all-start.1) | async-done | bytes 2097184 | tf_op jit(solution)/shard_map/all_to_all | solution.py:61
  80.2 5.6 %copy.148 = bf16[128,8,2,1024]{3,1,2,0:T(8,128)(2,1)} copy(bf16[128,8,2,1024]{3,2,1,0:T(2,128)(2,1)} %bitcast.117) | data formatting | bytes 8388608
  86.0 6.7 %all-gather.5.cloned.1.call-done = bf16[2048,1024]{1,0:T(8,128)(2,1)} async-done(((bf16[2048,512]{1,0:T(8,128)(2,1)}), bf16[2048,1024]{1,0:T(8,128)(2,1)}) %all-gather.5.cloned.1.call-update) | async-done | bytes 4194320 | tf_op jit(solution)/shard_map/all_gather | solution.py:72
  92.7 3.4 fusion.48
  96.9 12.4 %convolution_convert_fusion = bf16[2048,2048]{0,1:T(8,128)(2,1)S(1)} fusion(bf16[2048,1024]{1,0:T(8,128)(2,1)} %all-gather.5.cloned.1.call-done, bf16[1024,2048]{1,0:T(8,128)(2,1)} %bitcast.118), kind=kOutput, calls=%fused_computation.29 | convolution fusion | flops 8594128896 | bytes 16777216 | tf_op jit(solution)/shard_map/dot_general | solution.py:74
  114.1 3.9 collective-permute-start.1
  121.5 4.0 %collective-permute-done.1 = bf16[3,1280]{0,1:T(8,128)(2,1)S(1)} collective-permute-done((bf16[3,1280]{0,1:T(8,128)(2,1)}, bf16[3,1280]{0,1:T(8,128)(2,1)S(1)}, u32[]{:S(2)}, u32[]{:S(2)}) %collective-permute-start.1) | collective-permute-done | bytes 7712 | tf_op jit(solution)/shard_map/ppermute | solution.py:15
  125.5 9.0 %maximum_maximum_fusion = bf16[2051,1280]{0,1:T(8,128)(2,1)S(1)} fusion(bf16[2048,256]{0,1:T(8,128)(2,1)} %copy-done.7, bf16[2048,1024]{0,1:T(8,128)(2,1)} %copy-done.2, bf16[3,1280]{0,1:T(8,128)(2,1)S(1)} %collective-permute-done.1), kind=kLoop, calls=%fused_computation.32 | loop fusion | flops 15751680 | bytes 10501120 | tf_op jit(solution)/shard_map/concatenate | solution.py:89
  134.5 15.1 %multiply_convert_fusion.1 = bf16[2048,1280]{0,1:T(8,128)(2,1)S(1)} fusion(bf16[2048,256]{0,1:T(8,128)(2,1)S(1)} %copy-done.8, bf16[2051,1280]{0,1:T(8,128)(2,1)S(1)} %maximum_maximum_fusion, f32[1280]{0:T(1024)S(1)} %get-tuple-element.54, f32[1280]{0:T(1024)S(1)} %get-tuple-element.55, f32[1280]{0:T(1024)S(1)} %get-tuple-element.56, ...), kind=kLoop, calls=%fused_computation.9 | loop fusion | flops 60293120 | bytes 26246144 | tf_op jit(solution)/shard_map/convert_element_type | solution.py:102
  155.0 4.5 %fusion.17 = f32[16,16,64,128]{3,2,1,0:T(8,128)} fusion(f32[16,128,16]{1,2,0:T(8,128)S(1)} %copy.132, bf16[16,128,16,64]{1,0,3,2:T(8,128)(2,1)S(1)} %bitcast.111, bf16[16,128,128,1]{1,0,2,3:T(8,128)(2,1)S(1)} %bitcast.121), kind=kOutput, calls=%fused_computation.35 | convolution fusion | flops 543162368 | bytes 13238272 | tf_op jit(solution)/shard_map/jshp,jsn->jhpn/dot_general | solution.py:125
  159.5 33.0 %while.13 = (s32[]{:T(128)}, f32[16,64,128]{2,1,0:T(8,128)S(1)}, f32[16,16,64,128]{3,2,1,0:T(8,128)}, f32[16,16]{1,0:T(8,128)S(1)}, f32[16,16,64,128]{3,2,1,0:T(8,128)}, /*index=5*/s32[]{:T(128)}, s32[]{:T(128)}) while((s32[]{:T(128)}, f32[16,64,128]{2,1,0:T(8,128)S(1)}, f32[16,16,64,128]{3,2,1,0:T(8,128)}, ...), condition=%wide.region_3.4_spmd.clone, body=%wide.region_2.3_spmd.clone.sunk | while | flops 524291 | bytes 2621740 | solution.py:127
  194.4 42.1 %all-gather.1 = f32[16,1,16]{2,1,0:T(1,128)S(1)} all-gather(f32[1,1,16]{2,1,0:T(1,128)S(1)} %slice_bitcast_fusion.6), channel_id=1, replica_groups=mesh['seq'=16,'head'=2] {'seq'}, dimensions={0}, use_global_device_ids=true | all-gather | bytes 1088 | tf_op jit(solution)/shard_map/all_gather | solution.py:133
  239.9 68.2 %all-gather.7.cloned.1.call-done = f32[256,64,128]{2,1,0:T(8,128)} async-done(((f32[16,64,128]{2,1,0:T(8,128)}), f32[256,64,128]{2,1,0:T(8,128)}) %all-gather.7.cloned.1.call-update) | async-done | bytes 8388624 | tf_op jit(solution)/shard_map/all_gather | solution.py:134
  308.1 9.4 %reshape.254 = f32[16,16,8192]{2,1,0:T(8,128)} reshape(f32[256,64,128]{2,1,0:T(8,128)} %all-gather.7.cloned.1.call-done) | data formatting | bytes 16777216 | tf_op jit(solution)/shard_map/reshape | solution.py:144
  317.5 12.5 %fusion.8 = f32[16,1,8192]{2,1,0:T(1,128)S(1)} fusion(f32[16,16,1]{0,2,1:T(1,128)S(1)} %copy.138, f32[16,16,8192]{2,1,0:T(8,128)} %reshape.254), kind=kOutput, calls=%fused_computation.18 | convolution fusion | flops 25165824 | bytes 8913920 | tf_op jit(solution)/shard_map/jh,jhq->hq/dot_general | solution.py:141
  330.5 4.8 %fusion.16 = f32[16,128,16,64]{1,3,2,0:T(8,128)S(1)} fusion(f32[16,16,64,128]{3,2,1,0:T(8,128)} %get-tuple-element.33, f32[16,64,128]{2,1,0:T(8,128)S(1)} %bitcast.120, f32[16,16]{1,0:T(8,128)S(1)} %concatenate.23, bf16[16,128,128,1]{1,0,2,3:T(8,128)(2,1)S(1)} %bitcast.119), kind=kOutput, calls=%fused_computation.34 | convolution fusion | flops 543162368 | bytes 17826816 | tf_op jit(solution)/shard_map/jin,jhpn->jihp/dot_general | solution.py:152
  335.4 10.7 %fusion.3 = f32[16,128,16,64]{1,3,2,0:T(8,128)} fusion(f32[16,128,16,64]{1,3,2,0:T(8,128)S(1)} %fusion.16, f32[16]{0:T(128)S(1)} %copy-done.25, f32[16,128,16]{1,2,0:T(8,128)S(1)} %copy-done.13, f32[16,16,128]{2,1,0:T(8,128)S(1)} %copy-done.14, f32[16,16,128]{2,1,0:T(8,128)S(1)} %copy.123, f32[16,128,128]{2,1,0:T(8,128)S(1)} %fusion.39, ...), kind=kOutput, calls=%fused_computation.12 | convolution fusion | flops 572522496 | bytes 22675520 | tf_op jit(solution)/shard_map/jhis,jshp->jihp/dot_general | solution.py:120
  346.1 9.9 %copy.135 = f32[16,128,16,64]{1,0,3,2:T(8,128)S(1)} copy(f32[16,128,16,64]{1,3,2,0:T(8,128)} %fusion.3) | data formatting | bytes 16777216 | tf_op jit(solution)/shard_map/add | solution.py:154
  356.1 7.0 %multiply_reduce_fusion = (f32[2048]{0:T(1024)S(1)}, f32[2048,1024]{0,1:T(8,128)}) fusion(bf16[2048,2048]{0,1:T(8,128)(2,1)S(1)} %bitcast.115, f32[128,8,16,128]{3,2,1,0:T(8,128)S(1)} %bitcast.110), kind=kLoop, calls=%fused_computation.21 | loop fusion | flops 16775168 | bytes 20979712 | tf_op jit(solution)/shard_map/reduce_sum | solution.py:156
  365.5 6.3 %multiply_convert_fusion.3 = bf16[2048,1024]{0,1:T(8,128)(2,1)} fusion(f32[2048,1024]{0,1:T(8,128)} %get-tuple-element.68, f32[1024]{0:T(1024)S(1)} %copy-done.18, f32[2048]{0:T(1024)S(1)} %add_rsqrt_fusion), kind=kLoop, calls=%fused_computation.20 | loop fusion | flops 6291456 | bytes 12595200 | tf_op jit(solution)/shard_map/convert_element_type | solution.py:157
  371.8 6.4 %copy.136 = bf16[2048,1024]{1,0:T(8,128)(2,1)} copy(bf16[2048,1024]{0,1:T(8,128)(2,1)} %multiply_convert_fusion.3) | data formatting | bytes 8388608 | tf_op jit(solution)/shard_map/convert_element_type | solution.py:157
  (174 shorter events, 70.9 us)
Async XLA Ops:
  6.5 10.6 %copy-start = (bf16[16,128,512]{2,1,0:T(8,128)(2,1)S(1)}, bf16[16,128,512]{2,1,0:T(8,128)(2,1)}, u32[]{:S(2)}) copy-start(bf16[16,128,512]{2,1,0:T(8,128)(2,1)} %param.16) | copy-start | bytes 6291460
  8.8 15.6 %all-to-all-start = ((bf16[16,1,1]{2,1,0:T(2,128)(2,1)}), bf16[16,1,1]{2,1,0:T(2,128)(2,1)S(1)}, u32[]{:S(2)}, u32[]{:S(2)}) async-start(bf16[16,1,1]{2,1,0:T(2,128)(2,1)} %copy.114), calls=%async_computation | async-start | bytes 16384 | tf_op jit(solution)/shard_map/all_to_all | solution.py:62
  21.0 53.8 %copy-start.17 = (s32[16]{0:T(128)S(1)}, s32[16]{0:T(128)}, u32[]{:S(2)}) copy-start(s32[16]{0:T(128)} %param.18) | copy-start | bytes 196
  24.4 46.4 %all-to-all-start.1 = ((bf16[16,128,512]{2,1,0:T(8,128)(2,1)}), bf16[16,128,512]{2,1,0:T(8,128)(2,1)S(1)}, u32[]{:S(2)}, u32[]{:S(2)}) async-start(bf16[16,128,512]{2,1,0:T(8,128)(2,1)} %copy.116), calls=%async_computation.1 | async-start | bytes 4194304 | tf_op jit(solution)/shard_map/all_to_all | solution.py:61
  28.2 64.6 %all-gather.5.cloned.1.call-start = ((), (), s32[]{:S(2)}) async-start(), calls=%async_computation.2 | async-start | bytes 6291456 | tf_op jit(solution)/shard_map/all_gather | solution.py:72
  72.2 13.6 %copy-start.16 = (f32[4,1024]{1,0:T(4,128)S(1)}, f32[4,1024]{1,0:T(4,128)}, u32[]{:S(2)}) copy-start(f32[4,1024]{1,0:T(4,128)} %param.24) | copy-start | bytes 49156
  72.2 13.6 %copy-start.19 = (f32[4,256]{1,0:T(4,128)S(1)}, f32[4,256]{1,0:T(4,128)}, u32[]{:S(2)}) copy-start(f32[4,256]{1,0:T(4,128)} %param.25) | copy-start | bytes 12292
  72.2 13.6 %copy-start.20 = (f32[1024]{0:T(1024)S(1)}, f32[1024]{0:T(1024)}, u32[]{:S(2)}) copy-start(f32[1024]{0:T(1024)} %param.26) | copy-start | bytes 12292
  72.2 13.6 %copy-start.22 = (f32[256]{0:T(256)S(1)}, f32[256]{0:T(256)}, u32[]{:S(2)}) copy-start(f32[256]{0:T(256)} %param.27) | copy-start | bytes 3076
  72.2 13.7 %copy-start.24 = (f32[16]{0:T(128)S(1)}, f32[16]{0:T(128)}, u32[]{:S(2)}) copy-start(f32[16]{0:T(128)} %param.23) | copy-start | bytes 196
  72.2 20.5 %copy-start.15 = (bf16[1024,16]{0,1:T(8,128)(2,1)S(1)}, bf16[1024,16]{0,1:T(8,128)(2,1)}, u32[]{:S(2)}) copy-start(bf16[1024,16]{0,1:T(8,128)(2,1)} %param.21) | copy-start | bytes 98308
  72.3 20.5 %copy-start.21 = (f32[16]{0:T(128)S(1)}, f32[16]{0:T(128)}, u32[]{:S(2)}) copy-start(f32[16]{0:T(128)} %param.22) | copy-start | bytes 196
  74.8 233.3 %all-gather.7.cloned.1.call-start = ((), (), s32[]{:S(2)}) async-start(), calls=%async_computation.3 | async-start | bytes 8912896 | tf_op jit(solution)/shard_map/all_gather | solution.py:134
  76.5 9.4 %collective-permute-start = (bf16[3]{0:T(256)(128)(2,1)S(1)}, bf16[3]{0:T(256)(128)(2,1)S(1)}, u32[]{:S(2)}, u32[]{:S(2)}) collective-permute-start(bf16[3]{0:T(256)(128)(2,1)S(1)} %fusion.69), channel_id=1, source_target_pairs={{0,2},{2,4},{4,6},{6,8},{8,10},{10,12},{12,14},{14,16},{16,18},{18... | collective-permute-start | bytes 26 | tf_op jit(solution)/shard_map/ppermute | solution.py:15
  96.9 12.7 %copy-start.10 = (bf16[2048,1024]{1,0:T(8,128)(2,1)S(1)}, bf16[2048,1024]{1,0:T(8,128)(2,1)}, u32[]{:S(2)}) copy-start(bf16[2048,1024]{1,0:T(8,128)(2,1)} %all-gather.5.cloned.1.call-done) | copy-start | bytes 12582916
  96.9 12.7 %copy-start.23 = (bf16[1024,256]{1,0:T(8,128)(2,1)S(1)}, bf16[1024,256]{1,0:T(8,128)(2,1)}, u32[]{:S(2)}) copy-start(bf16[1024,256]{1,0:T(8,128)(2,1)} %param.20) | copy-start | bytes 1572868
  114.1 11.4 %collective-permute-start.1 = (bf16[3,1280]{0,1:T(8,128)(2,1)}, bf16[3,1280]{0,1:T(8,128)(2,1)S(1)}, u32[]{:S(2)}, u32[]{:S(2)}) collective-permute-start(bf16[3,1280]{0,1:T(8,128)(2,1)} %fusion.47), channel_id=1, source_target_pairs={{0,2},{2,4},{4,6},{6,8},{8,10},{10,12},{12,14},{14,16},{16,18},{18... | collective-permute-start | bytes 23048 | tf_op jit(solution)/shard_map/ppermute | solution.py:15
  119.7 14.8 %copy-start.8 = (bf16[2048,256]{0,1:T(8,128)(2,1)S(1)}, bf16[2048,256]{0,1:T(8,128)(2,1)}, u32[]{:S(2)}) copy-start(bf16[2048,256]{0,1:T(8,128)(2,1)} %copy-done.7) | copy-start | bytes 3145732
  121.5 13.0 %copy-start.3 = (bf16[2048,1024]{0,1:T(8,128)(2,1)S(1)}, bf16[2048,1024]{0,1:T(8,128)(2,1)}, u32[]{:S(2)}) copy-start(bf16[2048,1024]{0,1:T(8,128)(2,1)} %copy-done.2) | copy-start | bytes 12582916
  159.5 77.7 %copy-start.11 = (f32[16,128,16]{2,0,1:T(8,128)S(1)}, f32[16,128,16]{2,0,1:T(8,128)}, u32[]{:S(2)}) copy-start(f32[16,128,16]{2,0,1:T(8,128)} %get-tuple-element.73) | copy-start | bytes 393220
  159.5 78.7 %copy-start.12 = (bf16[16,8,16,128]{3,1,2,0:T(8,128)(2,1)S(1)}, bf16[16,8,16,128]{3,1,2,0:T(8,128)(2,1)}, u32[]{:S(2)}) copy-start(bf16[16,8,16,128]{3,1,2,0:T(8,128)(2,1)} %get-tuple-element.72) | copy-start | bytes 1572868
  330.5 25.6 %slice-start = ((s8[8388608]{0:T(1024)(128)(4,1)}), s8[4194304]{0:T(1024)(128)(4,1)S(1)}, s32[]{:S(2)}) async-start(s8[8388608]{0:T(1024)(128)(4,1)} %bitcast.114), calls=%async_computation.4 | async-start | bytes 8388608
  335.3 20.7 %slice-start.1 = ((s8[8388608]{0:T(1024)(128)(4,1)}), s8[4194304]{0:T(1024)(128)(4,1)S(1)}, s32[]{:S(2)}) async-start(s8[8388608]{0:T(1024)(128)(4,1)} %bitcast.114), calls=%async_computation.5 | async-start | bytes 8388608
  365.5 12.7 %copy-start.1 = (bf16[16,128,512]{2,1,0:T(8,128)(2,1)S(1)}, bf16[16,128,512]{2,1,0:T(8,128)(2,1)}, u32[]{:S(2)}) copy-start(bf16[16,128,512]{2,1,0:T(8,128)(2,1)} %param.16) | copy-start | bytes 6291460
  (10 other events, 46.8 us)
Sparse Core Ops, SparseCore 0:
  74.9 17.7 all-gather.4
  193.4 114.6 all-gather.6
where the time goes:
time: 392 us; the launch traced here: 385 us
  waiting for transfers between devices  125 us (32%)
  other arithmetic  76.1 us (19%)
  matrix products  54.6 us (14%)
  local copies, waits for them, and re-layouts  51.5 us (13%)
  blocking collectives  44.5 us (11%)
  starting transfers between devices  19.1 us (5%)
  between operations  14.2 us (4%)
    all_gather x1, waiting for transfers between devices, shards(): lax.all_gather(final[None], 'seq', axis=0, tiled=True)  68.2 us
    all_to_all x1, waiting for transfers between devices, shards(): lax.all_to_all(outgoing, 'seq', split_axis=0, concat_axis=0, tiled=True)  42.4 us
    all_gather x1, blocking collectives, shards(): lax.all_gather(through[tiles_dev - 1:], 'seq', axis=0, tiled=True)  42.1 us
    add x16, other arithmetic, advance(): return (passing[:, None, None] * carry + contrib, carry)  18.5 us
    dot_general x3, matrix products, shards(): jnp.dot(piece, weight, preferred_element_type=jnp.float32)  17.1 us
    convert_element_type x1, other arithmetic, shards(): conv_out = jax.nn.silu(total).astype(jnp.bfloat16)  15.1 us
    dynamic_update_slice x16, other arithmetic, shards(): lax.scan(advance, jnp.zeros((heads_here, head_dim, state_dim), jnp.float3...  13.9 us
    unnamed x66, local copies, waits for them, and re-layouts  13.7 us
  transfers between devices with their start and end apart: 6, of which 5 were waited for; matrix products, arithmetic and copies ran while one was open for 5% of the time, Pallas kernels for 0%

commit v1 on v0

--- a/solution.py
+++ b/solution.py
@@ -13,11 +13,6 @@
     devices = lax.axis_size(axis)
     pairs = [(i, i + by) for i in range(devices) if 0 <= i + by < devices]
     return lax.ppermute(x, axis, pairs)
-
-
-def advance(carry, item):
-    passing, contrib = item
-    return (passing[:, None, None] * carry + contrib, carry)
 
 
 def shards(
@@ -124,26 +119,31 @@
     scaled = (x_heads.astype(jnp.float32) * to_end[:, :, :, None]).astype(jnp.bfloat16)
     contrib = jnp.einsum("jshp,jsn->jhpn", scaled, b_part, preferred_element_type=jnp.float32)
     passing = jnp.exp(cumul[:, tile_len - 1, :]) * (1.0 - has_bound)[:, None]
-    final, before_tile = lax.scan(
-        advance, jnp.zeros((heads_here, head_dim, state_dim), jnp.float32), (passing, contrib)
+    tile_ids = jnp.arange(tiles_dev + 1, dtype=jnp.int32)
+    src_ids = jnp.arange(tiles_dev, dtype=jnp.int32)
+    between_tiles = (src_ids[None, :, None] < src_ids[None, None, :]) & (
+        src_ids[None, None, :] < tile_ids[:, None, None]
     )
+    spans = jnp.prod(
+        jnp.where(between_tiles[:, :, :, None], passing[None, None, :, :], 1.0), 2
+    ) * (src_ids[None, :] < tile_ids[:, None]).astype(jnp.float32)[:, :, None]
+    flat_contrib = contrib.reshape(tiles_dev, heads_here, head_dim * state_dim)
+    local_state = jnp.einsum(
+        "cjh,jhq->chq", spans, flat_contrib, precision=lax.Precision.HIGHEST
+    ).reshape(tiles_dev + 1, heads_here, head_dim, state_dim)
+    before_tile = local_state[:tiles_dev]
     through = jnp.cumprod(passing, 0)
     prefix = jnp.concatenate([jnp.ones((1, heads_here), jnp.float32), through[:-1]], 0)
-    all_decay, all_state = (
-        lax.all_gather(through[tiles_dev - 1 :], "seq", axis=0, tiled=True),
-        lax.all_gather(final[None], "seq", axis=0, tiled=True),
-    )
     position = lax.axis_index("seq")
-    index = jnp.arange(seq_count, dtype=jnp.int32)
-    between = (index[None, :] > index[:, None]) & (index[None, :] < position)
-    factors = jnp.where(between[:, :, None], all_decay[None, :, :], 1.0)
-    reach = jnp.prod(factors, 1) * (index < position).astype(jnp.float32)[:, None]
-    entering = jnp.einsum(
-        "jh,jhq->hq",
-        reach,
-        all_state.reshape(seq_count, heads_here, head_dim * state_dim),
-        precision=lax.Precision.HIGHEST,
-    ).reshape(heads_here, head_dim, state_dim)
+    run_decay = through[tiles_dev - 1]
+    run_state = local_state[tiles_dev]
+    distance = 1
+    while distance < seq_count:
+        got_decay, got_state = shifted((run_decay, run_state), "seq", distance)
+        run_state = run_state + run_decay[:, None, None] * got_state
+        run_decay = jnp.where(position >= distance, run_decay * got_decay, run_decay)
+        distance *= 2
+    entering = shifted(run_state, "seq", 1)
     tile_state = before_tile + prefix[:, :, None, None] * entering[None]
     carried = tile_state.astype(jnp.bfloat16)
     inter = (

time: 392 us -> 346 us (0.88)
  the two profiles are of different devices: /device:TPU:0 before, /device:TPU:15 now
where the time goes in v1:
time: 346 us; the launch traced here: 340 us
  waiting for transfers between devices  86 us (25%)
  local copies, waits for them, and re-layouts  66.1 us (19%)
  matrix products  62 us (18%)
  starting transfers between devices  57.6 us (17%)
  other arithmetic  50.6 us (15%)
  between operations  14.3 us (4%)
    all_to_all x1, waiting for transfers between devices, shards(): lax.all_to_all(outgoing, 'seq', split_axis=0, concat_axis=0, tiled=True)  47.5 us
    ppermute x10, starting transfers between devices, shifted(): return lax.ppermute(x, axis, pairs)  44.5 us
    ppermute x10, waiting for transfers between devices, shifted(): return lax.ppermute(x, axis, pairs)  36.4 us
    unnamed x69, local copies, waits for them, and re-layouts  25.9 us
    dot_general x1, matrix products, shards(): jnp.einsum('cjh,jhq->chq', spans, flat_contrib, precision=lax.Precision.H...  18.9 us
    convert_element_type x1, other arithmetic, shards(): conv_out = jax.nn.silu(total).astype(jnp.bfloat16)  15.1 us
    dot_general x3, matrix products, shards(): jnp.dot(piece, weight, preferred_element_type=jnp.float32)  14.5 us
    add x1, local copies, waits for them, and re-layouts, shards(): intra + inter + d_skip[None, None, :, None] * x_heads.astype(jnp.float32)  9.92 us
  transfers between devices with their start and end apart: 13, of which 7 were waited for; matrix products, arithmetic and copies ran while one was open for 11% of the time, Pallas kernels for 0%

profile of v1, /device:TPU:15, one launch (start us, length us, event | category | flops | bytes accessed | tf_op | source)
XLA Modules:
  0.0 339.7 jit_solution(17381698858752543710)
XLA Ops:
  8.8 6.6 %all-to-all-start = ((bf16[16,1,1]{2,1,0:T(2,128)(2,1)}), bf16[16,1,1]{2,1,0:T(2,128)(2,1)S(1)}, u32[]{:S(2)}, u32[]{:S(2)}) async-start(bf16[16,1,1]{2,1,0:T(2,128)(2,1)} %copy.129), calls=%async_computation | async-start | bytes 16384 | tf_op jit(solution)/shard_map/all_to_all | solution.py:57
  19.3 6.5 %all-to-all-start.1 = ((bf16[16,128,512]{2,1,0:T(8,128)(2,1)}), bf16[16,128,512]{2,1,0:T(8,128)(2,1)S(1)}, u32[]{:S(2)}, u32[]{:S(2)}) async-start(bf16[16,128,512]{2,1,0:T(8,128)(2,1)} %copy.131), calls=%async_computation.1 | async-start | bytes 4194304 | tf_op jit(solution)/shard_map/all_to_all | solution.py:56
  26.0 47.5 %all-to-all-done.1 = bf16[16,128,512]{2,1,0:T(8,128)(2,1)S(1)} async-done(((bf16[16,128,512]{2,1,0:T(8,128)(2,1)}), bf16[16,128,512]{2,1,0:T(8,128)(2,1)S(1)}, u32[]{:S(2)}, u32[]{:S(2)}) %all-to-all-start.1) | async-done | bytes 2097184 | tf_op jit(solution)/shard_map/all_to_all | solution.py:56
  81.4 5.7 %copy.163 = bf16[128,8,2,1024]{3,1,2,0:T(8,128)(2,1)} copy(bf16[128,8,2,1024]{3,2,1,0:T(2,128)(2,1)} %bitcast.110) | data formatting | bytes 8388608
  91.8 12.0 %convolution_convert_fusion = bf16[2048,2048]{0,1:T(8,128)(2,1)S(1)} fusion(bf16[2048,1024]{1,0:T(8,128)(2,1)} %all-gather.2.cloned.1.call-done, bf16[1024,2048]{1,0:T(8,128)(2,1)} %bitcast.111), kind=kOutput, calls=%fused_computation.26 | convolution fusion | flops 8594128896 | bytes 16777216 | tf_op jit(solution)/shard_map/dot_general | solution.py:69
  104.2 4.9 %copy-done.8 = bf16[2048,1024]{1,0:T(8,128)(2,1)S(1)} copy-done((bf16[2048,1024]{1,0:T(8,128)(2,1)S(1)}, bf16[2048,1024]{1,0:T(8,128)(2,1)}, u32[]{:S(2)}) %copy-start.8) | copy-done | bytes 4194328
  121.9 8.8 %maximum_maximum_fusion = bf16[2051,1280]{0,1:T(8,128)(2,1)S(1)} fusion(bf16[2048,256]{0,1:T(8,128)(2,1)S(1)} %convolution_convert_fusion.1, bf16[2048,1024]{0,1:T(8,128)(2,1)} %copy-done.3, bf16[3,1280]{0,1:T(8,128)(2,1)} %collective-permute-done.1), kind=kLoop, calls=%fused_computation.29 | loop fusion | flops 15751680 | bytes 10501120 | tf_op jit(solution)/shard_map/concatenate | solution.py:84
  130.8 15.1 %multiply_convert_fusion.1 = bf16[2048,1280]{0,1:T(8,128)(2,1)S(1)} fusion(bf16[2048,256]{0,1:T(8,128)(2,1)S(1)} %convolution_convert_fusion.1, bf16[2051,1280]{0,1:T(8,128)(2,1)S(1)} %maximum_maximum_fusion, f32[1280]{0:T(1024)S(1)} %copy-done.14, f32[1280]{0:T(1024)S(1)} %copy-done.15, f32[1280]{0:T(1024)S(1)} %copy-done.16, f32[1280]{0:T(1024)S(1)} %copy-done.13, ...), kind=kLoop, calls=%fused_computation.6 | loop fusion | flops 60293120 | bytes 26246144 | tf_op jit(solution)/shard_map/convert_element_type | solution.py:97
  156.0 9.4 %reshape.283 = f32[16,16,8192]{2,1,0:T(8,128)} reshape(f32[16,16,64,128]{3,2,1,0:T(8,128)} %fusion.17) | data formatting | bytes 16777216 | tf_op jit(solution)/shard_map/reshape | solution.py:130
  165.4 18.9 %convolution_bitcast_fusion = f32[17,16,8192]{2,0,1:T(8,128)S(1)} fusion(f32[16,16,8192]{2,1,0:T(8,128)} %reshape.283, f32[17,16,16]{0,2,1:T(8,128)S(1)} %broadcast_multiply_fusion), kind=kOutput, calls=%fused_computation.1 | convolution fusion | flops 427819008 | bytes 17318912 | tf_op jit(solution)/shard_map/cjh,jhq->chq/dot_general | solution.py:131
  189.1 4.9 %collective-permute-start.2 = (f32[16,64,128]{2,1,0:T(8,128)S(1)}, f32[16,64,128]{2,1,0:T(8,128)}, u32[]{:S(2)}, u32[]{:S(2)}) collective-permute-start(f32[16,64,128]{2,1,0:T(8,128)S(1)} %bitcast.114), channel_id=1, source_target_pairs={{0,2},{2,4},{4,6},{6,8},{8,10},{10,12},{12,14},{14,16},{16,18},{18... | collective-permute-start | bytes 1572872 | tf_op jit(solution)/shard_map/ppermute | solution.py:15
  194.1 9.3 %collective-permute-done.2 = f32[16,64,128]{2,1,0:T(8,128)} collective-permute-done((f32[16,64,128]{2,1,0:T(8,128)S(1)}, f32[16,64,128]{2,1,0:T(8,128)}, u32[]{:S(2)}, u32[]{:S(2)}) %collective-permute-start.2) | collective-permute-done | bytes 524320 | tf_op jit(solution)/shard_map/ppermute | solution.py:15
  208.4 5.1 %collective-permute-start.3 = (f32[16]{0:T(128)S(1)}, f32[16]{0:T(128)S(1)}, u32[]{:S(2)}, u32[]{:S(2)}) collective-permute-start(f32[16]{0:T(128)S(1)} %slice_bitcast_fusion.6), channel_id=1, source_target_pairs={{0,2},{2,4},{4,6},{6,8},{8,10},{10,12},{12,14},{14,16},{16,18},{18... | collective-permute-start | bytes 200 | tf_op jit(solution)/shard_map/ppermute | solution.py:15
  218.6 5.3 %collective-permute-start.6 = (f32[16,64,128]{2,1,0:T(8,128)S(1)}, f32[16,64,128]{2,1,0:T(8,128)}, u32[]{:S(2)}, u32[]{:S(2)}) collective-permute-start(f32[16,64,128]{2,1,0:T(8,128)S(1)} %multiply_add_fusion.2), channel_id=1, source_target_pairs={{0,8},{2,10},{4,12},{6,14},{8,16},{10,18},{12,20},{14,22},{16,24},... | collective-permute-start | bytes 1572872 | tf_op jit(solution)/shard_map/ppermute | solution.py:15
  233.5 5.1 %collective-permute-start.8 = (f32[16,64,128]{2,1,0:T(8,128)S(1)}, f32[16,64,128]{2,1,0:T(8,128)}, u32[]{:S(2)}, u32[]{:S(2)}) collective-permute-start(f32[16,64,128]{2,1,0:T(8,128)S(1)} %multiply_add_fusion.1), channel_id=1, source_target_pairs={{0,16},{2,18},{4,20},{6,22},{8,24},{10,26},{12,28},{14,30},{1,17},... | collective-permute-start | bytes 1572872 | tf_op jit(solution)/shard_map/ppermute | solution.py:15
  241.7 18.1 %collective-permute-done.7 = f32[16]{0:T(128)S(1)} collective-permute-done((f32[16]{0:T(128)S(1)}, f32[16]{0:T(128)S(1)}, u32[]{:S(2)}, u32[]{:S(2)}) %collective-permute-start.7) | collective-permute-done | bytes 96 | tf_op jit(solution)/shard_map/ppermute | solution.py:15
  262.5 8.1 %collective-permute-start.9 = (f32[16,64,128]{2,1,0:T(8,128)S(1)}, f32[16,64,128]{2,1,0:T(8,128)S(1)}, u32[]{:S(2)}, u32[]{:S(2)}) collective-permute-start(f32[16,64,128]{2,1,0:T(8,128)S(1)} %multiply_add_fusion), channel_id=1, source_target_pairs={{0,2},{2,4},{4,6},{6,8},{8,10},{10,12},{12,14},{14,16},{16,18},{18... | collective-permute-start | bytes 1572872 | tf_op jit(solution)/shard_map/ppermute | solution.py:15
  270.6 9.7 %fusion = f32[16,16,64,128]{3,2,1,0:T(8,128)} fusion(f32[16,16,128]{2,1,0:T(8,128)S(1)} %copy.140, f32[16,16,128]{2,1,0:T(8,128)S(1)} %copy.138, f32[16,128,128]{2,1,0:T(8,128)S(1)} %fusion.41, pred[16,128,128]{2,1,0:T(8,128)(4,1)S(1)} %compare_and_fusion, bf16[16,128,16,64]{1,0,3,2:T(8,128)(2,1)} %bitcast.104), kind=kOutput, calls=%fused_computation.7 | convolution fusion | flops 562036736 | bytes 14155776 | tf_op jit(solution)/shard_map/jhis,jshp->jihp/dot_general | solution.py:115
  283.7 4.9 %copy.168 = f32[32,8,64,128]{3,2,1,0:T(8,128)} copy(f32[32,8,64,128]{3,1,2,0:T(8,128)S(1)} %bitcast.102) | data formatting | bytes 16777216
  288.7 9.4 %fusion.2 = f32[16,128,16,64]{1,3,2,0:T(8,128)} fusion(f32[16,16,64,128]{3,2,1,0:T(8,128)} %fusion, f32[16]{0:T(128)S(1)} %copy-done.27, f32[16,128,16]{1,2,0:T(8,128)S(1)} %copy.143, bf16[16,128,16,64]{1,0,3,2:T(8,128)(2,1)S(1)} %bitcast.105, f32[16,16,64,128]{3,2,0,1:T(8,128)} %bitcast.106, f32[16,64,128]{2,1,0:T(8,128)S(1)} %collective-permute-done.9, ...), kind=kOutput, calls=%fused_computation.9 | convolution fusion | flops 553648128 | bytes 30540864 | tf_op jit(solution)/shard_map/jin,jhpn->jihp/dot_general | solution.py:152
  298.1 9.9 %copy.153 = f32[16,128,16,64]{1,0,3,2:T(8,128)S(1)} copy(f32[16,128,16,64]{1,3,2,0:T(8,128)} %fusion.2) | data formatting | bytes 16777216 | tf_op jit(solution)/shard_map/add | solution.py:154
  308.0 8.7 %multiply_reduce_fusion = (f32[2048]{0:T(1024)S(1)}, f32[2048,1024]{0,1:T(8,128)}) fusion(bf16[2048,2048]{0,1:T(8,128)(2,1)} %copy-done.7, f32[128,8,16,128]{3,2,1,0:T(8,128)S(1)} %bitcast.107), kind=kLoop, calls=%fused_computation.19 | loop fusion | flops 16775168 | bytes 20979712 | tf_op jit(solution)/shard_map/reduce_sum | solution.py:156
  319.9 6.3 %multiply_convert_fusion.3 = bf16[2048,1024]{0,1:T(8,128)(2,1)} fusion(f32[2048,1024]{0,1:T(8,128)} %get-tuple-element.10, f32[1024]{0:T(1024)S(1)} %copy-done.22, f32[2048]{0:T(1024)S(1)} %add_rsqrt_fusion), kind=kLoop, calls=%fused_computation.18 | loop fusion | flops 6291456 | bytes 12595200 | tf_op jit(solution)/shard_map/convert_element_type | solution.py:157
  326.2 6.4 %copy.154 = bf16[2048,1024]{1,0:T(8,128)(2,1)} copy(bf16[2048,1024]{0,1:T(8,128)(2,1)} %multiply_convert_fusion.3) | data formatting | bytes 8388608 | tf_op jit(solution)/shard_map/convert_element_type | solution.py:157
  (148 shorter events, 78.9 us)
Async XLA Ops:
  8.8 10.4 %all-to-all-start = ((bf16[16,1,1]{2,1,0:T(2,128)(2,1)}), bf16[16,1,1]{2,1,0:T(2,128)(2,1)S(1)}, u32[]{:S(2)}, u32[]{:S(2)}) async-start(bf16[16,1,1]{2,1,0:T(2,128)(2,1)} %copy.129), calls=%async_computation | async-start | bytes 16384 | tf_op jit(solution)/shard_map/all_to_all | solution.py:57
  19.3 58.2 %copy-start.18 = (s32[16]{0:T(128)S(1)}, s32[16]{0:T(128)}, u32[]{:S(2)}) copy-start(s32[16]{0:T(128)} %param.16) | copy-start | bytes 196
  19.3 54.2 %all-to-all-start.1 = ((bf16[16,128,512]{2,1,0:T(8,128)(2,1)}), bf16[16,128,512]{2,1,0:T(8,128)(2,1)S(1)}, u32[]{:S(2)}, u32[]{:S(2)}) async-start(bf16[16,128,512]{2,1,0:T(8,128)(2,1)} %copy.131), calls=%async_computation.1 | async-start | bytes 4194304 | tf_op jit(solution)/shard_map/all_to_all | solution.py:56
  25.8 66.1 %all-gather.2.cloned.1.call-start = ((), (), s32[]{:S(2)}) async-start(), calls=%async_computation.2 | async-start | bytes 6291456 | tf_op jit(solution)/shard_map/all_gather | solution.py:67
  74.8 12.8 %copy-start.17 = (f32[4,1024]{1,0:T(4,128)S(1)}, f32[4,1024]{1,0:T(4,128)}, u32[]{:S(2)}) copy-start(f32[4,1024]{1,0:T(4,128)} %param.22) | copy-start | bytes 49156
  74.8 12.8 %copy-start.23 = (f32[4,256]{1,0:T(4,128)S(1)}, f32[4,256]{1,0:T(4,128)}, u32[]{:S(2)}) copy-start(f32[4,256]{1,0:T(4,128)} %param.23) | copy-start | bytes 12292
  74.9 12.8 %copy-start.24 = (f32[1024]{0:T(1024)S(1)}, f32[1024]{0:T(1024)}, u32[]{:S(2)}) copy-start(f32[1024]{0:T(1024)} %param.24) | copy-start | bytes 12292
  74.9 12.8 %copy-start.26 = (f32[256]{0:T(256)S(1)}, f32[256]{0:T(256)}, u32[]{:S(2)}) copy-start(f32[256]{0:T(256)} %param.25) | copy-start | bytes 3076
  74.9 14.1 %copy-start.29 = (f32[16]{0:T(128)S(1)}, f32[16]{0:T(128)}, u32[]{:S(2)}) copy-start(f32[16]{0:T(128)} %param.21) | copy-start | bytes 196
  79.1 10.0 %collective-permute-start = (bf16[3]{0:T(256)(128)(2,1)S(1)}, bf16[3]{0:T(256)(128)(2,1)S(1)}, u32[]{:S(2)}, u32[]{:S(2)}) collective-permute-start(bf16[3]{0:T(256)(128)(2,1)S(1)} %fusion.72), channel_id=1, source_target_pairs={{0,2},{2,4},{4,6},{6,8},{8,10},{10,12},{12,14},{14,16},{16,18},{18... | collective-permute-start | bytes 26 | tf_op jit(solution)/shard_map/ppermute | solution.py:15
  111.4 10.4 %collective-permute-start.1 = (bf16[3,1280]{0,1:T(8,128)(2,1)}, bf16[3,1280]{0,1:T(8,128)(2,1)}, u32[]{:S(2)}, u32[]{:S(2)}) collective-permute-start(bf16[3,1280]{0,1:T(8,128)(2,1)} %fusion.49), channel_id=1, source_target_pairs={{0,2},{2,4},{4,6},{6,8},{8,10},{10,12},{12,14},{14,16},{16,18},{18... | collective-permute-start | bytes 23048 | tf_op jit(solution)/shard_map/ppermute | solution.py:15
  118.9 11.8 %copy-start.16 = (f32[1280]{0:T(1024)S(1)}, f32[1280]{0:T(1024)}, u32[]{:S(2)}) copy-start(f32[1280]{0:T(1024)} %get-tuple-element.8) | copy-start | bytes 15364
  118.9 11.8 %copy-start.19 = (pred[2048]{0:T(1024)(128)(4,1)S(1)}, pred[2048]{0:T(1024)(128)(4,1)}, u32[]{:S(2)}) copy-start(pred[2048]{0:T(1024)(128)(4,1)} %get-tuple-element.17) | copy-start | bytes 6148
  165.4 74.0 %copy-start.9 = (f32[16,128,16]{2,0,1:T(8,128)S(1)}, f32[16,128,16]{2,0,1:T(8,128)}, u32[]{:S(2)}) copy-start(f32[16,128,16]{2,0,1:T(8,128)} %get-tuple-element.16) | copy-start | bytes 393220
  189.1 14.3 %collective-permute-start.2 = (f32[16,64,128]{2,1,0:T(8,128)S(1)}, f32[16,64,128]{2,1,0:T(8,128)}, u32[]{:S(2)}, u32[]{:S(2)}) collective-permute-start(f32[16,64,128]{2,1,0:T(8,128)S(1)} %bitcast.114), channel_id=1, source_target_pairs={{0,2},{2,4},{4,6},{6,8},{8,10},{10,12},{12,14},{14,16},{16,18},{18... | collective-permute-start | bytes 1572872 | tf_op jit(solution)/shard_map/ppermute | solution.py:15
  204.6 12.8 %collective-permute-start.4 = (f32[16,64,128]{2,1,0:T(8,128)S(1)}, f32[16,64,128]{2,1,0:T(8,128)}, u32[]{:S(2)}, u32[]{:S(2)}) collective-permute-start(f32[16,64,128]{2,1,0:T(8,128)S(1)} %multiply_add_fusion.3), channel_id=1, source_target_pairs={{0,4},{2,6},{4,8},{6,10},{8,12},{10,14},{12,16},{14,18},{16,20},{1... | collective-permute-start | bytes 1572872 | tf_op jit(solution)/shard_map/ppermute | solution.py:15
  208.4 9.0 %collective-permute-start.3 = (f32[16]{0:T(128)S(1)}, f32[16]{0:T(128)S(1)}, u32[]{:S(2)}, u32[]{:S(2)}) collective-permute-start(f32[16]{0:T(128)S(1)} %slice_bitcast_fusion.6), channel_id=1, source_target_pairs={{0,2},{2,4},{4,6},{6,8},{8,10},{10,12},{12,14},{14,16},{16,18},{18... | collective-permute-start | bytes 200 | tf_op jit(solution)/shard_map/ppermute | solution.py:15
  218.6 13.7 %collective-permute-start.6 = (f32[16,64,128]{2,1,0:T(8,128)S(1)}, f32[16,64,128]{2,1,0:T(8,128)}, u32[]{:S(2)}, u32[]{:S(2)}) collective-permute-start(f32[16,64,128]{2,1,0:T(8,128)S(1)} %multiply_add_fusion.2), channel_id=1, source_target_pairs={{0,8},{2,10},{4,12},{6,14},{8,16},{10,18},{12,20},{14,22},{16,24},... | collective-permute-start | bytes 1572872 | tf_op jit(solution)/shard_map/ppermute | solution.py:15
  224.0 8.4 %collective-permute-start.5 = (f32[16]{0:T(128)S(1)}, f32[16]{0:T(128)S(1)}, u32[]{:S(2)}, u32[]{:S(2)}) collective-permute-start(f32[16]{0:T(128)S(1)} %broadcast_select_fusion.2), channel_id=1, source_target_pairs={{0,4},{2,6},{4,8},{6,10},{8,12},{10,14},{12,16},{14,18},{16,20},{1... | collective-permute-start | bytes 200 | tf_op jit(solution)/shard_map/ppermute | solution.py:15
  233.5 27.8 %collective-permute-start.8 = (f32[16,64,128]{2,1,0:T(8,128)S(1)}, f32[16,64,128]{2,1,0:T(8,128)}, u32[]{:S(2)}, u32[]{:S(2)}) collective-permute-start(f32[16,64,128]{2,1,0:T(8,128)S(1)} %multiply_add_fusion.1), channel_id=1, source_target_pairs={{0,16},{2,18},{4,20},{6,22},{8,24},{10,26},{12,28},{14,30},{1,17},... | collective-permute-start | bytes 1572872 | tf_op jit(solution)/shard_map/ppermute | solution.py:15
  239.8 20.0 %collective-permute-start.7 = (f32[16]{0:T(128)S(1)}, f32[16]{0:T(128)S(1)}, u32[]{:S(2)}, u32[]{:S(2)}) collective-permute-start(f32[16]{0:T(128)S(1)} %broadcast_select_fusion.1), channel_id=1, source_target_pairs={{0,8},{2,10},{4,12},{6,14},{8,16},{10,18},{12,20},{14,22},{16,24},... | collective-permute-start | bytes 200 | tf_op jit(solution)/shard_map/ppermute | solution.py:15
  262.5 26.2 %collective-permute-start.9 = (f32[16,64,128]{2,1,0:T(8,128)S(1)}, f32[16,64,128]{2,1,0:T(8,128)S(1)}, u32[]{:S(2)}, u32[]{:S(2)}) collective-permute-start(f32[16,64,128]{2,1,0:T(8,128)S(1)} %multiply_add_fusion), channel_id=1, source_target_pairs={{0,2},{2,4},{4,6},{6,8},{8,10},{10,12},{12,14},{14,16},{16,18},{18... | collective-permute-start | bytes 1572872 | tf_op jit(solution)/shard_map/ppermute | solution.py:15
  308.0 11.9 %copy-start.22 = (f32[1024]{0:T(1024)S(1)}, f32[1024]{0:T(1024)}, u32[]{:S(2)}) copy-start(f32[1024]{0:T(1024)} %param.27) | copy-start | bytes 12292
  319.9 12.7 %copy-start.1 = (bf16[16,128,512]{2,1,0:T(8,128)(2,1)S(1)}, bf16[16,128,512]{2,1,0:T(8,128)(2,1)}, u32[]{:S(2)}) copy-start(bf16[16,128,512]{2,1,0:T(8,128)(2,1)} %param.14) | copy-start | bytes 6291460
  (20 other events, 145.6 us)
Sparse Core Ops, SparseCore 0:
  77.6 14.2 all-gather.1

commit v2 on v1

--- a/solution.py
+++ b/solution.py
@@ -119,24 +119,22 @@
     scaled = (x_heads.astype(jnp.float32) * to_end[:, :, :, None]).astype(jnp.bfloat16)
     contrib = jnp.einsum("jshp,jsn->jhpn", scaled, b_part, preferred_element_type=jnp.float32)
     passing = jnp.exp(cumul[:, tile_len - 1, :]) * (1.0 - has_bound)[:, None]
-    tile_ids = jnp.arange(tiles_dev + 1, dtype=jnp.int32)
-    src_ids = jnp.arange(tiles_dev, dtype=jnp.int32)
-    between_tiles = (src_ids[None, :, None] < src_ids[None, None, :]) & (
-        src_ids[None, None, :] < tile_ids[:, None, None]
-    )
-    spans = jnp.prod(
-        jnp.where(between_tiles[:, :, :, None], passing[None, None, :, :], 1.0), 2
-    ) * (src_ids[None, :] < tile_ids[:, None]).astype(jnp.float32)[:, :, None]
     flat_contrib = contrib.reshape(tiles_dev, heads_here, head_dim * state_dim)
-    local_state = jnp.einsum(
-        "cjh,jhq->chq", spans, flat_contrib, precision=lax.Precision.HIGHEST
-    ).reshape(tiles_dev + 1, heads_here, head_dim, state_dim)
-    before_tile = local_state[:tiles_dev]
     through = jnp.cumprod(passing, 0)
     prefix = jnp.concatenate([jnp.ones((1, heads_here), jnp.float32), through[:-1]], 0)
+    reverse = jnp.cumprod(passing[::-1], 0)[::-1]
+    to_last = jnp.concatenate([reverse[1:], jnp.ones((1, heads_here), jnp.float32)], 0)
+    run_state = jnp.sum(to_last[:, :, None] * flat_contrib, 0).reshape(
+        heads_here, head_dim, state_dim
+    )
+    running = jnp.zeros((heads_here, head_dim * state_dim), jnp.float32)
+    states = []
+    for tile in range(tiles_dev):
+        states.append(running)
+        running = passing[tile][:, None] * running + flat_contrib[tile]
+    before_tile = jnp.stack(states).reshape(tiles_dev, heads_here, head_dim, state_dim)
     position = lax.axis_index("seq")
     run_decay = through[tiles_dev - 1]
-    run_state = local_state[tiles_dev]
     distance = 1
     while distance < seq_count:
         got_decay, got_state = shifted((run_decay, run_state), "seq", distance)

time: 346 us -> 302 us (0.87)
  the two profiles are of different devices: /device:TPU:15 before, /device:TPU:29 now
where the time goes in v2:
time: 302 us; the launch traced here: 297 us
  waiting for transfers between devices  115 us (38%)
  other arithmetic  48.7 us (16%)
  local copies, waits for them, and re-layouts  42.3 us (14%)
  matrix products  40.5 us (13%)
  starting transfers between devices  31.2 us (10%)
  between operations  14.9 us (5%)
  blocking collectives  3.76 us (1%)
    ppermute x10, waiting for transfers between devices, shifted(): return lax.ppermute(x, axis, pairs)  67 us
    all_to_all x1, waiting for transfers between devices, shards(): lax.all_to_all(outgoing, 'seq', split_axis=0, concat_axis=0, tiled=True)  45 us
    ppermute x10, starting transfers between devices, shifted(): return lax.ppermute(x, axis, pairs)  18.2 us
    dot_general x3, matrix products, shards(): jnp.dot(piece, weight, preferred_element_type=jnp.float32)  16.7 us
    convert_element_type x1, other arithmetic, shards(): conv_out = jax.nn.silu(total).astype(jnp.bfloat16)  15.1 us
    unnamed x101, local copies, waits for them, and re-layouts  14.1 us
    add x1, local copies, waits for them, and re-layouts, shards(): intra + inter + d_skip[None, None, :, None] * x_heads.astype(jnp.float32)  9.82 us
    dot_general x1, matrix products, shards(): jnp.einsum('jhis,jshp->jihp', weights, x_heads, preferred_element_type=jn...  9.58 us
  transfers between devices with their start and end apart: 13, of which 9 were waited for; matrix products, arithmetic and copies ran while one was open for 11% of the time, Pallas kernels for 0%

profile of v2, /device:TPU:29, one launch (start us, length us, event | category | flops | bytes accessed | tf_op | source)
XLA Modules:
  0.0 296.7 jit_solution(11866421167262159055)
XLA Ops:
  8.8 6.4 %all-to-all-start = ((bf16[16,1,1]{2,1,0:T(2,128)(2,1)}), bf16[16,1,1]{2,1,0:T(2,128)(2,1)S(1)}, u32[]{:S(2)}, u32[]{:S(2)}) async-start(bf16[16,1,1]{2,1,0:T(2,128)(2,1)} %copy.91), calls=%async_computation | async-start | bytes 16384 | tf_op jit(solution)/shard_map/all_to_all | solution.py:57
  19.1 6.5 %all-to-all-start.1 = ((bf16[16,128,512]{2,1,0:T(8,128)(2,1)}), bf16[16,128,512]{2,1,0:T(8,128)(2,1)S(1)}, u32[]{:S(2)}, u32[]{:S(2)}) async-start(bf16[16,128,512]{2,1,0:T(8,128)(2,1)} %copy.93), calls=%async_computation.1 | async-start | bytes 4194304 | tf_op jit(solution)/shard_map/all_to_all | solution.py:56
  25.8 45.0 %all-to-all-done.1 = bf16[16,128,512]{2,1,0:T(8,128)(2,1)S(1)} async-done(((bf16[16,128,512]{2,1,0:T(8,128)(2,1)}), bf16[16,128,512]{2,1,0:T(8,128)(2,1)S(1)}, u32[]{:S(2)}, u32[]{:S(2)}) %all-to-all-start.1) | async-done | bytes 2097184 | tf_op jit(solution)/shard_map/all_to_all | solution.py:56
  78.8 5.6 %copy.122 = bf16[128,8,2,1024]{3,1,2,0:T(8,128)(2,1)} copy(bf16[128,8,2,1024]{3,2,1,0:T(2,128)(2,1)} %bitcast.130) | data formatting | bytes 8388608
  88.4 3.3 %all-gather.2.cloned.1.call-done = bf16[2048,1024]{1,0:T(8,128)(2,1)} async-done(((bf16[2048,512]{1,0:T(8,128)(2,1)}), bf16[2048,1024]{1,0:T(8,128)(2,1)}) %all-gather.2.cloned.1.call-update) | async-done | bytes 4194320 | tf_op jit(solution)/shard_map/all_gather | solution.py:67
  91.7 3.4 %fusion.47 = f32[2,8,16,128]{3,1,2,0:T(8,128)S(1)} fusion(bf16[2048,1024]{1,0:T(8,128)(2,1)} %all-gather.2.cloned.1.call-done, bf16[1024,16]{0,1:T(8,128)(2,1)S(1)} %copy-done.8, f32[16]{0:T(128)S(1)} %copy-done.29), kind=kOutput, calls=%fused_computation.90 | convolution fusion | flops 67338240 | bytes 4358208 | tf_op jit(solution)/shard_map/dot_general | solution.py:69
  96.6 12.0 %convolution_convert_fusion = bf16[2048,2048]{0,1:T(8,128)(2,1)S(1)} fusion(bf16[2048,1024]{1,0:T(8,128)(2,1)} %all-gather.2.cloned.1.call-done, bf16[1024,2048]{1,0:T(8,128)(2,1)} %bitcast.131), kind=kOutput, calls=%fused_computation.24 | convolution fusion | flops 8594128896 | bytes 16777216 | tf_op jit(solution)/shard_map/dot_general | solution.py:69
  108.9 4.9 %copy-done.6 = bf16[2048,1024]{1,0:T(8,128)(2,1)S(1)} copy-done((bf16[2048,1024]{1,0:T(8,128)(2,1)S(1)}, bf16[2048,1024]{1,0:T(8,128)(2,1)}, u32[]{:S(2)}) %copy-start.6) | copy-done | bytes 4194328
  125.1 3.3 %collective-permute-done.3 = f32[16]{0:T(128)S(1)} collective-permute-done((f32[16]{0:T(128)S(1)}, f32[16]{0:T(128)S(1)}, u32[]{:S(2)}, u32[]{:S(2)}) %collective-permute-start.3) | collective-permute-done | bytes 96 | tf_op jit(solution)/shard_map/ppermute | solution.py:15
  134.2 3.2 %collective-permute-done.7 = f32[16]{0:T(128)S(1)} collective-permute-done((f32[16]{0:T(128)S(1)}, f32[16]{0:T(128)S(1)}, u32[]{:S(2)}, u32[]{:S(2)}) %collective-permute-start.7) | collective-permute-done | bytes 96 | tf_op jit(solution)/shard_map/ppermute | solution.py:15
  137.4 8.8 %maximum_maximum_fusion = bf16[2051,1280]{0,1:T(8,128)(2,1)S(1)} fusion(bf16[2048,256]{0,1:T(8,128)(2,1)S(1)} %convolution_convert_fusion.1, bf16[2048,1024]{0,1:T(8,128)(2,1)} %copy-done.2, bf16[3,1280]{0,1:T(8,128)(2,1)} %collective-permute-done.1), kind=kLoop, calls=%fused_computation.27 | loop fusion | flops 15751680 | bytes 10501120 | tf_op jit(solution)/shard_map/concatenate | solution.py:84
  146.2 15.1 %multiply_convert_fusion.1 = bf16[2048,1280]{0,1:T(8,128)(2,1)S(1)} fusion(bf16[2048,256]{0,1:T(8,128)(2,1)S(1)} %convolution_convert_fusion.1, bf16[2051,1280]{0,1:T(8,128)(2,1)S(1)} %maximum_maximum_fusion, f32[1280]{0:T(1024)S(1)} %copy-done.9, f32[1280]{0:T(1024)S(1)} %copy-done.10, f32[1280]{0:T(1024)S(1)} %copy-done.11, f32[1280]{0:T(1024)S(1)} %get-tuple-element.5, ...), kind=kLoop, calls=%fused_computation.5 | loop fusion | flops 60293120 | bytes 26246144 | tf_op jit(solution)/shard_map/convert_element_type | solution.py:97
  163.7 3.1 %multiply_reduce_fusion.1 = (f32[16,64,128]{2,1,0:T(8,128)S(1)}, f32[16,16,64,128]{3,2,1,0:T(8,128)S(1)}) fusion(f32[16,16]{1,0:T(8,128)S(1)} %concatenate.28, bf16[16,128,128,1]{1,0,2,3:T(8,128)(2,1)S(1)} %bitcast.133, f32[16,128,16]{1,2,0:T(8,128)S(1)} %copy.109, bf16[16,128,16,64]{1,0,3,2:T(8,128)(2,1)S(1)} %bitcast.122), kind=kOutput, calls=%fused_computation.17 | convolution fusion | flops 547225600 | bytes 13763584 | tf_op jit(solution)/shard_map/jshp,jsn->jhpn/dot_general | solution.py:120
  170.2 9.6 %fusion = f32[16,16,64,128]{3,2,1,0:T(8,128)} fusion(f32[16,16,128]{2,1,0:T(8,128)S(1)} %copy.102, f32[16,16,128]{2,1,0:T(8,128)S(1)} %copy.100, f32[16,128,128]{2,1,0:T(8,128)S(1)} %fusion.36, pred[16,128,128]{2,1,0:T(8,128)(4,1)S(1)} %copy-done.7, bf16[16,128,16,64]{1,0,3,2:T(8,128)(2,1)S(1)} %bitcast.123), kind=kOutput, calls=%fused_computation.6 | convolution fusion | flops 562036736 | bytes 14155776 | tf_op jit(solution)/shard_map/jhis,jshp->jihp/dot_general | solution.py:115
  182.0 9.4 %collective-permute-done.4 = f32[16,64,128]{2,1,0:T(8,128)S(1)} collective-permute-done((f32[16,64,128]{2,1,0:T(8,128)S(1)}, f32[16,64,128]{2,1,0:T(8,128)S(1)}, u32[]{:S(2)}, u32[]{:S(2)}) %collective-permute-start.4) | collective-permute-done | bytes 524320 | tf_op jit(solution)/shard_map/ppermute | solution.py:15
  193.2 11.1 %collective-permute-done.6 = f32[16,64,128]{2,1,0:T(8,128)S(1)} collective-permute-done((f32[16,64,128]{2,1,0:T(8,128)S(1)}, f32[16,64,128]{2,1,0:T(8,128)S(1)}, u32[]{:S(2)}, u32[]{:S(2)}) %collective-permute-start.6) | collective-permute-done | bytes 524320 | tf_op jit(solution)/shard_map/ppermute | solution.py:15
  206.1 25.8 %collective-permute-done.8 = f32[16,64,128]{2,1,0:T(8,128)S(1)} collective-permute-done((f32[16,64,128]{2,1,0:T(8,128)S(1)}, f32[16,64,128]{2,1,0:T(8,128)S(1)}, u32[]{:S(2)}, u32[]{:S(2)}) %collective-permute-start.8) | collective-permute-done | bytes 524320 | tf_op jit(solution)/shard_map/ppermute | solution.py:15
  234.6 12.9 %collective-permute-done.9 = f32[16,64,128]{2,1,0:T(8,128)S(1)} collective-permute-done((f32[16,64,128]{2,1,0:T(8,128)S(1)}, f32[16,64,128]{2,1,0:T(8,128)S(1)}, u32[]{:S(2)}, u32[]{:S(2)}) %collective-permute-start.9) | collective-permute-done | bytes 524320 | tf_op jit(solution)/shard_map/ppermute | solution.py:15
  247.5 7.3 %fusion.2 = f32[16,128,16,64]{1,3,2,0:T(8,128)S(1)} fusion(f32[16,16,64,128]{3,2,1,0:T(8,128)} %fusion, f32[16]{0:T(128)S(1)} %copy-done.39, f32[16,128,16]{1,2,0:T(8,128)S(1)} %copy.105, bf16[16,128,16,64]{1,0,3,2:T(8,128)(2,1)S(1)} %bitcast.124, f32[16,16,64,128]{3,2,1,0:T(8,128)} %copy-done.4, f32[16,64,128]{2,1,0:T(8,128)S(1)} %collective-permute-done.9, ...), kind=kOutput, calls=%fused_computation.8 | convolution fusion | flops 553648128 | bytes 30540864 | tf_op jit(solution)/shard_map/jin,jhpn->jihp/dot_general | solution.py:150
  254.8 9.8 %copy.112 = f32[16,128,16,64]{1,0,3,2:T(8,128)} copy(f32[16,128,16,64]{1,3,2,0:T(8,128)S(1)} %fusion.2) | data formatting | bytes 16777216 | tf_op jit(solution)/shard_map/add | solution.py:152
  264.7 8.3 %multiply_reduce_fusion = (f32[2048]{0:T(1024)S(1)}, f32[2048,1024]{0,1:T(8,128)}) fusion(bf16[2048,2048]{0,1:T(8,128)(2,1)} %copy-done.5, f32[128,8,16,128]{3,2,1,0:T(8,128)} %bitcast.125), kind=kLoop, calls=%fused_computation.15 | loop fusion | flops 16775168 | bytes 20979712 | tf_op jit(solution)/shard_map/reduce_sum | solution.py:154
  272.9 3.8 %psum.7 = f32[2048]{0:T(1024)S(1)} all-reduce(f32[2048]{0:T(1024)S(1)} %get-tuple-element.9), channel_id=1, replica_groups=mesh['seq'=16,'head'=2] {'head'}, use_global_device_ids=true, to_apply=%region_6.7 | all-reduce | flops 2048 | bytes 16384 | tf_op jit(solution)/shard_map/psum | solution.py:154
  276.7 6.3 %multiply_convert_fusion.3 = bf16[2048,1024]{0,1:T(8,128)(2,1)} fusion(f32[2048,1024]{0,1:T(8,128)} %get-tuple-element.10, f32[1024]{0:T(1024)S(1)} %copy-done.26, f32[2048]{0:T(1024)S(1)} %add_rsqrt_fusion), kind=kLoop, calls=%fused_computation.14 | loop fusion | flops 6291456 | bytes 12595200 | tf_op jit(solution)/shard_map/convert_element_type | solution.py:155
  283.0 6.4 %copy.113 = bf16[2048,1024]{1,0:T(8,128)(2,1)} copy(bf16[2048,1024]{0,1:T(8,128)(2,1)} %multiply_convert_fusion.3) | data formatting | bytes 8388608 | tf_op jit(solution)/shard_map/convert_element_type | solution.py:155
  (190 shorter events, 50.7 us)
Async XLA Ops:
  8.8 10.2 %all-to-all-start = ((bf16[16,1,1]{2,1,0:T(2,128)(2,1)}), bf16[16,1,1]{2,1,0:T(2,128)(2,1)S(1)}, u32[]{:S(2)}, u32[]{:S(2)}) async-start(bf16[16,1,1]{2,1,0:T(2,128)(2,1)} %copy.91), calls=%async_computation | async-start | bytes 16384 | tf_op jit(solution)/shard_map/all_to_all | solution.py:57
  19.0 55.7 %copy-start.13 = (s32[16]{0:T(128)S(1)}, s32[16]{0:T(128)}, u32[]{:S(2)}) copy-start(s32[16]{0:T(128)} %param.16) | copy-start | bytes 196
  19.1 51.7 %all-to-all-start.1 = ((bf16[16,128,512]{2,1,0:T(8,128)(2,1)}), bf16[16,128,512]{2,1,0:T(8,128)(2,1)S(1)}, u32[]{:S(2)}, u32[]{:S(2)}) async-start(bf16[16,128,512]{2,1,0:T(8,128)(2,1)} %copy.93), calls=%async_computation.1 | async-start | bytes 4194304 | tf_op jit(solution)/shard_map/all_to_all | solution.py:56
  25.5 66.2 %all-gather.2.cloned.1.call-start = ((), (), s32[]{:S(2)}) async-start(), calls=%async_computation.2 | async-start | bytes 6291456 | tf_op jit(solution)/shard_map/all_gather | solution.py:67
  76.4 11.3 %collective-permute-start = (bf16[3]{0:T(256)(128)(2,1)S(1)}, bf16[3]{0:T(256)(128)(2,1)S(1)}, u32[]{:S(2)}, u32[]{:S(2)}) collective-permute-start(bf16[3]{0:T(256)(128)(2,1)S(1)} %fusion.74), channel_id=1, source_target_pairs={{0,2},{2,4},{4,6},{6,8},{8,10},{10,12},{12,14},{14,16},{16,18},{18... | collective-permute-start | bytes 26 | tf_op jit(solution)/shard_map/ppermute | solution.py:15
  116.1 21.3 %collective-permute-start.1 = (bf16[3,1280]{0,1:T(8,128)(2,1)}, bf16[3,1280]{0,1:T(8,128)(2,1)}, u32[]{:S(2)}, u32[]{:S(2)}) collective-permute-start(bf16[3,1280]{0,1:T(8,128)(2,1)} %fusion.46), channel_id=1, source_target_pairs={{0,2},{2,4},{4,6},{6,8},{8,10},{10,12},{12,14},{14,16},{16,18},{18... | collective-permute-start | bytes 23048 | tf_op jit(solution)/shard_map/ppermute | solution.py:15
  121.0 25.2 %copy-start.11 = (f32[1280]{0:T(1024)S(1)}, f32[1280]{0:T(1024)}, u32[]{:S(2)}) copy-start(f32[1280]{0:T(1024)} %get-tuple-element.8) | copy-start | bytes 15364
  121.0 25.2 %copy-start.14 = (pred[2048]{0:T(1024)(128)(4,1)S(1)}, pred[2048]{0:T(1024)(128)(4,1)}, u32[]{:S(2)}) copy-start(pred[2048]{0:T(1024)(128)(4,1)} %get-tuple-element.31) | copy-start | bytes 6148
  121.0 25.2 %copy-start.15 = (pred[2048]{0:T(1024)(128)(4,1)S(1)}, pred[2048]{0:T(1024)(128)(4,1)}, u32[]{:S(2)}) copy-start(pred[2048]{0:T(1024)(128)(4,1)} %get-tuple-element.32) | copy-start | bytes 6148
  121.0 25.2 %copy-start.16 = (pred[2048]{0:T(1024)(128)(4,1)S(1)}, pred[2048]{0:T(1024)(128)(4,1)}, u32[]{:S(2)}) copy-start(pred[2048]{0:T(1024)(128)(4,1)} %get-tuple-element.33) | copy-start | bytes 6148
  122.7 5.7 %collective-permute-start.3 = (f32[16]{0:T(128)S(1)}, f32[16]{0:T(128)S(1)}, u32[]{:S(2)}, u32[]{:S(2)}) collective-permute-start(f32[16]{0:T(128)S(1)} %slice_bitcast_fusion.6), channel_id=1, source_target_pairs={{0,2},{2,4},{4,6},{6,8},{8,10},{10,12},{12,14},{14,16},{16,18},{18... | collective-permute-start | bytes 200 | tf_op jit(solution)/shard_map/ppermute | solution.py:15
  128.4 33.0 %copy-start.23 = (f32[16]{0:T(128)}, f32[16]{0:T(128)S(1)}, u32[]{:S(2)}) copy-start(f32[16]{0:T(128)S(1)} %broadcast_select_fusion.2) | copy-start | bytes 196
  128.4 4.3 %collective-permute-start.5 = (f32[16]{0:T(128)S(1)}, f32[16]{0:T(128)S(1)}, u32[]{:S(2)}, u32[]{:S(2)}) collective-permute-start(f32[16]{0:T(128)S(1)} %broadcast_select_fusion.2), channel_id=1, source_target_pairs={{0,4},{2,6},{4,8},{6,10},{8,12},{10,14},{12,16},{14,18},{16,20},{1... | collective-permute-start | bytes 200 | tf_op jit(solution)/shard_map/ppermute | solution.py:15
  132.7 4.7 %collective-permute-start.7 = (f32[16]{0:T(128)S(1)}, f32[16]{0:T(128)S(1)}, u32[]{:S(2)}, u32[]{:S(2)}) collective-permute-start(f32[16]{0:T(128)S(1)} %broadcast_select_fusion.1), channel_id=1, source_target_pairs={{0,8},{2,10},{4,12},{6,14},{8,16},{10,18},{12,20},{14,22},{16,24},... | collective-permute-start | bytes 200 | tf_op jit(solution)/shard_map/ppermute | solution.py:15
  166.8 13.4 %collective-permute-start.2 = (f32[16,64,128]{2,1,0:T(8,128)S(1)}, f32[16,64,128]{2,1,0:T(8,128)S(1)}, u32[]{:S(2)}, u32[]{:S(2)}) collective-permute-start(f32[16,64,128]{2,1,0:T(8,128)S(1)} %get-tuple-element.53), channel_id=1, source_target_pairs={{0,2},{2,4},{4,6},{6,8},{8,10},{10,12},{12,14},{14,16},{16,18},{18... | collective-permute-start | bytes 1572872 | tf_op jit(solution)/shard_map/ppermute | solution.py:15
  179.8 25.9 %copy-start.32 = (f32[16]{0:T(128)S(1)}, f32[16]{0:T(128)}, u32[]{:S(2)}) copy-start(f32[16]{0:T(128)} %get-tuple-element.37) | copy-start | bytes 196
  180.0 25.9 %copy-start.17 = (f32[16]{0:T(128)S(1)}, f32[16]{0:T(128)}, u32[]{:S(2)}) copy-start(f32[16]{0:T(128)} %get-tuple-element.36) | copy-start | bytes 196
  180.3 11.1 %collective-permute-start.4 = (f32[16,64,128]{2,1,0:T(8,128)S(1)}, f32[16,64,128]{2,1,0:T(8,128)S(1)}, u32[]{:S(2)}, u32[]{:S(2)}) collective-permute-start(f32[16,64,128]{2,1,0:T(8,128)S(1)} %multiply_add_fusion.3), channel_id=1, source_target_pairs={{0,4},{2,6},{4,8},{6,10},{8,12},{10,14},{12,16},{14,18},{16,20},{1... | collective-permute-start | bytes 1572872 | tf_op jit(solution)/shard_map/ppermute | solution.py:15
  181.7 52.5 %copy-start.31 = (f32[16]{0:T(128)S(1)}, f32[16]{0:T(128)}, u32[]{:S(2)}) copy-start(f32[16]{0:T(128)} %get-tuple-element.35) | copy-start | bytes 196
  181.9 52.5 %copy-start.30 = (f32[16]{0:T(128)S(1)}, f32[16]{0:T(128)}, u32[]{:S(2)}) copy-start(f32[16]{0:T(128)} %get-tuple-element.34) | copy-start | bytes 196
  182.0 65.5 %copy-start.39 = (f32[16]{0:T(128)S(1)}, f32[16]{0:T(128)}, u32[]{:S(2)}) copy-start(f32[16]{0:T(128)} %param.26) | copy-start | bytes 196
  191.5 12.8 %collective-permute-start.6 = (f32[16,64,128]{2,1,0:T(8,128)S(1)}, f32[16,64,128]{2,1,0:T(8,128)S(1)}, u32[]{:S(2)}, u32[]{:S(2)}) collective-permute-start(f32[16,64,128]{2,1,0:T(8,128)S(1)} %multiply_add_fusion.2), channel_id=1, source_target_pairs={{0,8},{2,10},{4,12},{6,14},{8,16},{10,18},{12,20},{14,22},{16,24},... | collective-permute-start | bytes 1572872 | tf_op jit(solution)/shard_map/ppermute | solution.py:15
  204.4 27.4 %collective-permute-start.8 = (f32[16,64,128]{2,1,0:T(8,128)S(1)}, f32[16,64,128]{2,1,0:T(8,128)S(1)}, u32[]{:S(2)}, u32[]{:S(2)}) collective-permute-start(f32[16,64,128]{2,1,0:T(8,128)S(1)} %multiply_add_fusion.1), channel_id=1, source_target_pairs={{0,16},{2,18},{4,20},{6,22},{8,24},{10,26},{12,28},{14,30},{1,17},... | collective-permute-start | bytes 1572872 | tf_op jit(solution)/shard_map/ppermute | solution.py:15
  232.0 15.5 %collective-permute-start.9 = (f32[16,64,128]{2,1,0:T(8,128)S(1)}, f32[16,64,128]{2,1,0:T(8,128)S(1)}, u32[]{:S(2)}, u32[]{:S(2)}) collective-permute-start(f32[16,64,128]{2,1,0:T(8,128)S(1)} %multiply_add_fusion), channel_id=1, source_target_pairs={{0,2},{2,4},{4,6},{6,8},{8,10},{10,12},{12,14},{14,16},{16,18},{18... | collective-permute-start | bytes 1572872 | tf_op jit(solution)/shard_map/ppermute | solution.py:15
  (35 other events, 360.4 us)
Sparse Core Ops, SparseCore 0:
  74.9 16.7 all-gather.1

commit v3 on v2

--- a/solution.py
+++ b/solution.py
@@ -1,6 +1,8 @@
 import jax
 import jax.numpy as jnp
 from jax import lax
+from jax.experimental import pallas as pl
+from jax.experimental.pallas import tpu as pltpu
 from jax.sharding import PartitionSpec as P
 
 INNER = 2048
@@ -13,6 +15,104 @@
     devices = lax.axis_size(axis)
     pairs = [(i, i + by) for i in range(devices) if 0 <= i + by < devices]
     return lax.ppermute(x, axis, pairs)
+
+
+def mix_tile(
+    x_ref, b_ref, c_ref, cum_ref, cumt_ref, dtt_ref, partc_ref, partr_ref, car_ref, gate_ref, d_ref,
+    out_ref, sq_ref,
+):
+    f32 = jnp.float32
+    tile_len = x_ref.shape[0]
+    pairs = x_ref.shape[1] // 128
+    b_mat = b_ref[...]
+    c_mat = c_ref[...]
+    scores = lax.dot_general(
+        c_mat, b_mat, (((1,), (1,)), ((), ())), preferred_element_type=f32
+    )
+    cum = cum_ref[0]
+    cumt = cumt_ref[0]
+    dtt = dtt_ref[0]
+    part_col = partc_ref[0]
+    part_row = partr_ref[0]
+    row = lax.broadcasted_iota(jnp.int32, (tile_len, tile_len), 0)
+    col = lax.broadcasted_iota(jnp.int32, (tile_len, tile_len), 1)
+    keep = (row >= col) & (part_col == part_row)
+    earlier = 1.0 - part_col
+    first_half = lax.broadcasted_iota(jnp.int32, (tile_len, 128), 1) < 64
+    total_sq = jnp.zeros((tile_len, 1), f32)
+    for pair in range(pairs):
+        cols = pl.ds(pair * 128, 128)
+        x_pair = x_ref[:, cols]
+        slabs = []
+        for half in range(2):
+            head = 2 * pair + half
+            diff = cum[:, head : head + 1] - cumt[head : head + 1, :]
+            decay = jnp.where(keep, jnp.exp(jnp.where(keep, diff, 0.0)), 0.0)
+            slabs.append((scores * decay * dtt[head : head + 1, :]).astype(jnp.bfloat16))
+        weights = jnp.concatenate(slabs, axis=1)
+        zero = jnp.zeros_like(x_pair)
+        split_x = jnp.concatenate(
+            [jnp.where(first_half, x_pair, zero), jnp.where(first_half, zero, x_pair)], axis=0
+        )
+        intra = jnp.dot(weights, split_x, preferred_element_type=f32)
+        carried = car_ref[0, cols, :]
+        projected = lax.dot_general(
+            c_mat, carried, (((1,), (1,)), ((), ())), preferred_element_type=f32
+        )
+        grow = jnp.where(
+            first_half,
+            jnp.exp(cum[:, 2 * pair : 2 * pair + 1]),
+            jnp.exp(cum[:, 2 * pair + 1 : 2 * pair + 2]),
+        )
+        inter = grow * earlier * projected
+        mixed = intra + inter + d_ref[:, cols] * x_pair.astype(f32)
+        gate = gate_ref[:, cols].astype(f32)
+        gated = mixed * (gate / (1.0 + jnp.exp(-gate)))
+        out_ref[:, cols] = gated
+        total_sq = total_sq + jnp.sum(gated * gated, axis=1, keepdims=True)
+    sq_ref[...] = total_sq
+
+
+def mix_tiles(conv_out, zx, cumul, cumul_t, dt_t, later, carried, d_full):
+    tiles_dev, tile_len, heads_here = cumul.shape
+    inner_here = carried.shape[1]
+    state_dim = carried.shape[2]
+    rows = tiles_dev * tile_len
+    b_block = inner_here // 128
+    c_block = b_block + state_dim // 128
+    part_col = later.reshape(tiles_dev, tile_len, 1)
+    part_row = later.reshape(tiles_dev, 1, tile_len)
+    per_tile = lambda j: (j, 0, 0)
+    return pl.pallas_call(
+        mix_tile,
+        grid=(tiles_dev,),
+        in_specs=[
+            pl.BlockSpec((tile_len, inner_here), lambda j: (j, 0)),
+            pl.BlockSpec((tile_len, state_dim), lambda j: (j, b_block)),
+            pl.BlockSpec((tile_len, state_dim), lambda j: (j, c_block)),
+            pl.BlockSpec((1, tile_len, heads_here), per_tile),
+            pl.BlockSpec((1, heads_here, tile_len), per_tile),
+            pl.BlockSpec((1, heads_here, tile_len), per_tile),
+            pl.BlockSpec((1, tile_len, 1), per_tile),
+            pl.BlockSpec((1, 1, tile_len), per_tile),
+            pl.BlockSpec((1, inner_here, state_dim), per_tile),
+            pl.BlockSpec((tile_len, inner_here), lambda j: (j, 0)),
+            pl.BlockSpec((1, inner_here), lambda j: (0, 0)),
+        ],
+        out_specs=[
+            pl.BlockSpec((tile_len, inner_here), lambda j: (j, 0)),
+            pl.BlockSpec((tile_len, 1), lambda j: (j, 0)),
+        ],
+        out_shape=[
+            jax.ShapeDtypeStruct((rows, inner_here), jnp.float32),
+            jax.ShapeDtypeStruct((rows, 1), jnp.float32),
+        ],
+        cost_estimate=pl.CostEstimate(
+            flops=tiles_dev * (2 * tile_len * tile_len * (state_dim + 4 * inner_here + 2 * inner_here)),
+            transcendentals=tiles_dev * tile_len * (tile_len * heads_here + 2 * inner_here),
+            bytes_accessed=rows * inner_here * 10 + tiles_dev * inner_here * state_dim * 2,
+        ),
+    )(conv_out, conv_out, conv_out, cumul, cumul_t, dt_t, part_col, part_row, carried, zx, d_full)
 
 
 def shards(
@@ -68,8 +168,8 @@
     acc_zx, acc_bc, acc_dt = tuple(
         (jnp.dot(piece, weight, preferred_element_type=jnp.float32) for weight in weight_set)
     )
-    gate = acc_zx[:, :inner_here].astype(jnp.bfloat16)
-    x_in = acc_zx[:, inner_here:].astype(jnp.bfloat16)
+    zx = acc_zx.astype(jnp.bfloat16)
+    x_in = zx[:, inner_here:]
     bc_all = acc_bc.astype(jnp.bfloat16)
     step_dt = jax.nn.softplus(acc_dt + dt_bias[None, :])
     within = jnp.arange(tile_len, dtype=jnp.int32)
@@ -105,14 +205,6 @@
     cumul = jnp.cumsum(tile_dt * rate[None, None, :], 1)
     cumul_t = cumul.transpose(0, 2, 1)
     dt_t = tile_dt.transpose(0, 2, 1)
-    causal = within[:, None] >= within[None, :]
-    keep = causal[None, :, :] & (later[:, :, None] == later[:, None, :])
-    mask_four = keep[:, None, :, :]
-    diff = cumul_t[:, :, :, None] - cumul_t[:, :, None, :]
-    decay = jnp.where(mask_four, jnp.exp(jnp.where(mask_four, diff, 0.0)), 0.0)
-    scores = jnp.einsum("jin,jsn->jis", c_part, b_part, preferred_element_type=jnp.float32)
-    weights = (scores[:, None, :, :] * decay * dt_t[:, :, None, :]).astype(jnp.bfloat16)
-    intra = jnp.einsum("jhis,jshp->jihp", weights, x_heads, preferred_element_type=jnp.float32)
     last_part = later[:, tile_len - 1]
     tail_keep = (later == last_part[:, None]).astype(jnp.float32)
     to_end = jnp.exp(cumul[:, tile_len - 1 :, :] - cumul) * tile_dt * tail_keep[:, :, None]
@@ -143,18 +235,11 @@
         distance *= 2
     entering = shifted(run_state, "seq", 1)
     tile_state = before_tile + prefix[:, :, None, None] * entering[None]
-    carried = tile_state.astype(jnp.bfloat16)
-    inter = (
-        jnp.exp(cumul)[:, :, :, None]
-        * (1.0 - later)[:, :, None, None]
-        * jnp.einsum("jin,jhpn->jihp", c_part, carried, preferred_element_type=jnp.float32)
-    )
-    mixed = intra + inter + d_skip[None, None, :, None] * x_heads.astype(jnp.float32)
-    gated = mixed.reshape(row_count, inner_here) * jax.nn.silu(gate.astype(jnp.float32))
-    sums = lax.psum(jnp.sum(gated * gated, 1), "head")
-    return (gated * lax.rsqrt(sums / INNER + EPSILON)[:, None] * norm_gain[None, :]).astype(
-        jnp.bfloat16
-    )
+    carried = tile_state.astype(jnp.bfloat16).reshape(tiles_dev, inner_here, state_dim)
+    d_full = jnp.repeat(d_skip, head_dim)[None, :]
+    gated, row_sq = mix_tiles(conv_out, zx, cumul, cumul_t, dt_t, later, carried, d_full)
+    sums = lax.psum(row_sq, "head")
+    return (gated * lax.rsqrt(sums / INNER + EPSILON) * norm_gain[None, :]).astype(jnp.bfloat16)
 
 
 def solution(mesh):

time: 302 us -> 332 us (1.099)
  Pallas kernels: 0 us -> 31.5 us
  matrix products: 40.5 us -> 22 us
  other arithmetic: 48.7 us -> 66.3 us
  waiting for transfers between devices: 115 us -> 103 us
  local copies, waits for them, and re-layouts: 42.3 us -> 52.3 us
  blocking collectives: 3.76 us -> 8.25 us
    pallas_call x0 -> x1, Pallas kernels: none -> 31.5 us  [mix_tiles(): pl.pallas_call(mix_tile, grid=(tiles_dev,), in_specs=[pl.BlockSpec((tile_...]
    another operation x1, other arithmetic: 0.14 us -> 23.3 us  [shards(): cumul = jnp.cumsum(tile_dt * rate[None, None, :], 1)]
    dot_general x3 -> x0, matrix products: 17.3 us -> none  [the longest x1 9.58 us: shards(): jnp.einsum('jhis,jshp->jihp', weights, x_heads, preferred_element_type=jn...]
    unnamed x101 -> x55, local copies, waits for them, and re-layouts: 14.1 us -> 28.4 us
    ppermute x10, waiting for transfers between devices: 67 us -> 54.9 us  [shifted(): return lax.ppermute(x, axis, pairs)]
    convert_element_type x1 -> x4, other arithmetic: 6.29 us -> 17.9 us  [the longest x1 6.83 us: shards(): tile_state.astype(jnp.bfloat16).reshape(tiles_dev, inner_here, state_dim)]
    add x1 -> x0, local copies, waits for them, and re-layouts: 9.82 us -> none  [shards(): intra + inter + d_skip[None, None, :, None] * x_heads.astype(jnp.float32)]
    reduce_sum x1 -> x0, other arithmetic: 8.26 us -> none  [shards(): sums = lax.psum(jnp.sum(gated * gated, 1), 'head')]
  transfers between devices with their start and end apart: 13 -> 13, of which waited for: 9 -> 9; matrix products, arithmetic and copies ran while one was open for 11% -> 19% of each run, Pallas kernels for 0% -> 0%
where the time goes in v3:
time: 332 us; the launch traced here: 330 us
  waiting for transfers between devices  103 us (31%)
  other arithmetic  66.3 us (20%)
  local copies, waits for them, and re-layouts  52.3 us (16%)
  starting transfers between devices  32.5 us (10%)
  Pallas kernels  31.5 us (9%)
  matrix products  22 us (7%)
  between operations  14 us (4%)
  blocking collectives  8.25 us (2%)
    ppermute x10, waiting for transfers between devices, shifted(): return lax.ppermute(x, axis, pairs)  54.9 us
    all_to_all x1, waiting for transfers between devices, shards(): lax.all_to_all(outgoing, 'seq', split_axis=0, concat_axis=0, tiled=True)  45 us
    pallas_call x1, Pallas kernels, mix_tiles(): pl.pallas_call(mix_tile, grid=(tiles_dev,), in_specs=[pl.BlockSpec((tile_...  31.5 us
    unnamed x55, local copies, waits for them, and re-layouts  28.4 us
    another operation x1, other arithmetic, shards(): cumul = jnp.cumsum(tile_dt * rate[None, None, :], 1)  23.3 us
    ppermute x10, starting transfers between devices, shifted(): return lax.ppermute(x, axis, pairs)  19.6 us
    dot_general x3, matrix products, shards(): jnp.dot(piece, weight, preferred_element_type=jnp.float32)  14.4 us
    convert_element_type x1, other arithmetic, shards(): conv_out = jax.nn.silu(total).astype(jnp.bfloat16)  10.8 us
  transfers between devices with their start and end apart: 13, of which 9 were waited for; matrix products, arithmetic and copies ran while one was open for 19% of the time, Pallas kernels for 0%

profile of v3, /device:TPU:29, one launch (start us, length us, event | category | flops | bytes accessed | tf_op | source)
XLA Modules:
  0.0 330.0 jit_solution(16109042618297783482)
XLA Ops:
  8.8 6.4 %all-to-all-start = ((bf16[16,1,1]{2,1,0:T(2,128)(2,1)}), bf16[16,1,1]{2,1,0:T(2,128)(2,1)S(1)}, u32[]{:S(2)}, u32[]{:S(2)}) async-start(bf16[16,1,1]{2,1,0:T(2,128)(2,1)} %copy.68), calls=%async_computation | async-start | bytes 16384 | tf_op jit(solution)/shard_map/all_to_all | solution.py:157
  19.1 6.5 %all-to-all-start.1 = ((bf16[16,128,512]{2,1,0:T(8,128)(2,1)}), bf16[16,128,512]{2,1,0:T(8,128)(2,1)S(1)}, u32[]{:S(2)}, u32[]{:S(2)}) async-start(bf16[16,128,512]{2,1,0:T(8,128)(2,1)} %copy.70), calls=%async_computation.1 | async-start | bytes 4194304 | tf_op jit(solution)/shard_map/all_to_all | solution.py:156
  25.8 45.0 %all-to-all-done.1 = bf16[16,128,512]{2,1,0:T(8,128)(2,1)S(1)} async-done(((bf16[16,128,512]{2,1,0:T(8,128)(2,1)}), bf16[16,128,512]{2,1,0:T(8,128)(2,1)S(1)}, u32[]{:S(2)}, u32[]{:S(2)}) %all-to-all-start.1) | async-done | bytes 2097184 | tf_op jit(solution)/shard_map/all_to_all | solution.py:156
  78.8 5.6 %copy.89 = bf16[128,8,2,1024]{3,1,2,0:T(8,128)(2,1)} copy(bf16[128,8,2,1024]{3,2,1,0:T(2,128)(2,1)} %bitcast.118) | data formatting | bytes 8388608
  91.7 11.9 %convolution_convert_fusion.gate_ref = bf16[2048,2048]{1,0:T(8,128)(2,1)S(1)} fusion(bf16[2048,1024]{1,0:T(8,128)(2,1)} %all-gather.2.cloned.1.call-done, bf16[1024,2048]{1,0:T(8,128)(2,1)} %bitcast.119), kind=kOutput, calls=%fused_computation.5 | convolution fusion | flops 8594128896 | bytes 16777216 | tf_op jit(solution)/shard_map/dot_general | solution.py:169
  104.3 4.5 %copy-done.6 = bf16[2048,1024]{1,0:T(8,128)(2,1)S(1)} copy-done((bf16[2048,1024]{1,0:T(8,128)(2,1)S(1)}, bf16[2048,1024]{1,0:T(8,128)(2,1)}, u32[]{:S(2)}) %copy-start.6) | copy-done | bytes 4194328
  116.2 23.3 %fusion.44 = f32[16,128,16]{2,0,1:T(8,128)S(1)} fusion(f32[16,128,16]{2,0,1:T(8,128)S(1)} %copy.76), kind=kOutput, calls=%fused_computation.143 | output fusion | flops 4161536 | bytes 262144 | tf_op jit(solution)/shard_map/jit(cumsum)/reduce_window_sum | solution.py:205
  143.1 4.0 %maximum_maximum_fusion = bf16[2051,1280]{1,0:T(8,128)(2,1)S(1)} fusion(bf16[2048,256]{1,0:T(8,128)(2,1)S(1)} %convolution_convert_fusion.1, bf16[2048,1024]{1,0:T(8,128)(2,1)} %copy-done.3, bf16[3,1280]{1,0:T(4,128)(2,1)S(1)} %collective-permute-done.1), kind=kLoop, calls=%fused_computation.8 | loop fusion | flops 15751680 | bytes 10501120 | tf_op jit(solution)/shard_map/concatenate | solution.py:184
  147.1 10.8 %multiply_convert_fusion.x_ref.b_ref.c_ref = bf16[2048,1280]{1,0:T(8,128)(2,1)S(1)} fusion(bf16[2048,256]{1,0:T(8,128)(2,1)S(1)} %convolution_convert_fusion.1, bf16[2051,1280]{1,0:T(8,128)(2,1)S(1)} %maximum_maximum_fusion, f32[1280]{0:T(1024)S(1)} %get-tuple-element.10, f32[1280]{0:T(1024)S(1)} %get-tuple-element.11, f32[1280]{0:T(1024)S(1)} %get-tuple-element.12, ...), kind=kLoop, calls=%fused_computation | loop fusion | flops 60293120 | bytes 26246144 | tf_op jit(solution)/shard_map/convert_element_type | solution.py:197
  157.9 4.8 %slice_convert_fusion = f32[2048,1024]{1,0:T(8,128)} fusion(bf16[2048,1280]{1,0:T(8,128)(2,1)S(1)} %multiply_convert_fusion.x_ref.b_ref.c_ref), kind=kLoop, calls=%fused_computation.10 | loop fusion | flops 2097152 | bytes 12582912 | tf_op jit(solution)/shard_map/convert_element_type | solution.py:211
  162.8 9.2 %copy.79 = f32[2048,1024]{0,1:T(8,128)} copy(f32[2048,1024]{1,0:T(8,128)} %slice_convert_fusion) | data formatting | bytes 16777216 | tf_op jit(solution)/shard_map/convert_element_type | solution.py:211
  171.9 5.4 %copy.91 = f32[128,8,16,128]{3,2,1,0:T(8,128)S(1)} copy(f32[128,8,16,128]{3,1,2,0:T(8,128)} %bitcast.116) | data formatting | bytes 16777216
  178.4 4.1 %multiply_reduce_fusion = (f32[16,64,128]{2,1,0:T(8,128)S(1)}, f32[16,16,64,128]{3,2,1,0:T(8,128)}) fusion(f32[16,16]{1,0:T(8,128)S(1)} %concatenate.29, bf16[16,128,128,1]{2,1,3,0:T(8,128)(2,1)S(1)} %bitcast.114, bf16[16,128,16,64]{1,0,3,2:T(8,128)(2,1)S(1)} %multiply_convert_fusion.2), kind=kOutput, calls=%fused_computation.3 | convolution fusion | flops 540934144 | bytes 13632512 | tf_op jit(solution)/shard_map/jshp,jsn->jhpn/dot_general | solution.py:212
  188.8 9.4 %collective-permute-done.3 = f32[16]{0:T(128)S(1)} collective-permute-done((f32[16]{0:T(128)S(1)}, f32[16]{0:T(128)S(1)}, u32[]{:S(2)}, u32[]{:S(2)}) %collective-permute-start.3) | collective-permute-done | bytes 96 | tf_op jit(solution)/shard_map/ppermute | solution.py:17
  206.7 3.7 %slice_add_fusion = (f32[1,16,64,128]{3,2,1,0:T(8,128)S(1)}, f32[1,16,64,128]{3,2,1,0:T(8,128)S(1)}, f32[1,16,64,128]{3,2,1,0:T(8,128)S(1)}, f32[1,16,64,128]{3,...) fusion(f32[16,16,64,128]{3,2,1,0:T(8,128)} %get-tuple-element.4, ...), kind=kLoop, calls=%fused_computation.29 | loop fusion | flops 3801088 | bytes 15729600 | tf_op jit(solution)/shard_map/add | solution.py:226
  210.5 5.8 %collective-permute-done.4 = f32[16,64,128]{2,1,0:T(8,128)S(1)} collective-permute-done((f32[16,64,128]{2,1,0:T(8,128)S(1)}, f32[16,64,128]{2,1,0:T(8,128)S(1)}, u32[]{:S(2)}, u32[]{:S(2)}) %collective-permute-start.4) | collective-permute-done | bytes 524320 | tf_op jit(solution)/shard_map/ppermute | solution.py:17
  221.8 6.2 %collective-permute-done.6 = f32[16,64,128]{2,1,0:T(8,128)S(1)} collective-permute-done((f32[16,64,128]{2,1,0:T(8,128)S(1)}, f32[16,64,128]{2,1,0:T(8,128)S(1)}, u32[]{:S(2)}, u32[]{:S(2)}) %collective-permute-start.6) | collective-permute-done | bytes 524320 | tf_op jit(solution)/shard_map/ppermute | solution.py:17
  234.0 21.2 %collective-permute-done.8 = f32[16,64,128]{2,1,0:T(8,128)S(1)} collective-permute-done((f32[16,64,128]{2,1,0:T(8,128)S(1)}, f32[16,64,128]{2,1,0:T(8,128)S(1)}, u32[]{:S(2)}, u32[]{:S(2)}) %collective-permute-start.8) | collective-permute-done | bytes 524320 | tf_op jit(solution)/shard_map/ppermute | solution.py:17
  255.2 3.4 %collective-permute-start.9 = (f32[16,64,128]{2,1,0:T(8,128)S(1)}, f32[16,64,128]{2,1,0:T(8,128)S(1)}, u32[]{:S(2)}, u32[]{:S(2)}) collective-permute-start(f32[16,64,128]{2,1,0:T(8,128)S(1)} %multiply_add_fusion), channel_id=1, source_target_pairs={{0,2},{2,4},{4,6},{6,8},{8,10},{10,12},{12,14},{14,16},{16,18},{18... | collective-permute-start | bytes 1572872 | tf_op jit(solution)/shard_map/ppermute | solution.py:17
  262.9 8.1 %collective-permute-done.9 = f32[16,64,128]{2,1,0:T(8,128)S(1)} collective-permute-done((f32[16,64,128]{2,1,0:T(8,128)S(1)}, f32[16,64,128]{2,1,0:T(8,128)S(1)}, u32[]{:S(2)}, u32[]{:S(2)}) %collective-permute-start.9) | collective-permute-done | bytes 524320 | tf_op jit(solution)/shard_map/ppermute | solution.py:17
  271.0 6.8 %add_convert_fusion.car_ref = bf16[16,1024,128]{2,1,0:T(8,128)(2,1)} fusion(f32[16,1024,128]{2,1,0:T(8,128)} %constant_dynamic-update-slice_fusion.2, f32[1024,128]{1,0:T(8,128)S(1)} %bitcast.138, f32[16,1024]{1,0:T(8,128)S(1)} %mul.568), kind=kLoop, calls=%fused_computation.2 | loop fusion | flops 6291456 | bytes 13172736 | tf_op jit(solution)/shard_map/convert_element_type | solution.py:238
  277.8 31.5 %shard_map.136 = (f32[2048,1024]{1,0:T(8,128)}, f32[2048,1]{1,0:T(8,128)}) custom-call(bf16[2048,1280]{1,0:T(8,128)(2,1)} %copy-done.2, bf16[2048,1280]{1,0:T(8,128)(2,1)} %copy-done.2, bf16[2048,1280]{1,0:T(8,128)(2,1)} %copy-done.2, f32[16,128,16]{2,1,0:T(8,128)} %copy.84.cum_ref, f32[16,16,128]{2,1,0:T(8,128)} %bitcast.137, ...), custom_call_target="tpu_custom_call" | custom-call | flops 3288334336 | bytes 25165824 | tf_op jit(solution)/shard_map/pallas_call | solution.py:86
  309.3 8.2 %psum.7 = f32[2048,1]{1,0:T(8,128)S(1)} all-reduce(f32[2048,1]{1,0:T(8,128)} %get-tuple-element.8), channel_id=1, replica_groups=mesh['seq'=16,'head'=2] {'head'}, use_global_device_ids=true, to_apply=%region_5.6 | all-reduce | flops 2048 | bytes 16384 | tf_op jit(solution)/shard_map/psum | solution.py:241
  317.9 5.2 %multiply_convert_fusion.1 = bf16[2048,1024]{1,0:T(8,128)(2,1)} fusion(f32[2048,1024]{1,0:T(8,128)} %get-tuple-element.7, f32[1024]{0:T(1024)S(1)} %copy-done.10, f32[2048]{0:T(1024)S(1)} %rsqrt_reduce_fusion), kind=kLoop, calls=%fused_computation.1 | loop fusion | flops 6291456 | bytes 12595200 | tf_op jit(solution)/shard_map/convert_element_type | solution.py:242
  (136 shorter events, 64.9 us)
Async XLA Ops:
  6.5 8.7 %copy-start = (bf16[16,128,512]{2,1,0:T(8,128)(2,1)S(1)}, bf16[16,128,512]{2,1,0:T(8,128)(2,1)}, u32[]{:S(2)}) copy-start(bf16[16,128,512]{2,1,0:T(8,128)(2,1)} %param.14) | copy-start | bytes 6291460
  8.8 10.2 %all-to-all-start = ((bf16[16,1,1]{2,1,0:T(2,128)(2,1)}), bf16[16,1,1]{2,1,0:T(2,128)(2,1)S(1)}, u32[]{:S(2)}, u32[]{:S(2)}) async-start(bf16[16,1,1]{2,1,0:T(2,128)(2,1)} %copy.68), calls=%async_computation | async-start | bytes 16384 | tf_op jit(solution)/shard_map/all_to_all | solution.py:157
  19.1 55.7 %copy-start.8 = (s32[16]{0:T(128)S(1)}, s32[16]{0:T(128)}, u32[]{:S(2)}) copy-start(s32[16]{0:T(128)} %param.16) | copy-start | bytes 196
  19.1 51.8 %all-to-all-start.1 = ((bf16[16,128,512]{2,1,0:T(8,128)(2,1)}), bf16[16,128,512]{2,1,0:T(8,128)(2,1)S(1)}, u32[]{:S(2)}, u32[]{:S(2)}) async-start(bf16[16,128,512]{2,1,0:T(8,128)(2,1)} %copy.70), calls=%async_computation.1 | async-start | bytes 4194304 | tf_op jit(solution)/shard_map/all_to_all | solution.py:156
  25.6 66.1 %all-gather.2.cloned.1.call-start = ((), (), s32[]{:S(2)}) async-start(), calls=%async_computation.2 | async-start | bytes 6291456 | tf_op jit(solution)/shard_map/all_gather | solution.py:167
  72.2 12.7 %copy-start.15 = (f32[16]{0:T(128)S(1)}, f32[16]{0:T(128)}, u32[]{:S(2)}) copy-start(f32[16]{0:T(128)} %param.26) | copy-start | bytes 196
  72.2 13.4 %copy-start.9 = (f32[4,1024]{1,0:T(4,128)S(1)}, f32[4,1024]{1,0:T(4,128)}, u32[]{:S(2)}) copy-start(f32[4,1024]{1,0:T(4,128)} %param.22) | copy-start | bytes 49156
  72.2 13.4 %copy-start.11 = (f32[4,256]{1,0:T(4,128)S(1)}, f32[4,256]{1,0:T(4,128)}, u32[]{:S(2)}) copy-start(f32[4,256]{1,0:T(4,128)} %param.23) | copy-start | bytes 12292
  72.2 13.4 %copy-start.12 = (f32[1024]{0:T(1024)S(1)}, f32[1024]{0:T(1024)}, u32[]{:S(2)}) copy-start(f32[1024]{0:T(1024)} %param.24) | copy-start | bytes 12292
  72.2 13.4 %copy-start.14 = (f32[256]{0:T(256)S(1)}, f32[256]{0:T(256)}, u32[]{:S(2)}) copy-start(f32[256]{0:T(256)} %param.25) | copy-start | bytes 3076
  72.2 14.4 %copy-start.17 = (f32[16]{0:T(128)S(1)}, f32[16]{0:T(128)}, u32[]{:S(2)}) copy-start(f32[16]{0:T(128)} %param.21) | copy-start | bytes 196
  76.4 12.0 %collective-permute-start = (bf16[3]{0:T(256)(128)(2,1)S(1)}, bf16[3]{0:T(256)(128)(2,1)S(1)}, u32[]{:S(2)}, u32[]{:S(2)}) collective-permute-start(bf16[3]{0:T(256)(128)(2,1)S(1)} %fusion.35), channel_id=1, source_target_pairs={{0,2},{2,4},{4,6},{6,8},{8,10},{10,12},{12,14},{14,16},{16,18},{18... | collective-permute-start | bytes 26 | tf_op jit(solution)/shard_map/ppermute | solution.py:17
  103.6 6.7 %copy-start.5 = (bf16[2048,2048]{1,0:T(8,128)(2,1)}, bf16[2048,2048]{1,0:T(8,128)(2,1)S(1)}, u32[]{:S(2)}) copy-start(bf16[2048,2048]{1,0:T(8,128)(2,1)S(1)} %convolution_convert_fusion.gate_ref) | copy-start | bytes 25165828
  110.3 32.8 %collective-permute-start.1 = (bf16[3,1280]{1,0:T(4,128)(2,1)S(1)}, bf16[3,1280]{1,0:T(4,128)(2,1)S(1)}, u32[]{:S(2)}, u32[]{:S(2)}) collective-permute-start(bf16[3,1280]{1,0:T(4,128)(2,1)S(1)} %fusion.16), channel_id=1, source_target_pairs={{0,2},{2,4},{4,6},{6,8},{8,10},{10,12},{12,14},{14,16},{16,18},{18... | collective-permute-start | bytes 23048 | tf_op jit(solution)/shard_map/ppermute | solution.py:17
  182.5 21.3 %collective-permute-start.2 = (f32[16,64,128]{2,1,0:T(8,128)S(1)}, f32[16,64,128]{2,1,0:T(8,128)S(1)}, u32[]{:S(2)}, u32[]{:S(2)}) collective-permute-start(f32[16,64,128]{2,1,0:T(8,128)S(1)} %get-tuple-element.48), channel_id=1, source_target_pairs={{0,2},{2,4},{4,6},{6,8},{8,10},{10,12},{12,14},{14,16},{16,18},{18... | collective-permute-start | bytes 1572872 | tf_op jit(solution)/shard_map/ppermute | solution.py:17
  186.9 11.3 %collective-permute-start.3 = (f32[16]{0:T(128)S(1)}, f32[16]{0:T(128)S(1)}, u32[]{:S(2)}, u32[]{:S(2)}) collective-permute-start(f32[16]{0:T(128)S(1)} %slice_bitcast_fusion.1), channel_id=1, source_target_pairs={{0,2},{2,4},{4,6},{6,8},{8,10},{10,12},{12,14},{14,16},{16,18},{18... | collective-permute-start | bytes 200 | tf_op jit(solution)/shard_map/ppermute | solution.py:17
  198.2 4.3 %collective-permute-start.5 = (f32[16]{0:T(128)S(1)}, f32[16]{0:T(128)S(1)}, u32[]{:S(2)}, u32[]{:S(2)}) collective-permute-start(f32[16]{0:T(128)S(1)} %broadcast_select_fusion.2), channel_id=1, source_target_pairs={{0,4},{2,6},{4,8},{6,10},{8,12},{10,14},{12,16},{14,18},{16,20},{1... | collective-permute-start | bytes 200 | tf_op jit(solution)/shard_map/ppermute | solution.py:17
  202.5 4.3 %collective-permute-start.7 = (f32[16]{0:T(128)S(1)}, f32[16]{0:T(128)S(1)}, u32[]{:S(2)}, u32[]{:S(2)}) collective-permute-start(f32[16]{0:T(128)S(1)} %broadcast_select_fusion.1), channel_id=1, source_target_pairs={{0,8},{2,10},{4,12},{6,14},{8,16},{10,18},{12,20},{14,22},{16,24},... | collective-permute-start | bytes 200 | tf_op jit(solution)/shard_map/ppermute | solution.py:17
  203.9 12.3 %collective-permute-start.4 = (f32[16,64,128]{2,1,0:T(8,128)S(1)}, f32[16,64,128]{2,1,0:T(8,128)S(1)}, u32[]{:S(2)}, u32[]{:S(2)}) collective-permute-start(f32[16,64,128]{2,1,0:T(8,128)S(1)} %multiply_add_fusion.3), channel_id=1, source_target_pairs={{0,4},{2,6},{4,8},{6,10},{8,12},{10,14},{12,16},{14,18},{16,20},{1... | collective-permute-start | bytes 1572872 | tf_op jit(solution)/shard_map/ppermute | solution.py:17
  216.3 11.7 %collective-permute-start.6 = (f32[16,64,128]{2,1,0:T(8,128)S(1)}, f32[16,64,128]{2,1,0:T(8,128)S(1)}, u32[]{:S(2)}, u32[]{:S(2)}) collective-permute-start(f32[16,64,128]{2,1,0:T(8,128)S(1)} %multiply_add_fusion.2), channel_id=1, source_target_pairs={{0,8},{2,10},{4,12},{6,14},{8,16},{10,18},{12,20},{14,22},{16,24},... | collective-permute-start | bytes 1572872 | tf_op jit(solution)/shard_map/ppermute | solution.py:17
  228.2 26.9 %collective-permute-start.8 = (f32[16,64,128]{2,1,0:T(8,128)S(1)}, f32[16,64,128]{2,1,0:T(8,128)S(1)}, u32[]{:S(2)}, u32[]{:S(2)}) collective-permute-start(f32[16,64,128]{2,1,0:T(8,128)S(1)} %multiply_add_fusion.1), channel_id=1, source_target_pairs={{0,16},{2,18},{4,20},{6,22},{8,24},{10,26},{12,28},{14,30},{1,17},... | collective-permute-start | bytes 1572872 | tf_op jit(solution)/shard_map/ppermute | solution.py:17
  255.2 15.7 %collective-permute-start.9 = (f32[16,64,128]{2,1,0:T(8,128)S(1)}, f32[16,64,128]{2,1,0:T(8,128)S(1)}, u32[]{:S(2)}, u32[]{:S(2)}) collective-permute-start(f32[16,64,128]{2,1,0:T(8,128)S(1)} %multiply_add_fusion), channel_id=1, source_target_pairs={{0,2},{2,4},{4,6},{6,8},{8,10},{10,12},{12,14},{14,16},{16,18},{18... | collective-permute-start | bytes 1572872 | tf_op jit(solution)/shard_map/ppermute | solution.py:17
  277.8 40.1 %copy-start.10 = (f32[1024]{0:T(1024)S(1)}, f32[1024]{0:T(1024)}, u32[]{:S(2)}) copy-start(f32[1024]{0:T(1024)} %param.27) | copy-start | bytes 12292
  277.8 45.3 %copy-start.1 = (bf16[16,128,512]{2,1,0:T(8,128)(2,1)S(1)}, bf16[16,128,512]{2,1,0:T(8,128)(2,1)}, u32[]{:S(2)}) copy-start(bf16[16,128,512]{2,1,0:T(8,128)(2,1)} %param.14) | copy-start | bytes 6291460
  (8 other events, 35.6 us)
Sparse Core Ops, SparseCore 0:
  74.9 16.7 all-gather.1

commit v4 on v3

--- a/solution.py
+++ b/solution.py
@@ -39,7 +39,7 @@
     keep = (row >= col) & (part_col == part_row)
     earlier = 1.0 - part_col
     first_half = lax.broadcasted_iota(jnp.int32, (tile_len, 128), 1) < 64
-    total_sq = jnp.zeros((tile_len, 1), f32)
+    total_sq = jnp.zeros((tile_len, 128), f32)
     for pair in range(pairs):
         cols = pl.ds(pair * 128, 128)
         x_pair = x_ref[:, cols]
@@ -67,10 +67,49 @@
         inter = grow * earlier * projected
         mixed = intra + inter + d_ref[:, cols] * x_pair.astype(f32)
         gate = gate_ref[:, cols].astype(f32)
-        gated = mixed * (gate / (1.0 + jnp.exp(-gate)))
+        gated = mixed * (gate * (0.5 + 0.5 * jnp.tanh(0.5 * gate)))
         out_ref[:, cols] = gated
-        total_sq = total_sq + jnp.sum(gated * gated, axis=1, keepdims=True)
-    sq_ref[...] = total_sq
+        total_sq = total_sq + gated * gated
+    sq_ref[...] = jnp.sum(total_sq, axis=1, keepdims=True)
+
+
+def contrib_tile(x_ref, b_ref, end_ref, out_ref):
+    f32 = jnp.float32
+    tile_len = x_ref.shape[0]
+    pairs = x_ref.shape[1] // 128
+    b_mat = b_ref[...]
+    to_end = end_ref[0]
+    first_half = lax.broadcasted_iota(jnp.int32, (tile_len, 128), 1) < 64
+    for pair in range(pairs):
+        cols = pl.ds(pair * 128, 128)
+        scale = jnp.where(
+            first_half, to_end[:, 2 * pair : 2 * pair + 1], to_end[:, 2 * pair + 1 : 2 * pair + 2]
+        )
+        scaled = (x_ref[:, cols].astype(f32) * scale).astype(jnp.bfloat16)
+        out_ref[0, cols, :] = lax.dot_general(
+            scaled, b_mat, (((0,), (0,)), ((), ())), preferred_element_type=f32
+        )
+
+
+def contrib_tiles(conv_out, to_end, inner_here, state_dim):
+    tiles_dev, tile_len, heads_here = to_end.shape
+    b_block = inner_here // 128
+    return pl.pallas_call(
+        contrib_tile,
+        grid=(tiles_dev,),
+        in_specs=[
+            pl.BlockSpec((tile_len, inner_here), lambda j: (j, 0)),
+            pl.BlockSpec((tile_len, state_dim), lambda j: (j, b_block)),
+            pl.BlockSpec((1, tile_len, heads_here), lambda j: (j, 0, 0)),
+        ],
+        out_specs=pl.BlockSpec((1, inner_here, state_dim), lambda j: (j, 0, 0)),
+        out_shape=jax.ShapeDtypeStruct((tiles_dev, inner_here, state_dim), jnp.float32),
+        cost_estimate=pl.CostEstimate(
+            flops=tiles_dev * 2 * tile_len * inner_here * state_dim,
+            transcendentals=0,
+            bytes_accessed=tiles_dev * (tile_len * (inner_here + state_dim) * 2 + inner_here * state_dim * 4),
+        ),
+    )(conv_out, conv_out, to_end)
 
 
 def mix_tiles(conv_out, zx, cumul, cumul_t, dt_t, later, carried, d_full):
@@ -195,36 +234,32 @@
             0.0,
         )
     conv_out = jax.nn.silu(total).astype(jnp.bfloat16)
-    x_heads = conv_out[:, :inner_here].reshape(tiles_dev, tile_len, heads_here, head_dim)
-    b_part = conv_out[:, inner_here : inner_here + state_dim].reshape(
-        tiles_dev, tile_len, state_dim
-    )
-    c_part = conv_out[:, inner_here + state_dim :].reshape(tiles_dev, tile_len, state_dim)
     rate = -jnp.exp(a_log)
     tile_dt = step_dt.reshape(tiles_dev, tile_len, heads_here)
-    cumul = jnp.cumsum(tile_dt * rate[None, None, :], 1)
+    lower = (within[:, None] >= within[None, :]).astype(jnp.float32)
+    cumul = jnp.einsum(
+        "is,jsh->jih", lower, tile_dt * rate[None, None, :], precision=lax.Precision.HIGHEST
+    )
     cumul_t = cumul.transpose(0, 2, 1)
     dt_t = tile_dt.transpose(0, 2, 1)
     last_part = later[:, tile_len - 1]
     tail_keep = (later == last_part[:, None]).astype(jnp.float32)
     to_end = jnp.exp(cumul[:, tile_len - 1 :, :] - cumul) * tile_dt * tail_keep[:, :, None]
-    scaled = (x_heads.astype(jnp.float32) * to_end[:, :, :, None]).astype(jnp.bfloat16)
-    contrib = jnp.einsum("jshp,jsn->jhpn", scaled, b_part, preferred_element_type=jnp.float32)
+    contrib = contrib_tiles(conv_out, to_end, inner_here, state_dim).reshape(
+        tiles_dev, heads_here, head_dim, state_dim
+    )
     passing = jnp.exp(cumul[:, tile_len - 1, :]) * (1.0 - has_bound)[:, None]
-    flat_contrib = contrib.reshape(tiles_dev, heads_here, head_dim * state_dim)
     through = jnp.cumprod(passing, 0)
     prefix = jnp.concatenate([jnp.ones((1, heads_here), jnp.float32), through[:-1]], 0)
     reverse = jnp.cumprod(passing[::-1], 0)[::-1]
     to_last = jnp.concatenate([reverse[1:], jnp.ones((1, heads_here), jnp.float32)], 0)
-    run_state = jnp.sum(to_last[:, :, None] * flat_contrib, 0).reshape(
-        heads_here, head_dim, state_dim
-    )
-    running = jnp.zeros((heads_here, head_dim * state_dim), jnp.float32)
+    run_state = jnp.sum(to_last[:, :, None, None] * contrib, 0)
+    running = jnp.zeros((heads_here, head_dim, state_dim), jnp.float32)
     states = []
     for tile in range(tiles_dev):
         states.append(running)
-        running = passing[tile][:, None] * running + flat_contrib[tile]
-    before_tile = jnp.stack(states).reshape(tiles_dev, heads_here, head_dim, state_dim)
+        running = passing[tile][:, None, None] * running + contrib[tile]
+    before_tile = jnp.stack(states)
     position = lax.axis_index("seq")
     run_decay = through[tiles_dev - 1]
     distance = 1

time: 332 us -> 307 us (0.925)
  local copies, waits for them, and re-layouts: 52.3 us -> 27.5 us
  other arithmetic: 66.3 us -> 56.3 us
  waiting for transfers between devices: 103 us -> 110 us
  Pallas kernels: 31.5 us -> 37.6 us
    another operation x4, other arithmetic: 23.5 us -> 1.17 us  [the longest x1 1.01 us: shards(): before_tile = jnp.stack(states)]
    pallas_call x0 -> x1, Pallas kernels: none -> 17 us  [contrib_tiles(): pl.pallas_call(contrib_tile, grid=(tiles_dev,), in_specs=[pl.BlockSpec((t...]
    unnamed x55 -> x44, local copies, waits for them, and re-layouts: 28.4 us -> 12 us
    unnamed x0 -> x14, other arithmetic: none -> 15.2 us
    pallas_call x1, Pallas kernels: 31.5 us -> 20.6 us  [mix_tiles(): pl.pallas_call(mix_tile, grid=(tiles_dev,), in_specs=[pl.BlockSpec((tile_...]
    convert_element_type x2 -> x0, local copies, waits for them, and re-layouts: 9.29 us -> none  [the longest x1 9.18 us: shards(): x_heads.astype(jnp.float32) * to_end[:, :, :, None]]
    ppermute x10, waiting for transfers between devices: 54.9 us -> 61.2 us  [shifted(): return lax.ppermute(x, axis, pairs)]
    convert_element_type x2 -> x0, other arithmetic: 5.83 us -> none  [the longest x1 4.82 us: shards(): x_heads.astype(jnp.float32) * to_end[:, :, :, None]]
  transfers between devices with their start and end apart: 13 -> 13, of which waited for: 9 -> 9; matrix products, arithmetic and copies ran while one was open for 19% -> 13% of each run, Pallas kernels for 0% -> 0%
where the time goes in v4:
time: 307 us; the launch traced here: 305 us
  waiting for transfers between devices  110 us (36%)
  other arithmetic  56.3 us (18%)
  Pallas kernels  37.6 us (12%)
  starting transfers between devices  32 us (10%)
  local copies, waits for them, and re-layouts  27.5 us (9%)
  matrix products  20.3 us (7%)
  between operations  13.9 us (5%)
  blocking collectives  7.91 us (3%)
    ppermute x10, waiting for transfers between devices, shifted(): return lax.ppermute(x, axis, pairs)  61.2 us
    all_to_all x1, waiting for transfers between devices, shards(): lax.all_to_all(outgoing, 'seq', split_axis=0, concat_axis=0, tiled=True)  45 us
    pallas_call x1, Pallas kernels, mix_tiles(): pl.pallas_call(mix_tile, grid=(tiles_dev,), in_specs=[pl.BlockSpec((tile_...  20.6 us
    ppermute x10, starting transfers between devices, shifted(): return lax.ppermute(x, axis, pairs)  19.1 us
    pallas_call x1, Pallas kernels, contrib_tiles(): pl.pallas_call(contrib_tile, grid=(tiles_dev,), in_specs=[pl.BlockSpec((t...  17 us
    dot_general x3, matrix products, shards(): jnp.dot(piece, weight, preferred_element_type=jnp.float32)  16.6 us
    unnamed x14, other arithmetic  15.2 us
    unnamed x44, local copies, waits for them, and re-layouts  12 us
  transfers between devices with their start and end apart: 13, of which 9 were waited for; matrix products, arithmetic and copies ran while one was open for 13% of the time, Pallas kernels for 0%

profile of v4, /device:TPU:29, one launch (start us, length us, event | category | flops | bytes accessed | tf_op | source)
XLA Modules:
  0.0 305.1 jit_solution(11497379833335220157)
XLA Ops:
  8.8 6.4 %all-to-all-start = ((bf16[16,1,1]{2,1,0:T(2,128)(2,1)}), bf16[16,1,1]{2,1,0:T(2,128)(2,1)S(1)}, u32[]{:S(2)}, u32[]{:S(2)}) async-start(bf16[16,1,1]{2,1,0:T(2,128)(2,1)} %copy.62), calls=%async_computation | async-start | bytes 16384 | tf_op jit(solution)/shard_map/all_to_all | solution.py:196
  19.1 6.5 %all-to-all-start.1 = ((bf16[16,128,512]{2,1,0:T(8,128)(2,1)}), bf16[16,128,512]{2,1,0:T(8,128)(2,1)S(1)}, u32[]{:S(2)}, u32[]{:S(2)}) async-start(bf16[16,128,512]{2,1,0:T(8,128)(2,1)} %copy.64), calls=%async_computation.1 | async-start | bytes 4194304 | tf_op jit(solution)/shard_map/all_to_all | solution.py:195
  25.8 45.0 %all-to-all-done.1 = bf16[16,128,512]{2,1,0:T(8,128)(2,1)S(1)} async-done(((bf16[16,128,512]{2,1,0:T(8,128)(2,1)}), bf16[16,128,512]{2,1,0:T(8,128)(2,1)S(1)}, u32[]{:S(2)}, u32[]{:S(2)}) %all-to-all-start.1) | async-done | bytes 2097184 | tf_op jit(solution)/shard_map/all_to_all | solution.py:195
  78.8 5.6 %copy.77 = bf16[128,8,2,1024]{3,1,2,0:T(8,128)(2,1)} copy(bf16[128,8,2,1024]{3,2,1,0:T(2,128)(2,1)} %bitcast.92) | data formatting | bytes 8388608
  88.4 3.3 %all-gather.2.cloned.1.call-done = bf16[2048,1024]{1,0:T(8,128)(2,1)} async-done(((bf16[2048,512]{1,0:T(8,128)(2,1)}), bf16[2048,1024]{1,0:T(8,128)(2,1)}) %all-gather.2.cloned.1.call-update) | async-done | bytes 4194320 | tf_op jit(solution)/shard_map/all_gather | solution.py:206
  91.7 3.4 %compare_select_fusion = f32[2048,16]{0,1:T(8,128)S(1)} fusion(bf16[2048,1024]{1,0:T(8,128)(2,1)} %all-gather.2.cloned.1.call-done, bf16[1024,16]{0,1:T(8,128)(2,1)S(1)} %copy-done.9, f32[16]{0:T(128)S(1)} %copy-done.15), kind=kOutput, calls=%fused_computation.46 | convolution fusion | flops 67338240 | bytes 4358208 | tf_op jit(solution)/shard_map/dot_general | solution.py:208
  97.3 11.9 %convolution_convert_fusion.gate_ref = bf16[2048,2048]{1,0:T(8,128)(2,1)S(1)} fusion(bf16[2048,1024]{1,0:T(8,128)(2,1)} %all-gather.2.cloned.1.call-done, bf16[1024,2048]{1,0:T(8,128)(2,1)} %bitcast.93), kind=kOutput, calls=%fused_computation.4 | convolution fusion | flops 8594128896 | bytes 16777216 | tf_op jit(solution)/shard_map/dot_general | solution.py:208
  109.9 4.5 %copy-done.7 = bf16[2048,1024]{1,0:T(8,128)(2,1)S(1)} copy-done((bf16[2048,1024]{1,0:T(8,128)(2,1)S(1)}, bf16[2048,1024]{1,0:T(8,128)(2,1)}, u32[]{:S(2)}) %copy-start.7) | copy-done | bytes 4194328
  116.6 3.1 %collective-permute-start.1 = (bf16[3,1280]{1,0:T(4,128)(2,1)S(1)}, bf16[3,1280]{1,0:T(4,128)(2,1)S(1)}, u32[]{:S(2)}, u32[]{:S(2)}) collective-permute-start(bf16[3,1280]{1,0:T(4,128)(2,1)S(1)} %fusion.26), channel_id=1, source_target_pairs={{0,2},{2,4},{4,6},{6,8},{8,10},{10,12},{12,14},{14,16},{16,18},{18... | collective-permute-start | bytes 23048 | tf_op jit(solution)/shard_map/ppermute | solution.py:17
  130.7 3.0 collective-permute-done.5
  137.9 3.8 %maximum_maximum_fusion = bf16[2051,1280]{1,0:T(8,128)(2,1)S(1)} fusion(bf16[2048,256]{1,0:T(8,128)(2,1)S(1)} %convolution_convert_fusion.1, bf16[2048,1024]{1,0:T(8,128)(2,1)} %copy-done.3, bf16[3,1280]{1,0:T(4,128)(2,1)S(1)} %collective-permute-done.1), kind=kLoop, calls=%fused_computation.7 | loop fusion | flops 15751680 | bytes 10501120 | tf_op jit(solution)/shard_map/concatenate | solution.py:223
  141.7 11.7 %multiply_convert_fusion.x_ref.b_ref.c_ref = bf16[2048,1280]{1,0:T(8,128)(2,1)} fusion(bf16[2048,256]{1,0:T(8,128)(2,1)S(1)} %convolution_convert_fusion.1, bf16[2051,1280]{1,0:T(8,128)(2,1)S(1)} %maximum_maximum_fusion, f32[1280]{0:T(1024)S(1)} %get-tuple-element.10, f32[1280]{0:T(1024)S(1)} %get-tuple-element.11, f32[1280]{0:T(1024)S(1)} %get-tuple-element.12, ...), kind=kLoop, calls=%fused_computation | loop fusion | flops 60293120 | bytes 26246144 | tf_op jit(solution)/shard_map/convert_element_type | solution.py:236
  153.4 17.0 %shard_map.136 = f32[16,1024,128]{2,1,0:T(8,128)} custom-call(bf16[2048,1280]{1,0:T(8,128)(2,1)} %multiply_convert_fusion.x_ref.b_ref.c_ref, bf16[2048,1280]{1,0:T(8,128)(2,1)} %multiply_convert_fusion.x_ref.b_ref.c_ref, f32[16,128,16]{2,1,0:T(8,128)} %multiply_multiply_fusion.end_ref), custom_call_target="tpu_custom_call" | custom-call | flops 536870912 | bytes 13107200 | tf_op jit(solution)/shard_map/pallas_call | solution.py:97
  170.4 5.6 %multiply_reduce_fusion = f32[1024,128]{1,0:T(8,128)S(1)} fusion(f32[16,1024,128]{2,1,0:T(8,128)} %shard_map.136, f32[16,1024]{1,0:T(8,128)S(1)} %mul.808), kind=kLoop, calls=%fused_computation.3 | loop fusion | flops 4063232 | bytes 8978432 | tf_op jit(solution)/shard_map/reduce_sum | solution.py:256
  176.0 3.1 %collective-permute-start.2 = (f32[16,64,128]{2,1,0:T(8,128)S(1)}, f32[16,64,128]{2,1,0:T(8,128)S(1)}, u32[]{:S(2)}, u32[]{:S(2)}) collective-permute-start(f32[16,64,128]{2,1,0:T(8,128)S(1)} %bitcast.94), channel_id=1, source_target_pairs={{0,2},{2,4},{4,6},{6,8},{8,10},{10,12},{12,14},{14,16},{16,18},{18... | collective-permute-start | bytes 1572872 | tf_op jit(solution)/shard_map/ppermute | solution.py:17
  186.6 3.7 %collective-permute-done.2 = f32[16,64,128]{2,1,0:T(8,128)S(1)} collective-permute-done((f32[16,64,128]{2,1,0:T(8,128)S(1)}, f32[16,64,128]{2,1,0:T(8,128)S(1)}, u32[]{:S(2)}, u32[]{:S(2)}) %collective-permute-start.2) | collective-permute-done | bytes 524320 | tf_op jit(solution)/shard_map/ppermute | solution.py:17
  194.0 8.7 %collective-permute-done.4 = f32[16,64,128]{2,1,0:T(8,128)S(1)} collective-permute-done((f32[16,64,128]{2,1,0:T(8,128)S(1)}, f32[16,64,128]{2,1,0:T(8,128)S(1)}, u32[]{:S(2)}, u32[]{:S(2)}) %collective-permute-start.4) | collective-permute-done | bytes 524320 | tf_op jit(solution)/shard_map/ppermute | solution.py:17
  206.3 8.6 %collective-permute-done.6 = f32[16,64,128]{2,1,0:T(8,128)S(1)} collective-permute-done((f32[16,64,128]{2,1,0:T(8,128)S(1)}, f32[16,64,128]{2,1,0:T(8,128)S(1)}, u32[]{:S(2)}, u32[]{:S(2)}) %collective-permute-start.6) | collective-permute-done | bytes 524320 | tf_op jit(solution)/shard_map/ppermute | solution.py:17
  218.4 23.4 %collective-permute-done.8 = f32[16,64,128]{2,1,0:T(8,128)S(1)} collective-permute-done((f32[16,64,128]{2,1,0:T(8,128)S(1)}, f32[16,64,128]{2,1,0:T(8,128)S(1)}, u32[]{:S(2)}, u32[]{:S(2)}) %collective-permute-start.8) | collective-permute-done | bytes 524320 | tf_op jit(solution)/shard_map/ppermute | solution.py:17
  246.0 11.3 %collective-permute-done.9 = f32[16,64,128]{2,1,0:T(8,128)S(1)} collective-permute-done((f32[16,64,128]{2,1,0:T(8,128)S(1)}, f32[16,64,128]{2,1,0:T(8,128)S(1)}, u32[]{:S(2)}, u32[]{:S(2)}) %collective-permute-start.9) | collective-permute-done | bytes 524320 | tf_op jit(solution)/shard_map/ppermute | solution.py:17
  257.3 6.8 %add_convert_fusion.car_ref = bf16[16,1024,128]{2,1,0:T(8,128)(2,1)} fusion(f32[16,1024,128]{2,1,0:T(8,128)} %fusion.14, f32[1024,128]{1,0:T(8,128)S(1)} %bitcast.98, f32[16,1024]{1,0:T(8,128)S(1)} %mul.805), kind=kLoop, calls=%fused_computation.2 | loop fusion | flops 6291456 | bytes 13172736 | tf_op jit(solution)/shard_map/convert_element_type | solution.py:273
  264.1 20.6 %shard_map.137 = (f32[2048,1024]{1,0:T(8,128)}, f32[2048,1]{1,0:T(8,128)}) custom-call(bf16[2048,1280]{1,0:T(8,128)(2,1)} %multiply_convert_fusion.x_ref.b_ref.c_ref, bf16[2048,1280]{1,0:T(8,128)(2,1)} %multiply_convert_fusion.x_ref.b_ref.c_ref, bf16[2048,1280]{1,0:T(8,128)(2,1)} %multiply_convert_fusion.x_ref.b_ref.c_ref, f32[16,128,16]{2,1,0:T(8,128)} %bitcast.90, ...), custom_call_target="tpu_custom_call" | custom-call | flops 3288334336 | bytes 25165824 | tf_op jit(solution)/shard_map/pallas_call | solution.py:125
  284.7 7.9 %psum.7 = f32[2048,1]{1,0:T(8,128)S(1)} all-reduce(f32[2048,1]{1,0:T(8,128)} %get-tuple-element.8), channel_id=1, replica_groups=mesh['seq'=16,'head'=2] {'head'}, use_global_device_ids=true, to_apply=%region_4.5 | all-reduce | flops 2048 | bytes 16384 | tf_op jit(solution)/shard_map/psum | solution.py:276
  293.0 5.2 %multiply_convert_fusion.1 = bf16[2048,1024]{1,0:T(8,128)(2,1)} fusion(f32[2048,1024]{1,0:T(8,128)} %get-tuple-element.7, f32[1024]{0:T(1024)S(1)} %copy-done.12, f32[2048]{0:T(1024)S(1)} %rsqrt_reduce_fusion), kind=kLoop, calls=%fused_computation.1 | loop fusion | flops 6291456 | bytes 12595200 | tf_op jit(solution)/shard_map/convert_element_type | solution.py:277
  (162 shorter events, 61.0 us)
Async XLA Ops:
  8.8 10.2 %all-to-all-start = ((bf16[16,1,1]{2,1,0:T(2,128)(2,1)}), bf16[16,1,1]{2,1,0:T(2,128)(2,1)S(1)}, u32[]{:S(2)}, u32[]{:S(2)}) async-start(bf16[16,1,1]{2,1,0:T(2,128)(2,1)} %copy.62), calls=%async_computation | async-start | bytes 16384 | tf_op jit(solution)/shard_map/all_to_all | solution.py:196
  19.1 55.7 %copy-start.10 = (s32[16]{0:T(128)S(1)}, s32[16]{0:T(128)}, u32[]{:S(2)}) copy-start(s32[16]{0:T(128)} %param.16) | copy-start | bytes 196
  19.1 51.7 %all-to-all-start.1 = ((bf16[16,128,512]{2,1,0:T(8,128)(2,1)}), bf16[16,128,512]{2,1,0:T(8,128)(2,1)S(1)}, u32[]{:S(2)}, u32[]{:S(2)}) async-start(bf16[16,128,512]{2,1,0:T(8,128)(2,1)} %copy.64), calls=%async_computation.1 | async-start | bytes 4194304 | tf_op jit(solution)/shard_map/all_to_all | solution.py:195
  25.6 66.1 %all-gather.2.cloned.1.call-start = ((), (), s32[]{:S(2)}) async-start(), calls=%async_computation.2 | async-start | bytes 6291456 | tf_op jit(solution)/shard_map/all_gather | solution.py:206
  72.2 13.0 %copy-start.11 = (f32[4,1024]{1,0:T(4,128)S(1)}, f32[4,1024]{1,0:T(4,128)}, u32[]{:S(2)}) copy-start(f32[4,1024]{1,0:T(4,128)} %param.22) | copy-start | bytes 49156
  72.2 13.0 %copy-start.13 = (f32[4,256]{1,0:T(4,128)S(1)}, f32[4,256]{1,0:T(4,128)}, u32[]{:S(2)}) copy-start(f32[4,256]{1,0:T(4,128)} %param.23) | copy-start | bytes 12292
  72.2 13.0 %copy-start.14 = (f32[1024]{0:T(1024)S(1)}, f32[1024]{0:T(1024)}, u32[]{:S(2)}) copy-start(f32[1024]{0:T(1024)} %param.24) | copy-start | bytes 12292
  72.2 14.2 %copy-start.19 = (f32[16]{0:T(128)S(1)}, f32[16]{0:T(128)}, u32[]{:S(2)}) copy-start(f32[16]{0:T(128)} %param.21) | copy-start | bytes 196
  72.2 19.5 %copy-start.9 = (bf16[1024,16]{0,1:T(8,128)(2,1)S(1)}, bf16[1024,16]{0,1:T(8,128)(2,1)}, u32[]{:S(2)}) copy-start(bf16[1024,16]{0,1:T(8,128)(2,1)} %param.19) | copy-start | bytes 98308
  72.3 19.4 %copy-start.15 = (f32[16]{0:T(128)S(1)}, f32[16]{0:T(128)}, u32[]{:S(2)}) copy-start(f32[16]{0:T(128)} %param.20) | copy-start | bytes 196
  76.4 11.9 %collective-permute-start = (bf16[3]{0:T(256)(128)(2,1)S(1)}, bf16[3]{0:T(256)(128)(2,1)S(1)}, u32[]{:S(2)}, u32[]{:S(2)}) collective-permute-start(bf16[3]{0:T(256)(128)(2,1)S(1)} %fusion.45), channel_id=1, source_target_pairs={{0,2},{2,4},{4,6},{6,8},{8,10},{10,12},{12,14},{14,16},{16,18},{18... | collective-permute-start | bytes 26 | tf_op jit(solution)/shard_map/ppermute | solution.py:17
  95.5 13.7 %copy-start.8 = (f32[16,16,128]{2,1,0:T(8,128)}, f32[16,16,128]{2,1,0:T(8,128)S(1)}, u32[]{:S(2)}) copy-start(f32[16,16,128]{2,1,0:T(8,128)S(1)} %fusion.16.cumt_ref) | copy-start | bytes 393220
  95.8 32.0 %copy-start.6 = (f32[16,16,128]{1,2,0:T(8,128)}, f32[16,16,128]{1,2,0:T(8,128)S(1)}, u32[]{:S(2)}) copy-start(f32[16,16,128]{1,2,0:T(8,128)S(1)} %copy.71) | copy-start | bytes 393220
  116.6 21.3 %collective-permute-start.1 = (bf16[3,1280]{1,0:T(4,128)(2,1)S(1)}, bf16[3,1280]{1,0:T(4,128)(2,1)S(1)}, u32[]{:S(2)}, u32[]{:S(2)}) collective-permute-start(bf16[3,1280]{1,0:T(4,128)(2,1)S(1)} %fusion.26), channel_id=1, source_target_pairs={{0,2},{2,4},{4,6},{6,8},{8,10},{10,12},{12,14},{14,16},{16,18},{18... | collective-permute-start | bytes 23048 | tf_op jit(solution)/shard_map/ppermute | solution.py:17
  120.4 9.0 %collective-permute-start.3 = (f32[16]{0:T(128)S(1)}, f32[16]{0:T(128)S(1)}, u32[]{:S(2)}, u32[]{:S(2)}) collective-permute-start(f32[16]{0:T(128)S(1)} %slice_bitcast_fusion), channel_id=1, source_target_pairs={{0,2},{2,4},{4,6},{6,8},{8,10},{10,12},{12,14},{14,16},{16,18},{18... | collective-permute-start | bytes 200 | tf_op jit(solution)/shard_map/ppermute | solution.py:17
  129.4 4.3 %collective-permute-start.5 = (f32[16]{0:T(128)S(1)}, f32[16]{0:T(128)S(1)}, u32[]{:S(2)}, u32[]{:S(2)}) collective-permute-start(f32[16]{0:T(128)S(1)} %broadcast_select_fusion.2), channel_id=1, source_target_pairs={{0,4},{2,6},{4,8},{6,10},{8,12},{10,14},{12,16},{14,18},{16,20},{1... | collective-permute-start | bytes 200 | tf_op jit(solution)/shard_map/ppermute | solution.py:17
  133.7 4.3 %collective-permute-start.7 = (f32[16]{0:T(128)S(1)}, f32[16]{0:T(128)S(1)}, u32[]{:S(2)}, u32[]{:S(2)}) collective-permute-start(f32[16]{0:T(128)S(1)} %broadcast_select_fusion.1), channel_id=1, source_target_pairs={{0,8},{2,10},{4,12},{6,14},{8,16},{10,18},{12,20},{14,22},{16,24},... | collective-permute-start | bytes 200 | tf_op jit(solution)/shard_map/ppermute | solution.py:17
  176.0 14.3 %collective-permute-start.2 = (f32[16,64,128]{2,1,0:T(8,128)S(1)}, f32[16,64,128]{2,1,0:T(8,128)S(1)}, u32[]{:S(2)}, u32[]{:S(2)}) collective-permute-start(f32[16,64,128]{2,1,0:T(8,128)S(1)} %bitcast.94), channel_id=1, source_target_pairs={{0,2},{2,4},{4,6},{6,8},{8,10},{10,12},{12,14},{14,16},{16,18},{18... | collective-permute-start | bytes 1572872 | tf_op jit(solution)/shard_map/ppermute | solution.py:17
  190.5 12.2 %collective-permute-start.4 = (f32[16,64,128]{2,1,0:T(8,128)S(1)}, f32[16,64,128]{2,1,0:T(8,128)S(1)}, u32[]{:S(2)}, u32[]{:S(2)}) collective-permute-start(f32[16,64,128]{2,1,0:T(8,128)S(1)} %multiply_add_fusion.3), channel_id=1, source_target_pairs={{0,4},{2,6},{4,8},{6,10},{8,12},{10,14},{12,16},{14,18},{16,20},{1... | collective-permute-start | bytes 1572872 | tf_op jit(solution)/shard_map/ppermute | solution.py:17
  202.8 12.0 %collective-permute-start.6 = (f32[16,64,128]{2,1,0:T(8,128)S(1)}, f32[16,64,128]{2,1,0:T(8,128)S(1)}, u32[]{:S(2)}, u32[]{:S(2)}) collective-permute-start(f32[16,64,128]{2,1,0:T(8,128)S(1)} %multiply_add_fusion.2), channel_id=1, source_target_pairs={{0,8},{2,10},{4,12},{6,14},{8,16},{10,18},{12,20},{14,22},{16,24},... | collective-permute-start | bytes 1572872 | tf_op jit(solution)/shard_map/ppermute | solution.py:17
  215.0 26.8 %collective-permute-start.8 = (f32[16,64,128]{2,1,0:T(8,128)S(1)}, f32[16,64,128]{2,1,0:T(8,128)S(1)}, u32[]{:S(2)}, u32[]{:S(2)}) collective-permute-start(f32[16,64,128]{2,1,0:T(8,128)S(1)} %multiply_add_fusion.1), channel_id=1, source_target_pairs={{0,16},{2,18},{4,20},{6,22},{8,24},{10,26},{12,28},{14,30},{1,17},... | collective-permute-start | bytes 1572872 | tf_op jit(solution)/shard_map/ppermute | solution.py:17
  241.9 15.4 %collective-permute-start.9 = (f32[16,64,128]{2,1,0:T(8,128)S(1)}, f32[16,64,128]{2,1,0:T(8,128)S(1)}, u32[]{:S(2)}, u32[]{:S(2)}) collective-permute-start(f32[16,64,128]{2,1,0:T(8,128)S(1)} %multiply_add_fusion), channel_id=1, source_target_pairs={{0,2},{2,4},{4,6},{6,8},{8,10},{10,12},{12,14},{14,16},{16,18},{18... | collective-permute-start | bytes 1572872 | tf_op jit(solution)/shard_map/ppermute | solution.py:17
  264.1 28.9 %copy-start.12 = (f32[1024]{0:T(1024)S(1)}, f32[1024]{0:T(1024)}, u32[]{:S(2)}) copy-start(f32[1024]{0:T(1024)} %param.27) | copy-start | bytes 12292
  264.1 34.1 %copy-start.1 = (bf16[16,128,512]{2,1,0:T(8,128)(2,1)S(1)}, bf16[16,128,512]{2,1,0:T(8,128)(2,1)}, u32[]{:S(2)}) copy-start(bf16[16,128,512]{2,1,0:T(8,128)(2,1)} %param.14) | copy-start | bytes 6291460
  (9 other events, 69.0 us)
Sparse Core Ops, SparseCore 0:
  74.9 16.7 all-gather.1

commit v5 on v4

--- a/solution.py
+++ b/solution.py
@@ -55,10 +55,7 @@
             [jnp.where(first_half, x_pair, zero), jnp.where(first_half, zero, x_pair)], axis=0
         )
         intra = jnp.dot(weights, split_x, preferred_element_type=f32)
-        carried = car_ref[0, cols, :]
-        projected = lax.dot_general(
-            c_mat, carried, (((1,), (1,)), ((), ())), preferred_element_type=f32
-        )
+        projected = jnp.dot(c_mat, car_ref[0, :, cols], preferred_element_type=f32)
         grow = jnp.where(
             first_half,
             jnp.exp(cum[:, 2 * pair : 2 * pair + 1]),
@@ -73,11 +70,11 @@
     sq_ref[...] = jnp.sum(total_sq, axis=1, keepdims=True)
 
 
-def contrib_tile(x_ref, b_ref, end_ref, out_ref):
+def contrib_tile(x_ref, bt_ref, end_ref, out_ref):
     f32 = jnp.float32
     tile_len = x_ref.shape[0]
     pairs = x_ref.shape[1] // 128
-    b_mat = b_ref[...]
+    b_t = bt_ref[0]
     to_end = end_ref[0]
     first_half = lax.broadcasted_iota(jnp.int32, (tile_len, 128), 1) < 64
     for pair in range(pairs):
@@ -86,36 +83,33 @@
             first_half, to_end[:, 2 * pair : 2 * pair + 1], to_end[:, 2 * pair + 1 : 2 * pair + 2]
         )
         scaled = (x_ref[:, cols].astype(f32) * scale).astype(jnp.bfloat16)
-        out_ref[0, cols, :] = lax.dot_general(
-            scaled, b_mat, (((0,), (0,)), ((), ())), preferred_element_type=f32
-        )
-
-
-def contrib_tiles(conv_out, to_end, inner_here, state_dim):
+        out_ref[0, :, cols] = jnp.dot(b_t, scaled, preferred_element_type=f32)
+
+
+def contrib_tiles(conv_out, b_t, to_end, inner_here, state_dim):
     tiles_dev, tile_len, heads_here = to_end.shape
-    b_block = inner_here // 128
     return pl.pallas_call(
         contrib_tile,
         grid=(tiles_dev,),
         in_specs=[
             pl.BlockSpec((tile_len, inner_here), lambda j: (j, 0)),
-            pl.BlockSpec((tile_len, state_dim), lambda j: (j, b_block)),
+            pl.BlockSpec((1, state_dim, tile_len), lambda j: (j, 0, 0)),
             pl.BlockSpec((1, tile_len, heads_here), lambda j: (j, 0, 0)),
         ],
-        out_specs=pl.BlockSpec((1, inner_here, state_dim), lambda j: (j, 0, 0)),
-        out_shape=jax.ShapeDtypeStruct((tiles_dev, inner_here, state_dim), jnp.float32),
+        out_specs=pl.BlockSpec((1, state_dim, inner_here), lambda j: (j, 0, 0)),
+        out_shape=jax.ShapeDtypeStruct((tiles_dev, state_dim, inner_here), jnp.float32),
         cost_estimate=pl.CostEstimate(
             flops=tiles_dev * 2 * tile_len * inner_here * state_dim,
             transcendentals=0,
             bytes_accessed=tiles_dev * (tile_len * (inner_here + state_dim) * 2 + inner_here * state_dim * 4),
         ),
-    )(conv_out, conv_out, to_end)
+    )(conv_out, b_t, to_end)
 
 
 def mix_tiles(conv_out, zx, cumul, cumul_t, dt_t, later, carried, d_full):
     tiles_dev, tile_len, heads_here = cumul.shape
-    inner_here = carried.shape[1]
-    state_dim = carried.shape[2]
+    inner_here = carried.shape[2]
+    state_dim = carried.shape[1]
     rows = tiles_dev * tile_len
     b_block = inner_here // 128
     c_block = b_block + state_dim // 128
@@ -134,7 +128,7 @@
             pl.BlockSpec((1, heads_here, tile_len), per_tile),
             pl.BlockSpec((1, tile_len, 1), per_tile),
             pl.BlockSpec((1, 1, tile_len), per_tile),
-            pl.BlockSpec((1, inner_here, state_dim), per_tile),
+            pl.BlockSpec((1, state_dim, inner_here), per_tile),
             pl.BlockSpec((tile_len, inner_here), lambda j: (j, 0)),
             pl.BlockSpec((1, inner_here), lambda j: (0, 0)),
         ],
@@ -245,32 +239,35 @@
     last_part = later[:, tile_len - 1]
     tail_keep = (later == last_part[:, None]).astype(jnp.float32)
     to_end = jnp.exp(cumul[:, tile_len - 1 :, :] - cumul) * tile_dt * tail_keep[:, :, None]
-    contrib = contrib_tiles(conv_out, to_end, inner_here, state_dim).reshape(
-        tiles_dev, heads_here, head_dim, state_dim
-    )
+    b_t = conv_out[:, inner_here : inner_here + state_dim].reshape(
+        tiles_dev, tile_len, state_dim
+    ).transpose(0, 2, 1)
+    contrib = contrib_tiles(conv_out, b_t, to_end, inner_here, state_dim)
     passing = jnp.exp(cumul[:, tile_len - 1, :]) * (1.0 - has_bound)[:, None]
     through = jnp.cumprod(passing, 0)
     prefix = jnp.concatenate([jnp.ones((1, heads_here), jnp.float32), through[:-1]], 0)
     reverse = jnp.cumprod(passing[::-1], 0)[::-1]
     to_last = jnp.concatenate([reverse[1:], jnp.ones((1, heads_here), jnp.float32)], 0)
-    run_state = jnp.sum(to_last[:, :, None, None] * contrib, 0)
-    running = jnp.zeros((heads_here, head_dim, state_dim), jnp.float32)
+    widen = lambda per_head: jnp.repeat(per_head, head_dim, axis=-1)
+    run_state = jnp.sum(widen(to_last)[:, None, :] * contrib, 0)
+    passing_wide = widen(passing)
+    running = jnp.zeros((state_dim, inner_here), jnp.float32)
     states = []
     for tile in range(tiles_dev):
         states.append(running)
-        running = passing[tile][:, None, None] * running + contrib[tile]
+        running = passing_wide[tile][None, :] * running + contrib[tile]
     before_tile = jnp.stack(states)
     position = lax.axis_index("seq")
-    run_decay = through[tiles_dev - 1]
+    run_decay = widen(through[tiles_dev - 1])
     distance = 1
     while distance < seq_count:
         got_decay, got_state = shifted((run_decay, run_state), "seq", distance)
-        run_state = run_state + run_decay[:, None, None] * got_state
+        run_state = run_state + run_decay[None, :] * got_state
         run_decay = jnp.where(position >= distance, run_decay * got_decay, run_decay)
         distance *= 2
     entering = shifted(run_state, "seq", 1)
-    tile_state = before_tile + prefix[:, :, None, None] * entering[None]
-    carried = tile_state.astype(jnp.bfloat16).reshape(tiles_dev, inner_here, state_dim)
+    tile_state = before_tile + widen(prefix)[:, None, :] * entering[None]
+    carried = tile_state.astype(jnp.bfloat16)
     d_full = jnp.repeat(d_skip, head_dim)[None, :]
     gated, row_sq = mix_tiles(conv_out, zx, cumul, cumul_t, dt_t, later, carried, d_full)
     sums = lax.psum(row_sq, "head")

time: 307 us -> 300 us (0.977)
  other arithmetic: 56.3 us -> 51.3 us
    mul x35 -> x4, local copies, waits for them, and re-layouts: 6.09 us -> 0.34 us  [the longest x1 0.1 us: shards(): tile_state = before_tile + widen(prefix)[:, None, :] * entering[None]]
    unnamed x44 -> x46, local copies, waits for them, and re-layouts: 12 us -> 13.7 us
  transfers between devices with their start and end apart: 13 -> 13, of which waited for: 9 -> 8; matrix products, arithmetic and copies ran while one was open for 13% -> 19% of each run, Pallas kernels for 0% -> 5%
where the time goes in v5:
time: 300 us; the launch traced here: 295 us
  waiting for transfers between devices  109 us (36%)
  other arithmetic  51.3 us (17%)
  Pallas kernels  35.8 us (12%)
  starting transfers between devices  32.2 us (11%)
  local copies, waits for them, and re-layouts  26.8 us (9%)
  matrix products  18.1 us (6%)
  between operations  14 us (5%)
  blocking collectives  8.34 us (3%)
    ppermute x10, waiting for transfers between devices, shifted(): return lax.ppermute(x, axis, pairs)  60.4 us
    all_to_all x1, waiting for transfers between devices, shards(): lax.all_to_all(outgoing, 'seq', split_axis=0, concat_axis=0, tiled=True)  45 us
    pallas_call x1, Pallas kernels, mix_tiles(): pl.pallas_call(mix_tile, grid=(tiles_dev,), in_specs=[pl.BlockSpec((tile_...  20.4 us
    ppermute x10, starting transfers between devices, shifted(): return lax.ppermute(x, axis, pairs)  19.3 us
    pallas_call x1, Pallas kernels, contrib_tiles(): pl.pallas_call(contrib_tile, grid=(tiles_dev,), in_specs=[pl.BlockSpec((t...  15.4 us
    dot_general x3, matrix products, shards(): jnp.dot(piece, weight, preferred_element_type=jnp.float32)  14.4 us
    unnamed x46, local copies, waits for them, and re-layouts  13.7 us
    unnamed x14, other arithmetic  12.9 us
  transfers between devices with their start and end apart: 13, of which 8 were waited for; matrix products, arithmetic and copies ran while one was open for 19% of the time, Pallas kernels for 5%

profile of v5, /device:TPU:29, one launch (start us, length us, event | category | flops | bytes accessed | tf_op | source)
XLA Modules:
  0.0 295.2 jit_solution(1349861984413214292)
XLA Ops:
  8.8 6.4 %all-to-all-start = ((bf16[16,1,1]{2,1,0:T(2,128)(2,1)}), bf16[16,1,1]{2,1,0:T(2,128)(2,1)S(1)}, u32[]{:S(2)}, u32[]{:S(2)}) async-start(bf16[16,1,1]{2,1,0:T(2,128)(2,1)} %copy.67), calls=%async_computation | async-start | bytes 16384 | tf_op jit(solution)/shard_map/all_to_all | solution.py:190
  16.6 2.5 copy.69
  19.1 6.5 %all-to-all-start.1 = ((bf16[16,128,512]{2,1,0:T(8,128)(2,1)}), bf16[16,128,512]{2,1,0:T(8,128)(2,1)S(1)}, u32[]{:S(2)}, u32[]{:S(2)}) async-start(bf16[16,128,512]{2,1,0:T(8,128)(2,1)} %copy.69), calls=%async_computation.1 | async-start | bytes 4194304 | tf_op jit(solution)/shard_map/all_to_all | solution.py:189
  25.8 45.0 %all-to-all-done.1 = bf16[16,128,512]{2,1,0:T(8,128)(2,1)S(1)} async-done(((bf16[16,128,512]{2,1,0:T(8,128)(2,1)}), bf16[16,128,512]{2,1,0:T(8,128)(2,1)S(1)}, u32[]{:S(2)}, u32[]{:S(2)}) %all-to-all-start.1) | async-done | bytes 2097184 | tf_op jit(solution)/shard_map/all_to_all | solution.py:189
  72.3 2.5 copy.71
  78.8 5.6 %copy.83 = bf16[128,8,2,1024]{3,1,2,0:T(8,128)(2,1)} copy(bf16[128,8,2,1024]{3,2,1,0:T(2,128)(2,1)} %bitcast.90) | data formatting | bytes 8388608
  88.4 3.3 %all-gather.2.cloned.1.call-done = bf16[2048,1024]{1,0:T(8,128)(2,1)} async-done(((bf16[2048,512]{1,0:T(8,128)(2,1)}), bf16[2048,1024]{1,0:T(8,128)(2,1)}) %all-gather.2.cloned.1.call-update) | async-done | bytes 4194320 | tf_op jit(solution)/shard_map/all_gather | solution.py:200
  91.7 11.9 %convolution_convert_fusion.gate_ref = bf16[2048,2048]{1,0:T(8,128)(2,1)S(1)} fusion(bf16[2048,1024]{1,0:T(8,128)(2,1)} %all-gather.2.cloned.1.call-done, bf16[1024,2048]{1,0:T(8,128)(2,1)} %bitcast.91), kind=kOutput, calls=%fused_computation.4 | convolution fusion | flops 8594128896 | bytes 16777216 | tf_op jit(solution)/shard_map/dot_general | solution.py:202
  104.3 4.5 %copy-done.8 = bf16[2048,1024]{1,0:T(8,128)(2,1)S(1)} copy-done((bf16[2048,1024]{1,0:T(8,128)(2,1)S(1)}, bf16[2048,1024]{1,0:T(8,128)(2,1)}, u32[]{:S(2)}) %copy-start.8) | copy-done | bytes 4194328
  110.3 3.1 %collective-permute-start.1 = (bf16[3,1280]{1,0:T(4,128)(2,1)S(1)}, bf16[3,1280]{1,0:T(4,128)(2,1)S(1)}, u32[]{:S(2)}, u32[]{:S(2)}) collective-permute-start(bf16[3,1280]{1,0:T(4,128)(2,1)S(1)} %fusion.26), channel_id=1, source_target_pairs={{0,2},{2,4},{4,6},{6,8},{8,10},{10,12},{12,14},{14,16},{16,18},{18... | collective-permute-start | bytes 23048 | tf_op jit(solution)/shard_map/ppermute | solution.py:17
  124.4 3.8 %maximum_maximum_fusion = bf16[2051,1280]{1,0:T(8,128)(2,1)S(1)} fusion(bf16[2048,256]{1,0:T(8,128)(2,1)S(1)} %convolution_convert_fusion.1, bf16[2048,1024]{1,0:T(8,128)(2,1)} %copy-done.4, bf16[3,1280]{1,0:T(4,128)(2,1)S(1)} %collective-permute-done.1), kind=kLoop, calls=%fused_computation.7 | loop fusion | flops 15751680 | bytes 10501120 | tf_op jit(solution)/shard_map/concatenate | solution.py:217
  128.2 10.8 %multiply_convert_fusion.x_ref.b_ref.c_ref = bf16[2048,1280]{1,0:T(8,128)(2,1)S(1)} fusion(bf16[2048,256]{1,0:T(8,128)(2,1)S(1)} %convolution_convert_fusion.1, bf16[2051,1280]{1,0:T(8,128)(2,1)S(1)} %maximum_maximum_fusion, f32[1280]{0:T(1024)S(1)} %get-tuple-element.10, f32[1280]{0:T(1024)S(1)} %get-tuple-element.11, f32[1280]{0:T(1024)S(1)} %get-tuple-element.12, ...), kind=kLoop, calls=%fused_computation | loop fusion | flops 60293120 | bytes 26246144 | tf_op jit(solution)/shard_map/convert_element_type | solution.py:230
  142.5 15.4 %shard_map.136 = f32[16,128,1024]{2,1,0:T(8,128)} custom-call(bf16[2048,1280]{1,0:T(8,128)(2,1)} %copy-done.2, bf16[16,128,128]{2,1,0:T(8,128)(2,1)} %bitcast.93, f32[16,128,16]{2,1,0:T(8,128)} %multiply_multiply_fusion.end_ref), custom_call_target="tpu_custom_call" | custom-call | flops 536870912 | bytes 13107200 | tf_op jit(solution)/shard_map/pallas_call | solution.py:91
  157.8 4.7 %multiply_reduce_fusion = f32[128,1024]{1,0:T(8,128)S(1)} fusion(f32[16,128,1024]{2,1,0:T(8,128)} %shard_map.136, f32[16,1024]{1,0:T(8,128)S(1)} %mul.447), kind=kLoop, calls=%fused_computation.3 | loop fusion | flops 4063232 | bytes 8978432 | tf_op jit(solution)/shard_map/reduce_sum | solution.py:252
  171.0 8.1 %collective-permute-done.2 = f32[128,1024]{1,0:T(8,128)S(1)} collective-permute-done((f32[128,1024]{1,0:T(8,128)S(1)}, f32[128,1024]{1,0:T(8,128)S(1)}, u32[]{:S(2)}, u32[]{:S(2)}) %collective-permute-start.2) | collective-permute-done | bytes 524320 | tf_op jit(solution)/shard_map/ppermute | solution.py:17
  182.3 10.2 %collective-permute-done.4 = f32[128,1024]{1,0:T(8,128)S(1)} collective-permute-done((f32[128,1024]{1,0:T(8,128)S(1)}, f32[128,1024]{1,0:T(8,128)S(1)}, u32[]{:S(2)}, u32[]{:S(2)}) %collective-permute-start.4) | collective-permute-done | bytes 524320 | tf_op jit(solution)/shard_map/ppermute | solution.py:17
  195.8 9.3 %collective-permute-done.6 = f32[128,1024]{1,0:T(8,128)S(1)} collective-permute-done((f32[128,1024]{1,0:T(8,128)S(1)}, f32[128,1024]{1,0:T(8,128)S(1)}, u32[]{:S(2)}, u32[]{:S(2)}) %collective-permute-start.6) | collective-permute-done | bytes 524320 | tf_op jit(solution)/shard_map/ppermute | solution.py:17
  211.7 20.4 %collective-permute-done.8 = f32[128,1024]{1,0:T(8,128)S(1)} collective-permute-done((f32[128,1024]{1,0:T(8,128)S(1)}, f32[128,1024]{1,0:T(8,128)S(1)}, u32[]{:S(2)}, u32[]{:S(2)}) %collective-permute-start.8) | collective-permute-done | bytes 524320 | tf_op jit(solution)/shard_map/ppermute | solution.py:17
  232.2 2.9 collective-permute-start.9
  237.0 10.3 %collective-permute-done.9 = f32[128,1024]{1,0:T(8,128)S(1)} collective-permute-done((f32[128,1024]{1,0:T(8,128)S(1)}, f32[128,1024]{1,0:T(8,128)S(1)}, u32[]{:S(2)}, u32[]{:S(2)}) %collective-permute-start.9) | collective-permute-done | bytes 524320 | tf_op jit(solution)/shard_map/ppermute | solution.py:17
  247.3 6.8 %add_convert_fusion.car_ref = bf16[16,128,1024]{2,1,0:T(8,128)(2,1)} fusion(f32[16,128,1024]{2,1,0:T(8,128)} %fusion.14, f32[128,1024]{1,0:T(8,128)S(1)} %collective-permute-done.9, f32[16,1024]{1,0:T(8,128)S(1)} %mul.445), kind=kLoop, calls=%fused_computation.2 | loop fusion | flops 6291456 | bytes 13172736 | tf_op jit(solution)/shard_map/convert_element_type | solution.py:270
  254.1 20.4 %shard_map.137 = (f32[2048,1024]{1,0:T(8,128)}, f32[2048,1]{1,0:T(8,128)}) custom-call(bf16[2048,1280]{1,0:T(8,128)(2,1)} %copy-done.2, bf16[2048,1280]{1,0:T(8,128)(2,1)} %copy-done.2, bf16[2048,1280]{1,0:T(8,128)(2,1)} %copy-done.2, f32[16,128,16]{2,1,0:T(8,128)} %bitcast.88, f32[16,16,128]{2,1,0:T(8,128)} %copy-done.9, ...), custom_call_target="tpu_custom_call" | custom-call | flops 3288334336 | bytes 25165824 | tf_op jit(solution)/shard_map/pallas_call | solution.py:119
  274.5 8.3 %psum.7 = f32[2048,1]{1,0:T(8,128)S(1)} all-reduce(f32[2048,1]{1,0:T(8,128)} %get-tuple-element.8), channel_id=1, replica_groups=mesh['seq'=16,'head'=2] {'head'}, use_global_device_ids=true, to_apply=%region_4.5 | all-reduce | flops 2048 | bytes 16384 | tf_op jit(solution)/shard_map/psum | solution.py:273
  283.2 5.2 %multiply_convert_fusion.1 = bf16[2048,1024]{1,0:T(8,128)(2,1)} fusion(f32[2048,1024]{1,0:T(8,128)} %get-tuple-element.7, f32[1024]{0:T(1024)S(1)} %copy-done.13, f32[2048]{0:T(1024)S(1)} %rsqrt_reduce_fusion), kind=kLoop, calls=%fused_computation.1 | loop fusion | flops 6291456 | bytes 12595200 | tf_op jit(solution)/shard_map/convert_element_type | solution.py:274
  (168 shorter events, 53.3 us)
Async XLA Ops:
  8.8 10.2 %all-to-all-start = ((bf16[16,1,1]{2,1,0:T(2,128)(2,1)}), bf16[16,1,1]{2,1,0:T(2,128)(2,1)S(1)}, u32[]{:S(2)}, u32[]{:S(2)}) async-start(bf16[16,1,1]{2,1,0:T(2,128)(2,1)} %copy.67), calls=%async_computation | async-start | bytes 16384 | tf_op jit(solution)/shard_map/all_to_all | solution.py:190
  19.1 55.7 %copy-start.11 = (s32[16]{0:T(128)S(1)}, s32[16]{0:T(128)}, u32[]{:S(2)}) copy-start(s32[16]{0:T(128)} %param.16) | copy-start | bytes 196
  19.1 51.8 %all-to-all-start.1 = ((bf16[16,128,512]{2,1,0:T(8,128)(2,1)}), bf16[16,128,512]{2,1,0:T(8,128)(2,1)S(1)}, u32[]{:S(2)}, u32[]{:S(2)}) async-start(bf16[16,128,512]{2,1,0:T(8,128)(2,1)} %copy.69), calls=%async_computation.1 | async-start | bytes 4194304 | tf_op jit(solution)/shard_map/all_to_all | solution.py:189
  25.6 66.1 %all-gather.2.cloned.1.call-start = ((), (), s32[]{:S(2)}) async-start(), calls=%async_computation.2 | async-start | bytes 6291456 | tf_op jit(solution)/shard_map/all_gather | solution.py:200
  72.2 12.3 %copy-start.18 = (f32[16]{0:T(128)S(1)}, f32[16]{0:T(128)}, u32[]{:S(2)}) copy-start(f32[16]{0:T(128)} %param.26) | copy-start | bytes 196
  72.2 13.0 %copy-start.12 = (f32[4,1024]{1,0:T(4,128)S(1)}, f32[4,1024]{1,0:T(4,128)}, u32[]{:S(2)}) copy-start(f32[4,1024]{1,0:T(4,128)} %param.22) | copy-start | bytes 49156
  72.2 13.0 %copy-start.14 = (f32[4,256]{1,0:T(4,128)S(1)}, f32[4,256]{1,0:T(4,128)}, u32[]{:S(2)}) copy-start(f32[4,256]{1,0:T(4,128)} %param.23) | copy-start | bytes 12292
  72.2 13.0 %copy-start.15 = (f32[1024]{0:T(1024)S(1)}, f32[1024]{0:T(1024)}, u32[]{:S(2)}) copy-start(f32[1024]{0:T(1024)} %param.24) | copy-start | bytes 12292
  72.2 13.0 %copy-start.17 = (f32[256]{0:T(256)S(1)}, f32[256]{0:T(256)}, u32[]{:S(2)}) copy-start(f32[256]{0:T(256)} %param.25) | copy-start | bytes 3076
  72.2 14.2 %copy-start.20 = (f32[16]{0:T(128)S(1)}, f32[16]{0:T(128)}, u32[]{:S(2)}) copy-start(f32[16]{0:T(128)} %param.21) | copy-start | bytes 196
  76.4 11.9 %collective-permute-start = (bf16[3]{0:T(256)(128)(2,1)S(1)}, bf16[3]{0:T(256)(128)(2,1)S(1)}, u32[]{:S(2)}, u32[]{:S(2)}) collective-permute-start(bf16[3]{0:T(256)(128)(2,1)S(1)} %fusion.45), channel_id=1, source_target_pairs={{0,2},{2,4},{4,6},{6,8},{8,10},{10,12},{12,14},{14,16},{16,18},{18... | collective-permute-start | bytes 26 | tf_op jit(solution)/shard_map/ppermute | solution.py:17
  110.3 14.1 %collective-permute-start.1 = (bf16[3,1280]{1,0:T(4,128)(2,1)S(1)}, bf16[3,1280]{1,0:T(4,128)(2,1)S(1)}, u32[]{:S(2)}, u32[]{:S(2)}) collective-permute-start(bf16[3,1280]{1,0:T(4,128)(2,1)S(1)} %fusion.26), channel_id=1, source_target_pairs={{0,2},{2,4},{4,6},{6,8},{8,10},{10,12},{12,14},{14,16},{16,18},{18... | collective-permute-start | bytes 23048 | tf_op jit(solution)/shard_map/ppermute | solution.py:17
  115.6 12.5 %copy-start.9 = (f32[16,16,128]{2,1,0:T(8,128)}, f32[16,16,128]{2,1,0:T(8,128)S(1)}, u32[]{:S(2)}) copy-start(f32[16,16,128]{2,1,0:T(8,128)S(1)} %fusion.22.cumt_ref) | copy-start | bytes 393220
  116.0 23.0 %copy-start.7 = (f32[16,16,128]{1,2,0:T(8,128)}, f32[16,16,128]{1,2,0:T(8,128)S(1)}, u32[]{:S(2)}) copy-start(f32[16,16,128]{1,2,0:T(8,128)S(1)} %copy.76) | copy-start | bytes 393220
  116.6 5.9 %collective-permute-start.3 = (f32[1024]{0:T(1024)S(1)}, f32[1024]{0:T(1024)S(1)}, u32[]{:S(2)}, u32[]{:S(2)}) collective-permute-start(f32[1024]{0:T(1024)S(1)} %mul.450), channel_id=1, source_target_pairs={{0,2},{2,4},{4,6},{6,8},{8,10},{10,12},{12,14},{14,16},{16,18},{18... | collective-permute-start | bytes 12296 | tf_op jit(solution)/shard_map/ppermute | solution.py:17
  122.6 73.2 %collective-permute-start.5 = (f32[1024]{0:T(1024)S(1)}, f32[1024]{0:T(1024)S(1)}, u32[]{:S(2)}, u32[]{:S(2)}) collective-permute-start(f32[1024]{0:T(1024)S(1)} %multiply_select_fusion.2), channel_id=1, source_target_pairs={{0,4},{2,6},{4,8},{6,10},{8,12},{10,14},{12,16},{14,18},{16,20},{1... | collective-permute-start | bytes 12296 | tf_op jit(solution)/shard_map/ppermute | solution.py:17
  162.5 16.6 %collective-permute-start.2 = (f32[128,1024]{1,0:T(8,128)S(1)}, f32[128,1024]{1,0:T(8,128)S(1)}, u32[]{:S(2)}, u32[]{:S(2)}) collective-permute-start(f32[128,1024]{1,0:T(8,128)S(1)} %multiply_reduce_fusion), channel_id=1, source_target_pairs={{0,2},{2,4},{4,6},{6,8},{8,10},{10,12},{12,14},{14,16},{16,18},{18... | collective-permute-start | bytes 1572872 | tf_op jit(solution)/shard_map/ppermute | solution.py:17
  179.2 13.4 %collective-permute-start.4 = (f32[128,1024]{1,0:T(8,128)S(1)}, f32[128,1024]{1,0:T(8,128)S(1)}, u32[]{:S(2)}, u32[]{:S(2)}) collective-permute-start(f32[128,1024]{1,0:T(8,128)S(1)} %multiply_add_fusion.3), channel_id=1, source_target_pairs={{0,4},{2,6},{4,8},{6,10},{8,12},{10,14},{12,16},{14,18},{16,20},{1... | collective-permute-start | bytes 1572872 | tf_op jit(solution)/shard_map/ppermute | solution.py:17
  192.6 12.4 %collective-permute-start.6 = (f32[128,1024]{1,0:T(8,128)S(1)}, f32[128,1024]{1,0:T(8,128)S(1)}, u32[]{:S(2)}, u32[]{:S(2)}) collective-permute-start(f32[128,1024]{1,0:T(8,128)S(1)} %multiply_add_fusion.2), channel_id=1, source_target_pairs={{0,8},{2,10},{4,12},{6,14},{8,16},{10,18},{12,20},{14,22},{16,24},... | collective-permute-start | bytes 1572872 | tf_op jit(solution)/shard_map/ppermute | solution.py:17
  205.1 27.0 %collective-permute-start.8 = (f32[128,1024]{1,0:T(8,128)S(1)}, f32[128,1024]{1,0:T(8,128)S(1)}, u32[]{:S(2)}, u32[]{:S(2)}) collective-permute-start(f32[128,1024]{1,0:T(8,128)S(1)} %multiply_add_fusion.1), channel_id=1, source_target_pairs={{0,16},{2,18},{4,20},{6,22},{8,24},{10,26},{12,28},{14,30},{1,17},... | collective-permute-start | bytes 1572872 | tf_op jit(solution)/shard_map/ppermute | solution.py:17
  207.4 4.3 %collective-permute-start.7 = (f32[1024]{0:T(1024)S(1)}, f32[1024]{0:T(1024)S(1)}, u32[]{:S(2)}, u32[]{:S(2)}) collective-permute-start(f32[1024]{0:T(1024)S(1)} %multiply_select_fusion.1), channel_id=1, source_target_pairs={{0,8},{2,10},{4,12},{6,14},{8,16},{10,18},{12,20},{14,22},{16,24},... | collective-permute-start | bytes 12296 | tf_op jit(solution)/shard_map/ppermute | solution.py:17
  232.2 15.1 %collective-permute-start.9 = (f32[128,1024]{1,0:T(8,128)S(1)}, f32[128,1024]{1,0:T(8,128)S(1)}, u32[]{:S(2)}, u32[]{:S(2)}) collective-permute-start(f32[128,1024]{1,0:T(8,128)S(1)} %multiply_add_fusion), channel_id=1, source_target_pairs={{0,2},{2,4},{4,6},{6,8},{8,10},{10,12},{12,14},{14,16},{16,18},{18... | collective-permute-start | bytes 1572872 | tf_op jit(solution)/shard_map/ppermute | solution.py:17
  254.0 29.1 %copy-start.13 = (f32[1024]{0:T(1024)S(1)}, f32[1024]{0:T(1024)}, u32[]{:S(2)}) copy-start(f32[1024]{0:T(1024)} %param.27) | copy-start | bytes 12292
  254.0 34.3 %copy-start.1 = (bf16[16,128,512]{2,1,0:T(8,128)(2,1)S(1)}, bf16[16,128,512]{2,1,0:T(8,128)(2,1)}, u32[]{:S(2)}) copy-start(bf16[16,128,512]{2,1,0:T(8,128)(2,1)} %param.14) | copy-start | bytes 6291460
  (10 other events, 55.2 us)
Sparse Core Ops, SparseCore 0:
  74.9 16.7 all-gather.1

commit v6 on v5

--- a/solution.py
+++ b/solution.py
@@ -17,29 +17,20 @@
     return lax.ppermute(x, axis, pairs)
 
 
-def mix_tile(
-    x_ref, b_ref, c_ref, cum_ref, cumt_ref, dtt_ref, partc_ref, partr_ref, car_ref, gate_ref, d_ref,
-    out_ref, sq_ref,
-):
+def intra_tile(x_ref, b_ref, c_ref, cumc_ref, cumt_ref, dtt_ref, partc_ref, partr_ref, d_ref, out_ref):
     f32 = jnp.float32
     tile_len = x_ref.shape[0]
     pairs = x_ref.shape[1] // 128
-    b_mat = b_ref[...]
-    c_mat = c_ref[...]
     scores = lax.dot_general(
-        c_mat, b_mat, (((1,), (1,)), ((), ())), preferred_element_type=f32
-    )
-    cum = cum_ref[0]
+        c_ref[...], b_ref[...], (((1,), (1,)), ((), ())), preferred_element_type=f32
+    )
+    cum = cumc_ref[0]
     cumt = cumt_ref[0]
     dtt = dtt_ref[0]
-    part_col = partc_ref[0]
-    part_row = partr_ref[0]
     row = lax.broadcasted_iota(jnp.int32, (tile_len, tile_len), 0)
     col = lax.broadcasted_iota(jnp.int32, (tile_len, tile_len), 1)
-    keep = (row >= col) & (part_col == part_row)
-    earlier = 1.0 - part_col
+    keep = (row >= col) & (partc_ref[0] == partr_ref[0])
     first_half = lax.broadcasted_iota(jnp.int32, (tile_len, 128), 1) < 64
-    total_sq = jnp.zeros((tile_len, 128), f32)
     for pair in range(pairs):
         cols = pl.ds(pair * 128, 128)
         x_pair = x_ref[:, cols]
@@ -55,14 +46,27 @@
             [jnp.where(first_half, x_pair, zero), jnp.where(first_half, zero, x_pair)], axis=0
         )
         intra = jnp.dot(weights, split_x, preferred_element_type=f32)
+        out_ref[:, cols] = intra + d_ref[:, cols] * x_pair.astype(f32)
+
+
+def finish_tile(part_ref, c_ref, cumc_ref, partc_ref, car_ref, gate_ref, out_ref, sq_ref):
+    f32 = jnp.float32
+    tile_len = part_ref.shape[0]
+    pairs = part_ref.shape[1] // 128
+    c_mat = c_ref[...]
+    cum = cumc_ref[0]
+    earlier = 1.0 - partc_ref[0]
+    first_half = lax.broadcasted_iota(jnp.int32, (tile_len, 128), 1) < 64
+    total_sq = jnp.zeros((tile_len, 128), f32)
+    for pair in range(pairs):
+        cols = pl.ds(pair * 128, 128)
         projected = jnp.dot(c_mat, car_ref[0, :, cols], preferred_element_type=f32)
         grow = jnp.where(
             first_half,
             jnp.exp(cum[:, 2 * pair : 2 * pair + 1]),
             jnp.exp(cum[:, 2 * pair + 1 : 2 * pair + 2]),
         )
-        inter = grow * earlier * projected
-        mixed = intra + inter + d_ref[:, cols] * x_pair.astype(f32)
+        mixed = part_ref[:, cols] + grow * earlier * projected
         gate = gate_ref[:, cols].astype(f32)
         gated = mixed * (gate * (0.5 + 0.5 * jnp.tanh(0.5 * gate)))
         out_ref[:, cols] = gated
@@ -106,18 +110,16 @@
     )(conv_out, b_t, to_end)
 
 
-def mix_tiles(conv_out, zx, cumul, cumul_t, dt_t, later, carried, d_full):
+def intra_tiles(conv_out, cumul, cumul_t, dt_t, later, d_full):
     tiles_dev, tile_len, heads_here = cumul.shape
-    inner_here = carried.shape[2]
-    state_dim = carried.shape[1]
+    inner_here = d_full.shape[1]
+    state_dim = 128
     rows = tiles_dev * tile_len
     b_block = inner_here // 128
-    c_block = b_block + state_dim // 128
-    part_col = later.reshape(tiles_dev, tile_len, 1)
-    part_row = later.reshape(tiles_dev, 1, tile_len)
+    c_block = b_block + 1
     per_tile = lambda j: (j, 0, 0)
     return pl.pallas_call(
-        mix_tile,
+        intra_tile,
         grid=(tiles_dev,),
         in_specs=[
             pl.BlockSpec((tile_len, inner_here), lambda j: (j, 0)),
@@ -128,9 +130,37 @@
             pl.BlockSpec((1, heads_here, tile_len), per_tile),
             pl.BlockSpec((1, tile_len, 1), per_tile),
             pl.BlockSpec((1, 1, tile_len), per_tile),
+            pl.BlockSpec((1, inner_here), lambda j: (0, 0)),
+        ],
+        out_specs=pl.BlockSpec((tile_len, inner_here), lambda j: (j, 0)),
+        out_shape=jax.ShapeDtypeStruct((rows, inner_here), jnp.float32),
+        cost_estimate=pl.CostEstimate(
+            flops=tiles_dev * 2 * tile_len * tile_len * (state_dim + 4 * inner_here),
+            transcendentals=tiles_dev * tile_len * tile_len * heads_here,
+            bytes_accessed=rows * inner_here * 6,
+        ),
+    )(
+        conv_out, conv_out, conv_out, cumul, cumul_t, dt_t,
+        later.reshape(tiles_dev, tile_len, 1), later.reshape(tiles_dev, 1, tile_len), d_full,
+    )
+
+
+def finish_tiles(partial, conv_out, zx, cumul, later, carried):
+    tiles_dev, tile_len, heads_here = cumul.shape
+    state_dim, inner_here = carried.shape[1], carried.shape[2]
+    rows = tiles_dev * tile_len
+    c_block = inner_here // 128 + 1
+    per_tile = lambda j: (j, 0, 0)
+    return pl.pallas_call(
+        finish_tile,
+        grid=(tiles_dev,),
+        in_specs=[
+            pl.BlockSpec((tile_len, inner_here), lambda j: (j, 0)),
+            pl.BlockSpec((tile_len, state_dim), lambda j: (j, c_block)),
+            pl.BlockSpec((1, tile_len, heads_here), per_tile),
+            pl.BlockSpec((1, tile_len, 1), per_tile),
             pl.BlockSpec((1, state_dim, inner_here), per_tile),
             pl.BlockSpec((tile_len, inner_here), lambda j: (j, 0)),
-            pl.BlockSpec((1, inner_here), lambda j: (0, 0)),
         ],
         out_specs=[
             pl.BlockSpec((tile_len, inner_here), lambda j: (j, 0)),
@@ -141,12 +171,11 @@
             jax.ShapeDtypeStruct((rows, 1), jnp.float32),
         ],
         cost_estimate=pl.CostEstimate(
-            flops=tiles_dev * (2 * tile_len * tile_len * (state_dim + 4 * inner_here + 2 * inner_here)),
-            transcendentals=tiles_dev * tile_len * (tile_len * heads_here + 2 * inner_here),
+            flops=tiles_dev * 2 * tile_len * state_dim * inner_here,
+            transcendentals=rows * inner_here * 2,
             bytes_accessed=rows * inner_here * 10 + tiles_dev * inner_here * state_dim * 2,
         ),
-    )(conv_out, conv_out, conv_out, cumul, cumul_t, dt_t, part_col, part_row, carried, zx, d_full)
-
+    )(partial, conv_out, cumul, later.reshape(tiles_dev, tile_len, 1), carried, zx)
 
 def shards(
     ingest,
@@ -257,19 +286,26 @@
         states.append(running)
         running = passing_wide[tile][None, :] * running + contrib[tile]
     before_tile = jnp.stack(states)
+    d_full = jnp.repeat(d_skip, head_dim)[None, :]
+    partial = intra_tiles(conv_out, cumul, cumul_t, dt_t, later, d_full)
     position = lax.axis_index("seq")
-    run_decay = widen(through[tiles_dev - 1])
-    distance = 1
-    while distance < seq_count:
-        got_decay, got_state = shifted((run_decay, run_state), "seq", distance)
-        run_state = run_state + run_decay[None, :] * got_state
-        run_decay = jnp.where(position >= distance, run_decay * got_decay, run_decay)
-        distance *= 2
-    entering = shifted(run_state, "seq", 1)
+    all_decay = widen(through[tiles_dev - 1])
+    halves = []
+    width = inner_here // 2
+    for group in range(2):
+        run_decay = all_decay[group * width : (group + 1) * width]
+        group_state = run_state[:, group * width : (group + 1) * width]
+        distance = 1
+        while distance < seq_count:
+            got_decay, got_state = shifted((run_decay, group_state), "seq", distance)
+            group_state = group_state + run_decay[None, :] * got_state
+            run_decay = jnp.where(position >= distance, run_decay * got_decay, run_decay)
+            distance *= 2
+        halves.append(shifted(group_state, "seq", 1))
+    entering = jnp.concatenate(halves, 1)
     tile_state = before_tile + widen(prefix)[:, None, :] * entering[None]
     carried = tile_state.astype(jnp.bfloat16)
-    d_full = jnp.repeat(d_skip, head_dim)[None, :]
-    gated, row_sq = mix_tiles(conv_out, zx, cumul, cumul_t, dt_t, later, carried, d_full)
+    gated, row_sq = finish_tiles(partial, conv_out, zx, cumul, later, carried)
     sums = lax.psum(row_sq, "head")
     return (gated * lax.rsqrt(sums / INNER + EPSILON) * norm_gain[None, :]).astype(jnp.bfloat16)
 

time: 300 us -> 317 us (1.057)
  the two profiles are of different devices: /device:TPU:29 before, /device:TPU:5 now
where the time goes in v6:
time: 317 us; the launch traced here: 315 us
  starting transfers between devices  65 us (21%)
  waiting for transfers between devices  60.5 us (19%)
  other arithmetic  52.5 us (17%)
  Pallas kernels  48.7 us (15%)
  local copies, waits for them, and re-layouts  28 us (9%)
  blocking collectives  24.9 us (8%)
  matrix products  21.3 us (7%)
  between operations  14.1 us (4%)
    ppermute x18, starting transfers between devices, shifted(): return lax.ppermute(x, axis, pairs)  53 us
    all_to_all x1, waiting for transfers between devices, shards(): lax.all_to_all(outgoing, 'seq', split_axis=0, concat_axis=0, tiled=True)  43.2 us
    psum x1, blocking collectives, shards(): sums = lax.psum(row_sq, 'head')  24.9 us
    pallas_call x1, Pallas kernels, finish_tiles(): pl.pallas_call(finish_tile, grid=(tiles_dev,), in_specs=[pl.BlockSpec((ti...  17.2 us
    dot_general x3, matrix products, shards(): jnp.dot(piece, weight, preferred_element_type=jnp.float32)  16.9 us
    pallas_call x1, Pallas kernels, intra_tiles(): pl.pallas_call(intra_tile, grid=(tiles_dev,), in_specs=[pl.BlockSpec((til...  16.2 us
    pallas_call x1, Pallas kernels, contrib_tiles(): pl.pallas_call(contrib_tile, grid=(tiles_dev,), in_specs=[pl.BlockSpec((t...  15.4 us
    unnamed x45, local copies, waits for them, and re-layouts  14.4 us
  transfers between devices with their start and end apart: 21, of which 10 were waited for; matrix products, arithmetic and copies ran while one was open for 11% of the time, Pallas kernels for 5%

profile of v6, /device:TPU:5, one launch (start us, length us, event | category | flops | bytes accessed | tf_op | source)
XLA Modules:
  0.0 315.1 jit_solution(5994049931052443947)
XLA Ops:
  8.8 6.7 %all-to-all-start = ((bf16[16,1,1]{2,1,0:T(2,128)(2,1)}), bf16[16,1,1]{2,1,0:T(2,128)(2,1)S(1)}, u32[]{:S(2)}, u32[]{:S(2)}) async-start(bf16[16,1,1]{2,1,0:T(2,128)(2,1)} %copy.56), calls=%async_computation | async-start | bytes 16384 | tf_op jit(solution)/shard_map/all_to_all | solution.py:219
  20.6 5.3 %all-to-all-start.1 = ((bf16[16,128,512]{2,1,0:T(8,128)(2,1)}), bf16[16,128,512]{2,1,0:T(8,128)(2,1)S(1)}, u32[]{:S(2)}, u32[]{:S(2)}) async-start(bf16[16,128,512]{2,1,0:T(8,128)(2,1)} %copy.58), calls=%async_computation.1 | async-start | bytes 4194304 | tf_op jit(solution)/shard_map/all_to_all | solution.py:218
  26.1 43.2 %all-to-all-done.1 = bf16[16,128,512]{2,1,0:T(8,128)(2,1)S(1)} async-done(((bf16[16,128,512]{2,1,0:T(8,128)(2,1)}), bf16[16,128,512]{2,1,0:T(8,128)(2,1)S(1)}, u32[]{:S(2)}, u32[]{:S(2)}) %all-to-all-start.1) | async-done | bytes 2097184 | tf_op jit(solution)/shard_map/all_to_all | solution.py:218
  77.8 5.6 %copy.72 = bf16[128,8,2,1024]{3,1,2,0:T(8,128)(2,1)} copy(bf16[128,8,2,1024]{3,2,1,0:T(2,128)(2,1)} %bitcast.87) | data formatting | bytes 8388608
  87.4 4.6 %all-gather.2.cloned.1.call-done = bf16[2048,1024]{1,0:T(8,128)(2,1)} async-done(((bf16[2048,512]{1,0:T(8,128)(2,1)}), bf16[2048,1024]{1,0:T(8,128)(2,1)}) %all-gather.2.cloned.1.call-update) | async-done | bytes 4194320 | tf_op jit(solution)/shard_map/all_gather | solution.py:229
  92.0 3.4 %compare_select_fusion = f32[2048,16]{0,1:T(8,128)S(1)} fusion(bf16[2048,1024]{1,0:T(8,128)(2,1)} %all-gather.2.cloned.1.call-done, bf16[1024,16]{0,1:T(8,128)(2,1)S(1)} %copy-done.10, f32[16]{0:T(128)S(1)} %copy-done.16), kind=kOutput, calls=%fused_computation.46 | convolution fusion | flops 67338240 | bytes 4358208 | tf_op jit(solution)/shard_map/dot_general | solution.py:231
  97.2 12.2 %convolution_convert_fusion.gate_ref = bf16[2048,2048]{1,0:T(8,128)(2,1)S(1)} fusion(bf16[2048,1024]{1,0:T(8,128)(2,1)} %all-gather.2.cloned.1.call-done, bf16[1024,2048]{1,0:T(8,128)(2,1)} %bitcast.88), kind=kOutput, calls=%fused_computation.4 | convolution fusion | flops 8594128896 | bytes 16777216 | tf_op jit(solution)/shard_map/dot_general | solution.py:231
  110.1 4.5 %copy-done.8 = bf16[2048,1024]{1,0:T(8,128)(2,1)S(1)} copy-done((bf16[2048,1024]{1,0:T(8,128)(2,1)S(1)}, bf16[2048,1024]{1,0:T(8,128)(2,1)}, u32[]{:S(2)}) %copy-start.8) | copy-done | bytes 4194328
  125.0 4.3 %collective-permute-start.11 = (f32[512]{0:T(512)S(1)}, f32[512]{0:T(512)S(1)}, u32[]{:S(2)}, u32[]{:S(2)}) collective-permute-start(f32[512]{0:T(512)S(1)} %mul.505), channel_id=1, source_target_pairs={{0,2},{2,4},{4,6},{6,8},{8,10},{10,12},{12,14},{14,16},{16,18},{18... | collective-permute-start | bytes 6152 | tf_op jit(solution)/shard_map/ppermute | solution.py:17
  143.8 3.8 %maximum_maximum_fusion = bf16[2051,1280]{1,0:T(8,128)(2,1)S(1)} fusion(bf16[2048,256]{1,0:T(8,128)(2,1)S(1)} %convolution_convert_fusion.1, bf16[2048,1024]{1,0:T(8,128)(2,1)} %copy-done.4, bf16[3,1280]{1,0:T(4,128)(2,1)S(1)} %collective-permute-done.1), kind=kLoop, calls=%fused_computation.7 | loop fusion | flops 15751680 | bytes 10501120 | tf_op jit(solution)/shard_map/concatenate | solution.py:246
  147.6 10.8 %multiply_convert_fusion.x_ref.b_ref.c_ref = bf16[2048,1280]{1,0:T(8,128)(2,1)S(1)} fusion(bf16[2048,256]{1,0:T(8,128)(2,1)S(1)} %convolution_convert_fusion.1, bf16[2051,1280]{1,0:T(8,128)(2,1)S(1)} %maximum_maximum_fusion, f32[1280]{0:T(1024)S(1)} %get-tuple-element.10, f32[1280]{0:T(1024)S(1)} %get-tuple-element.11, f32[1280]{0:T(1024)S(1)} %get-tuple-element.12, ...), kind=kLoop, calls=%fused_computation | loop fusion | flops 60293120 | bytes 26246144 | tf_op jit(solution)/shard_map/convert_element_type | solution.py:259
  161.8 15.4 %shard_map.137 = f32[16,128,1024]{2,1,0:T(8,128)} custom-call(bf16[2048,1280]{1,0:T(8,128)(2,1)} %copy-done.2, bf16[16,128,128]{2,1,0:T(8,128)(2,1)} %bitcast.90, f32[16,128,16]{2,1,0:T(8,128)} %multiply_multiply_fusion.end_ref), custom_call_target="tpu_custom_call" | custom-call | flops 536870912 | bytes 13107200 | tf_op jit(solution)/shard_map/pallas_call | solution.py:95
  177.2 4.7 %multiply_reduce_fusion = f32[128,1024]{1,0:T(8,128)S(1)} fusion(f32[16,128,1024]{2,1,0:T(8,128)} %shard_map.137, f32[16,1024]{1,0:T(8,128)S(1)} %mul.490), kind=kLoop, calls=%fused_computation.3 | loop fusion | flops 4063232 | bytes 8978432 | tf_op jit(solution)/shard_map/reduce_sum | solution.py:281
  185.2 4.8 %collective-permute-start.2 = (f32[128,512]{1,0:T(8,128)S(1)}, f32[128,512]{1,0:T(8,128)S(1)}, u32[]{:S(2)}, u32[]{:S(2)}) collective-permute-start(f32[128,512]{1,0:T(8,128)S(1)} %get-tuple-element.29), channel_id=1, source_target_pairs={{0,2},{2,4},{4,6},{6,8},{8,10},{10,12},{12,14},{14,16},{16,18},{18... | collective-permute-start | bytes 786440 | tf_op jit(solution)/shard_map/ppermute | solution.py:17
  203.2 3.2 %collective-permute-start.12 = (f32[128,512]{1,0:T(8,128)S(1)}, f32[128,512]{1,0:T(8,128)S(1)}, u32[]{:S(2)}, u32[]{:S(2)}) collective-permute-start(f32[128,512]{1,0:T(8,128)S(1)} %get-tuple-element.28), channel_id=1, source_target_pairs={{0,4},{2,6},{4,8},{6,10},{8,12},{10,14},{12,16},{14,18},{16,20},{1... | collective-permute-start | bytes 786440 | tf_op jit(solution)/shard_map/ppermute | solution.py:17
  216.7 3.6 %collective-permute-start.8 = (f32[128,512]{1,0:T(8,128)S(1)}, f32[128,512]{1,0:T(8,128)S(1)}, u32[]{:S(2)}, u32[]{:S(2)}) collective-permute-start(f32[128,512]{1,0:T(8,128)S(1)} %multiply_add_fusion.5), channel_id=1, source_target_pairs={{0,16},{2,18},{4,20},{6,22},{8,24},{10,26},{12,28},{14,30},{1,17},... | collective-permute-start | bytes 786440 | tf_op jit(solution)/shard_map/ppermute | solution.py:17
  222.3 3.8 %collective-permute-start.16 = (f32[128,512]{1,0:T(8,128)S(1)}, f32[128,512]{1,0:T(8,128)S(1)}, u32[]{:S(2)}, u32[]{:S(2)}) collective-permute-start(f32[128,512]{1,0:T(8,128)S(1)} %multiply_add_fusion.1), channel_id=1, source_target_pairs={{0,16},{2,18},{4,20},{6,22},{8,24},{10,26},{12,28},{14,30},{1,17},... | collective-permute-start | bytes 786440 | tf_op jit(solution)/shard_map/ppermute | solution.py:17
  226.2 16.2 %shard_map.136.part_ref = f32[2048,1024]{1,0:T(8,128)} custom-call(bf16[2048,1280]{1,0:T(8,128)(2,1)} %copy-done.2, bf16[2048,1280]{1,0:T(8,128)(2,1)} %copy-done.2, bf16[2048,1280]{1,0:T(8,128)(2,1)} %copy-done.2, f32[16,128,16]{2,1,0:T(8,128)} %bitcast.81, f32[16,16,128]{2,1,0:T(8,128)} %copy-done.9, f32[16,16,128]{2,1,0:T(8,128)} %copy.67.dtt_ref, ...), custom_call_target="tpu_custom_call" | custom-call | flops 2214592512 | bytes 12582912 | tf_op jit(solution)/shard_map/pallas_call | solution.py:121
  242.4 3.3 %collective-permute-start.9 = (f32[128,512]{1,0:T(8,128)S(1)}, f32[128,512]{1,0:T(8,128)S(1)}, u32[]{:S(2)}, u32[]{:S(2)}) collective-permute-start(f32[128,512]{1,0:T(8,128)S(1)} %multiply_add_fusion.4), channel_id=1, source_target_pairs={{0,2},{2,4},{4,6},{6,8},{8,10},{10,12},{12,14},{14,16},{16,18},{18... | collective-permute-start | bytes 786440 | tf_op jit(solution)/shard_map/ppermute | solution.py:17
  250.4 3.3 %collective-permute-done.17 = f32[128,512]{1,0:T(8,128)S(1)} collective-permute-done((f32[128,512]{1,0:T(8,128)S(1)}, f32[128,512]{1,0:T(8,128)S(1)}, u32[]{:S(2)}, u32[]{:S(2)}) %collective-permute-start.17) | collective-permute-done | bytes 262176 | tf_op jit(solution)/shard_map/ppermute | solution.py:17
  253.8 6.8 %add_convert_fusion.car_ref = bf16[16,128,1024]{2,1,0:T(8,128)(2,1)} fusion(f32[16,128,1024]{2,1,0:T(8,128)} %fusion.16, f32[128,1024]{1,0:T(8,128)S(1)} %pad_maximum_fusion.1, f32[16,1024]{1,0:T(8,128)S(1)} %mul.488), kind=kLoop, calls=%fused_computation.2 | loop fusion | flops 6291456 | bytes 13172736 | tf_op jit(solution)/shard_map/convert_element_type | solution.py:307
  260.5 17.2 %shard_map.138 = (f32[2048,1024]{1,0:T(8,128)}, f32[2048,1]{1,0:T(8,128)}) custom-call(f32[2048,1024]{1,0:T(8,128)} %shard_map.136.part_ref, bf16[2048,1280]{1,0:T(8,128)(2,1)} %copy-done.2, f32[16,128,16]{2,1,0:T(8,128)} %bitcast.82, f32[16,128,1]{2,1,0:T(8,128)} %fusion.15.partc_ref, bf16[16,128,1024]{2,1,0:T(8,128)(2,1)} %add_convert_fusion.car_ref, ...), custom_call_target="tpu_custom_call" | custom-call | flops 536870912 | bytes 25165824 | tf_op jit(solution)/shard_map/pallas_call | solution.py:154
  277.7 24.9 %psum.7 = f32[2048,1]{1,0:T(8,128)S(1)} all-reduce(f32[2048,1]{1,0:T(8,128)} %get-tuple-element.8), channel_id=1, replica_groups=mesh['seq'=16,'head'=2] {'head'}, use_global_device_ids=true, to_apply=%region_4.5 | all-reduce | flops 2048 | bytes 16384 | tf_op jit(solution)/shard_map/psum | solution.py:309
  303.0 5.2 %multiply_convert_fusion.1 = bf16[2048,1024]{1,0:T(8,128)(2,1)} fusion(f32[2048,1024]{1,0:T(8,128)} %get-tuple-element.7, f32[1024]{0:T(1024)S(1)} %copy-done.13, f32[2048]{0:T(1024)S(1)} %rsqrt_reduce_fusion), kind=kLoop, calls=%fused_computation.1 | loop fusion | flops 6291456 | bytes 12595200 | tf_op jit(solution)/shard_map/convert_element_type | solution.py:310
  (193 shorter events, 84.2 us)
Async XLA Ops:
  8.8 11.8 %all-to-all-start = ((bf16[16,1,1]{2,1,0:T(2,128)(2,1)}), bf16[16,1,1]{2,1,0:T(2,128)(2,1)S(1)}, u32[]{:S(2)}, u32[]{:S(2)}) async-start(bf16[16,1,1]{2,1,0:T(2,128)(2,1)} %copy.56), calls=%async_computation | async-start | bytes 16384 | tf_op jit(solution)/shard_map/all_to_all | solution.py:219
  19.4 53.9 %copy-start.11 = (s32[16]{0:T(128)S(1)}, s32[16]{0:T(128)}, u32[]{:S(2)}) copy-start(s32[16]{0:T(128)} %param.16) | copy-start | bytes 196
  20.6 48.7 %all-to-all-start.1 = ((bf16[16,128,512]{2,1,0:T(8,128)(2,1)}), bf16[16,128,512]{2,1,0:T(8,128)(2,1)S(1)}, u32[]{:S(2)}, u32[]{:S(2)}) async-start(bf16[16,128,512]{2,1,0:T(8,128)(2,1)} %copy.58), calls=%async_computation.1 | async-start | bytes 4194304 | tf_op jit(solution)/shard_map/all_to_all | solution.py:218
  25.9 66.1 %all-gather.2.cloned.1.call-start = ((), (), s32[]{:S(2)}) async-start(), calls=%async_computation.2 | async-start | bytes 6291456 | tf_op jit(solution)/shard_map/all_gather | solution.py:229
  75.0 12.4 %collective-permute-start = (bf16[3]{0:T(256)(128)(2,1)S(1)}, bf16[3]{0:T(256)(128)(2,1)S(1)}, u32[]{:S(2)}, u32[]{:S(2)}) collective-permute-start(bf16[3]{0:T(256)(128)(2,1)S(1)} %fusion.46), channel_id=1, source_target_pairs={{0,2},{2,4},{4,6},{6,8},{8,10},{10,12},{12,14},{14,16},{16,18},{18... | collective-permute-start | bytes 26 | tf_op jit(solution)/shard_map/ppermute | solution.py:17
  116.7 27.0 %collective-permute-start.1 = (bf16[3,1280]{1,0:T(4,128)(2,1)S(1)}, bf16[3,1280]{1,0:T(4,128)(2,1)S(1)}, u32[]{:S(2)}, u32[]{:S(2)}) collective-permute-start(bf16[3,1280]{1,0:T(4,128)(2,1)S(1)} %fusion.27), channel_id=1, source_target_pairs={{0,2},{2,4},{4,6},{6,8},{8,10},{10,12},{12,14},{14,16},{16,18},{18... | collective-permute-start | bytes 23048 | tf_op jit(solution)/shard_map/ppermute | solution.py:17
  121.9 10.7 %collective-permute-start.3 = (f32[512]{0:T(512)S(1)}, f32[512]{0:T(512)S(1)}, u32[]{:S(2)}, u32[]{:S(2)}) collective-permute-start(f32[512]{0:T(512)S(1)} %mul.493), channel_id=1, source_target_pairs={{0,2},{2,4},{4,6},{6,8},{8,10},{10,12},{12,14},{14,16},{16,18},{18... | collective-permute-start | bytes 6152 | tf_op jit(solution)/shard_map/ppermute | solution.py:17
  125.0 9.8 %collective-permute-start.11 = (f32[512]{0:T(512)S(1)}, f32[512]{0:T(512)S(1)}, u32[]{:S(2)}, u32[]{:S(2)}) collective-permute-start(f32[512]{0:T(512)S(1)} %mul.505), channel_id=1, source_target_pairs={{0,2},{2,4},{4,6},{6,8},{8,10},{10,12},{12,14},{14,16},{16,18},{18... | collective-permute-start | bytes 6152 | tf_op jit(solution)/shard_map/ppermute | solution.py:17
  132.6 5.3 %collective-permute-start.5 = (f32[512]{0:T(512)S(1)}, f32[512]{0:T(512)S(1)}, u32[]{:S(2)}, u32[]{:S(2)}) collective-permute-start(f32[512]{0:T(512)S(1)} %multiply_select_fusion.5), channel_id=1, source_target_pairs={{0,4},{2,6},{4,8},{6,10},{8,12},{10,14},{12,16},{14,18},{16,20},{1... | collective-permute-start | bytes 6152 | tf_op jit(solution)/shard_map/ppermute | solution.py:17
  134.8 6.2 %collective-permute-start.13 = (f32[512]{0:T(512)S(1)}, f32[512]{0:T(512)S(1)}, u32[]{:S(2)}, u32[]{:S(2)}) collective-permute-start(f32[512]{0:T(512)S(1)} %multiply_select_fusion.2), channel_id=1, source_target_pairs={{0,4},{2,6},{4,8},{6,10},{8,12},{10,14},{12,16},{14,18},{16,20},{1... | collective-permute-start | bytes 6152 | tf_op jit(solution)/shard_map/ppermute | solution.py:17
  138.0 5.3 %collective-permute-start.7 = (f32[512]{0:T(512)S(1)}, f32[512]{0:T(512)S(1)}, u32[]{:S(2)}, u32[]{:S(2)}) collective-permute-start(f32[512]{0:T(512)S(1)} %multiply_select_fusion.4), channel_id=1, source_target_pairs={{0,8},{2,10},{4,12},{6,14},{8,16},{10,18},{12,20},{14,22},{16,24},... | collective-permute-start | bytes 6152 | tf_op jit(solution)/shard_map/ppermute | solution.py:17
  141.1 2.7 collective-permute-start.15
  182.0 19.2 %collective-permute-start.10 = (f32[128,512]{1,0:T(8,128)S(1)}, f32[128,512]{1,0:T(8,128)S(1)}, u32[]{:S(2)}, u32[]{:S(2)}) collective-permute-start(f32[128,512]{1,0:T(8,128)S(1)} %get-tuple-element.30), channel_id=1, source_target_pairs={{0,2},{2,4},{4,6},{6,8},{8,10},{10,12},{12,14},{14,16},{16,18},{18... | collective-permute-start | bytes 786440 | tf_op jit(solution)/shard_map/ppermute | solution.py:17
  185.2 15.9 %collective-permute-start.2 = (f32[128,512]{1,0:T(8,128)S(1)}, f32[128,512]{1,0:T(8,128)S(1)}, u32[]{:S(2)}, u32[]{:S(2)}) collective-permute-start(f32[128,512]{1,0:T(8,128)S(1)} %get-tuple-element.29), channel_id=1, source_target_pairs={{0,2},{2,4},{4,6},{6,8},{8,10},{10,12},{12,14},{14,16},{16,18},{18... | collective-permute-start | bytes 786440 | tf_op jit(solution)/shard_map/ppermute | solution.py:17
  201.2 7.1 %collective-permute-start.4 = (f32[128,512]{1,0:T(8,128)S(1)}, f32[128,512]{1,0:T(8,128)S(1)}, u32[]{:S(2)}, u32[]{:S(2)}) collective-permute-start(f32[128,512]{1,0:T(8,128)S(1)} %get-tuple-element.27), channel_id=1, source_target_pairs={{0,4},{2,6},{4,8},{6,10},{8,12},{10,14},{12,16},{14,18},{16,20},{1... | collective-permute-start | bytes 786440 | tf_op jit(solution)/shard_map/ppermute | solution.py:17
  203.2 9.7 %collective-permute-start.12 = (f32[128,512]{1,0:T(8,128)S(1)}, f32[128,512]{1,0:T(8,128)S(1)}, u32[]{:S(2)}, u32[]{:S(2)}) collective-permute-start(f32[128,512]{1,0:T(8,128)S(1)} %get-tuple-element.28), channel_id=1, source_target_pairs={{0,4},{2,6},{4,8},{6,10},{8,12},{10,14},{12,16},{14,18},{16,20},{1... | collective-permute-start | bytes 786440 | tf_op jit(solution)/shard_map/ppermute | solution.py:17
  208.4 8.2 %collective-permute-start.6 = (f32[128,512]{1,0:T(8,128)S(1)}, f32[128,512]{1,0:T(8,128)S(1)}, u32[]{:S(2)}, u32[]{:S(2)}) collective-permute-start(f32[128,512]{1,0:T(8,128)S(1)} %multiply_add_fusion.6), channel_id=1, source_target_pairs={{0,8},{2,10},{4,12},{6,14},{8,16},{10,18},{12,20},{14,22},{16,24},... | collective-permute-start | bytes 786440 | tf_op jit(solution)/shard_map/ppermute | solution.py:17
  212.9 9.4 %collective-permute-start.14 = (f32[128,512]{1,0:T(8,128)S(1)}, f32[128,512]{1,0:T(8,128)S(1)}, u32[]{:S(2)}, u32[]{:S(2)}) collective-permute-start(f32[128,512]{1,0:T(8,128)S(1)} %multiply_add_fusion.2), channel_id=1, source_target_pairs={{0,8},{2,10},{4,12},{6,14},{8,16},{10,18},{12,20},{14,22},{16,24},... | collective-permute-start | bytes 786440 | tf_op jit(solution)/shard_map/ppermute | solution.py:17
  216.7 25.6 %collective-permute-start.8 = (f32[128,512]{1,0:T(8,128)S(1)}, f32[128,512]{1,0:T(8,128)S(1)}, u32[]{:S(2)}, u32[]{:S(2)}) collective-permute-start(f32[128,512]{1,0:T(8,128)S(1)} %multiply_add_fusion.5), channel_id=1, source_target_pairs={{0,16},{2,18},{4,20},{6,22},{8,24},{10,26},{12,28},{14,30},{1,17},... | collective-permute-start | bytes 786440 | tf_op jit(solution)/shard_map/ppermute | solution.py:17
  222.3 23.3 %collective-permute-start.16 = (f32[128,512]{1,0:T(8,128)S(1)}, f32[128,512]{1,0:T(8,128)S(1)}, u32[]{:S(2)}, u32[]{:S(2)}) collective-permute-start(f32[128,512]{1,0:T(8,128)S(1)} %multiply_add_fusion.1), channel_id=1, source_target_pairs={{0,16},{2,18},{4,20},{6,22},{8,24},{10,26},{12,28},{14,30},{1,17},... | collective-permute-start | bytes 786440 | tf_op jit(solution)/shard_map/ppermute | solution.py:17
  242.4 8.0 %collective-permute-start.9 = (f32[128,512]{1,0:T(8,128)S(1)}, f32[128,512]{1,0:T(8,128)S(1)}, u32[]{:S(2)}, u32[]{:S(2)}) collective-permute-start(f32[128,512]{1,0:T(8,128)S(1)} %multiply_add_fusion.4), channel_id=1, source_target_pairs={{0,2},{2,4},{4,6},{6,8},{8,10},{10,12},{12,14},{14,16},{16,18},{18... | collective-permute-start | bytes 786440 | tf_op jit(solution)/shard_map/ppermute | solution.py:17
  245.7 8.0 %collective-permute-start.17 = (f32[128,512]{1,0:T(8,128)S(1)}, f32[128,512]{1,0:T(8,128)S(1)}, u32[]{:S(2)}, u32[]{:S(2)}) collective-permute-start(f32[128,512]{1,0:T(8,128)S(1)} %multiply_add_fusion), channel_id=1, source_target_pairs={{0,2},{2,4},{4,6},{6,8},{8,10},{10,12},{12,14},{14,16},{16,18},{18... | collective-permute-start | bytes 786440 | tf_op jit(solution)/shard_map/ppermute | solution.py:17
  260.5 42.5 %copy-start.13 = (f32[1024]{0:T(1024)S(1)}, f32[1024]{0:T(1024)}, u32[]{:S(2)}) copy-start(f32[1024]{0:T(1024)} %param.27) | copy-start | bytes 12292
  260.5 47.7 %copy-start.1 = (bf16[16,128,512]{2,1,0:T(8,128)(2,1)S(1)}, bf16[16,128,512]{2,1,0:T(8,128)(2,1)}, u32[]{:S(2)}) copy-start(bf16[16,128,512]{2,1,0:T(8,128)(2,1)} %param.14) | copy-start | bytes 6291460
  (18 other events, 218.3 us)
Sparse Core Ops, SparseCore 0:
  73.4 18.4 all-gather.1

commit v7 on v5

--- a/solution.py
+++ b/solution.py
@@ -261,11 +261,11 @@
     run_decay = widen(through[tiles_dev - 1])
     distance = 1
     while distance < seq_count:
-        got_decay, got_state = shifted((run_decay, run_state), "seq", distance)
-        run_state = run_state + run_decay[None, :] * got_state
+        got_decay, got_state = shifted((run_decay, run_state.astype(jnp.bfloat16)), "seq", distance)
+        run_state = run_state + run_decay[None, :] * got_state.astype(jnp.float32)
         run_decay = jnp.where(position >= distance, run_decay * got_decay, run_decay)
         distance *= 2
-    entering = shifted(run_state, "seq", 1)
+    entering = shifted(run_state.astype(jnp.bfloat16), "seq", 1).astype(jnp.float32)
     tile_state = before_tile + widen(prefix)[:, None, :] * entering[None]
     carried = tile_state.astype(jnp.bfloat16)
     d_full = jnp.repeat(d_skip, head_dim)[None, :]

time: 300 us -> 270 us (0.900)
  waiting for transfers between devices: 109 us -> 81.3 us
    ppermute x10, waiting for transfers between devices: 60.4 us -> 33 us  [shifted(): return lax.ppermute(x, axis, pairs)]
  transfers between devices with their start and end apart: 13 -> 13, of which waited for: 8 -> 6; matrix products, arithmetic and copies ran while one was open for 19% -> 21% of each run, Pallas kernels for 5% -> 6%
where the time goes in v7:
time: 270 us; the launch traced here: 267 us
  waiting for transfers between devices  81.3 us (30%)
  other arithmetic  51.6 us (19%)
  Pallas kernels  35.8 us (13%)
  starting transfers between devices  31.2 us (12%)
  local copies, waits for them, and re-layouts  26.8 us (10%)
  matrix products  18.1 us (7%)
  between operations  14 us (5%)
  blocking collectives  8.53 us (3%)
    all_to_all x1, waiting for transfers between devices, shards(): lax.all_to_all(outgoing, 'seq', split_axis=0, concat_axis=0, tiled=True)  45 us
    ppermute x10, waiting for transfers between devices, shifted(): return lax.ppermute(x, axis, pairs)  33 us
    pallas_call x1, Pallas kernels, mix_tiles(): pl.pallas_call(mix_tile, grid=(tiles_dev,), in_specs=[pl.BlockSpec((tile_...  20.4 us
    ppermute x10, starting transfers between devices, shifted(): return lax.ppermute(x, axis, pairs)  18.3 us
    pallas_call x1, Pallas kernels, contrib_tiles(): pl.pallas_call(contrib_tile, grid=(tiles_dev,), in_specs=[pl.BlockSpec((t...  15.4 us
    dot_general x3, matrix products, shards(): jnp.dot(piece, weight, preferred_element_type=jnp.float32)  14.4 us
    unnamed x46, local copies, waits for them, and re-layouts  13.7 us
    unnamed x14, other arithmetic  13 us
  transfers between devices with their start and end apart: 13, of which 6 were waited for; matrix products, arithmetic and copies ran while one was open for 21% of the time, Pallas kernels for 6%

profile of v7, /device:TPU:29, one launch (start us, length us, event | category | flops | bytes accessed | tf_op | source)
XLA Modules:
  0.0 267.3 jit_solution(8706879328199236733)
XLA Ops:
  8.8 6.4 %all-to-all-start = ((bf16[16,1,1]{2,1,0:T(2,128)(2,1)}), bf16[16,1,1]{2,1,0:T(2,128)(2,1)S(1)}, u32[]{:S(2)}, u32[]{:S(2)}) async-start(bf16[16,1,1]{2,1,0:T(2,128)(2,1)} %copy.67), calls=%async_computation | async-start | bytes 16384 | tf_op jit(solution)/shard_map/all_to_all | solution.py:190
  16.6 2.5 copy.69
  19.1 6.5 %all-to-all-start.1 = ((bf16[16,128,512]{2,1,0:T(8,128)(2,1)}), bf16[16,128,512]{2,1,0:T(8,128)(2,1)S(1)}, u32[]{:S(2)}, u32[]{:S(2)}) async-start(bf16[16,128,512]{2,1,0:T(8,128)(2,1)} %copy.69), calls=%async_computation.1 | async-start | bytes 4194304 | tf_op jit(solution)/shard_map/all_to_all | solution.py:189
  25.8 45.0 %all-to-all-done.1 = bf16[16,128,512]{2,1,0:T(8,128)(2,1)S(1)} async-done(((bf16[16,128,512]{2,1,0:T(8,128)(2,1)}), bf16[16,128,512]{2,1,0:T(8,128)(2,1)S(1)}, u32[]{:S(2)}, u32[]{:S(2)}) %all-to-all-start.1) | async-done | bytes 2097184 | tf_op jit(solution)/shard_map/all_to_all | solution.py:189
  72.2 2.5 copy.71
  76.4 2.4 collective-permute-start
  78.8 5.6 %copy.83 = bf16[128,8,2,1024]{3,1,2,0:T(8,128)(2,1)} copy(bf16[128,8,2,1024]{3,2,1,0:T(2,128)(2,1)} %bitcast.90) | data formatting | bytes 8388608
  88.4 3.3 %all-gather.2.cloned.1.call-done = bf16[2048,1024]{1,0:T(8,128)(2,1)} async-done(((bf16[2048,512]{1,0:T(8,128)(2,1)}), bf16[2048,1024]{1,0:T(8,128)(2,1)}) %all-gather.2.cloned.1.call-update) | async-done | bytes 4194320 | tf_op jit(solution)/shard_map/all_gather | solution.py:200
  91.7 11.9 %convolution_convert_fusion.gate_ref = bf16[2048,2048]{1,0:T(8,128)(2,1)S(1)} fusion(bf16[2048,1024]{1,0:T(8,128)(2,1)} %all-gather.2.cloned.1.call-done, bf16[1024,2048]{1,0:T(8,128)(2,1)} %bitcast.91), kind=kOutput, calls=%fused_computation.4 | convolution fusion | flops 8594128896 | bytes 16777216 | tf_op jit(solution)/shard_map/dot_general | solution.py:202
  104.3 4.5 %copy-done.8 = bf16[2048,1024]{1,0:T(8,128)(2,1)S(1)} copy-done((bf16[2048,1024]{1,0:T(8,128)(2,1)S(1)}, bf16[2048,1024]{1,0:T(8,128)(2,1)}, u32[]{:S(2)}) %copy-start.8) | copy-done | bytes 4194328
  110.3 3.1 %collective-permute-start.1 = (bf16[3,1280]{1,0:T(4,128)(2,1)S(1)}, bf16[3,1280]{1,0:T(4,128)(2,1)S(1)}, u32[]{:S(2)}, u32[]{:S(2)}) collective-permute-start(bf16[3,1280]{1,0:T(4,128)(2,1)S(1)} %fusion.28), channel_id=1, source_target_pairs={{0,2},{2,4},{4,6},{6,8},{8,10},{10,12},{12,14},{14,16},{16,18},{18... | collective-permute-start | bytes 23048 | tf_op jit(solution)/shard_map/ppermute | solution.py:17
  124.4 3.8 %maximum_maximum_fusion = bf16[2051,1280]{1,0:T(8,128)(2,1)S(1)} fusion(bf16[2048,256]{1,0:T(8,128)(2,1)S(1)} %convolution_convert_fusion.1, bf16[2048,1024]{1,0:T(8,128)(2,1)} %copy-done.4, bf16[3,1280]{1,0:T(4,128)(2,1)S(1)} %collective-permute-done.1), kind=kLoop, calls=%fused_computation.7 | loop fusion | flops 15751680 | bytes 10501120 | tf_op jit(solution)/shard_map/concatenate | solution.py:217
  128.2 10.8 %multiply_convert_fusion.x_ref.b_ref.c_ref = bf16[2048,1280]{1,0:T(8,128)(2,1)S(1)} fusion(bf16[2048,256]{1,0:T(8,128)(2,1)S(1)} %convolution_convert_fusion.1, bf16[2051,1280]{1,0:T(8,128)(2,1)S(1)} %maximum_maximum_fusion, f32[1280]{0:T(1024)S(1)} %get-tuple-element.10, f32[1280]{0:T(1024)S(1)} %get-tuple-element.11, f32[1280]{0:T(1024)S(1)} %get-tuple-element.12, ...), kind=kLoop, calls=%fused_computation | loop fusion | flops 60293120 | bytes 26246144 | tf_op jit(solution)/shard_map/convert_element_type | solution.py:230
  139.0 2.4 copy-done.2
  142.5 15.4 %shard_map.136 = f32[16,128,1024]{2,1,0:T(8,128)} custom-call(bf16[2048,1280]{1,0:T(8,128)(2,1)} %copy-done.2, bf16[16,128,128]{2,1,0:T(8,128)(2,1)} %bitcast.93, f32[16,128,16]{2,1,0:T(8,128)} %multiply_multiply_fusion.end_ref), custom_call_target="tpu_custom_call" | custom-call | flops 536870912 | bytes 13107200 | tf_op jit(solution)/shard_map/pallas_call | solution.py:91
  157.9 4.7 %multiply_reduce_fusion = f32[128,1024]{1,0:T(8,128)S(1)} fusion(f32[16,128,1024]{2,1,0:T(8,128)} %shard_map.136, f32[16,1024]{1,0:T(8,128)S(1)} %mul.447), kind=kLoop, calls=%fused_computation.3 | loop fusion | flops 4063232 | bytes 8978432 | tf_op jit(solution)/shard_map/reduce_sum | solution.py:252
  177.2 8.5 %collective-permute-done.4 = bf16[128,1024]{1,0:T(8,128)(2,1)S(1)} collective-permute-done((bf16[128,1024]{1,0:T(8,128)(2,1)S(1)}, bf16[128,1024]{1,0:T(8,128)(2,1)S(1)}, u32[]{:S(2)}, u32[]{:S(2)}) %collective-permute-start.4) | collective-permute-done | bytes 262176 | tf_op jit(solution)/shard_map/ppermute | solution.py:17
  189.3 4.8 %collective-permute-done.6 = bf16[128,1024]{1,0:T(8,128)(2,1)S(1)} collective-permute-done((bf16[128,1024]{1,0:T(8,128)(2,1)S(1)}, bf16[128,1024]{1,0:T(8,128)(2,1)S(1)}, u32[]{:S(2)}, u32[]{:S(2)}) %collective-permute-start.6) | collective-permute-done | bytes 262176 | tf_op jit(solution)/shard_map/ppermute | solution.py:17
  196.5 13.4 %collective-permute-done.8 = bf16[128,1024]{1,0:T(8,128)(2,1)S(1)} collective-permute-done((bf16[128,1024]{1,0:T(8,128)(2,1)S(1)}, bf16[128,1024]{1,0:T(8,128)(2,1)S(1)}, u32[]{:S(2)}, u32[]{:S(2)}) %collective-permute-start.8) | collective-permute-done | bytes 262176 | tf_op jit(solution)/shard_map/ppermute | solution.py:17
  212.8 6.3 %collective-permute-done.9 = bf16[128,1024]{1,0:T(8,128)(2,1)S(1)} collective-permute-done((bf16[128,1024]{1,0:T(8,128)(2,1)S(1)}, bf16[128,1024]{1,0:T(8,128)(2,1)S(1)}, u32[]{:S(2)}, u32[]{:S(2)}) %collective-permute-start.9) | collective-permute-done | bytes 262176 | tf_op jit(solution)/shard_map/ppermute | solution.py:17
  219.2 6.8 %add_convert_fusion.car_ref = bf16[16,128,1024]{2,1,0:T(8,128)(2,1)} fusion(f32[16,128,1024]{2,1,0:T(8,128)} %fusion.14, f32[128,1024]{1,0:T(8,128)S(1)} %convert_element_type.160, f32[16,1024]{1,0:T(8,128)S(1)} %mul.445), kind=kLoop, calls=%fused_computation.2 | loop fusion | flops 6291456 | bytes 13172736 | tf_op jit(solution)/shard_map/convert_element_type | solution.py:270
  226.0 20.4 %shard_map.137 = (f32[2048,1024]{1,0:T(8,128)}, f32[2048,1]{1,0:T(8,128)}) custom-call(bf16[2048,1280]{1,0:T(8,128)(2,1)} %copy-done.2, bf16[2048,1280]{1,0:T(8,128)(2,1)} %copy-done.2, bf16[2048,1280]{1,0:T(8,128)(2,1)} %copy-done.2, f32[16,128,16]{2,1,0:T(8,128)} %bitcast.88, f32[16,16,128]{2,1,0:T(8,128)} %copy-done.9, ...), custom_call_target="tpu_custom_call" | custom-call | flops 3288334336 | bytes 25165824 | tf_op jit(solution)/shard_map/pallas_call | solution.py:119
  246.3 8.5 %psum.7 = f32[2048,1]{1,0:T(8,128)S(1)} all-reduce(f32[2048,1]{1,0:T(8,128)} %get-tuple-element.8), channel_id=1, replica_groups=mesh['seq'=16,'head'=2] {'head'}, use_global_device_ids=true, to_apply=%region_4.5 | all-reduce | flops 2048 | bytes 16384 | tf_op jit(solution)/shard_map/psum | solution.py:273
  255.2 5.2 %multiply_convert_fusion.1 = bf16[2048,1024]{1,0:T(8,128)(2,1)} fusion(f32[2048,1024]{1,0:T(8,128)} %get-tuple-element.7, f32[1024]{0:T(1024)S(1)} %copy-done.13, f32[2048]{0:T(1024)S(1)} %rsqrt_reduce_fusion), kind=kLoop, calls=%fused_computation.1 | loop fusion | flops 6291456 | bytes 12595200 | tf_op jit(solution)/shard_map/convert_element_type | solution.py:274
  (170 shorter events, 48.6 us)
Async XLA Ops:
  8.8 10.2 %all-to-all-start = ((bf16[16,1,1]{2,1,0:T(2,128)(2,1)}), bf16[16,1,1]{2,1,0:T(2,128)(2,1)S(1)}, u32[]{:S(2)}, u32[]{:S(2)}) async-start(bf16[16,1,1]{2,1,0:T(2,128)(2,1)} %copy.67), calls=%async_computation | async-start | bytes 16384 | tf_op jit(solution)/shard_map/all_to_all | solution.py:190
  19.1 55.7 %copy-start.11 = (s32[16]{0:T(128)S(1)}, s32[16]{0:T(128)}, u32[]{:S(2)}) copy-start(s32[16]{0:T(128)} %param.16) | copy-start | bytes 196
  19.1 51.7 %all-to-all-start.1 = ((bf16[16,128,512]{2,1,0:T(8,128)(2,1)}), bf16[16,128,512]{2,1,0:T(8,128)(2,1)S(1)}, u32[]{:S(2)}, u32[]{:S(2)}) async-start(bf16[16,128,512]{2,1,0:T(8,128)(2,1)} %copy.69), calls=%async_computation.1 | async-start | bytes 4194304 | tf_op jit(solution)/shard_map/all_to_all | solution.py:189
  25.6 66.1 %all-gather.2.cloned.1.call-start = ((), (), s32[]{:S(2)}) async-start(), calls=%async_computation.2 | async-start | bytes 6291456 | tf_op jit(solution)/shard_map/all_gather | solution.py:200
  72.2 12.3 %copy-start.18 = (f32[16]{0:T(128)S(1)}, f32[16]{0:T(128)}, u32[]{:S(2)}) copy-start(f32[16]{0:T(128)} %param.26) | copy-start | bytes 196
  72.2 13.0 %copy-start.12 = (f32[4,1024]{1,0:T(4,128)S(1)}, f32[4,1024]{1,0:T(4,128)}, u32[]{:S(2)}) copy-start(f32[4,1024]{1,0:T(4,128)} %param.22) | copy-start | bytes 49156
  72.2 13.0 %copy-start.14 = (f32[4,256]{1,0:T(4,128)S(1)}, f32[4,256]{1,0:T(4,128)}, u32[]{:S(2)}) copy-start(f32[4,256]{1,0:T(4,128)} %param.23) | copy-start | bytes 12292
  72.2 13.0 %copy-start.15 = (f32[1024]{0:T(1024)S(1)}, f32[1024]{0:T(1024)}, u32[]{:S(2)}) copy-start(f32[1024]{0:T(1024)} %param.24) | copy-start | bytes 12292
  72.2 13.0 %copy-start.17 = (f32[256]{0:T(256)S(1)}, f32[256]{0:T(256)}, u32[]{:S(2)}) copy-start(f32[256]{0:T(256)} %param.25) | copy-start | bytes 3076
  72.2 14.2 %copy-start.20 = (f32[16]{0:T(128)S(1)}, f32[16]{0:T(128)}, u32[]{:S(2)}) copy-start(f32[16]{0:T(128)} %param.21) | copy-start | bytes 196
  76.4 11.9 %collective-permute-start = (bf16[3]{0:T(256)(128)(2,1)S(1)}, bf16[3]{0:T(256)(128)(2,1)S(1)}, u32[]{:S(2)}, u32[]{:S(2)}) collective-permute-start(bf16[3]{0:T(256)(128)(2,1)S(1)} %fusion.47), channel_id=1, source_target_pairs={{0,2},{2,4},{4,6},{6,8},{8,10},{10,12},{12,14},{14,16},{16,18},{18... | collective-permute-start | bytes 26 | tf_op jit(solution)/shard_map/ppermute | solution.py:17
  110.3 14.1 %collective-permute-start.1 = (bf16[3,1280]{1,0:T(4,128)(2,1)S(1)}, bf16[3,1280]{1,0:T(4,128)(2,1)S(1)}, u32[]{:S(2)}, u32[]{:S(2)}) collective-permute-start(bf16[3,1280]{1,0:T(4,128)(2,1)S(1)} %fusion.28), channel_id=1, source_target_pairs={{0,2},{2,4},{4,6},{6,8},{8,10},{10,12},{12,14},{14,16},{16,18},{18... | collective-permute-start | bytes 23048 | tf_op jit(solution)/shard_map/ppermute | solution.py:17
  115.7 12.5 %copy-start.9 = (f32[16,16,128]{2,1,0:T(8,128)}, f32[16,16,128]{2,1,0:T(8,128)S(1)}, u32[]{:S(2)}) copy-start(f32[16,16,128]{2,1,0:T(8,128)S(1)} %fusion.24.cumt_ref) | copy-start | bytes 393220
  116.0 23.0 %copy-start.7 = (f32[16,16,128]{1,2,0:T(8,128)}, f32[16,16,128]{1,2,0:T(8,128)S(1)}, u32[]{:S(2)}) copy-start(f32[16,16,128]{1,2,0:T(8,128)S(1)} %copy.76) | copy-start | bytes 393220
  116.6 5.9 %collective-permute-start.3 = (f32[1024]{0:T(1024)S(1)}, f32[1024]{0:T(1024)S(1)}, u32[]{:S(2)}, u32[]{:S(2)}) collective-permute-start(f32[1024]{0:T(1024)S(1)} %mul.450), channel_id=1, source_target_pairs={{0,2},{2,4},{4,6},{6,8},{8,10},{10,12},{12,14},{14,16},{16,18},{18... | collective-permute-start | bytes 12296 | tf_op jit(solution)/shard_map/ppermute | solution.py:17
  122.6 65.4 %collective-permute-start.5 = (f32[1024]{0:T(1024)S(1)}, f32[1024]{0:T(1024)S(1)}, u32[]{:S(2)}, u32[]{:S(2)}) collective-permute-start(f32[1024]{0:T(1024)S(1)} %multiply_select_fusion.2), channel_id=1, source_target_pairs={{0,4},{2,6},{4,8},{6,10},{8,12},{10,14},{12,16},{14,18},{16,20},{1... | collective-permute-start | bytes 12296 | tf_op jit(solution)/shard_map/ppermute | solution.py:17
  162.6 12.2 %collective-permute-start.2 = (bf16[128,1024]{1,0:T(8,128)(2,1)S(1)}, bf16[128,1024]{1,0:T(8,128)(2,1)S(1)}, u32[]{:S(2)}, u32[]{:S(2)}) collective-permute-start(bf16[128,1024]{1,0:T(8,128)(2,1)S(1)} %convert_element_type.151), channel_id=1, source_target_pairs={{0,2},{2,4},{4,6},{6,8},{8,10},{10,12},{12,14},{14,16},{16,18},{18... | collective-permute-start | bytes 786440 | tf_op jit(solution)/shard_map/ppermute | solution.py:17
  174.9 10.8 %collective-permute-start.4 = (bf16[128,1024]{1,0:T(8,128)(2,1)S(1)}, bf16[128,1024]{1,0:T(8,128)(2,1)S(1)}, u32[]{:S(2)}, u32[]{:S(2)}) collective-permute-start(bf16[128,1024]{1,0:T(8,128)(2,1)S(1)} %fusion.16), channel_id=1, source_target_pairs={{0,4},{2,6},{4,8},{6,10},{8,12},{10,14},{12,16},{14,18},{16,20},{1... | collective-permute-start | bytes 786440 | tf_op jit(solution)/shard_map/ppermute | solution.py:17
  185.8 8.3 %collective-permute-start.6 = (bf16[128,1024]{1,0:T(8,128)(2,1)S(1)}, bf16[128,1024]{1,0:T(8,128)(2,1)S(1)}, u32[]{:S(2)}, u32[]{:S(2)}) collective-permute-start(bf16[128,1024]{1,0:T(8,128)(2,1)S(1)} %get-tuple-element.13), channel_id=1, source_target_pairs={{0,8},{2,10},{4,12},{6,14},{8,16},{10,18},{12,20},{14,22},{16,24},... | collective-permute-start | bytes 786440 | tf_op jit(solution)/shard_map/ppermute | solution.py:17
  188.0 8.5 %collective-permute-start.7 = (f32[1024]{0:T(1024)S(1)}, f32[1024]{0:T(1024)S(1)}, u32[]{:S(2)}, u32[]{:S(2)}) collective-permute-start(f32[1024]{0:T(1024)S(1)} %multiply_select_fusion.1), channel_id=1, source_target_pairs={{0,8},{2,10},{4,12},{6,14},{8,16},{10,18},{12,20},{14,22},{16,24},... | collective-permute-start | bytes 12296 | tf_op jit(solution)/shard_map/ppermute | solution.py:17
  194.2 15.7 %collective-permute-start.8 = (bf16[128,1024]{1,0:T(8,128)(2,1)S(1)}, bf16[128,1024]{1,0:T(8,128)(2,1)S(1)}, u32[]{:S(2)}, u32[]{:S(2)}) collective-permute-start(bf16[128,1024]{1,0:T(8,128)(2,1)S(1)} %fusion.17), channel_id=1, source_target_pairs={{0,16},{2,18},{4,20},{6,22},{8,24},{10,26},{12,28},{14,30},{1,17},... | collective-permute-start | bytes 786440 | tf_op jit(solution)/shard_map/ppermute | solution.py:17
  210.0 9.1 %collective-permute-start.9 = (bf16[128,1024]{1,0:T(8,128)(2,1)S(1)}, bf16[128,1024]{1,0:T(8,128)(2,1)S(1)}, u32[]{:S(2)}, u32[]{:S(2)}) collective-permute-start(bf16[128,1024]{1,0:T(8,128)(2,1)S(1)} %add_convert_fusion.1), channel_id=1, source_target_pairs={{0,2},{2,4},{4,6},{6,8},{8,10},{10,12},{12,14},{14,16},{16,18},{18... | collective-permute-start | bytes 786440 | tf_op jit(solution)/shard_map/ppermute | solution.py:17
  225.9 29.3 %copy-start.13 = (f32[1024]{0:T(1024)S(1)}, f32[1024]{0:T(1024)}, u32[]{:S(2)}) copy-start(f32[1024]{0:T(1024)} %param.27) | copy-start | bytes 12292
  225.9 34.5 %copy-start.1 = (bf16[16,128,512]{2,1,0:T(8,128)(2,1)S(1)}, bf16[16,128,512]{2,1,0:T(8,128)(2,1)}, u32[]{:S(2)}) copy-start(bf16[16,128,512]{2,1,0:T(8,128)(2,1)} %param.14) | copy-start | bytes 6291460
  (10 other events, 55.3 us)
Sparse Core Ops, SparseCore 0:
  74.9 16.7 all-gather.1

commit v8 on v7

--- a/solution.py
+++ b/solution.py
@@ -176,21 +176,17 @@
     taps = conv_x.shape[0]
     keep_rows = taps - 1
     owner = dest_tile // tiles_dev
-    offset = dest_tile % tiles_dev
     slots = jnp.arange(seq_count, dtype=jnp.int32)
     pick = (owner[None, :] == slots[:, None]).astype(jnp.float32)
     outgoing = jnp.einsum(
         "sj,jrc->src", pick.astype(jnp.bfloat16), ingest, preferred_element_type=jnp.float32
     ).astype(jnp.bfloat16)
-    marks = (
-        jnp.dot(pick, (offset + 1).astype(jnp.float32), precision=lax.Precision.HIGHEST) - 1.0
-    ).astype(jnp.bfloat16)
-    incoming, got_marks = (
-        lax.all_to_all(outgoing, "seq", split_axis=0, concat_axis=0, tiled=True),
-        lax.all_to_all(marks, "seq", split_axis=0, concat_axis=0, tiled=True),
-    )
-    local_slots = jnp.arange(tiles_dev, dtype=jnp.float32)
-    place = (got_marks.astype(jnp.float32)[None, :] == local_slots[:, None]).astype(jnp.bfloat16)
+    incoming = lax.all_to_all(outgoing, "seq", split_axis=0, concat_axis=0, tiled=True)
+    every_dest = lax.all_gather(dest_tile, "seq", tiled=True).reshape(seq_count, tiles_dev)
+    mine = every_dest // tiles_dev == lax.axis_index("seq")
+    got_slot = jnp.sum(jnp.where(mine, every_dest % tiles_dev, 0), 1)
+    local_slots = jnp.arange(tiles_dev, dtype=jnp.int32)
+    place = (got_slot[None, :] == local_slots[:, None]).astype(jnp.bfloat16)
     arrived = jnp.einsum("js,src->jrc", place, incoming, preferred_element_type=jnp.float32).astype(
         jnp.bfloat16
     )
@@ -270,7 +266,7 @@
     carried = tile_state.astype(jnp.bfloat16)
     d_full = jnp.repeat(d_skip, head_dim)[None, :]
     gated, row_sq = mix_tiles(conv_out, zx, cumul, cumul_t, dt_t, later, carried, d_full)
-    sums = lax.psum(row_sq, "head")
+    sums = jnp.sum(lax.all_gather(row_sq, "head"), 0)
     return (gated * lax.rsqrt(sums / INNER + EPSILON) * norm_gain[None, :]).astype(jnp.bfloat16)
 
 

time: 270 us -> 266 us (0.985)
  waiting for transfers between devices: 81.3 us -> 35.2 us
  blocking collectives: 8.53 us -> 54 us
  starting transfers between devices: 31.2 us -> 25.1 us
    all_to_all x1, waiting for transfers between devices: 45 us -> 0.01 us  [shards(): lax.all_to_all(outgoing, 'seq', split_axis=0, concat_axis=0, tiled=True)]
    unnamed x0 -> x1, blocking collectives: none -> 45 us
    all_gather x0 -> x1, blocking collectives: none -> 8.99 us  [shards(): sums = jnp.sum(lax.all_gather(row_sq, 'head'), 0)]
    psum x1 -> x0, blocking collectives: 8.53 us -> none  [shards(): sums = lax.psum(row_sq, 'head')]
    all_to_all x1 -> x0, starting transfers between devices: 6.38 us -> none  [shards(): lax.all_to_all(marks, 'seq', split_axis=0, concat_axis=0, tiled=True)]
    unnamed x46 -> x53, local copies, waits for them, and re-layouts: 13.7 us -> 15.4 us
  transfers between devices with their start and end apart: 13 -> 12, of which waited for: 6 -> 5; matrix products, arithmetic and copies ran while one was open for 21% -> 20% of each run, Pallas kernels for 6% -> 6%
where the time goes in v8:
time: 266 us; the launch traced here: 263 us
  blocking collectives  54 us (20%)
  other arithmetic  53.3 us (20%)
  Pallas kernels  35.6 us (13%)
  waiting for transfers between devices  35.2 us (13%)
  local copies, waits for them, and re-layouts  27.8 us (10%)
  starting transfers between devices  25.1 us (9%)
  matrix products  17.3 us (7%)
  between operations  14.7 us (6%)
    unnamed x1, blocking collectives  45 us
    ppermute x10, waiting for transfers between devices, shifted(): return lax.ppermute(x, axis, pairs)  33 us
    pallas_call x1, Pallas kernels, mix_tiles(): pl.pallas_call(mix_tile, grid=(tiles_dev,), in_specs=[pl.BlockSpec((tile_...  20.3 us
    ppermute x10, starting transfers between devices, shifted(): return lax.ppermute(x, axis, pairs)  18.5 us
    unnamed x53, local copies, waits for them, and re-layouts  15.4 us
    pallas_call x1, Pallas kernels, contrib_tiles(): pl.pallas_call(contrib_tile, grid=(tiles_dev,), in_specs=[pl.BlockSpec((t...  15.4 us
    dot_general x3, matrix products, shards(): jnp.dot(piece, weight, preferred_element_type=jnp.float32)  14.4 us
    unnamed x14, other arithmetic  12.9 us
  transfers between devices with their start and end apart: 12, of which 5 were waited for; matrix products, arithmetic and copies ran while one was open for 20% of the time, Pallas kernels for 6%

profile of v8, /device:TPU:29, one launch (start us, length us, event | category | flops | bytes accessed | tf_op | source)
XLA Modules:
  0.0 263.0 jit_solution(6354571044917996798)
XLA Ops:
  9.5 2.5 copy.66
  12.0 6.5 %all-to-all-start = ((bf16[16,128,512]{2,1,0:T(8,128)(2,1)}), bf16[16,128,512]{2,1,0:T(8,128)(2,1)S(1)}, u32[]{:S(2)}, u32[]{:S(2)}) async-start(bf16[16,128,512]{2,1,0:T(8,128)(2,1)} %copy.66), calls=%async_computation | async-start | bytes 4194304 | tf_op jit(solution)/shard_map/all_to_all | solution.py:184
  20.1 45.0 %all-reduce.2 = s32[256]{0:T(256)S(1)} all-reduce(s32[256]{0:T(256)S(1)} %dynamic-update-slice), channel_id=1, replica_groups=mesh['seq'=16,'head'=2] {'seq'}, use_global_device_ids=true, to_apply=%add.2 | all-reduce | flops 256 | bytes 2048
  66.7 2.5 copy.68
  70.9 2.6 collective-permute-start
  73.5 5.6 %copy.80 = bf16[128,8,2,1024]{3,1,2,0:T(8,128)(2,1)} copy(bf16[128,8,2,1024]{3,2,1,0:T(2,128)(2,1)} %bitcast.78) | data formatting | bytes 8388608
  83.1 2.1 all-gather.3.cloned.1.call-done
  85.3 11.9 %convolution_convert_fusion.gate_ref = bf16[2048,2048]{1,0:T(8,128)(2,1)S(1)} fusion(bf16[2048,1024]{1,0:T(8,128)(2,1)} %all-gather.3.cloned.1.call-done, bf16[1024,2048]{1,0:T(8,128)(2,1)} %bitcast.79), kind=kOutput, calls=%fused_computation.4 | convolution fusion | flops 8594128896 | bytes 16777216 | tf_op jit(solution)/shard_map/dot_general | solution.py:198
  97.9 4.5 %copy-done.8 = bf16[2048,1024]{1,0:T(8,128)(2,1)S(1)} copy-done((bf16[2048,1024]{1,0:T(8,128)(2,1)S(1)}, bf16[2048,1024]{1,0:T(8,128)(2,1)}, u32[]{:S(2)}) %copy-start.8) | copy-done | bytes 4194328
  103.8 3.1 %collective-permute-start.1 = (bf16[3,1280]{1,0:T(4,128)(2,1)S(1)}, bf16[3,1280]{1,0:T(4,128)(2,1)S(1)}, u32[]{:S(2)}, u32[]{:S(2)}) collective-permute-start(bf16[3,1280]{1,0:T(4,128)(2,1)S(1)} %fusion.25), channel_id=1, source_target_pairs={{0,2},{2,4},{4,6},{6,8},{8,10},{10,12},{12,14},{14,16},{16,18},{18... | collective-permute-start | bytes 23048 | tf_op jit(solution)/shard_map/ppermute | solution.py:17
  117.9 3.8 %maximum_maximum_fusion = bf16[2051,1280]{1,0:T(8,128)(2,1)S(1)} fusion(bf16[2048,256]{1,0:T(8,128)(2,1)S(1)} %convolution_convert_fusion.1, bf16[2048,1024]{1,0:T(8,128)(2,1)} %copy-done.4, bf16[3,1280]{1,0:T(4,128)(2,1)S(1)} %collective-permute-done.1), kind=kLoop, calls=%fused_computation.7 | loop fusion | flops 15751680 | bytes 10501120 | tf_op jit(solution)/shard_map/concatenate | solution.py:213
  121.8 10.8 %multiply_convert_fusion.x_ref.b_ref.c_ref = bf16[2048,1280]{1,0:T(8,128)(2,1)S(1)} fusion(bf16[2048,256]{1,0:T(8,128)(2,1)S(1)} %convolution_convert_fusion.1, bf16[2051,1280]{1,0:T(8,128)(2,1)S(1)} %maximum_maximum_fusion, f32[1280]{0:T(1024)S(1)} %get-tuple-element.10, f32[1280]{0:T(1024)S(1)} %get-tuple-element.11, f32[1280]{0:T(1024)S(1)} %get-tuple-element.12, ...), kind=kLoop, calls=%fused_computation | loop fusion | flops 60293120 | bytes 26246144 | tf_op jit(solution)/shard_map/convert_element_type | solution.py:226
  132.6 2.4 copy-done.2
  136.0 15.4 %shard_map.136 = f32[16,128,1024]{2,1,0:T(8,128)} custom-call(bf16[2048,1280]{1,0:T(8,128)(2,1)} %copy-done.2, bf16[16,128,128]{2,1,0:T(8,128)(2,1)} %bitcast.81, f32[16,128,16]{2,1,0:T(8,128)} %multiply_multiply_fusion.end_ref), custom_call_target="tpu_custom_call" | custom-call | flops 536870912 | bytes 13107200 | tf_op jit(solution)/shard_map/pallas_call | solution.py:91
  151.4 4.7 %multiply_reduce_fusion = f32[128,1024]{1,0:T(8,128)S(1)} fusion(f32[16,128,1024]{2,1,0:T(8,128)} %shard_map.136, f32[16,1024]{1,0:T(8,128)S(1)} %mul.445), kind=kLoop, calls=%fused_computation.3 | loop fusion | flops 4063232 | bytes 8978432 | tf_op jit(solution)/shard_map/reduce_sum | solution.py:248
  170.6 8.5 %collective-permute-done.4 = bf16[128,1024]{1,0:T(8,128)(2,1)S(1)} collective-permute-done((bf16[128,1024]{1,0:T(8,128)(2,1)S(1)}, bf16[128,1024]{1,0:T(8,128)(2,1)S(1)}, u32[]{:S(2)}, u32[]{:S(2)}) %collective-permute-start.4) | collective-permute-done | bytes 262176 | tf_op jit(solution)/shard_map/ppermute | solution.py:17
  182.7 4.8 %collective-permute-done.6 = bf16[128,1024]{1,0:T(8,128)(2,1)S(1)} collective-permute-done((bf16[128,1024]{1,0:T(8,128)(2,1)S(1)}, bf16[128,1024]{1,0:T(8,128)(2,1)S(1)}, u32[]{:S(2)}, u32[]{:S(2)}) %collective-permute-start.6) | collective-permute-done | bytes 262176 | tf_op jit(solution)/shard_map/ppermute | solution.py:17
  189.9 13.4 %collective-permute-done.8 = bf16[128,1024]{1,0:T(8,128)(2,1)S(1)} collective-permute-done((bf16[128,1024]{1,0:T(8,128)(2,1)S(1)}, bf16[128,1024]{1,0:T(8,128)(2,1)S(1)}, u32[]{:S(2)}, u32[]{:S(2)}) %collective-permute-start.8) | collective-permute-done | bytes 262176 | tf_op jit(solution)/shard_map/ppermute | solution.py:17
  206.3 6.3 %collective-permute-done.9 = bf16[128,1024]{1,0:T(8,128)(2,1)S(1)} collective-permute-done((bf16[128,1024]{1,0:T(8,128)(2,1)S(1)}, bf16[128,1024]{1,0:T(8,128)(2,1)S(1)}, u32[]{:S(2)}, u32[]{:S(2)}) %collective-permute-start.9) | collective-permute-done | bytes 262176 | tf_op jit(solution)/shard_map/ppermute | solution.py:17
  212.6 6.8 %add_convert_fusion.car_ref = bf16[16,128,1024]{2,1,0:T(8,128)(2,1)} fusion(f32[16,128,1024]{2,1,0:T(8,128)} %fusion.11, f32[128,1024]{1,0:T(8,128)S(1)} %convert_element_type.140, f32[16,1024]{1,0:T(8,128)S(1)} %mul.443), kind=kLoop, calls=%fused_computation.2 | loop fusion | flops 6291456 | bytes 13172736 | tf_op jit(solution)/shard_map/convert_element_type | solution.py:266
  219.4 20.3 %shard_map.137 = (f32[2048,1024]{1,0:T(8,128)}, f32[2048,1]{1,0:T(8,128)}) custom-call(bf16[2048,1280]{1,0:T(8,128)(2,1)} %copy-done.2, bf16[2048,1280]{1,0:T(8,128)(2,1)} %copy-done.2, bf16[2048,1280]{1,0:T(8,128)(2,1)} %copy-done.2, f32[16,128,16]{2,1,0:T(8,128)} %bitcast.76, f32[16,16,128]{2,1,0:T(8,128)} %copy-done.9, ...), custom_call_target="tpu_custom_call" | custom-call | flops 3288334336 | bytes 25165824 | tf_op jit(solution)/shard_map/pallas_call | solution.py:119
  239.7 9.0 %all-gather = f32[4096,1]{1,0:T(8,128)} all-gather(f32[2048,1]{1,0:T(8,128)} %get-tuple-element.8), channel_id=2, replica_groups=mesh['seq'=16,'head'=2] {'head'}, dimensions={0}, use_global_device_ids=true | all-gather | bytes 24576 | tf_op jit(solution)/shard_map/all_gather | solution.py:269
  248.7 2.2 reduce.8
  251.0 5.2 %multiply_convert_fusion.1 = bf16[2048,1024]{1,0:T(8,128)(2,1)} fusion(f32[2048,1024]{1,0:T(8,128)} %get-tuple-element.7, f32[1024]{0:T(1024)S(1)} %copy-done.13, f32[2048]{0:T(1024)S(1)} %add_rsqrt_fusion), kind=kLoop, calls=%fused_computation.1 | loop fusion | flops 6291456 | bytes 12595200 | tf_op jit(solution)/shard_map/convert_element_type | solution.py:270
  (178 shorter events, 48.4 us)
Async XLA Ops:
  6.5 13.3 %copy-start.20 = (s32[16]{0:T(128)S(1)}, s32[16]{0:T(128)}, u32[]{:S(2)}) copy-start(s32[16]{0:T(128)} %param.15) | copy-start | bytes 196
  12.0 57.3 %copy-start.11 = (s32[16]{0:T(128)S(1)}, s32[16]{0:T(128)}, u32[]{:S(2)}) copy-start(s32[16]{0:T(128)} %param.16) | copy-start | bytes 196
  12.0 53.3 %all-to-all-start = ((bf16[16,128,512]{2,1,0:T(8,128)(2,1)}), bf16[16,128,512]{2,1,0:T(8,128)(2,1)S(1)}, u32[]{:S(2)}, u32[]{:S(2)}) async-start(bf16[16,128,512]{2,1,0:T(8,128)(2,1)} %copy.66), calls=%async_computation | async-start | bytes 4194304 | tf_op jit(solution)/shard_map/all_to_all | solution.py:184
  18.5 66.8 %all-gather.3.cloned.1.call-start = ((), (), s32[]{:S(2)}) async-start(), calls=%async_computation.1 | async-start | bytes 6291456 | tf_op jit(solution)/shard_map/all_gather | solution.py:196
  66.6 12.5 %copy-start.18 = (f32[16]{0:T(128)S(1)}, f32[16]{0:T(128)}, u32[]{:S(2)}) copy-start(f32[16]{0:T(128)} %param.26) | copy-start | bytes 196
  66.7 13.2 %copy-start.12 = (f32[4,1024]{1,0:T(4,128)S(1)}, f32[4,1024]{1,0:T(4,128)}, u32[]{:S(2)}) copy-start(f32[4,1024]{1,0:T(4,128)} %param.22) | copy-start | bytes 49156
  66.7 13.2 %copy-start.14 = (f32[4,256]{1,0:T(4,128)S(1)}, f32[4,256]{1,0:T(4,128)}, u32[]{:S(2)}) copy-start(f32[4,256]{1,0:T(4,128)} %param.23) | copy-start | bytes 12292
  66.7 13.2 %copy-start.15 = (f32[1024]{0:T(1024)S(1)}, f32[1024]{0:T(1024)}, u32[]{:S(2)}) copy-start(f32[1024]{0:T(1024)} %param.24) | copy-start | bytes 12292
  66.7 13.2 %copy-start.17 = (f32[256]{0:T(256)S(1)}, f32[256]{0:T(256)}, u32[]{:S(2)}) copy-start(f32[256]{0:T(256)} %param.25) | copy-start | bytes 3076
  66.7 14.5 %copy-start.21 = (f32[16]{0:T(128)S(1)}, f32[16]{0:T(128)}, u32[]{:S(2)}) copy-start(f32[16]{0:T(128)} %param.21) | copy-start | bytes 196
  70.9 12.1 %collective-permute-start = (bf16[3]{0:T(256)(128)(2,1)S(1)}, bf16[3]{0:T(256)(128)(2,1)S(1)}, u32[]{:S(2)}, u32[]{:S(2)}) collective-permute-start(bf16[3]{0:T(256)(128)(2,1)S(1)} %fusion.44), channel_id=1, source_target_pairs={{0,2},{2,4},{4,6},{6,8},{8,10},{10,12},{12,14},{14,16},{16,18},{18... | collective-permute-start | bytes 26 | tf_op jit(solution)/shard_map/ppermute | solution.py:17
  103.8 14.1 %collective-permute-start.1 = (bf16[3,1280]{1,0:T(4,128)(2,1)S(1)}, bf16[3,1280]{1,0:T(4,128)(2,1)S(1)}, u32[]{:S(2)}, u32[]{:S(2)}) collective-permute-start(bf16[3,1280]{1,0:T(4,128)(2,1)S(1)} %fusion.25), channel_id=1, source_target_pairs={{0,2},{2,4},{4,6},{6,8},{8,10},{10,12},{12,14},{14,16},{16,18},{18... | collective-permute-start | bytes 23048 | tf_op jit(solution)/shard_map/ppermute | solution.py:17
  109.2 12.5 %copy-start.9 = (f32[16,16,128]{2,1,0:T(8,128)}, f32[16,16,128]{2,1,0:T(8,128)S(1)}, u32[]{:S(2)}) copy-start(f32[16,16,128]{2,1,0:T(8,128)S(1)} %fusion.21.cumt_ref) | copy-start | bytes 393220
  109.6 23.0 %copy-start.7 = (f32[16,16,128]{1,2,0:T(8,128)}, f32[16,16,128]{1,2,0:T(8,128)S(1)}, u32[]{:S(2)}) copy-start(f32[16,16,128]{1,2,0:T(8,128)S(1)} %copy.73) | copy-start | bytes 393220
  110.2 5.9 %collective-permute-start.3 = (f32[1024]{0:T(1024)S(1)}, f32[1024]{0:T(1024)S(1)}, u32[]{:S(2)}, u32[]{:S(2)}) collective-permute-start(f32[1024]{0:T(1024)S(1)} %mul.448), channel_id=1, source_target_pairs={{0,2},{2,4},{4,6},{6,8},{8,10},{10,12},{12,14},{14,16},{16,18},{18... | collective-permute-start | bytes 12296 | tf_op jit(solution)/shard_map/ppermute | solution.py:17
  116.1 65.3 %collective-permute-start.5 = (f32[1024]{0:T(1024)S(1)}, f32[1024]{0:T(1024)S(1)}, u32[]{:S(2)}, u32[]{:S(2)}) collective-permute-start(f32[1024]{0:T(1024)S(1)} %multiply_select_fusion.2), channel_id=1, source_target_pairs={{0,4},{2,6},{4,8},{6,10},{8,12},{10,14},{12,16},{14,18},{16,20},{1... | collective-permute-start | bytes 12296 | tf_op jit(solution)/shard_map/ppermute | solution.py:17
  156.1 12.1 %collective-permute-start.2 = (bf16[128,1024]{1,0:T(8,128)(2,1)S(1)}, bf16[128,1024]{1,0:T(8,128)(2,1)S(1)}, u32[]{:S(2)}, u32[]{:S(2)}) collective-permute-start(bf16[128,1024]{1,0:T(8,128)(2,1)S(1)} %convert_element_type.131), channel_id=1, source_target_pairs={{0,2},{2,4},{4,6},{6,8},{8,10},{10,12},{12,14},{14,16},{16,18},{18... | collective-permute-start | bytes 786440 | tf_op jit(solution)/shard_map/ppermute | solution.py:17
  168.4 10.8 %collective-permute-start.4 = (bf16[128,1024]{1,0:T(8,128)(2,1)S(1)}, bf16[128,1024]{1,0:T(8,128)(2,1)S(1)}, u32[]{:S(2)}, u32[]{:S(2)}) collective-permute-start(bf16[128,1024]{1,0:T(8,128)(2,1)S(1)} %fusion.13), channel_id=1, source_target_pairs={{0,4},{2,6},{4,8},{6,10},{8,12},{10,14},{12,16},{14,18},{16,20},{1... | collective-permute-start | bytes 786440 | tf_op jit(solution)/shard_map/ppermute | solution.py:17
  179.3 8.3 %collective-permute-start.6 = (bf16[128,1024]{1,0:T(8,128)(2,1)S(1)}, bf16[128,1024]{1,0:T(8,128)(2,1)S(1)}, u32[]{:S(2)}, u32[]{:S(2)}) collective-permute-start(bf16[128,1024]{1,0:T(8,128)(2,1)S(1)} %get-tuple-element.13), channel_id=1, source_target_pairs={{0,8},{2,10},{4,12},{6,14},{8,16},{10,18},{12,20},{14,22},{16,24},... | collective-permute-start | bytes 786440 | tf_op jit(solution)/shard_map/ppermute | solution.py:17
  181.4 8.5 %collective-permute-start.7 = (f32[1024]{0:T(1024)S(1)}, f32[1024]{0:T(1024)S(1)}, u32[]{:S(2)}, u32[]{:S(2)}) collective-permute-start(f32[1024]{0:T(1024)S(1)} %multiply_select_fusion.1), channel_id=1, source_target_pairs={{0,8},{2,10},{4,12},{6,14},{8,16},{10,18},{12,20},{14,22},{16,24},... | collective-permute-start | bytes 12296 | tf_op jit(solution)/shard_map/ppermute | solution.py:17
  187.6 15.7 %collective-permute-start.8 = (bf16[128,1024]{1,0:T(8,128)(2,1)S(1)}, bf16[128,1024]{1,0:T(8,128)(2,1)S(1)}, u32[]{:S(2)}, u32[]{:S(2)}) collective-permute-start(bf16[128,1024]{1,0:T(8,128)(2,1)S(1)} %fusion.14), channel_id=1, source_target_pairs={{0,16},{2,18},{4,20},{6,22},{8,24},{10,26},{12,28},{14,30},{1,17},... | collective-permute-start | bytes 786440 | tf_op jit(solution)/shard_map/ppermute | solution.py:17
  203.4 9.1 %collective-permute-start.9 = (bf16[128,1024]{1,0:T(8,128)(2,1)S(1)}, bf16[128,1024]{1,0:T(8,128)(2,1)S(1)}, u32[]{:S(2)}, u32[]{:S(2)}) collective-permute-start(bf16[128,1024]{1,0:T(8,128)(2,1)S(1)} %add_convert_fusion.1), channel_id=1, source_target_pairs={{0,2},{2,4},{4,6},{6,8},{8,10},{10,12},{12,14},{14,16},{16,18},{18... | collective-permute-start | bytes 786440 | tf_op jit(solution)/shard_map/ppermute | solution.py:17
  219.4 31.5 %copy-start.13 = (f32[1024]{0:T(1024)S(1)}, f32[1024]{0:T(1024)}, u32[]{:S(2)}) copy-start(f32[1024]{0:T(1024)} %param.27) | copy-start | bytes 12292
  239.7 16.5 %copy-start.1 = (bf16[16,128,512]{2,1,0:T(8,128)(2,1)S(1)}, bf16[16,128,512]{2,1,0:T(8,128)(2,1)}, u32[]{:S(2)}) copy-start(bf16[16,128,512]{2,1,0:T(8,128)(2,1)} %param.14) | copy-start | bytes 6291460
  (11 other events, 60.2 us)
Sparse Core Ops, SparseCore 0:
  69.4 15.8 all-gather.2

commit v9 on v8

--- a/solution.py
+++ b/solution.py
@@ -257,8 +257,16 @@
     run_decay = widen(through[tiles_dev - 1])
     distance = 1
     while distance < seq_count:
-        got_decay, got_state = shifted((run_decay, run_state.astype(jnp.bfloat16)), "seq", distance)
-        run_state = run_state + run_decay[None, :] * got_state.astype(jnp.float32)
+        high = run_decay.astype(jnp.bfloat16)
+        rest = run_decay - high.astype(jnp.float32)
+        middle = rest.astype(jnp.bfloat16)
+        low = (rest - middle.astype(jnp.float32)).astype(jnp.bfloat16)
+        payload = jnp.concatenate(
+            [run_state.astype(jnp.bfloat16), high[None], middle[None], low[None]], 0
+        )
+        got = shifted(payload, "seq", distance).astype(jnp.float32)
+        got_decay = got[state_dim] + got[state_dim + 1] + got[state_dim + 2]
+        run_state = run_state + run_decay[None, :] * got[:state_dim]
         run_decay = jnp.where(position >= distance, run_decay * got_decay, run_decay)
         distance *= 2
     entering = shifted(run_state.astype(jnp.bfloat16), "seq", 1).astype(jnp.float32)

time: 266 us -> 261 us (0.981)
  starting transfers between devices: 25.1 us -> 22.3 us
    ppermute x10 -> x7, starting transfers between devices: 18.5 us -> 15.7 us  [shifted(): return lax.ppermute(x, axis, pairs)]
    ppermute x10 -> x7, waiting for transfers between devices: 33 us -> 32.9 us  [shifted(): return lax.ppermute(x, axis, pairs)]
  transfers between devices with their start and end apart: 12 -> 9, of which waited for: 5 -> 6; matrix products, arithmetic and copies ran while one was open for 20% -> 13% of each run, Pallas kernels for 6% -> 0%
where the time goes in v9:
time: 261 us; the launch traced here: 260 us
  other arithmetic  53.9 us (21%)
  blocking collectives  52.8 us (20%)
  Pallas kernels  35.6 us (14%)
  waiting for transfers between devices  35.1 us (13%)
  local copies, waits for them, and re-layouts  27.9 us (11%)
  starting transfers between devices  22.3 us (9%)
  matrix products  17.3 us (7%)
  between operations  14.7 us (6%)
    unnamed x1, blocking collectives  45.1 us
    ppermute x7, waiting for transfers between devices, shifted(): return lax.ppermute(x, axis, pairs)  32.9 us
    pallas_call x1, Pallas kernels, mix_tiles(): pl.pallas_call(mix_tile, grid=(tiles_dev,), in_specs=[pl.BlockSpec((tile_...  20.2 us
    ppermute x7, starting transfers between devices, shifted(): return lax.ppermute(x, axis, pairs)  15.7 us
    pallas_call x1, Pallas kernels, contrib_tiles(): pl.pallas_call(contrib_tile, grid=(tiles_dev,), in_specs=[pl.BlockSpec((t...  15.3 us
    unnamed x53, local copies, waits for them, and re-layouts  15.3 us
    dot_general x3, matrix products, shards(): jnp.dot(piece, weight, preferred_element_type=jnp.float32)  14.4 us
    unnamed x14, other arithmetic  13 us
  transfers between devices with their start and end apart: 9, of which 6 were waited for; matrix products, arithmetic and copies ran while one was open for 13% of the time, Pallas kernels for 0%

profile of v9, /device:TPU:29, one launch (start us, length us, event | category | flops | bytes accessed | tf_op | source)
XLA Modules:
  0.0 259.5 jit_solution(1407406184075775000)
XLA Ops:
  9.5 2.5 copy.66
  12.0 6.5 %all-to-all-start = ((bf16[16,128,512]{2,1,0:T(8,128)(2,1)}), bf16[16,128,512]{2,1,0:T(8,128)(2,1)S(1)}, u32[]{:S(2)}, u32[]{:S(2)}) async-start(bf16[16,128,512]{2,1,0:T(8,128)(2,1)} %copy.66), calls=%async_computation | async-start | bytes 4194304 | tf_op jit(solution)/shard_map/all_to_all | solution.py:184
  20.0 45.1 %all-reduce.2 = s32[256]{0:T(256)S(1)} all-reduce(s32[256]{0:T(256)S(1)} %dynamic-update-slice), channel_id=1, replica_groups=mesh['seq'=16,'head'=2] {'seq'}, use_global_device_ids=true, to_apply=%add.2 | all-reduce | flops 256 | bytes 2048
  66.7 2.5 copy.68
  70.9 2.6 %collective-permute-start = (bf16[3]{0:T(256)(128)(2,1)S(1)}, bf16[3]{0:T(256)(128)(2,1)S(1)}, u32[]{:S(2)}, u32[]{:S(2)}) collective-permute-start(bf16[3]{0:T(256)(128)(2,1)S(1)} %fusion.47), channel_id=1, source_target_pairs={{0,2},{2,4},{4,6},{6,8},{8,10},{10,12},{12,14},{14,16},{16,18},{18... | collective-permute-start | bytes 26 | tf_op jit(solution)/shard_map/ppermute | solution.py:17
  73.5 5.6 %copy.80 = bf16[128,8,2,1024]{3,1,2,0:T(8,128)(2,1)} copy(bf16[128,8,2,1024]{3,2,1,0:T(2,128)(2,1)} %bitcast.81) | data formatting | bytes 8388608
  85.2 11.9 %convolution_convert_fusion.gate_ref = bf16[2048,2048]{1,0:T(8,128)(2,1)S(1)} fusion(bf16[2048,1024]{1,0:T(8,128)(2,1)} %all-gather.3.cloned.1.call-done, bf16[1024,2048]{1,0:T(8,128)(2,1)} %bitcast.82), kind=kOutput, calls=%fused_computation.4 | convolution fusion | flops 8594128896 | bytes 16777216 | tf_op jit(solution)/shard_map/dot_general | solution.py:198
  97.9 4.5 %copy-done.8 = bf16[2048,1024]{1,0:T(8,128)(2,1)S(1)} copy-done((bf16[2048,1024]{1,0:T(8,128)(2,1)S(1)}, bf16[2048,1024]{1,0:T(8,128)(2,1)}, u32[]{:S(2)}) %copy-start.8) | copy-done | bytes 4194328
  103.8 3.3 %collective-permute-start.1 = (bf16[3,1280]{1,0:T(4,128)(2,1)S(1)}, bf16[3,1280]{1,0:T(4,128)(2,1)S(1)}, u32[]{:S(2)}, u32[]{:S(2)}) collective-permute-start(bf16[3,1280]{1,0:T(4,128)(2,1)S(1)} %fusion.28), channel_id=1, source_target_pairs={{0,2},{2,4},{4,6},{6,8},{8,10},{10,12},{12,14},{14,16},{16,18},{18... | collective-permute-start | bytes 23048 | tf_op jit(solution)/shard_map/ppermute | solution.py:17
  114.5 4.0 %maximum_maximum_fusion = bf16[2051,1280]{1,0:T(8,128)(2,1)S(1)} fusion(bf16[2048,256]{1,0:T(8,128)(2,1)S(1)} %convolution_convert_fusion.1, bf16[2048,1024]{1,0:T(8,128)(2,1)} %copy-done.4, bf16[3,1280]{1,0:T(4,128)(2,1)S(1)} %collective-permute-done.1), kind=kLoop, calls=%fused_computation.7 | loop fusion | flops 15751680 | bytes 10501120 | tf_op jit(solution)/shard_map/concatenate | solution.py:213
  118.5 10.8 %multiply_convert_fusion.x_ref.b_ref.c_ref = bf16[2048,1280]{1,0:T(8,128)(2,1)S(1)} fusion(bf16[2048,256]{1,0:T(8,128)(2,1)S(1)} %convolution_convert_fusion.1, bf16[2051,1280]{1,0:T(8,128)(2,1)S(1)} %maximum_maximum_fusion, f32[1280]{0:T(1024)S(1)} %get-tuple-element.10, f32[1280]{0:T(1024)S(1)} %get-tuple-element.11, f32[1280]{0:T(1024)S(1)} %get-tuple-element.12, ...), kind=kLoop, calls=%fused_computation | loop fusion | flops 60293120 | bytes 26246144 | tf_op jit(solution)/shard_map/convert_element_type | solution.py:226
  129.4 2.4 copy-done.2
  132.8 15.3 %shard_map.136 = f32[16,128,1024]{2,1,0:T(8,128)} custom-call(bf16[2048,1280]{1,0:T(8,128)(2,1)} %copy-done.2, bf16[16,128,128]{2,1,0:T(8,128)(2,1)} %bitcast.84, f32[16,128,16]{2,1,0:T(8,128)} %multiply_multiply_fusion.end_ref), custom_call_target="tpu_custom_call" | custom-call | flops 536870912 | bytes 13107200 | tf_op jit(solution)/shard_map/pallas_call | solution.py:91
  148.2 4.7 %multiply_reduce_fusion = f32[128,1024]{1,0:T(8,128)S(1)} fusion(f32[16,128,1024]{2,1,0:T(8,128)} %shard_map.136, f32[16,1024]{1,0:T(8,128)S(1)} %mul.475), kind=kLoop, calls=%fused_computation.3 | loop fusion | flops 4063232 | bytes 8978432 | tf_op jit(solution)/shard_map/reduce_sum | solution.py:248
  166.8 5.6 %collective-permute-done.3 = bf16[131,1024]{1,0:T(8,128)(2,1)S(1)} collective-permute-done((bf16[131,1024]{1,0:T(8,128)(2,1)S(1)}, bf16[131,1024]{1,0:T(8,128)(2,1)S(1)}, u32[]{:S(2)}, u32[]{:S(2)}) %collective-permute-start.3) | collective-permute-done | bytes 268320 | tf_op jit(solution)/shard_map/ppermute | solution.py:17
  175.8 5.1 %collective-permute-done.4 = bf16[131,1024]{1,0:T(8,128)(2,1)S(1)} collective-permute-done((bf16[131,1024]{1,0:T(8,128)(2,1)S(1)}, bf16[131,1024]{1,0:T(8,128)(2,1)S(1)}, u32[]{:S(2)}, u32[]{:S(2)}) %collective-permute-start.4) | collective-permute-done | bytes 268320 | tf_op jit(solution)/shard_map/ppermute | solution.py:17
  183.5 13.5 %collective-permute-done.5 = bf16[131,1024]{1,0:T(8,128)(2,1)S(1)} collective-permute-done((bf16[131,1024]{1,0:T(8,128)(2,1)S(1)}, bf16[131,1024]{1,0:T(8,128)(2,1)S(1)}, u32[]{:S(2)}, u32[]{:S(2)}) %collective-permute-start.5) | collective-permute-done | bytes 268320 | tf_op jit(solution)/shard_map/ppermute | solution.py:17
  197.1 4.0 %collective-permute-start.6 = (bf16[128,1024]{1,0:T(8,128)(2,1)S(1)}, bf16[128,1024]{1,0:T(8,128)(2,1)S(1)}, u32[]{:S(2)}, u32[]{:S(2)}) collective-permute-start(bf16[128,1024]{1,0:T(8,128)(2,1)S(1)} %add_convert_fusion.1), channel_id=1, source_target_pairs={{0,2},{2,4},{4,6},{6,8},{8,10},{10,12},{12,14},{14,16},{16,18},{18... | collective-permute-start | bytes 786440 | tf_op jit(solution)/shard_map/ppermute | solution.py:17
  202.0 8.5 %collective-permute-done.6 = bf16[128,1024]{1,0:T(8,128)(2,1)S(1)} collective-permute-done((bf16[128,1024]{1,0:T(8,128)(2,1)S(1)}, bf16[128,1024]{1,0:T(8,128)(2,1)S(1)}, u32[]{:S(2)}, u32[]{:S(2)}) %collective-permute-start.6) | collective-permute-done | bytes 262176 | tf_op jit(solution)/shard_map/ppermute | solution.py:17
  210.5 6.8 %add_convert_fusion.car_ref = bf16[16,128,1024]{2,1,0:T(8,128)(2,1)} fusion(f32[16,128,1024]{2,1,0:T(8,128)} %fusion.14, f32[128,1024]{1,0:T(8,128)S(1)} %convert_element_type.295, f32[16,1024]{1,0:T(8,128)S(1)} %mul.473), kind=kLoop, calls=%fused_computation.2 | loop fusion | flops 6291456 | bytes 13172736 | tf_op jit(solution)/shard_map/convert_element_type | solution.py:274
  217.3 20.2 %shard_map.137 = (f32[2048,1024]{1,0:T(8,128)}, f32[2048,1]{1,0:T(8,128)}) custom-call(bf16[2048,1280]{1,0:T(8,128)(2,1)} %copy-done.2, bf16[2048,1280]{1,0:T(8,128)(2,1)} %copy-done.2, bf16[2048,1280]{1,0:T(8,128)(2,1)} %copy-done.2, f32[16,128,16]{2,1,0:T(8,128)} %bitcast.79, f32[16,16,128]{2,1,0:T(8,128)} %copy-done.9, ...), custom_call_target="tpu_custom_call" | custom-call | flops 3288334336 | bytes 25165824 | tf_op jit(solution)/shard_map/pallas_call | solution.py:119
  237.5 7.7 %all-gather = f32[4096,1]{1,0:T(8,128)} all-gather(f32[2048,1]{1,0:T(8,128)} %get-tuple-element.8), channel_id=2, replica_groups=mesh['seq'=16,'head'=2] {'head'}, dimensions={0}, use_global_device_ids=true | all-gather | bytes 24576 | tf_op jit(solution)/shard_map/all_gather | solution.py:277
  245.2 2.2 reduce.8
  247.4 5.2 %multiply_convert_fusion.1 = bf16[2048,1024]{1,0:T(8,128)(2,1)} fusion(f32[2048,1024]{1,0:T(8,128)} %get-tuple-element.7, f32[1024]{0:T(1024)S(1)} %copy-done.13, f32[2048]{0:T(1024)S(1)} %add_rsqrt_fusion), kind=kLoop, calls=%fused_computation.1 | loop fusion | flops 6291456 | bytes 12595200 | tf_op jit(solution)/shard_map/convert_element_type | solution.py:278
  (184 shorter events, 44.3 us)
Async XLA Ops:
  6.5 12.0 %copy-start.22 = (u32[32]{0:T(128)S(1)}, u32[32]{0:T(128)}, u32[]{:S(2)}) copy-start(u32[32]{0:T(128)} %constant.79) | copy-start | bytes 388
  6.5 13.2 %copy-start.20 = (s32[16]{0:T(128)S(1)}, s32[16]{0:T(128)}, u32[]{:S(2)}) copy-start(s32[16]{0:T(128)} %param.15) | copy-start | bytes 196
  12.0 57.3 %copy-start.11 = (s32[16]{0:T(128)S(1)}, s32[16]{0:T(128)}, u32[]{:S(2)}) copy-start(s32[16]{0:T(128)} %param.16) | copy-start | bytes 196
  12.0 53.3 %all-to-all-start = ((bf16[16,128,512]{2,1,0:T(8,128)(2,1)}), bf16[16,128,512]{2,1,0:T(8,128)(2,1)S(1)}, u32[]{:S(2)}, u32[]{:S(2)}) async-start(bf16[16,128,512]{2,1,0:T(8,128)(2,1)} %copy.66), calls=%async_computation | async-start | bytes 4194304 | tf_op jit(solution)/shard_map/all_to_all | solution.py:184
  18.5 66.7 %all-gather.3.cloned.1.call-start = ((), (), s32[]{:S(2)}) async-start(), calls=%async_computation.1 | async-start | bytes 6291456 | tf_op jit(solution)/shard_map/all_gather | solution.py:196
  66.6 12.5 %copy-start.18 = (f32[16]{0:T(128)S(1)}, f32[16]{0:T(128)}, u32[]{:S(2)}) copy-start(f32[16]{0:T(128)} %param.26) | copy-start | bytes 196
  66.7 13.2 %copy-start.12 = (f32[4,1024]{1,0:T(4,128)S(1)}, f32[4,1024]{1,0:T(4,128)}, u32[]{:S(2)}) copy-start(f32[4,1024]{1,0:T(4,128)} %param.22) | copy-start | bytes 49156
  66.7 13.2 %copy-start.14 = (f32[4,256]{1,0:T(4,128)S(1)}, f32[4,256]{1,0:T(4,128)}, u32[]{:S(2)}) copy-start(f32[4,256]{1,0:T(4,128)} %param.23) | copy-start | bytes 12292
  66.7 13.2 %copy-start.15 = (f32[1024]{0:T(1024)S(1)}, f32[1024]{0:T(1024)}, u32[]{:S(2)}) copy-start(f32[1024]{0:T(1024)} %param.24) | copy-start | bytes 12292
  66.7 13.2 %copy-start.17 = (f32[256]{0:T(256)S(1)}, f32[256]{0:T(256)}, u32[]{:S(2)}) copy-start(f32[256]{0:T(256)} %param.25) | copy-start | bytes 3076
  66.7 14.5 %copy-start.21 = (f32[16]{0:T(128)S(1)}, f32[16]{0:T(128)}, u32[]{:S(2)}) copy-start(f32[16]{0:T(128)} %param.21) | copy-start | bytes 196
  70.9 12.2 %collective-permute-start = (bf16[3]{0:T(256)(128)(2,1)S(1)}, bf16[3]{0:T(256)(128)(2,1)S(1)}, u32[]{:S(2)}, u32[]{:S(2)}) collective-permute-start(bf16[3]{0:T(256)(128)(2,1)S(1)} %fusion.47), channel_id=1, source_target_pairs={{0,2},{2,4},{4,6},{6,8},{8,10},{10,12},{12,14},{14,16},{16,18},{18... | collective-permute-start | bytes 26 | tf_op jit(solution)/shard_map/ppermute | solution.py:17
  97.2 6.7 %copy-start.6 = (bf16[2048,2048]{1,0:T(8,128)(2,1)}, bf16[2048,2048]{1,0:T(8,128)(2,1)S(1)}, u32[]{:S(2)}) copy-start(bf16[2048,2048]{1,0:T(8,128)(2,1)S(1)} %convolution_convert_fusion.gate_ref) | copy-start | bytes 25165828
  103.8 10.7 %collective-permute-start.1 = (bf16[3,1280]{1,0:T(4,128)(2,1)S(1)}, bf16[3,1280]{1,0:T(4,128)(2,1)S(1)}, u32[]{:S(2)}, u32[]{:S(2)}) collective-permute-start(bf16[3,1280]{1,0:T(4,128)(2,1)S(1)} %fusion.28), channel_id=1, source_target_pairs={{0,2},{2,4},{4,6},{6,8},{8,10},{10,12},{12,14},{14,16},{16,18},{18... | collective-permute-start | bytes 23048 | tf_op jit(solution)/shard_map/ppermute | solution.py:17
  109.4 9.1 %copy-start.9 = (f32[16,16,128]{2,1,0:T(8,128)}, f32[16,16,128]{2,1,0:T(8,128)S(1)}, u32[]{:S(2)}) copy-start(f32[16,16,128]{2,1,0:T(8,128)S(1)} %fusion.24.cumt_ref) | copy-start | bytes 393220
  109.8 19.6 %copy-start.7 = (f32[16,16,128]{1,2,0:T(8,128)}, f32[16,16,128]{1,2,0:T(8,128)S(1)}, u32[]{:S(2)}) copy-start(f32[16,16,128]{1,2,0:T(8,128)S(1)} %copy.73) | copy-start | bytes 393220
  148.2 6.7 %copy-start.3 = (f32[16,128,1024]{2,1,0:T(8,128)S(1)}, f32[16,128,1024]{2,1,0:T(8,128)}, u32[]{:S(2)}) copy-start(f32[16,128,1024]{2,1,0:T(8,128)} %shard_map.136) | copy-start | bytes 25165828
  152.9 10.5 %collective-permute-start.2 = (bf16[131,1024]{1,0:T(8,128)(2,1)S(1)}, bf16[131,1024]{1,0:T(8,128)(2,1)S(1)}, u32[]{:S(2)}, u32[]{:S(2)}) collective-permute-start(bf16[131,1024]{1,0:T(8,128)(2,1)S(1)} %pad_maximum_fusion.1), channel_id=1, source_target_pairs={{0,2},{2,4},{4,6},{6,8},{8,10},{10,12},{12,14},{14,16},{16,18},{18... | collective-permute-start | bytes 804872 | tf_op jit(solution)/shard_map/ppermute | solution.py:17
  163.7 8.7 %collective-permute-start.3 = (bf16[131,1024]{1,0:T(8,128)(2,1)S(1)}, bf16[131,1024]{1,0:T(8,128)(2,1)S(1)}, u32[]{:S(2)}, u32[]{:S(2)}) collective-permute-start(bf16[131,1024]{1,0:T(8,128)(2,1)S(1)} %pad_maximum_fusion.2), channel_id=1, source_target_pairs={{0,4},{2,6},{4,8},{6,10},{8,12},{10,14},{12,16},{14,18},{16,20},{1... | collective-permute-start | bytes 804872 | tf_op jit(solution)/shard_map/ppermute | solution.py:17
  172.7 8.3 %collective-permute-start.4 = (bf16[131,1024]{1,0:T(8,128)(2,1)S(1)}, bf16[131,1024]{1,0:T(8,128)(2,1)S(1)}, u32[]{:S(2)}, u32[]{:S(2)}) collective-permute-start(bf16[131,1024]{1,0:T(8,128)(2,1)S(1)} %pad_maximum_fusion.3), channel_id=1, source_target_pairs={{0,8},{2,10},{4,12},{6,14},{8,16},{10,18},{12,20},{14,22},{16,24},... | collective-permute-start | bytes 804872 | tf_op jit(solution)/shard_map/ppermute | solution.py:17
  181.2 15.8 %collective-permute-start.5 = (bf16[131,1024]{1,0:T(8,128)(2,1)S(1)}, bf16[131,1024]{1,0:T(8,128)(2,1)S(1)}, u32[]{:S(2)}, u32[]{:S(2)}) collective-permute-start(bf16[131,1024]{1,0:T(8,128)(2,1)S(1)} %pad_maximum_fusion.4), channel_id=1, source_target_pairs={{0,16},{2,18},{4,20},{6,22},{8,24},{10,26},{12,28},{14,30},{1,17},... | collective-permute-start | bytes 804872 | tf_op jit(solution)/shard_map/ppermute | solution.py:17
  197.1 13.4 %collective-permute-start.6 = (bf16[128,1024]{1,0:T(8,128)(2,1)S(1)}, bf16[128,1024]{1,0:T(8,128)(2,1)S(1)}, u32[]{:S(2)}, u32[]{:S(2)}) collective-permute-start(bf16[128,1024]{1,0:T(8,128)(2,1)S(1)} %add_convert_fusion.1), channel_id=1, source_target_pairs={{0,2},{2,4},{4,6},{6,8},{8,10},{10,12},{12,14},{14,16},{16,18},{18... | collective-permute-start | bytes 786440 | tf_op jit(solution)/shard_map/ppermute | solution.py:17
  217.3 30.2 %copy-start.13 = (f32[1024]{0:T(1024)S(1)}, f32[1024]{0:T(1024)}, u32[]{:S(2)}) copy-start(f32[1024]{0:T(1024)} %param.27) | copy-start | bytes 12292
  237.5 15.2 %copy-start.1 = (bf16[16,128,512]{2,1,0:T(8,128)(2,1)S(1)}, bf16[16,128,512]{2,1,0:T(8,128)(2,1)}, u32[]{:S(2)}) copy-start(bf16[16,128,512]{2,1,0:T(8,128)(2,1)} %param.14) | copy-start | bytes 6291460
  (8 other events, 33.8 us)
Sparse Core Ops, SparseCore 0:
  69.4 15.8 all-gather.2

commit v10 on v8

--- a/solution.py
+++ b/solution.py
@@ -256,17 +256,30 @@
     position = lax.axis_index("seq")
     run_decay = widen(through[tiles_dev - 1])
     distance = 1
-    while distance < seq_count:
-        got_decay, got_state = shifted((run_decay, run_state.astype(jnp.bfloat16)), "seq", distance)
-        run_state = run_state + run_decay[None, :] * got_state.astype(jnp.float32)
+    def with_decay(state, decay):
+        high = decay.astype(jnp.bfloat16)
+        rest = decay - high.astype(jnp.float32)
+        middle = rest.astype(jnp.bfloat16)
+        low = (rest - middle.astype(jnp.float32)).astype(jnp.bfloat16)
+        return jnp.concatenate([state.astype(jnp.bfloat16), high[None], middle[None], low[None]], 0)
+
+    def unpack(got):
+        got = got.astype(jnp.float32)
+        return got[:state_dim], got[state_dim] + got[state_dim + 1] + got[state_dim + 2]
+
+    while 2 * distance < seq_count:
+        got_state, got_decay = unpack(shifted(with_decay(run_state, run_decay), "seq", distance))
+        run_state = run_state + run_decay[None, :] * got_state
         run_decay = jnp.where(position >= distance, run_decay * got_decay, run_decay)
         distance *= 2
-    entering = shifted(run_state.astype(jnp.bfloat16), "seq", 1).astype(jnp.float32)
+    near_state, near_decay = unpack(shifted(with_decay(run_state, run_decay), "seq", 1))
+    far_state = shifted(run_state.astype(jnp.bfloat16), "seq", distance + 1).astype(jnp.float32)
+    entering = near_state + near_decay[None, :] * far_state
     tile_state = before_tile + widen(prefix)[:, None, :] * entering[None]
     carried = tile_state.astype(jnp.bfloat16)
     d_full = jnp.repeat(d_skip, head_dim)[None, :]
     gated, row_sq = mix_tiles(conv_out, zx, cumul, cumul_t, dt_t, later, carried, d_full)
-    sums = jnp.sum(lax.all_gather(row_sq, "head"), 0)
+    sums = lax.psum(row_sq, "head")
     return (gated * lax.rsqrt(sums / INNER + EPSILON) * norm_gain[None, :]).astype(jnp.bfloat16)
 
 

time: 266 us -> 252 us (0.947)
  waiting for transfers between devices: 35.2 us -> 27.7 us
  starting transfers between devices: 25.1 us -> 22.4 us
    all_gather x1 -> x0, blocking collectives: 8.99 us -> none  [shards(): sums = jnp.sum(lax.all_gather(row_sq, 'head'), 0)]
    psum x0 -> x1, blocking collectives: none -> 7.52 us  [shards(): sums = lax.psum(row_sq, 'head')]
    ppermute x10 -> x7, waiting for transfers between devices: 33 us -> 25.5 us  [shifted(): return lax.ppermute(x, axis, pairs)]
    ppermute x10 -> x7, starting transfers between devices: 18.5 us -> 15.9 us  [shifted(): return lax.ppermute(x, axis, pairs)]
  transfers between devices with their start and end apart: 12 -> 9, of which waited for: 5 -> 6; matrix products, arithmetic and copies ran while one was open for 20% -> 13% of each run, Pallas kernels for 6% -> 0%
where the time goes in v10:
time: 252 us; the launch traced here: 250 us
  blocking collectives  52.6 us (21%)
  other arithmetic  52 us (21%)
  Pallas kernels  35.7 us (14%)
  local copies, waits for them, and re-layouts  27.9 us (11%)
  waiting for transfers between devices  27.7 us (11%)
  starting transfers between devices  22.4 us (9%)
  matrix products  17.3 us (7%)
  between operations  14.7 us (6%)
    unnamed x1, blocking collectives  45.1 us
    ppermute x7, waiting for transfers between devices, shifted(): return lax.ppermute(x, axis, pairs)  25.5 us
    pallas_call x1, Pallas kernels, mix_tiles(): pl.pallas_call(mix_tile, grid=(tiles_dev,), in_specs=[pl.BlockSpec((tile_...  20.4 us
    ppermute x7, starting transfers between devices, shifted(): return lax.ppermute(x, axis, pairs)  15.9 us
    pallas_call x1, Pallas kernels, contrib_tiles(): pl.pallas_call(contrib_tile, grid=(tiles_dev,), in_specs=[pl.BlockSpec((t...  15.3 us
    unnamed x53, local copies, waits for them, and re-layouts  15.3 us
    dot_general x3, matrix products, shards(): jnp.dot(piece, weight, preferred_element_type=jnp.float32)  14.4 us
    unnamed x14, other arithmetic  13 us
  transfers between devices with their start and end apart: 9, of which 6 were waited for; matrix products, arithmetic and copies ran while one was open for 13% of the time, Pallas kernels for 0%

profile of v10, /device:TPU:29, one launch (start us, length us, event | category | flops | bytes accessed | tf_op | source)
XLA Modules:
  0.0 250.3 jit_solution(18432334379715238931)
XLA Ops:
  9.5 2.5 copy.66
  12.0 6.5 %all-to-all-start = ((bf16[16,128,512]{2,1,0:T(8,128)(2,1)}), bf16[16,128,512]{2,1,0:T(8,128)(2,1)S(1)}, u32[]{:S(2)}, u32[]{:S(2)}) async-start(bf16[16,128,512]{2,1,0:T(8,128)(2,1)} %copy.66), calls=%async_computation | async-start | bytes 4194304 | tf_op jit(solution)/shard_map/all_to_all | solution.py:184
  20.0 45.1 %all-reduce.2 = s32[256]{0:T(256)S(1)} all-reduce(s32[256]{0:T(256)S(1)} %dynamic-update-slice), channel_id=1, replica_groups=mesh['seq'=16,'head'=2] {'seq'}, use_global_device_ids=true, to_apply=%add.2 | all-reduce | flops 256 | bytes 2048
  66.7 2.5 copy.68
  70.9 2.6 %collective-permute-start = (bf16[3]{0:T(256)(128)(2,1)S(1)}, bf16[3]{0:T(256)(128)(2,1)S(1)}, u32[]{:S(2)}, u32[]{:S(2)}) collective-permute-start(bf16[3]{0:T(256)(128)(2,1)S(1)} %fusion.47), channel_id=1, source_target_pairs={{0,2},{2,4},{4,6},{6,8},{8,10},{10,12},{12,14},{14,16},{16,18},{18... | collective-permute-start | bytes 26 | tf_op jit(solution)/shard_map/ppermute | solution.py:17
  73.5 5.6 %copy.80 = bf16[128,8,2,1024]{3,1,2,0:T(8,128)(2,1)} copy(bf16[128,8,2,1024]{3,2,1,0:T(2,128)(2,1)} %bitcast.81) | data formatting | bytes 8388608
  83.1 2.1 all-gather.2.cloned.1.call-done
  85.2 11.9 %convolution_convert_fusion.gate_ref = bf16[2048,2048]{1,0:T(8,128)(2,1)S(1)} fusion(bf16[2048,1024]{1,0:T(8,128)(2,1)} %all-gather.2.cloned.1.call-done, bf16[1024,2048]{1,0:T(8,128)(2,1)} %bitcast.82), kind=kOutput, calls=%fused_computation.4 | convolution fusion | flops 8594128896 | bytes 16777216 | tf_op jit(solution)/shard_map/dot_general | solution.py:198
  97.9 4.5 %copy-done.8 = bf16[2048,1024]{1,0:T(8,128)(2,1)S(1)} copy-done((bf16[2048,1024]{1,0:T(8,128)(2,1)S(1)}, bf16[2048,1024]{1,0:T(8,128)(2,1)}, u32[]{:S(2)}) %copy-start.8) | copy-done | bytes 4194328
  103.8 3.3 %collective-permute-start.1 = (bf16[3,1280]{1,0:T(4,128)(2,1)S(1)}, bf16[3,1280]{1,0:T(4,128)(2,1)S(1)}, u32[]{:S(2)}, u32[]{:S(2)}) collective-permute-start(bf16[3,1280]{1,0:T(4,128)(2,1)S(1)} %fusion.28), channel_id=1, source_target_pairs={{0,2},{2,4},{4,6},{6,8},{8,10},{10,12},{12,14},{14,16},{16,18},{18... | collective-permute-start | bytes 23048 | tf_op jit(solution)/shard_map/ppermute | solution.py:17
  114.5 4.0 %maximum_maximum_fusion = bf16[2051,1280]{1,0:T(8,128)(2,1)S(1)} fusion(bf16[2048,256]{1,0:T(8,128)(2,1)S(1)} %convolution_convert_fusion.1, bf16[2048,1024]{1,0:T(8,128)(2,1)} %copy-done.4, bf16[3,1280]{1,0:T(4,128)(2,1)S(1)} %collective-permute-done.1), kind=kLoop, calls=%fused_computation.7 | loop fusion | flops 15751680 | bytes 10501120 | tf_op jit(solution)/shard_map/concatenate | solution.py:213
  118.5 10.8 %multiply_convert_fusion.x_ref.b_ref.c_ref = bf16[2048,1280]{1,0:T(8,128)(2,1)S(1)} fusion(bf16[2048,256]{1,0:T(8,128)(2,1)S(1)} %convolution_convert_fusion.1, bf16[2051,1280]{1,0:T(8,128)(2,1)S(1)} %maximum_maximum_fusion, f32[1280]{0:T(1024)S(1)} %get-tuple-element.10, f32[1280]{0:T(1024)S(1)} %get-tuple-element.11, f32[1280]{0:T(1024)S(1)} %get-tuple-element.12, ...), kind=kLoop, calls=%fused_computation | loop fusion | flops 60293120 | bytes 26246144 | tf_op jit(solution)/shard_map/convert_element_type | solution.py:226
  129.4 2.4 copy-done.2
  132.8 15.3 %shard_map.136 = f32[16,128,1024]{2,1,0:T(8,128)} custom-call(bf16[2048,1280]{1,0:T(8,128)(2,1)} %copy-done.2, bf16[16,128,128]{2,1,0:T(8,128)(2,1)} %bitcast.84, f32[16,128,16]{2,1,0:T(8,128)} %multiply_multiply_fusion.end_ref), custom_call_target="tpu_custom_call" | custom-call | flops 536870912 | bytes 13107200 | tf_op jit(solution)/shard_map/pallas_call | solution.py:91
  148.2 4.7 %multiply_reduce_fusion = f32[128,1024]{1,0:T(8,128)S(1)} fusion(f32[16,128,1024]{2,1,0:T(8,128)} %shard_map.136, f32[16,1024]{1,0:T(8,128)S(1)} %mul.474), kind=kLoop, calls=%fused_computation.3 | loop fusion | flops 4063232 | bytes 8978432 | tf_op jit(solution)/shard_map/reduce_sum | solution.py:248
  166.8 5.6 %collective-permute-done.3 = bf16[131,1024]{1,0:T(8,128)(2,1)S(1)} collective-permute-done((bf16[131,1024]{1,0:T(8,128)(2,1)S(1)}, bf16[131,1024]{1,0:T(8,128)(2,1)S(1)}, u32[]{:S(2)}, u32[]{:S(2)}) %collective-permute-start.3) | collective-permute-done | bytes 268320 | tf_op jit(solution)/shard_map/ppermute | solution.py:17
  175.8 5.1 %collective-permute-done.4 = bf16[131,1024]{1,0:T(8,128)(2,1)S(1)} collective-permute-done((bf16[131,1024]{1,0:T(8,128)(2,1)S(1)}, bf16[131,1024]{1,0:T(8,128)(2,1)S(1)}, u32[]{:S(2)}, u32[]{:S(2)}) %collective-permute-start.4) | collective-permute-done | bytes 268320 | tf_op jit(solution)/shard_map/ppermute | solution.py:17
  181.2 4.2 %collective-permute-start.5 = (bf16[131,1024]{1,0:T(8,128)(2,1)S(1)}, bf16[131,1024]{1,0:T(8,128)(2,1)S(1)}, u32[]{:S(2)}, u32[]{:S(2)}) collective-permute-start(bf16[131,1024]{1,0:T(8,128)(2,1)S(1)} %pad_maximum_fusion.4), channel_id=1, source_target_pairs={{0,2},{2,4},{4,6},{6,8},{8,10},{10,12},{12,14},{14,16},{16,18},{18... | collective-permute-start | bytes 804872 | tf_op jit(solution)/shard_map/ppermute | solution.py:17
  188.5 2.6 %collective-permute-done.5 = bf16[131,1024]{1,0:T(8,128)(2,1)S(1)} collective-permute-done((bf16[131,1024]{1,0:T(8,128)(2,1)S(1)}, bf16[131,1024]{1,0:T(8,128)(2,1)S(1)}, u32[]{:S(2)}, u32[]{:S(2)}) %collective-permute-start.5) | collective-permute-done | bytes 268320 | tf_op jit(solution)/shard_map/ppermute | solution.py:17
  191.2 11.9 %collective-permute-done.6 = bf16[128,1024]{1,0:T(8,128)(2,1)S(1)} collective-permute-done((bf16[128,1024]{1,0:T(8,128)(2,1)S(1)}, bf16[128,1024]{1,0:T(8,128)(2,1)S(1)}, u32[]{:S(2)}, u32[]{:S(2)}) %collective-permute-start.6) | collective-permute-done | bytes 262176 | tf_op jit(solution)/shard_map/ppermute | solution.py:17
  203.2 6.8 %add_convert_fusion.car_ref = bf16[16,128,1024]{2,1,0:T(8,128)(2,1)} fusion(f32[16,128,1024]{2,1,0:T(8,128)} %fusion.15, f32[128,1024]{1,0:T(8,128)S(1)} %slice_add_fusion, f32[16,1024]{1,0:T(8,128)S(1)} %mul.472), kind=kLoop, calls=%fused_computation.2 | loop fusion | flops 6291456 | bytes 13172736 | tf_op jit(solution)/shard_map/convert_element_type | solution.py:279
  210.0 20.4 %shard_map.137 = (f32[2048,1024]{1,0:T(8,128)}, f32[2048,1]{1,0:T(8,128)}) custom-call(bf16[2048,1280]{1,0:T(8,128)(2,1)} %copy-done.2, bf16[2048,1280]{1,0:T(8,128)(2,1)} %copy-done.2, bf16[2048,1280]{1,0:T(8,128)(2,1)} %copy-done.2, f32[16,128,16]{2,1,0:T(8,128)} %bitcast.79, f32[16,16,128]{2,1,0:T(8,128)} %copy-done.9, ...), custom_call_target="tpu_custom_call" | custom-call | flops 3288334336 | bytes 25165824 | tf_op jit(solution)/shard_map/pallas_call | solution.py:119
  230.4 7.5 %psum.7 = f32[2048,1]{1,0:T(8,128)S(1)} all-reduce(f32[2048,1]{1,0:T(8,128)} %get-tuple-element.8), channel_id=1, replica_groups=mesh['seq'=16,'head'=2] {'head'}, use_global_device_ids=true, to_apply=%region_5.6 | all-reduce | flops 2048 | bytes 16384 | tf_op jit(solution)/shard_map/psum | solution.py:282
  238.3 5.2 %multiply_convert_fusion.1 = bf16[2048,1024]{1,0:T(8,128)(2,1)} fusion(f32[2048,1024]{1,0:T(8,128)} %get-tuple-element.7, f32[1024]{0:T(1024)S(1)} %copy-done.13, f32[2048]{0:T(1024)S(1)} %rsqrt_reduce_fusion), kind=kLoop, calls=%fused_computation.1 | loop fusion | flops 6291456 | bytes 12595200 | tf_op jit(solution)/shard_map/convert_element_type | solution.py:283
  (182 shorter events, 42.4 us)
Async XLA Ops:
  6.5 12.0 %copy-start.22 = (u32[32]{0:T(128)S(1)}, u32[32]{0:T(128)}, u32[]{:S(2)}) copy-start(u32[32]{0:T(128)} %constant.79) | copy-start | bytes 388
  6.5 13.2 %copy-start.20 = (s32[16]{0:T(128)S(1)}, s32[16]{0:T(128)}, u32[]{:S(2)}) copy-start(s32[16]{0:T(128)} %param.15) | copy-start | bytes 196
  12.0 57.3 %copy-start.11 = (s32[16]{0:T(128)S(1)}, s32[16]{0:T(128)}, u32[]{:S(2)}) copy-start(s32[16]{0:T(128)} %param.16) | copy-start | bytes 196
  12.0 53.3 %all-to-all-start = ((bf16[16,128,512]{2,1,0:T(8,128)(2,1)}), bf16[16,128,512]{2,1,0:T(8,128)(2,1)S(1)}, u32[]{:S(2)}, u32[]{:S(2)}) async-start(bf16[16,128,512]{2,1,0:T(8,128)(2,1)} %copy.66), calls=%async_computation | async-start | bytes 4194304 | tf_op jit(solution)/shard_map/all_to_all | solution.py:184
  18.5 66.7 %all-gather.2.cloned.1.call-start = ((), (), s32[]{:S(2)}) async-start(), calls=%async_computation.1 | async-start | bytes 6291456 | tf_op jit(solution)/shard_map/all_gather | solution.py:196
  66.6 12.5 %copy-start.18 = (f32[16]{0:T(128)S(1)}, f32[16]{0:T(128)}, u32[]{:S(2)}) copy-start(f32[16]{0:T(128)} %param.26) | copy-start | bytes 196
  66.7 13.2 %copy-start.12 = (f32[4,1024]{1,0:T(4,128)S(1)}, f32[4,1024]{1,0:T(4,128)}, u32[]{:S(2)}) copy-start(f32[4,1024]{1,0:T(4,128)} %param.22) | copy-start | bytes 49156
  66.7 13.2 %copy-start.14 = (f32[4,256]{1,0:T(4,128)S(1)}, f32[4,256]{1,0:T(4,128)}, u32[]{:S(2)}) copy-start(f32[4,256]{1,0:T(4,128)} %param.23) | copy-start | bytes 12292
  66.7 13.2 %copy-start.15 = (f32[1024]{0:T(1024)S(1)}, f32[1024]{0:T(1024)}, u32[]{:S(2)}) copy-start(f32[1024]{0:T(1024)} %param.24) | copy-start | bytes 12292
  66.7 13.2 %copy-start.17 = (f32[256]{0:T(256)S(1)}, f32[256]{0:T(256)}, u32[]{:S(2)}) copy-start(f32[256]{0:T(256)} %param.25) | copy-start | bytes 3076
  66.7 14.5 %copy-start.21 = (f32[16]{0:T(128)S(1)}, f32[16]{0:T(128)}, u32[]{:S(2)}) copy-start(f32[16]{0:T(128)} %param.21) | copy-start | bytes 196
  70.9 12.2 %collective-permute-start = (bf16[3]{0:T(256)(128)(2,1)S(1)}, bf16[3]{0:T(256)(128)(2,1)S(1)}, u32[]{:S(2)}, u32[]{:S(2)}) collective-permute-start(bf16[3]{0:T(256)(128)(2,1)S(1)} %fusion.47), channel_id=1, source_target_pairs={{0,2},{2,4},{4,6},{6,8},{8,10},{10,12},{12,14},{14,16},{16,18},{18... | collective-permute-start | bytes 26 | tf_op jit(solution)/shard_map/ppermute | solution.py:17
  97.2 6.7 %copy-start.6 = (bf16[2048,2048]{1,0:T(8,128)(2,1)}, bf16[2048,2048]{1,0:T(8,128)(2,1)S(1)}, u32[]{:S(2)}) copy-start(bf16[2048,2048]{1,0:T(8,128)(2,1)S(1)} %convolution_convert_fusion.gate_ref) | copy-start | bytes 25165828
  103.8 10.7 %collective-permute-start.1 = (bf16[3,1280]{1,0:T(4,128)(2,1)S(1)}, bf16[3,1280]{1,0:T(4,128)(2,1)S(1)}, u32[]{:S(2)}, u32[]{:S(2)}) collective-permute-start(bf16[3,1280]{1,0:T(4,128)(2,1)S(1)} %fusion.28), channel_id=1, source_target_pairs={{0,2},{2,4},{4,6},{6,8},{8,10},{10,12},{12,14},{14,16},{16,18},{18... | collective-permute-start | bytes 23048 | tf_op jit(solution)/shard_map/ppermute | solution.py:17
  109.4 9.1 %copy-start.9 = (f32[16,16,128]{2,1,0:T(8,128)}, f32[16,16,128]{2,1,0:T(8,128)S(1)}, u32[]{:S(2)}) copy-start(f32[16,16,128]{2,1,0:T(8,128)S(1)} %fusion.24.cumt_ref) | copy-start | bytes 393220
  109.8 19.6 %copy-start.7 = (f32[16,16,128]{1,2,0:T(8,128)}, f32[16,16,128]{1,2,0:T(8,128)S(1)}, u32[]{:S(2)}) copy-start(f32[16,16,128]{1,2,0:T(8,128)S(1)} %copy.73) | copy-start | bytes 393220
  148.2 6.7 %copy-start.3 = (f32[16,128,1024]{2,1,0:T(8,128)S(1)}, f32[16,128,1024]{2,1,0:T(8,128)}, u32[]{:S(2)}) copy-start(f32[16,128,1024]{2,1,0:T(8,128)} %shard_map.136) | copy-start | bytes 25165828
  152.9 10.5 %collective-permute-start.2 = (bf16[131,1024]{1,0:T(8,128)(2,1)S(1)}, bf16[131,1024]{1,0:T(8,128)(2,1)S(1)}, u32[]{:S(2)}, u32[]{:S(2)}) collective-permute-start(bf16[131,1024]{1,0:T(8,128)(2,1)S(1)} %pad_maximum_fusion.1), channel_id=1, source_target_pairs={{0,2},{2,4},{4,6},{6,8},{8,10},{10,12},{12,14},{14,16},{16,18},{18... | collective-permute-start | bytes 804872 | tf_op jit(solution)/shard_map/ppermute | solution.py:17
  163.7 8.7 %collective-permute-start.3 = (bf16[131,1024]{1,0:T(8,128)(2,1)S(1)}, bf16[131,1024]{1,0:T(8,128)(2,1)S(1)}, u32[]{:S(2)}, u32[]{:S(2)}) collective-permute-start(bf16[131,1024]{1,0:T(8,128)(2,1)S(1)} %pad_maximum_fusion.2), channel_id=1, source_target_pairs={{0,4},{2,6},{4,8},{6,10},{8,12},{10,14},{12,16},{14,18},{16,20},{1... | collective-permute-start | bytes 804872 | tf_op jit(solution)/shard_map/ppermute | solution.py:17
  172.7 8.3 %collective-permute-start.4 = (bf16[131,1024]{1,0:T(8,128)(2,1)S(1)}, bf16[131,1024]{1,0:T(8,128)(2,1)S(1)}, u32[]{:S(2)}, u32[]{:S(2)}) collective-permute-start(bf16[131,1024]{1,0:T(8,128)(2,1)S(1)} %pad_maximum_fusion.3), channel_id=1, source_target_pairs={{0,8},{2,10},{4,12},{6,14},{8,16},{10,18},{12,20},{14,22},{16,24},... | collective-permute-start | bytes 804872 | tf_op jit(solution)/shard_map/ppermute | solution.py:17
  181.2 10.0 %collective-permute-start.5 = (bf16[131,1024]{1,0:T(8,128)(2,1)S(1)}, bf16[131,1024]{1,0:T(8,128)(2,1)S(1)}, u32[]{:S(2)}, u32[]{:S(2)}) collective-permute-start(bf16[131,1024]{1,0:T(8,128)(2,1)S(1)} %pad_maximum_fusion.4), channel_id=1, source_target_pairs={{0,2},{2,4},{4,6},{6,8},{8,10},{10,12},{12,14},{14,16},{16,18},{18... | collective-permute-start | bytes 804872 | tf_op jit(solution)/shard_map/ppermute | solution.py:17
  186.3 16.8 %collective-permute-start.6 = (bf16[128,1024]{1,0:T(8,128)(2,1)S(1)}, bf16[128,1024]{1,0:T(8,128)(2,1)S(1)}, u32[]{:S(2)}, u32[]{:S(2)}) collective-permute-start(bf16[128,1024]{1,0:T(8,128)(2,1)S(1)} %fusion.12), channel_id=1, source_target_pairs={{0,18},{2,20},{4,22},{6,24},{8,26},{10,28},{12,30},{1,19},{3,21},{... | collective-permute-start | bytes 786440 | tf_op jit(solution)/shard_map/ppermute | solution.py:17
  210.0 28.3 %copy-start.13 = (f32[1024]{0:T(1024)S(1)}, f32[1024]{0:T(1024)}, u32[]{:S(2)}) copy-start(f32[1024]{0:T(1024)} %param.27) | copy-start | bytes 12292
  210.0 33.5 %copy-start.1 = (bf16[16,128,512]{2,1,0:T(8,128)(2,1)S(1)}, bf16[16,128,512]{2,1,0:T(8,128)(2,1)}, u32[]{:S(2)}) copy-start(bf16[16,128,512]{2,1,0:T(8,128)(2,1)} %param.14) | copy-start | bytes 6291460
  (8 other events, 33.8 us)
Sparse Core Ops, SparseCore 0:
  69.4 15.8 all-gather.1

commit v11 on v10

--- a/solution.py
+++ b/solution.py
@@ -182,7 +182,8 @@
         "sj,jrc->src", pick.astype(jnp.bfloat16), ingest, preferred_element_type=jnp.float32
     ).astype(jnp.bfloat16)
     incoming = lax.all_to_all(outgoing, "seq", split_axis=0, concat_axis=0, tiled=True)
-    every_dest = lax.all_gather(dest_tile, "seq", tiled=True).reshape(seq_count, tiles_dev)
+    zx_cols, gather_dest = lax.optimization_barrier((w_zx.reshape(w_zx.shape[0], -1), dest_tile))
+    every_dest = lax.all_gather(gather_dest, "seq", tiled=True).reshape(seq_count, tiles_dev)
     mine = every_dest // tiles_dev == lax.axis_index("seq")
     got_slot = jnp.sum(jnp.where(mine, every_dest % tiles_dev, 0), 1)
     local_slots = jnp.arange(tiles_dev, dtype=jnp.int32)
@@ -191,7 +192,6 @@
         jnp.bfloat16
     )
     own_rows = arrived.reshape(row_count, columns)
-    zx_cols = w_zx.reshape(w_zx.shape[0], -1)
     weight_set = (zx_cols, w_bc, w_dt)
     piece = lax.all_gather(own_rows, "head", axis=1, tiled=True)
     acc_zx, acc_bc, acc_dt = tuple(

time: 252 us -> 252 us (level)
  waiting for transfers between devices: 27.7 us -> 34.4 us
  blocking collectives: 52.6 us -> 46.5 us
    unnamed x1, blocking collectives: 45.1 us -> 39.3 us
    all_gather x1, waiting for transfers between devices: 2.12 us -> 7.79 us  [shards(): piece = lax.all_gather(own_rows, 'head', axis=1, tiled=True)]
where the time goes in v11:
time: 252 us; the launch traced here: 251 us
  other arithmetic  52 us (21%)
  blocking collectives  46.5 us (18%)
  Pallas kernels  35.7 us (14%)
  waiting for transfers between devices  34.4 us (14%)
  local copies, waits for them, and re-layouts  28 us (11%)
  starting transfers between devices  22.2 us (9%)
  matrix products  17.3 us (7%)
  between operations  14.8 us (6%)
    unnamed x1, blocking collectives  39.3 us
    ppermute x7, waiting for transfers between devices, shifted(): return lax.ppermute(x, axis, pairs)  26.6 us
    pallas_call x1, Pallas kernels, mix_tiles(): pl.pallas_call(mix_tile, grid=(tiles_dev,), in_specs=[pl.BlockSpec((tile_...  20.4 us
    ppermute x7, starting transfers between devices, shifted(): return lax.ppermute(x, axis, pairs)  15.8 us
    unnamed x53, local copies, waits for them, and re-layouts  15.4 us
    pallas_call x1, Pallas kernels, contrib_tiles(): pl.pallas_call(contrib_tile, grid=(tiles_dev,), in_specs=[pl.BlockSpec((t...  15.3 us
    dot_general x3, matrix products, shards(): jnp.dot(piece, weight, preferred_element_type=jnp.float32)  14.4 us
    unnamed x14, other arithmetic  13 us
  transfers between devices with their start and end apart: 9, of which 6 were waited for; matrix products, arithmetic and copies ran while one was open for 13% of the time, Pallas kernels for 0%

profile of v11, /device:TPU:29, one launch (start us, length us, event | category | flops | bytes accessed | tf_op | source)
XLA Modules:
  0.0 250.9 jit_solution(3050686246002283748)
XLA Ops:
  9.5 2.5 copy.66
  12.0 6.4 %all-to-all-start = ((bf16[16,128,512]{2,1,0:T(8,128)(2,1)}), bf16[16,128,512]{2,1,0:T(8,128)(2,1)S(1)}, u32[]{:S(2)}, u32[]{:S(2)}) async-start(bf16[16,128,512]{2,1,0:T(8,128)(2,1)} %copy.66), calls=%async_computation | async-start | bytes 4194304 | tf_op jit(solution)/shard_map/all_to_all | solution.py:184
  18.5 5.7 %copy.80 = bf16[128,8,2,1024]{3,1,2,0:T(8,128)(2,1)} copy(bf16[128,8,2,1024]{3,2,1,0:T(2,128)(2,1)} %bitcast.81) | data formatting | bytes 8388608
  25.7 39.3 %all-reduce.2 = s32[256]{0:T(256)S(1)} all-reduce(s32[256]{0:T(256)S(1)} %dynamic-update-slice), channel_id=1, replica_groups=mesh['seq'=16,'head'=2] {'seq'}, use_global_device_ids=true, to_apply=%add.2 | all-reduce | flops 256 | bytes 2048
  66.5 2.5 copy.68
  70.7 2.6 %collective-permute-start = (bf16[3]{0:T(256)(128)(2,1)S(1)}, bf16[3]{0:T(256)(128)(2,1)S(1)}, u32[]{:S(2)}, u32[]{:S(2)}) collective-permute-start(bf16[3]{0:T(256)(128)(2,1)S(1)} %fusion.47), channel_id=1, source_target_pairs={{0,2},{2,4},{4,6},{6,8},{8,10},{10,12},{12,14},{14,16},{16,18},{18... | collective-permute-start | bytes 26 | tf_op jit(solution)/shard_map/ppermute | solution.py:17
  77.3 7.8 %all-gather.2.cloned.1.call-done = bf16[2048,1024]{1,0:T(8,128)(2,1)} async-done(((bf16[2048,512]{1,0:T(8,128)(2,1)}), bf16[2048,1024]{1,0:T(8,128)(2,1)}) %all-gather.2.cloned.1.call-update) | async-done | bytes 4194320 | tf_op jit(solution)/shard_map/all_gather | solution.py:196
  85.1 11.9 %convolution_convert_fusion.gate_ref = bf16[2048,2048]{1,0:T(8,128)(2,1)S(1)} fusion(bf16[2048,1024]{1,0:T(8,128)(2,1)} %all-gather.2.cloned.1.call-done, bf16[1024,2048]{1,0:T(8,128)(2,1)} %bitcast.82), kind=kOutput, calls=%fused_computation.4 | convolution fusion | flops 8594128896 | bytes 16777216 | tf_op jit(solution)/shard_map/dot_general | solution.py:198
  97.8 4.5 %copy-done.8 = bf16[2048,1024]{1,0:T(8,128)(2,1)S(1)} copy-done((bf16[2048,1024]{1,0:T(8,128)(2,1)S(1)}, bf16[2048,1024]{1,0:T(8,128)(2,1)}, u32[]{:S(2)}) %copy-start.8) | copy-done | bytes 4194328
  103.7 3.2 %collective-permute-start.1 = (bf16[3,1280]{1,0:T(4,128)(2,1)S(1)}, bf16[3,1280]{1,0:T(4,128)(2,1)S(1)}, u32[]{:S(2)}, u32[]{:S(2)}) collective-permute-start(bf16[3,1280]{1,0:T(4,128)(2,1)S(1)} %fusion.28), channel_id=1, source_target_pairs={{0,2},{2,4},{4,6},{6,8},{8,10},{10,12},{12,14},{14,16},{16,18},{18... | collective-permute-start | bytes 23048 | tf_op jit(solution)/shard_map/ppermute | solution.py:17
  114.3 4.0 %maximum_maximum_fusion = bf16[2051,1280]{1,0:T(8,128)(2,1)S(1)} fusion(bf16[2048,256]{1,0:T(8,128)(2,1)S(1)} %convolution_convert_fusion.1, bf16[2048,1024]{1,0:T(8,128)(2,1)} %copy-done.4, bf16[3,1280]{1,0:T(4,128)(2,1)S(1)} %collective-permute-done.1), kind=kLoop, calls=%fused_computation.7 | loop fusion | flops 15751680 | bytes 10501120 | tf_op jit(solution)/shard_map/concatenate | solution.py:213
  118.3 10.8 %multiply_convert_fusion.x_ref.b_ref.c_ref = bf16[2048,1280]{1,0:T(8,128)(2,1)S(1)} fusion(bf16[2048,256]{1,0:T(8,128)(2,1)S(1)} %convolution_convert_fusion.1, bf16[2051,1280]{1,0:T(8,128)(2,1)S(1)} %maximum_maximum_fusion, f32[1280]{0:T(1024)S(1)} %get-tuple-element.14, f32[1280]{0:T(1024)S(1)} %get-tuple-element.15, f32[1280]{0:T(1024)S(1)} %get-tuple-element.16, ...), kind=kLoop, calls=%fused_computation | loop fusion | flops 60293120 | bytes 26246144 | tf_op jit(solution)/shard_map/convert_element_type | solution.py:226
  129.2 2.4 copy-done.2
  132.6 15.3 %shard_map.136 = f32[16,128,1024]{2,1,0:T(8,128)} custom-call(bf16[2048,1280]{1,0:T(8,128)(2,1)} %copy-done.2, bf16[16,128,128]{2,1,0:T(8,128)(2,1)} %bitcast.84, f32[16,128,16]{2,1,0:T(8,128)} %multiply_multiply_fusion.end_ref), custom_call_target="tpu_custom_call" | custom-call | flops 536870912 | bytes 13107200 | tf_op jit(solution)/shard_map/pallas_call | solution.py:91
  148.0 4.7 %multiply_reduce_fusion = f32[128,1024]{1,0:T(8,128)S(1)} fusion(f32[16,128,1024]{2,1,0:T(8,128)} %shard_map.136, f32[16,1024]{1,0:T(8,128)S(1)} %mul.474), kind=kLoop, calls=%fused_computation.3 | loop fusion | flops 4063232 | bytes 8978432 | tf_op jit(solution)/shard_map/reduce_sum | solution.py:248
  166.7 5.6 %collective-permute-done.3 = bf16[131,1024]{1,0:T(8,128)(2,1)S(1)} collective-permute-done((bf16[131,1024]{1,0:T(8,128)(2,1)S(1)}, bf16[131,1024]{1,0:T(8,128)(2,1)S(1)}, u32[]{:S(2)}, u32[]{:S(2)}) %collective-permute-start.3) | collective-permute-done | bytes 268320 | tf_op jit(solution)/shard_map/ppermute | solution.py:17
  175.7 5.2 %collective-permute-done.4 = bf16[131,1024]{1,0:T(8,128)(2,1)S(1)} collective-permute-done((bf16[131,1024]{1,0:T(8,128)(2,1)S(1)}, bf16[131,1024]{1,0:T(8,128)(2,1)S(1)}, u32[]{:S(2)}, u32[]{:S(2)}) %collective-permute-start.4) | collective-permute-done | bytes 268320 | tf_op jit(solution)/shard_map/ppermute | solution.py:17
  181.0 4.1 %collective-permute-start.5 = (bf16[131,1024]{1,0:T(8,128)(2,1)S(1)}, bf16[131,1024]{1,0:T(8,128)(2,1)S(1)}, u32[]{:S(2)}, u32[]{:S(2)}) collective-permute-start(bf16[131,1024]{1,0:T(8,128)(2,1)S(1)} %pad_maximum_fusion.4), channel_id=1, source_target_pairs={{0,2},{2,4},{4,6},{6,8},{8,10},{10,12},{12,14},{14,16},{16,18},{18... | collective-permute-start | bytes 804872 | tf_op jit(solution)/shard_map/ppermute | solution.py:17
  188.3 2.6 %collective-permute-done.5 = bf16[131,1024]{1,0:T(8,128)(2,1)S(1)} collective-permute-done((bf16[131,1024]{1,0:T(8,128)(2,1)S(1)}, bf16[131,1024]{1,0:T(8,128)(2,1)S(1)}, u32[]{:S(2)}, u32[]{:S(2)}) %collective-permute-start.5) | collective-permute-done | bytes 268320 | tf_op jit(solution)/shard_map/ppermute | solution.py:17
  191.0 12.9 %collective-permute-done.6 = bf16[128,1024]{1,0:T(8,128)(2,1)S(1)} collective-permute-done((bf16[128,1024]{1,0:T(8,128)(2,1)S(1)}, bf16[128,1024]{1,0:T(8,128)(2,1)S(1)}, u32[]{:S(2)}, u32[]{:S(2)}) %collective-permute-start.6) | collective-permute-done | bytes 262176 | tf_op jit(solution)/shard_map/ppermute | solution.py:17
  204.0 6.8 %add_convert_fusion.car_ref = bf16[16,128,1024]{2,1,0:T(8,128)(2,1)} fusion(f32[16,128,1024]{2,1,0:T(8,128)} %fusion.15, f32[128,1024]{1,0:T(8,128)S(1)} %slice_add_fusion, f32[16,1024]{1,0:T(8,128)S(1)} %mul.472), kind=kLoop, calls=%fused_computation.2 | loop fusion | flops 6291456 | bytes 13172736 | tf_op jit(solution)/shard_map/convert_element_type | solution.py:279
  210.8 20.4 %shard_map.137 = (f32[2048,1024]{1,0:T(8,128)}, f32[2048,1]{1,0:T(8,128)}) custom-call(bf16[2048,1280]{1,0:T(8,128)(2,1)} %copy-done.2, bf16[2048,1280]{1,0:T(8,128)(2,1)} %copy-done.2, bf16[2048,1280]{1,0:T(8,128)(2,1)} %copy-done.2, f32[16,128,16]{2,1,0:T(8,128)} %bitcast.79, f32[16,16,128]{2,1,0:T(8,128)} %copy-done.9, ...), custom_call_target="tpu_custom_call" | custom-call | flops 3288334336 | bytes 25165824 | tf_op jit(solution)/shard_map/pallas_call | solution.py:119
  231.2 7.2 %psum.7 = f32[2048,1]{1,0:T(8,128)S(1)} all-reduce(f32[2048,1]{1,0:T(8,128)} %get-tuple-element.12), channel_id=1, replica_groups=mesh['seq'=16,'head'=2] {'head'}, use_global_device_ids=true, to_apply=%region_5.6 | all-reduce | flops 2048 | bytes 16384 | tf_op jit(solution)/shard_map/psum | solution.py:282
  238.8 5.2 %multiply_convert_fusion.1 = bf16[2048,1024]{1,0:T(8,128)(2,1)} fusion(f32[2048,1024]{1,0:T(8,128)} %get-tuple-element.11, f32[1024]{0:T(1024)S(1)} %copy-done.13, f32[2048]{0:T(1024)S(1)} %rsqrt_reduce_fusion), kind=kLoop, calls=%fused_computation.1 | loop fusion | flops 6291456 | bytes 12595200 | tf_op jit(solution)/shard_map/convert_element_type | solution.py:283
  (182 shorter events, 42.4 us)
Async XLA Ops:
  9.5 14.7 %copy-start.22 = (u32[32]{0:T(128)S(1)}, u32[32]{0:T(128)}, u32[]{:S(2)}) copy-start(u32[32]{0:T(128)} %constant.79) | copy-start | bytes 388
  9.5 16.0 %copy-start.20 = (s32[16]{0:T(128)S(1)}, s32[16]{0:T(128)}, u32[]{:S(2)}) copy-start(s32[16]{0:T(128)} %param.15) | copy-start | bytes 196
  12.0 53.2 %all-to-all-start = ((bf16[16,128,512]{2,1,0:T(8,128)(2,1)}), bf16[16,128,512]{2,1,0:T(8,128)(2,1)S(1)}, u32[]{:S(2)}, u32[]{:S(2)}) async-start(bf16[16,128,512]{2,1,0:T(8,128)(2,1)} %copy.66), calls=%async_computation | async-start | bytes 4194304 | tf_op jit(solution)/shard_map/all_to_all | solution.py:184
  18.4 66.7 %all-gather.2.cloned.1.call-start = ((), (), s32[]{:S(2)}) async-start(), calls=%async_computation.1 | async-start | bytes 6291456 | tf_op jit(solution)/shard_map/all_gather | solution.py:196
  18.4 50.6 %copy-start.11 = (s32[16]{0:T(128)S(1)}, s32[16]{0:T(128)}, u32[]{:S(2)}) copy-start(s32[16]{0:T(128)} %param.16) | copy-start | bytes 196
  18.5 54.9 %copy-start.18 = (f32[16]{0:T(128)S(1)}, f32[16]{0:T(128)}, u32[]{:S(2)}) copy-start(f32[16]{0:T(128)} %param.26) | copy-start | bytes 196
  18.5 55.7 %copy-start.12 = (f32[4,1024]{1,0:T(4,128)S(1)}, f32[4,1024]{1,0:T(4,128)}, u32[]{:S(2)}) copy-start(f32[4,1024]{1,0:T(4,128)} %param.22) | copy-start | bytes 49156
  18.5 55.6 %copy-start.14 = (f32[4,256]{1,0:T(4,128)S(1)}, f32[4,256]{1,0:T(4,128)}, u32[]{:S(2)}) copy-start(f32[4,256]{1,0:T(4,128)} %param.23) | copy-start | bytes 12292
  18.5 55.6 %copy-start.15 = (f32[1024]{0:T(1024)S(1)}, f32[1024]{0:T(1024)}, u32[]{:S(2)}) copy-start(f32[1024]{0:T(1024)} %param.24) | copy-start | bytes 12292
  18.5 55.6 %copy-start.17 = (f32[256]{0:T(256)S(1)}, f32[256]{0:T(256)}, u32[]{:S(2)}) copy-start(f32[256]{0:T(256)} %param.25) | copy-start | bytes 3076
  18.5 56.9 %copy-start.21 = (f32[16]{0:T(128)S(1)}, f32[16]{0:T(128)}, u32[]{:S(2)}) copy-start(f32[16]{0:T(128)} %param.21) | copy-start | bytes 196
  70.7 6.5 %collective-permute-start = (bf16[3]{0:T(256)(128)(2,1)S(1)}, bf16[3]{0:T(256)(128)(2,1)S(1)}, u32[]{:S(2)}, u32[]{:S(2)}) collective-permute-start(bf16[3]{0:T(256)(128)(2,1)S(1)} %fusion.47), channel_id=1, source_target_pairs={{0,2},{2,4},{4,6},{6,8},{8,10},{10,12},{12,14},{14,16},{16,18},{18... | collective-permute-start | bytes 26 | tf_op jit(solution)/shard_map/ppermute | solution.py:17
  97.1 6.7 %copy-start.6 = (bf16[2048,2048]{1,0:T(8,128)(2,1)}, bf16[2048,2048]{1,0:T(8,128)(2,1)S(1)}, u32[]{:S(2)}) copy-start(bf16[2048,2048]{1,0:T(8,128)(2,1)S(1)} %convolution_convert_fusion.gate_ref) | copy-start | bytes 25165828
  103.7 10.6 %collective-permute-start.1 = (bf16[3,1280]{1,0:T(4,128)(2,1)S(1)}, bf16[3,1280]{1,0:T(4,128)(2,1)S(1)}, u32[]{:S(2)}, u32[]{:S(2)}) collective-permute-start(bf16[3,1280]{1,0:T(4,128)(2,1)S(1)} %fusion.28), channel_id=1, source_target_pairs={{0,2},{2,4},{4,6},{6,8},{8,10},{10,12},{12,14},{14,16},{16,18},{18... | collective-permute-start | bytes 23048 | tf_op jit(solution)/shard_map/ppermute | solution.py:17
  109.3 9.1 %copy-start.9 = (f32[16,16,128]{2,1,0:T(8,128)}, f32[16,16,128]{2,1,0:T(8,128)S(1)}, u32[]{:S(2)}) copy-start(f32[16,16,128]{2,1,0:T(8,128)S(1)} %fusion.24.cumt_ref) | copy-start | bytes 393220
  109.6 19.6 %copy-start.7 = (f32[16,16,128]{1,2,0:T(8,128)}, f32[16,16,128]{1,2,0:T(8,128)S(1)}, u32[]{:S(2)}) copy-start(f32[16,16,128]{1,2,0:T(8,128)S(1)} %copy.73) | copy-start | bytes 393220
  148.0 6.7 %copy-start.3 = (f32[16,128,1024]{2,1,0:T(8,128)S(1)}, f32[16,128,1024]{2,1,0:T(8,128)}, u32[]{:S(2)}) copy-start(f32[16,128,1024]{2,1,0:T(8,128)} %shard_map.136) | copy-start | bytes 25165828
  152.8 10.5 %collective-permute-start.2 = (bf16[131,1024]{1,0:T(8,128)(2,1)S(1)}, bf16[131,1024]{1,0:T(8,128)(2,1)S(1)}, u32[]{:S(2)}, u32[]{:S(2)}) collective-permute-start(bf16[131,1024]{1,0:T(8,128)(2,1)S(1)} %pad_maximum_fusion.1), channel_id=1, source_target_pairs={{0,2},{2,4},{4,6},{6,8},{8,10},{10,12},{12,14},{14,16},{16,18},{18... | collective-permute-start | bytes 804872 | tf_op jit(solution)/shard_map/ppermute | solution.py:17
  163.5 8.7 %collective-permute-start.3 = (bf16[131,1024]{1,0:T(8,128)(2,1)S(1)}, bf16[131,1024]{1,0:T(8,128)(2,1)S(1)}, u32[]{:S(2)}, u32[]{:S(2)}) collective-permute-start(bf16[131,1024]{1,0:T(8,128)(2,1)S(1)} %pad_maximum_fusion.2), channel_id=1, source_target_pairs={{0,4},{2,6},{4,8},{6,10},{8,12},{10,14},{12,16},{14,18},{16,20},{1... | collective-permute-start | bytes 804872 | tf_op jit(solution)/shard_map/ppermute | solution.py:17
  172.5 8.3 %collective-permute-start.4 = (bf16[131,1024]{1,0:T(8,128)(2,1)S(1)}, bf16[131,1024]{1,0:T(8,128)(2,1)S(1)}, u32[]{:S(2)}, u32[]{:S(2)}) collective-permute-start(bf16[131,1024]{1,0:T(8,128)(2,1)S(1)} %pad_maximum_fusion.3), channel_id=1, source_target_pairs={{0,8},{2,10},{4,12},{6,14},{8,16},{10,18},{12,20},{14,22},{16,24},... | collective-permute-start | bytes 804872 | tf_op jit(solution)/shard_map/ppermute | solution.py:17
  181.0 9.9 %collective-permute-start.5 = (bf16[131,1024]{1,0:T(8,128)(2,1)S(1)}, bf16[131,1024]{1,0:T(8,128)(2,1)S(1)}, u32[]{:S(2)}, u32[]{:S(2)}) collective-permute-start(bf16[131,1024]{1,0:T(8,128)(2,1)S(1)} %pad_maximum_fusion.4), channel_id=1, source_target_pairs={{0,2},{2,4},{4,6},{6,8},{8,10},{10,12},{12,14},{14,16},{16,18},{18... | collective-permute-start | bytes 804872 | tf_op jit(solution)/shard_map/ppermute | solution.py:17
  186.1 17.8 %collective-permute-start.6 = (bf16[128,1024]{1,0:T(8,128)(2,1)S(1)}, bf16[128,1024]{1,0:T(8,128)(2,1)S(1)}, u32[]{:S(2)}, u32[]{:S(2)}) collective-permute-start(bf16[128,1024]{1,0:T(8,128)(2,1)S(1)} %fusion.12), channel_id=1, source_target_pairs={{0,18},{2,20},{4,22},{6,24},{8,26},{10,28},{12,30},{1,19},{3,21},{... | collective-permute-start | bytes 786440 | tf_op jit(solution)/shard_map/ppermute | solution.py:17
  210.8 28.0 %copy-start.13 = (f32[1024]{0:T(1024)S(1)}, f32[1024]{0:T(1024)}, u32[]{:S(2)}) copy-start(f32[1024]{0:T(1024)} %param.27) | copy-start | bytes 12292
  210.8 33.2 %copy-start.1 = (bf16[16,128,512]{2,1,0:T(8,128)(2,1)S(1)}, bf16[16,128,512]{2,1,0:T(8,128)(2,1)}, u32[]{:S(2)}) copy-start(bf16[16,128,512]{2,1,0:T(8,128)(2,1)} %param.14) | copy-start | bytes 6291460
  (8 other events, 33.6 us)
Sparse Core Ops, SparseCore 0:
  69.2 15.9 all-gather.1

commit v12 on v11

--- a/solution.py
+++ b/solution.py
@@ -18,8 +18,8 @@
 
 
 def mix_tile(
-    x_ref, b_ref, c_ref, cum_ref, cumt_ref, dtt_ref, partc_ref, partr_ref, car_ref, gate_ref, d_ref,
-    out_ref, sq_ref,
+    x_ref, b_ref, c_ref, cum_ref, cumt_ref, dtt_ref, partc_ref, partr_ref, before_ref, prefix_ref,
+    enter_ref, gate_ref, d_ref, out_ref, sq_ref,
 ):
     f32 = jnp.float32
     tile_len = x_ref.shape[0]
@@ -55,7 +55,10 @@
             [jnp.where(first_half, x_pair, zero), jnp.where(first_half, zero, x_pair)], axis=0
         )
         intra = jnp.dot(weights, split_x, preferred_element_type=f32)
-        projected = jnp.dot(c_mat, car_ref[0, :, cols], preferred_element_type=f32)
+        carried = (
+            before_ref[0, :, cols] + prefix_ref[0, :, cols] * enter_ref[:, cols]
+        ).astype(jnp.bfloat16)
+        projected = jnp.dot(c_mat, carried, preferred_element_type=f32)
         grow = jnp.where(
             first_half,
             jnp.exp(cum[:, 2 * pair : 2 * pair + 1]),
@@ -106,10 +109,10 @@
     )(conv_out, b_t, to_end)
 
 
-def mix_tiles(conv_out, zx, cumul, cumul_t, dt_t, later, carried, d_full):
+def mix_tiles(conv_out, zx, cumul, cumul_t, dt_t, later, before_tile, prefix_wide, entering, d_full):
     tiles_dev, tile_len, heads_here = cumul.shape
-    inner_here = carried.shape[2]
-    state_dim = carried.shape[1]
+    inner_here = before_tile.shape[2]
+    state_dim = before_tile.shape[1]
     rows = tiles_dev * tile_len
     b_block = inner_here // 128
     c_block = b_block + state_dim // 128
@@ -129,6 +132,8 @@
             pl.BlockSpec((1, tile_len, 1), per_tile),
             pl.BlockSpec((1, 1, tile_len), per_tile),
             pl.BlockSpec((1, state_dim, inner_here), per_tile),
+            pl.BlockSpec((1, 1, inner_here), per_tile),
+            pl.BlockSpec((state_dim, inner_here), lambda j: (0, 0)),
             pl.BlockSpec((tile_len, inner_here), lambda j: (j, 0)),
             pl.BlockSpec((1, inner_here), lambda j: (0, 0)),
         ],
@@ -143,9 +148,12 @@
         cost_estimate=pl.CostEstimate(
             flops=tiles_dev * (2 * tile_len * tile_len * (state_dim + 4 * inner_here + 2 * inner_here)),
             transcendentals=tiles_dev * tile_len * (tile_len * heads_here + 2 * inner_here),
-            bytes_accessed=rows * inner_here * 10 + tiles_dev * inner_here * state_dim * 2,
+            bytes_accessed=rows * inner_here * 10 + tiles_dev * inner_here * state_dim * 4,
         ),
-    )(conv_out, conv_out, conv_out, cumul, cumul_t, dt_t, part_col, part_row, carried, zx, d_full)
+    )(
+        conv_out, conv_out, conv_out, cumul, cumul_t, dt_t, part_col, part_row,
+        before_tile, prefix_wide, entering, zx, d_full,
+    )
 
 
 def shards(
@@ -275,10 +283,11 @@
     near_state, near_decay = unpack(shifted(with_decay(run_state, run_decay), "seq", 1))
     far_state = shifted(run_state.astype(jnp.bfloat16), "seq", distance + 1).astype(jnp.float32)
     entering = near_state + near_decay[None, :] * far_state
-    tile_state = before_tile + widen(prefix)[:, None, :] * entering[None]
-    carried = tile_state.astype(jnp.bfloat16)
     d_full = jnp.repeat(d_skip, head_dim)[None, :]
-    gated, row_sq = mix_tiles(conv_out, zx, cumul, cumul_t, dt_t, later, carried, d_full)
+    gated, row_sq = mix_tiles(
+        conv_out, zx, cumul, cumul_t, dt_t, later, before_tile, widen(prefix)[:, None, :],
+        entering, d_full,
+    )
     sums = lax.psum(row_sq, "head")
     return (gated * lax.rsqrt(sums / INNER + EPSILON) * norm_gain[None, :]).astype(jnp.bfloat16)
 

time: 252 us -> 248 us (0.984)
  other arithmetic: 52 us -> 46.1 us
    convert_element_type x1 -> x0, other arithmetic: 6.79 us -> none  [shards(): carried = tile_state.astype(jnp.bfloat16)]
  transfers between devices with their start and end apart: 9 -> 9, of which waited for: 6 -> 6; matrix products, arithmetic and copies ran while one was open for 13% -> 14% of each run, Pallas kernels for 0% -> 0%
where the time goes in v12:
time: 248 us; the launch traced here: 247 us
  blocking collectives  46.5 us (19%)
  other arithmetic  46.1 us (19%)
  Pallas kernels  36.9 us (15%)
  waiting for transfers between devices  34.5 us (14%)
  local copies, waits for them, and re-layouts  28.6 us (12%)
  starting transfers between devices  22.1 us (9%)
  matrix products  17.3 us (7%)
  between operations  14.7 us (6%)
    unnamed x1, blocking collectives  39.3 us
    ppermute x7, waiting for transfers between devices, shifted(): return lax.ppermute(x, axis, pairs)  26.7 us
    pallas_call x1, Pallas kernels, mix_tiles(): pl.pallas_call(mix_tile, grid=(tiles_dev,), in_specs=[pl.BlockSpec((tile_...  21.6 us
    ppermute x7, starting transfers between devices, shifted(): return lax.ppermute(x, axis, pairs)  15.7 us
    unnamed x53, local copies, waits for them, and re-layouts  15.4 us
    pallas_call x1, Pallas kernels, contrib_tiles(): pl.pallas_call(contrib_tile, grid=(tiles_dev,), in_specs=[pl.BlockSpec((t...  15.3 us
    dot_general x3, matrix products, shards(): jnp.dot(piece, weight, preferred_element_type=jnp.float32)  14.4 us
    unnamed x14, other arithmetic  13 us
  transfers between devices with their start and end apart: 9, of which 6 were waited for; matrix products, arithmetic and copies ran while one was open for 14% of the time, Pallas kernels for 0%

profile of v12, /device:TPU:29, one launch (start us, length us, event | category | flops | bytes accessed | tf_op | source)
XLA Modules:
  0.0 246.8 jit_solution(4732135842709168343)
XLA Ops:
  9.5 2.5 %copy.66 = bf16[16,128,512]{2,1,0:T(8,128)(2,1)} copy(bf16[16,128,512]{2,0,1:T(8,128)(2,1)S(1)} %fusion.4) | data formatting | bytes 4194304 | tf_op jit(solution)/shard_map/convert_element_type | solution.py:191
  12.0 6.4 %all-to-all-start = ((bf16[16,128,512]{2,1,0:T(8,128)(2,1)}), bf16[16,128,512]{2,1,0:T(8,128)(2,1)S(1)}, u32[]{:S(2)}, u32[]{:S(2)}) async-start(bf16[16,128,512]{2,1,0:T(8,128)(2,1)} %copy.66), calls=%async_computation | async-start | bytes 4194304 | tf_op jit(solution)/shard_map/all_to_all | solution.py:192
  18.5 5.7 %copy.80 = bf16[128,8,2,1024]{3,1,2,0:T(8,128)(2,1)} copy(bf16[128,8,2,1024]{3,2,1,0:T(2,128)(2,1)} %bitcast.81) | data formatting | bytes 8388608
  25.7 39.3 %all-reduce.2 = s32[256]{0:T(256)S(1)} all-reduce(s32[256]{0:T(256)S(1)} %dynamic-update-slice), channel_id=1, replica_groups=mesh['seq'=16,'head'=2] {'seq'}, use_global_device_ids=true, to_apply=%add.2 | all-reduce | flops 256 | bytes 2048
  66.5 2.5 %copy.68 = bf16[16,128,512]{2,1,0:T(8,128)(2,1)} copy(bf16[16,128,512]{2,0,1:T(8,128)(2,1)S(1)} %fusion.7) | data formatting | bytes 4194304 | tf_op jit(solution)/shard_map/convert_element_type | solution.py:199
  70.7 2.6 %collective-permute-start = (bf16[3]{0:T(256)(128)(2,1)S(1)}, bf16[3]{0:T(256)(128)(2,1)S(1)}, u32[]{:S(2)}, u32[]{:S(2)}) collective-permute-start(bf16[3]{0:T(256)(128)(2,1)S(1)} %fusion.47), channel_id=1, source_target_pairs={{0,2},{2,4},{4,6},{6,8},{8,10},{10,12},{12,14},{14,16},{16,18},{18... | collective-permute-start | bytes 26 | tf_op jit(solution)/shard_map/ppermute | solution.py:17
  77.3 7.8 %all-gather.2.cloned.1.call-done = bf16[2048,1024]{1,0:T(8,128)(2,1)} async-done(((bf16[2048,512]{1,0:T(8,128)(2,1)}), bf16[2048,1024]{1,0:T(8,128)(2,1)}) %all-gather.2.cloned.1.call-update) | async-done | bytes 4194320 | tf_op jit(solution)/shard_map/all_gather | solution.py:204
  85.1 11.9 %convolution_convert_fusion.gate_ref = bf16[2048,2048]{1,0:T(8,128)(2,1)S(1)} fusion(bf16[2048,1024]{1,0:T(8,128)(2,1)} %all-gather.2.cloned.1.call-done, bf16[1024,2048]{1,0:T(8,128)(2,1)} %bitcast.82), kind=kOutput, calls=%fused_computation.3 | convolution fusion | flops 8594128896 | bytes 16777216 | tf_op jit(solution)/shard_map/dot_general | solution.py:206
  97.7 4.5 %copy-done.8 = bf16[2048,1024]{1,0:T(8,128)(2,1)S(1)} copy-done((bf16[2048,1024]{1,0:T(8,128)(2,1)S(1)}, bf16[2048,1024]{1,0:T(8,128)(2,1)}, u32[]{:S(2)}) %copy-start.8) | copy-done | bytes 4194328
  103.7 3.3 %collective-permute-start.1 = (bf16[3,1280]{1,0:T(4,128)(2,1)S(1)}, bf16[3,1280]{1,0:T(4,128)(2,1)S(1)}, u32[]{:S(2)}, u32[]{:S(2)}) collective-permute-start(bf16[3,1280]{1,0:T(4,128)(2,1)S(1)} %fusion.28), channel_id=1, source_target_pairs={{0,2},{2,4},{4,6},{6,8},{8,10},{10,12},{12,14},{14,16},{16,18},{18... | collective-permute-start | bytes 23048 | tf_op jit(solution)/shard_map/ppermute | solution.py:17
  115.0 4.0 %maximum_maximum_fusion = bf16[2051,1280]{1,0:T(8,128)(2,1)S(1)} fusion(bf16[2048,256]{1,0:T(8,128)(2,1)S(1)} %convolution_convert_fusion.1, bf16[2048,1024]{1,0:T(8,128)(2,1)} %copy-done.4, bf16[3,1280]{1,0:T(4,128)(2,1)S(1)} %collective-permute-done.1), kind=kLoop, calls=%fused_computation.6 | loop fusion | flops 15751680 | bytes 10501120 | tf_op jit(solution)/shard_map/concatenate | solution.py:221
  119.0 10.8 %multiply_convert_fusion.x_ref.b_ref.c_ref = bf16[2048,1280]{1,0:T(8,128)(2,1)S(1)} fusion(bf16[2048,256]{1,0:T(8,128)(2,1)S(1)} %convolution_convert_fusion.1, bf16[2051,1280]{1,0:T(8,128)(2,1)S(1)} %maximum_maximum_fusion, f32[1280]{0:T(1024)S(1)} %get-tuple-element.14, f32[1280]{0:T(1024)S(1)} %get-tuple-element.15, f32[1280]{0:T(1024)S(1)} %get-tuple-element.16, ...), kind=kLoop, calls=%fused_computation | loop fusion | flops 60293120 | bytes 26246144 | tf_op jit(solution)/shard_map/convert_element_type | solution.py:234
  129.8 2.4 copy-done.2
  133.3 15.3 %shard_map.136 = f32[16,128,1024]{2,1,0:T(8,128)} custom-call(bf16[2048,1280]{1,0:T(8,128)(2,1)} %copy-done.2, bf16[16,128,128]{2,1,0:T(8,128)(2,1)} %bitcast.84, f32[16,128,16]{2,1,0:T(8,128)} %multiply_multiply_fusion.end_ref), custom_call_target="tpu_custom_call" | custom-call | flops 536870912 | bytes 13107200 | tf_op jit(solution)/shard_map/pallas_call | solution.py:94
  148.6 4.7 %multiply_reduce_fusion = f32[128,1024]{1,0:T(8,128)S(1)} fusion(f32[16,128,1024]{2,1,0:T(8,128)} %shard_map.136, f32[16,1024]{1,0:T(8,128)S(1)} %mul.457), kind=kLoop, calls=%fused_computation.2 | loop fusion | flops 4063232 | bytes 8978432 | tf_op jit(solution)/shard_map/reduce_sum | solution.py:256
  153.4 1.9 collective-permute-start.2
  167.3 5.6 %collective-permute-done.3 = bf16[131,1024]{1,0:T(8,128)(2,1)S(1)} collective-permute-done((bf16[131,1024]{1,0:T(8,128)(2,1)S(1)}, bf16[131,1024]{1,0:T(8,128)(2,1)S(1)}, u32[]{:S(2)}, u32[]{:S(2)}) %collective-permute-start.3) | collective-permute-done | bytes 268320 | tf_op jit(solution)/shard_map/ppermute | solution.py:17
  176.3 5.2 %collective-permute-done.4 = bf16[131,1024]{1,0:T(8,128)(2,1)S(1)} collective-permute-done((bf16[131,1024]{1,0:T(8,128)(2,1)S(1)}, bf16[131,1024]{1,0:T(8,128)(2,1)S(1)}, u32[]{:S(2)}, u32[]{:S(2)}) %collective-permute-start.4) | collective-permute-done | bytes 268320 | tf_op jit(solution)/shard_map/ppermute | solution.py:17
  181.7 4.1 %collective-permute-start.5 = (bf16[131,1024]{1,0:T(8,128)(2,1)S(1)}, bf16[131,1024]{1,0:T(8,128)(2,1)S(1)}, u32[]{:S(2)}, u32[]{:S(2)}) collective-permute-start(bf16[131,1024]{1,0:T(8,128)(2,1)S(1)} %pad_maximum_fusion.4), channel_id=1, source_target_pairs={{0,2},{2,4},{4,6},{6,8},{8,10},{10,12},{12,14},{14,16},{16,18},{18... | collective-permute-start | bytes 804872 | tf_op jit(solution)/shard_map/ppermute | solution.py:17
  189.0 2.6 %collective-permute-done.5 = bf16[131,1024]{1,0:T(8,128)(2,1)S(1)} collective-permute-done((bf16[131,1024]{1,0:T(8,128)(2,1)S(1)}, bf16[131,1024]{1,0:T(8,128)(2,1)S(1)}, u32[]{:S(2)}, u32[]{:S(2)}) %collective-permute-start.5) | collective-permute-done | bytes 268320 | tf_op jit(solution)/shard_map/ppermute | solution.py:17
  191.6 13.0 %collective-permute-done.6 = bf16[128,1024]{1,0:T(8,128)(2,1)S(1)} collective-permute-done((bf16[128,1024]{1,0:T(8,128)(2,1)S(1)}, bf16[128,1024]{1,0:T(8,128)(2,1)S(1)}, u32[]{:S(2)}, u32[]{:S(2)}) %collective-permute-start.6) | collective-permute-done | bytes 262176 | tf_op jit(solution)/shard_map/ppermute | solution.py:17
  205.5 21.6 %shard_map.137 = (f32[2048,1024]{1,0:T(8,128)}, f32[2048,1]{1,0:T(8,128)}) custom-call(bf16[2048,1280]{1,0:T(8,128)(2,1)} %copy-done.2, bf16[2048,1280]{1,0:T(8,128)(2,1)} %copy-done.2, bf16[2048,1280]{1,0:T(8,128)(2,1)} %copy-done.2, f32[16,128,16]{2,1,0:T(8,128)} %bitcast.79, f32[16,16,128]{2,1,0:T(8,128)} %copy-done.9, ...), custom_call_target="tpu_custom_call" | custom-call | flops 3288334336 | bytes 29360128 | tf_op jit(solution)/shard_map/pallas_call | solution.py:122
  227.1 7.2 %psum.7 = f32[2048,1]{1,0:T(8,128)S(1)} all-reduce(f32[2048,1]{1,0:T(8,128)} %get-tuple-element.12), channel_id=1, replica_groups=mesh['seq'=16,'head'=2] {'head'}, use_global_device_ids=true, to_apply=%region_5.6 | all-reduce | flops 2048 | bytes 16384 | tf_op jit(solution)/shard_map/psum | solution.py:291
  234.7 5.2 %multiply_convert_fusion.1 = bf16[2048,1024]{1,0:T(8,128)(2,1)} fusion(f32[2048,1024]{1,0:T(8,128)} %get-tuple-element.11, f32[1024]{0:T(1024)S(1)} %copy-done.13, f32[2048]{0:T(1024)S(1)} %rsqrt_reduce_fusion), kind=kLoop, calls=%fused_computation.1 | loop fusion | flops 6291456 | bytes 12595200 | tf_op jit(solution)/shard_map/convert_element_type | solution.py:292
  (181 shorter events, 42.0 us)
Async XLA Ops:
  9.5 14.7 %copy-start.22 = (u32[32]{0:T(128)S(1)}, u32[32]{0:T(128)}, u32[]{:S(2)}) copy-start(u32[32]{0:T(128)} %constant.79) | copy-start | bytes 388
  9.5 16.0 %copy-start.20 = (s32[16]{0:T(128)S(1)}, s32[16]{0:T(128)}, u32[]{:S(2)}) copy-start(s32[16]{0:T(128)} %param.15) | copy-start | bytes 196
  12.0 53.2 %all-to-all-start = ((bf16[16,128,512]{2,1,0:T(8,128)(2,1)}), bf16[16,128,512]{2,1,0:T(8,128)(2,1)S(1)}, u32[]{:S(2)}, u32[]{:S(2)}) async-start(bf16[16,128,512]{2,1,0:T(8,128)(2,1)} %copy.66), calls=%async_computation | async-start | bytes 4194304 | tf_op jit(solution)/shard_map/all_to_all | solution.py:192
  18.4 66.7 %all-gather.2.cloned.1.call-start = ((), (), s32[]{:S(2)}) async-start(), calls=%async_computation.1 | async-start | bytes 6291456 | tf_op jit(solution)/shard_map/all_gather | solution.py:204
  18.4 50.6 %copy-start.11 = (s32[16]{0:T(128)S(1)}, s32[16]{0:T(128)}, u32[]{:S(2)}) copy-start(s32[16]{0:T(128)} %param.16) | copy-start | bytes 196
  18.5 54.9 %copy-start.18 = (f32[16]{0:T(128)S(1)}, f32[16]{0:T(128)}, u32[]{:S(2)}) copy-start(f32[16]{0:T(128)} %param.26) | copy-start | bytes 196
  18.5 55.6 %copy-start.12 = (f32[4,1024]{1,0:T(4,128)S(1)}, f32[4,1024]{1,0:T(4,128)}, u32[]{:S(2)}) copy-start(f32[4,1024]{1,0:T(4,128)} %param.22) | copy-start | bytes 49156
  18.5 55.6 %copy-start.14 = (f32[4,256]{1,0:T(4,128)S(1)}, f32[4,256]{1,0:T(4,128)}, u32[]{:S(2)}) copy-start(f32[4,256]{1,0:T(4,128)} %param.23) | copy-start | bytes 12292
  18.5 55.6 %copy-start.15 = (f32[1024]{0:T(1024)S(1)}, f32[1024]{0:T(1024)}, u32[]{:S(2)}) copy-start(f32[1024]{0:T(1024)} %param.24) | copy-start | bytes 12292
  18.5 55.6 %copy-start.17 = (f32[256]{0:T(256)S(1)}, f32[256]{0:T(256)}, u32[]{:S(2)}) copy-start(f32[256]{0:T(256)} %param.25) | copy-start | bytes 3076
  18.5 56.9 %copy-start.21 = (f32[16]{0:T(128)S(1)}, f32[16]{0:T(128)}, u32[]{:S(2)}) copy-start(f32[16]{0:T(128)} %param.21) | copy-start | bytes 196
  70.7 6.5 %collective-permute-start = (bf16[3]{0:T(256)(128)(2,1)S(1)}, bf16[3]{0:T(256)(128)(2,1)S(1)}, u32[]{:S(2)}, u32[]{:S(2)}) collective-permute-start(bf16[3]{0:T(256)(128)(2,1)S(1)} %fusion.47), channel_id=1, source_target_pairs={{0,2},{2,4},{4,6},{6,8},{8,10},{10,12},{12,14},{14,16},{16,18},{18... | collective-permute-start | bytes 26 | tf_op jit(solution)/shard_map/ppermute | solution.py:17
  97.1 6.7 %copy-start.6 = (bf16[2048,2048]{1,0:T(8,128)(2,1)}, bf16[2048,2048]{1,0:T(8,128)(2,1)S(1)}, u32[]{:S(2)}) copy-start(bf16[2048,2048]{1,0:T(8,128)(2,1)S(1)} %convolution_convert_fusion.gate_ref) | copy-start | bytes 25165828
  103.7 11.2 %collective-permute-start.1 = (bf16[3,1280]{1,0:T(4,128)(2,1)S(1)}, bf16[3,1280]{1,0:T(4,128)(2,1)S(1)}, u32[]{:S(2)}, u32[]{:S(2)}) collective-permute-start(bf16[3,1280]{1,0:T(4,128)(2,1)S(1)} %fusion.28), channel_id=1, source_target_pairs={{0,2},{2,4},{4,6},{6,8},{8,10},{10,12},{12,14},{14,16},{16,18},{18... | collective-permute-start | bytes 23048 | tf_op jit(solution)/shard_map/ppermute | solution.py:17
  109.3 9.7 %copy-start.9 = (f32[16,16,128]{2,1,0:T(8,128)}, f32[16,16,128]{2,1,0:T(8,128)S(1)}, u32[]{:S(2)}) copy-start(f32[16,16,128]{2,1,0:T(8,128)S(1)} %fusion.24.cumt_ref) | copy-start | bytes 393220
  109.6 20.2 %copy-start.7 = (f32[16,16,128]{1,2,0:T(8,128)}, f32[16,16,128]{1,2,0:T(8,128)S(1)}, u32[]{:S(2)}) copy-start(f32[16,16,128]{1,2,0:T(8,128)S(1)} %copy.73) | copy-start | bytes 393220
  148.6 6.7 %copy-start.3 = (f32[16,128,1024]{2,1,0:T(8,128)S(1)}, f32[16,128,1024]{2,1,0:T(8,128)}, u32[]{:S(2)}) copy-start(f32[16,128,1024]{2,1,0:T(8,128)} %shard_map.136) | copy-start | bytes 25165828
  153.4 10.5 %collective-permute-start.2 = (bf16[131,1024]{1,0:T(8,128)(2,1)S(1)}, bf16[131,1024]{1,0:T(8,128)(2,1)S(1)}, u32[]{:S(2)}, u32[]{:S(2)}) collective-permute-start(bf16[131,1024]{1,0:T(8,128)(2,1)S(1)} %pad_maximum_fusion.1), channel_id=1, source_target_pairs={{0,2},{2,4},{4,6},{6,8},{8,10},{10,12},{12,14},{14,16},{16,18},{18... | collective-permute-start | bytes 804872 | tf_op jit(solution)/shard_map/ppermute | solution.py:17
  164.2 8.7 %collective-permute-start.3 = (bf16[131,1024]{1,0:T(8,128)(2,1)S(1)}, bf16[131,1024]{1,0:T(8,128)(2,1)S(1)}, u32[]{:S(2)}, u32[]{:S(2)}) collective-permute-start(bf16[131,1024]{1,0:T(8,128)(2,1)S(1)} %pad_maximum_fusion.2), channel_id=1, source_target_pairs={{0,4},{2,6},{4,8},{6,10},{8,12},{10,14},{12,16},{14,18},{16,20},{1... | collective-permute-start | bytes 804872 | tf_op jit(solution)/shard_map/ppermute | solution.py:17
  173.1 8.4 %collective-permute-start.4 = (bf16[131,1024]{1,0:T(8,128)(2,1)S(1)}, bf16[131,1024]{1,0:T(8,128)(2,1)S(1)}, u32[]{:S(2)}, u32[]{:S(2)}) collective-permute-start(bf16[131,1024]{1,0:T(8,128)(2,1)S(1)} %pad_maximum_fusion.3), channel_id=1, source_target_pairs={{0,8},{2,10},{4,12},{6,14},{8,16},{10,18},{12,20},{14,22},{16,24},... | collective-permute-start | bytes 804872 | tf_op jit(solution)/shard_map/ppermute | solution.py:17
  181.7 9.9 %collective-permute-start.5 = (bf16[131,1024]{1,0:T(8,128)(2,1)S(1)}, bf16[131,1024]{1,0:T(8,128)(2,1)S(1)}, u32[]{:S(2)}, u32[]{:S(2)}) collective-permute-start(bf16[131,1024]{1,0:T(8,128)(2,1)S(1)} %pad_maximum_fusion.4), channel_id=1, source_target_pairs={{0,2},{2,4},{4,6},{6,8},{8,10},{10,12},{12,14},{14,16},{16,18},{18... | collective-permute-start | bytes 804872 | tf_op jit(solution)/shard_map/ppermute | solution.py:17
  186.8 17.8 %collective-permute-start.6 = (bf16[128,1024]{1,0:T(8,128)(2,1)S(1)}, bf16[128,1024]{1,0:T(8,128)(2,1)S(1)}, u32[]{:S(2)}, u32[]{:S(2)}) collective-permute-start(bf16[128,1024]{1,0:T(8,128)(2,1)S(1)} %fusion.12), channel_id=1, source_target_pairs={{0,18},{2,20},{4,22},{6,24},{8,26},{10,28},{12,30},{1,19},{3,21},{... | collective-permute-start | bytes 786440 | tf_op jit(solution)/shard_map/ppermute | solution.py:17
  205.5 29.2 %copy-start.13 = (f32[1024]{0:T(1024)S(1)}, f32[1024]{0:T(1024)}, u32[]{:S(2)}) copy-start(f32[1024]{0:T(1024)} %param.27) | copy-start | bytes 12292
  205.5 34.4 %copy-start.1 = (bf16[16,128,512]{2,1,0:T(8,128)(2,1)S(1)}, bf16[16,128,512]{2,1,0:T(8,128)(2,1)}, u32[]{:S(2)}) copy-start(bf16[16,128,512]{2,1,0:T(8,128)(2,1)} %param.14) | copy-start | bytes 6291460
  (8 other events, 33.6 us)
Sparse Core Ops, SparseCore 0:
  69.2 15.9 all-gather.1

commit v13 on v12

--- a/solution.py
+++ b/solution.py
@@ -73,10 +73,15 @@
     sq_ref[...] = jnp.sum(total_sq, axis=1, keepdims=True)
 
 
-def contrib_tile(x_ref, bt_ref, end_ref, out_ref):
+def contrib_tile(x_ref, bt_ref, end_ref, pass_ref, before_ref, total_ref):
     f32 = jnp.float32
     tile_len = x_ref.shape[0]
     pairs = x_ref.shape[1] // 128
+
+    @pl.when(pl.program_id(0) == 0)
+    def _():
+        total_ref[...] = jnp.zeros_like(total_ref)
+
     b_t = bt_ref[0]
     to_end = end_ref[0]
     first_half = lax.broadcasted_iota(jnp.int32, (tile_len, 128), 1) < 64
@@ -86,10 +91,13 @@
             first_half, to_end[:, 2 * pair : 2 * pair + 1], to_end[:, 2 * pair + 1 : 2 * pair + 2]
         )
         scaled = (x_ref[:, cols].astype(f32) * scale).astype(jnp.bfloat16)
-        out_ref[0, :, cols] = jnp.dot(b_t, scaled, preferred_element_type=f32)
-
-
-def contrib_tiles(conv_out, b_t, to_end, inner_here, state_dim):
+        contrib = jnp.dot(b_t, scaled, preferred_element_type=f32)
+        state = total_ref[:, cols]
+        before_ref[0, :, cols] = state
+        total_ref[:, cols] = pass_ref[0, :, cols] * state + contrib
+
+
+def contrib_tiles(conv_out, b_t, to_end, passing_wide, inner_here, state_dim):
     tiles_dev, tile_len, heads_here = to_end.shape
     return pl.pallas_call(
         contrib_tile,
@@ -98,15 +106,23 @@
             pl.BlockSpec((tile_len, inner_here), lambda j: (j, 0)),
             pl.BlockSpec((1, state_dim, tile_len), lambda j: (j, 0, 0)),
             pl.BlockSpec((1, tile_len, heads_here), lambda j: (j, 0, 0)),
-        ],
-        out_specs=pl.BlockSpec((1, state_dim, inner_here), lambda j: (j, 0, 0)),
-        out_shape=jax.ShapeDtypeStruct((tiles_dev, state_dim, inner_here), jnp.float32),
+            pl.BlockSpec((1, 1, inner_here), lambda j: (j, 0, 0)),
+        ],
+        out_specs=[
+            pl.BlockSpec((1, state_dim, inner_here), lambda j: (j, 0, 0)),
+            pl.BlockSpec((state_dim, inner_here), lambda j: (0, 0)),
+        ],
+        out_shape=[
+            jax.ShapeDtypeStruct((tiles_dev, state_dim, inner_here), jnp.float32),
+            jax.ShapeDtypeStruct((state_dim, inner_here), jnp.float32),
+        ],
+        compiler_params=pltpu.CompilerParams(dimension_semantics=("arbitrary",)),
         cost_estimate=pl.CostEstimate(
             flops=tiles_dev * 2 * tile_len * inner_here * state_dim,
             transcendentals=0,
             bytes_accessed=tiles_dev * (tile_len * (inner_here + state_dim) * 2 + inner_here * state_dim * 4),
         ),
-    )(conv_out, b_t, to_end)
+    )(conv_out, b_t, to_end, passing_wide)
 
 
 def mix_tiles(conv_out, zx, cumul, cumul_t, dt_t, later, before_tile, prefix_wide, entering, d_full):
@@ -246,21 +262,13 @@
     b_t = conv_out[:, inner_here : inner_here + state_dim].reshape(
         tiles_dev, tile_len, state_dim
     ).transpose(0, 2, 1)
-    contrib = contrib_tiles(conv_out, b_t, to_end, inner_here, state_dim)
     passing = jnp.exp(cumul[:, tile_len - 1, :]) * (1.0 - has_bound)[:, None]
     through = jnp.cumprod(passing, 0)
     prefix = jnp.concatenate([jnp.ones((1, heads_here), jnp.float32), through[:-1]], 0)
-    reverse = jnp.cumprod(passing[::-1], 0)[::-1]
-    to_last = jnp.concatenate([reverse[1:], jnp.ones((1, heads_here), jnp.float32)], 0)
     widen = lambda per_head: jnp.repeat(per_head, head_dim, axis=-1)
-    run_state = jnp.sum(widen(to_last)[:, None, :] * contrib, 0)
-    passing_wide = widen(passing)
-    running = jnp.zeros((state_dim, inner_here), jnp.float32)
-    states = []
-    for tile in range(tiles_dev):
-        states.append(running)
-        running = passing_wide[tile][None, :] * running + contrib[tile]
-    before_tile = jnp.stack(states)
+    before_tile, run_state = contrib_tiles(
+        conv_out, b_t, to_end, widen(passing)[:, None, :], inner_here, state_dim
+    )
     position = lax.axis_index("seq")
     run_decay = widen(through[tiles_dev - 1])
     distance = 1

time: 248 us -> 242 us (0.976)
  other arithmetic: 46.1 us -> 29.6 us
  waiting for transfers between devices: 34.5 us -> 45.6 us
    unnamed x14 -> x0, other arithmetic: 13 us -> none
    ppermute x7, waiting for transfers between devices: 26.7 us -> 36.3 us  [shifted(): return lax.ppermute(x, axis, pairs)]
    reduce_sum x1 -> x0, other arithmetic: 4.7 us -> none  [shards(): run_state = jnp.sum(widen(to_last)[:, None, :] * contrib, 0)]
    unnamed x53 -> x52, local copies, waits for them, and re-layouts: 15.4 us -> 15.1 us
  transfers between devices with their start and end apart: 9 -> 9, of which waited for: 6 -> 7; matrix products, arithmetic and copies ran while one was open for 14% -> 6% of each run, Pallas kernels for 0% -> 0%
where the time goes in v13:
time: 242 us; the launch traced here: 240 us
  blocking collectives  47.5 us (20%)
  waiting for transfers between devices  45.6 us (19%)
  Pallas kernels  36.3 us (15%)
  other arithmetic  29.6 us (12%)
  local copies, waits for them, and re-layouts  26.8 us (11%)
  starting transfers between devices  20.5 us (8%)
  matrix products  19.6 us (8%)
  between operations  14.7 us (6%)
    unnamed x1, blocking collectives  39.5 us
    ppermute x7, waiting for transfers between devices, shifted(): return lax.ppermute(x, axis, pairs)  36.3 us
    pallas_call x1, Pallas kernels, mix_tiles(): pl.pallas_call(mix_tile, grid=(tiles_dev,), in_specs=[pl.BlockSpec((tile_...  21.5 us
    dot_general x3, matrix products, shards(): jnp.dot(piece, weight, preferred_element_type=jnp.float32)  16.6 us
    unnamed x52, local copies, waits for them, and re-layouts  15.1 us
    pallas_call x1, Pallas kernels, contrib_tiles(): pl.pallas_call(contrib_tile, grid=(tiles_dev,), in_specs=[pl.BlockSpec((t...  14.8 us
    ppermute x7, starting transfers between devices, shifted(): return lax.ppermute(x, axis, pairs)  14.1 us
    convert_element_type x1, other arithmetic, shards(): conv_out = jax.nn.silu(total).astype(jnp.bfloat16)  10.8 us
  transfers between devices with their start and end apart: 9, of which 7 were waited for; matrix products, arithmetic and copies ran while one was open for 6% of the time, Pallas kernels for 0%

profile of v13, /device:TPU:29, one launch (start us, length us, event | category | flops | bytes accessed | tf_op | source)
XLA Modules:
  0.0 240.4 jit_solution(6909390483613054867)
XLA Ops:
  9.5 2.5 %copy.66 = bf16[16,128,512]{2,1,0:T(8,128)(2,1)} copy(bf16[16,128,512]{2,0,1:T(8,128)(2,1)S(1)} %fusion.4) | data formatting | bytes 4194304 | tf_op jit(solution)/shard_map/convert_element_type | solution.py:207
  12.0 6.4 %all-to-all-start = ((bf16[16,128,512]{2,1,0:T(8,128)(2,1)}), bf16[16,128,512]{2,1,0:T(8,128)(2,1)S(1)}, u32[]{:S(2)}, u32[]{:S(2)}) async-start(bf16[16,128,512]{2,1,0:T(8,128)(2,1)} %copy.66), calls=%async_computation | async-start | bytes 4194304 | tf_op jit(solution)/shard_map/all_to_all | solution.py:208
  18.5 5.6 %copy.80 = bf16[128,8,2,1024]{3,1,2,0:T(8,128)(2,1)} copy(bf16[128,8,2,1024]{3,2,1,0:T(2,128)(2,1)} %bitcast.50) | data formatting | bytes 8388608
  25.5 39.5 %all-reduce.1 = s32[256]{0:T(256)S(1)} all-reduce(s32[256]{0:T(256)S(1)} %dynamic-update-slice), channel_id=1, replica_groups=mesh['seq'=16,'head'=2] {'seq'}, use_global_device_ids=true, to_apply=%add.1 | all-reduce | flops 256 | bytes 2048
  66.6 2.5 %copy.68 = bf16[16,128,512]{2,1,0:T(8,128)(2,1)} copy(bf16[16,128,512]{2,0,1:T(8,128)(2,1)S(1)} %fusion.7) | data formatting | bytes 4194304 | tf_op jit(solution)/shard_map/convert_element_type | solution.py:215
  70.7 2.6 %collective-permute-start = (bf16[3]{0:T(256)(128)(2,1)S(1)}, bf16[3]{0:T(256)(128)(2,1)S(1)}, u32[]{:S(2)}, u32[]{:S(2)}) collective-permute-start(bf16[3]{0:T(256)(128)(2,1)S(1)} %fusion.38), channel_id=1, source_target_pairs={{0,2},{2,4},{4,6},{6,8},{8,10},{10,12},{12,14},{14,16},{16,18},{18... | collective-permute-start | bytes 26 | tf_op jit(solution)/shard_map/ppermute | solution.py:17
  73.8 2.0 collective-permute-done
  75.9 9.2 %all-gather.2.cloned.1.call-done = bf16[2048,1024]{1,0:T(8,128)(2,1)} async-done(((bf16[2048,512]{1,0:T(8,128)(2,1)}), bf16[2048,1024]{1,0:T(8,128)(2,1)}) %all-gather.2.cloned.1.call-update) | async-done | bytes 4194320 | tf_op jit(solution)/shard_map/all_gather | solution.py:220
  85.2 3.4 %compare_select_fusion = f32[2048,16]{0,1:T(8,128)S(1)} fusion(bf16[2048,1024]{1,0:T(8,128)(2,1)} %all-gather.2.cloned.1.call-done, bf16[1024,16]{0,1:T(8,128)(2,1)S(1)} %copy-done.10, f32[16]{0:T(128)S(1)} %copy-done.16), kind=kOutput, calls=%fused_computation.27 | convolution fusion | flops 67338240 | bytes 4358208 | tf_op jit(solution)/shard_map/dot_general | solution.py:222
  89.9 11.9 %convolution_convert_fusion.gate_ref = bf16[2048,2048]{1,0:T(8,128)(2,1)S(1)} fusion(bf16[2048,1024]{1,0:T(8,128)(2,1)} %all-gather.2.cloned.1.call-done, bf16[1024,2048]{1,0:T(8,128)(2,1)} %bitcast.51), kind=kOutput, calls=%fused_computation.2 | convolution fusion | flops 8594128896 | bytes 16777216 | tf_op jit(solution)/shard_map/dot_general | solution.py:222
  102.6 4.5 %copy-done.7 = bf16[2048,1024]{1,0:T(8,128)(2,1)S(1)} copy-done((bf16[2048,1024]{1,0:T(8,128)(2,1)S(1)}, bf16[2048,1024]{1,0:T(8,128)(2,1)}, u32[]{:S(2)}) %copy-start.7) | copy-done | bytes 4194328
  109.2 3.1 %collective-permute-start.1 = (bf16[3,1280]{1,0:T(4,128)(2,1)S(1)}, bf16[3,1280]{1,0:T(4,128)(2,1)S(1)}, u32[]{:S(2)}, u32[]{:S(2)}) collective-permute-start(bf16[3,1280]{1,0:T(4,128)(2,1)S(1)} %fusion.20), channel_id=1, source_target_pairs={{0,2},{2,4},{4,6},{6,8},{8,10},{10,12},{12,14},{14,16},{16,18},{18... | collective-permute-start | bytes 23048 | tf_op jit(solution)/shard_map/ppermute | solution.py:17
  114.6 4.0 %maximum_maximum_fusion = bf16[2051,1280]{1,0:T(8,128)(2,1)S(1)} fusion(bf16[2048,256]{1,0:T(8,128)(2,1)S(1)} %convolution_convert_fusion.1, bf16[2048,1024]{1,0:T(8,128)(2,1)} %copy-done.3, bf16[3,1280]{1,0:T(4,128)(2,1)S(1)} %collective-permute-done.1), kind=kLoop, calls=%fused_computation.5 | loop fusion | flops 15751680 | bytes 10501120 | tf_op jit(solution)/shard_map/concatenate | solution.py:237
  118.6 10.8 %multiply_convert_fusion.x_ref.b_ref.c_ref = bf16[2048,1280]{1,0:T(8,128)(2,1)S(1)} fusion(bf16[2048,256]{1,0:T(8,128)(2,1)S(1)} %convolution_convert_fusion.1, bf16[2051,1280]{1,0:T(8,128)(2,1)S(1)} %maximum_maximum_fusion, f32[1280]{0:T(1024)S(1)} %get-tuple-element.18, f32[1280]{0:T(1024)S(1)} %get-tuple-element.19, f32[1280]{0:T(1024)S(1)} %get-tuple-element.20, ...), kind=kLoop, calls=%fused_computation | loop fusion | flops 60293120 | bytes 26246144 | tf_op jit(solution)/shard_map/convert_element_type | solution.py:250
  129.4 2.4 copy-done.2
  132.9 14.8 %shard_map.136 = (f32[16,128,1024]{2,1,0:T(8,128)}, f32[128,1024]{1,0:T(8,128)}) custom-call(bf16[2048,1280]{1,0:T(8,128)(2,1)} %copy-done.2, bf16[16,128,128]{2,1,0:T(8,128)(2,1)} %bitcast.53, f32[16,128,16]{2,1,0:T(8,128)} %multiply_multiply_fusion.end_ref, f32[16,1,1024]{2,1,0:T(1,128)} %broadcast_in_dim_reshape.10.pass_ref), custom_call_target="tpu_custom_call" | custom-call | flops 536870912 | bytes 13107200 | tf_op jit(solution)/shard_map/pallas_call | solution.py:102
  148.9 2.3 collective-permute-start.2
  151.3 7.0 %collective-permute-done.2 = bf16[131,1024]{1,0:T(8,128)(2,1)S(1)} collective-permute-done((bf16[131,1024]{1,0:T(8,128)(2,1)S(1)}, bf16[131,1024]{1,0:T(8,128)(2,1)S(1)}, u32[]{:S(2)}, u32[]{:S(2)}) %collective-permute-start.2) | collective-permute-done | bytes 268320 | tf_op jit(solution)/shard_map/ppermute | solution.py:17
  160.9 8.4 %collective-permute-done.3 = bf16[131,1024]{1,0:T(8,128)(2,1)S(1)} collective-permute-done((bf16[131,1024]{1,0:T(8,128)(2,1)S(1)}, bf16[131,1024]{1,0:T(8,128)(2,1)S(1)}, u32[]{:S(2)}, u32[]{:S(2)}) %collective-permute-start.3) | collective-permute-done | bytes 268320 | tf_op jit(solution)/shard_map/ppermute | solution.py:17
  172.0 4.9 %collective-permute-done.4 = bf16[131,1024]{1,0:T(8,128)(2,1)S(1)} collective-permute-done((bf16[131,1024]{1,0:T(8,128)(2,1)S(1)}, bf16[131,1024]{1,0:T(8,128)(2,1)S(1)}, u32[]{:S(2)}, u32[]{:S(2)}) %collective-permute-start.4) | collective-permute-done | bytes 268320 | tf_op jit(solution)/shard_map/ppermute | solution.py:17
  185.3 12.2 %collective-permute-done.6 = bf16[128,1024]{1,0:T(8,128)(2,1)S(1)} collective-permute-done((bf16[128,1024]{1,0:T(8,128)(2,1)S(1)}, bf16[128,1024]{1,0:T(8,128)(2,1)S(1)}, u32[]{:S(2)}, u32[]{:S(2)}) %collective-permute-start.6) | collective-permute-done | bytes 262176 | tf_op jit(solution)/shard_map/ppermute | solution.py:17
  198.4 21.5 %shard_map.137 = (f32[2048,1024]{1,0:T(8,128)}, f32[2048,1]{1,0:T(8,128)}) custom-call(bf16[2048,1280]{1,0:T(8,128)(2,1)} %copy-done.2, bf16[2048,1280]{1,0:T(8,128)(2,1)} %copy-done.2, bf16[2048,1280]{1,0:T(8,128)(2,1)} %copy-done.2, f32[16,128,16]{2,1,0:T(8,128)} %bitcast.48, f32[16,16,128]{2,1,0:T(8,128)} %copy-done.9, ...), custom_call_target="tpu_custom_call" | custom-call | flops 3288334336 | bytes 29360128 | tf_op jit(solution)/shard_map/pallas_call | solution.py:138
  219.9 8.0 %psum.7 = f32[2048,1]{1,0:T(8,128)S(1)} all-reduce(f32[2048,1]{1,0:T(8,128)} %get-tuple-element.16), channel_id=1, replica_groups=mesh['seq'=16,'head'=2] {'head'}, use_global_device_ids=true, to_apply=%region_3.4 | all-reduce | flops 2048 | bytes 16384 | tf_op jit(solution)/shard_map/psum | solution.py:299
  228.3 5.3 %multiply_convert_fusion.1 = bf16[2048,1024]{1,0:T(8,128)(2,1)} fusion(f32[2048,1024]{1,0:T(8,128)} %get-tuple-element.15, f32[1024]{0:T(1024)S(1)} %copy-done.13, f32[2048]{0:T(1024)S(1)} %rsqrt_reduce_fusion), kind=kLoop, calls=%fused_computation.1 | loop fusion | flops 6291456 | bytes 12595200 | tf_op jit(solution)/shard_map/convert_element_type | solution.py:300
  (129 shorter events, 30.8 us)
Async XLA Ops:
  12.0 53.3 %all-to-all-start = ((bf16[16,128,512]{2,1,0:T(8,128)(2,1)}), bf16[16,128,512]{2,1,0:T(8,128)(2,1)S(1)}, u32[]{:S(2)}, u32[]{:S(2)}) async-start(bf16[16,128,512]{2,1,0:T(8,128)(2,1)} %copy.66), calls=%async_computation | async-start | bytes 4194304 | tf_op jit(solution)/shard_map/all_to_all | solution.py:208
  18.4 5.7 %copy-start.22 = (u32[32]{0:T(128)S(1)}, u32[32]{0:T(128)}, u32[]{:S(2)}) copy-start(u32[32]{0:T(128)} %constant.74) | copy-start | bytes 388
  18.4 6.8 %copy-start.20 = (s32[16]{0:T(128)S(1)}, s32[16]{0:T(128)}, u32[]{:S(2)}) copy-start(s32[16]{0:T(128)} %param.15) | copy-start | bytes 196
  18.4 66.7 %all-gather.2.cloned.1.call-start = ((), (), s32[]{:S(2)}) async-start(), calls=%async_computation.1 | async-start | bytes 6291456 | tf_op jit(solution)/shard_map/all_gather | solution.py:220
  65.2 8.1 %copy-start.12 = (f32[4,1024]{1,0:T(4,128)S(1)}, f32[4,1024]{1,0:T(4,128)}, u32[]{:S(2)}) copy-start(f32[4,1024]{1,0:T(4,128)} %param.22) | copy-start | bytes 49156
  65.2 8.1 %copy-start.14 = (f32[4,256]{1,0:T(4,128)S(1)}, f32[4,256]{1,0:T(4,128)}, u32[]{:S(2)}) copy-start(f32[4,256]{1,0:T(4,128)} %param.23) | copy-start | bytes 12292
  65.2 8.1 %copy-start.15 = (f32[1024]{0:T(1024)S(1)}, f32[1024]{0:T(1024)}, u32[]{:S(2)}) copy-start(f32[1024]{0:T(1024)} %param.24) | copy-start | bytes 12292
  65.2 8.1 %copy-start.17 = (f32[256]{0:T(256)S(1)}, f32[256]{0:T(256)}, u32[]{:S(2)}) copy-start(f32[256]{0:T(256)} %param.25) | copy-start | bytes 3076
  65.2 8.5 %copy-start.21 = (f32[16]{0:T(128)S(1)}, f32[16]{0:T(128)}, u32[]{:S(2)}) copy-start(f32[16]{0:T(128)} %param.21) | copy-start | bytes 196
  65.2 19.9 %copy-start.10 = (bf16[1024,16]{0,1:T(8,128)(2,1)S(1)}, bf16[1024,16]{0,1:T(8,128)(2,1)}, u32[]{:S(2)}) copy-start(bf16[1024,16]{0,1:T(8,128)(2,1)} %param.19) | copy-start | bytes 98308
  65.2 19.9 %copy-start.16 = (f32[16]{0:T(128)S(1)}, f32[16]{0:T(128)}, u32[]{:S(2)}) copy-start(f32[16]{0:T(128)} %param.20) | copy-start | bytes 196
  70.7 5.2 %collective-permute-start = (bf16[3]{0:T(256)(128)(2,1)S(1)}, bf16[3]{0:T(256)(128)(2,1)S(1)}, u32[]{:S(2)}, u32[]{:S(2)}) collective-permute-start(bf16[3]{0:T(256)(128)(2,1)S(1)} %fusion.38), channel_id=1, source_target_pairs={{0,2},{2,4},{4,6},{6,8},{8,10},{10,12},{12,14},{14,16},{16,18},{18... | collective-permute-start | bytes 26 | tf_op jit(solution)/shard_map/ppermute | solution.py:17
  88.9 12.9 %copy-start.9 = (f32[16,16,128]{2,1,0:T(8,128)}, f32[16,16,128]{2,1,0:T(8,128)S(1)}, u32[]{:S(2)}) copy-start(f32[16,16,128]{2,1,0:T(8,128)S(1)} %fusion.16.cumt_ref) | copy-start | bytes 393220
  89.3 23.1 %copy-start.6 = (f32[16,16,128]{1,2,0:T(8,128)}, f32[16,16,128]{1,2,0:T(8,128)S(1)}, u32[]{:S(2)}) copy-start(f32[16,16,128]{1,2,0:T(8,128)S(1)} %copy.73) | copy-start | bytes 393220
  101.9 6.6 %copy-start.5 = (bf16[2048,2048]{1,0:T(8,128)(2,1)}, bf16[2048,2048]{1,0:T(8,128)(2,1)S(1)}, u32[]{:S(2)}) copy-start(bf16[2048,2048]{1,0:T(8,128)(2,1)S(1)} %convolution_convert_fusion.gate_ref) | copy-start | bytes 25165828
  109.2 5.3 %collective-permute-start.1 = (bf16[3,1280]{1,0:T(4,128)(2,1)S(1)}, bf16[3,1280]{1,0:T(4,128)(2,1)S(1)}, u32[]{:S(2)}, u32[]{:S(2)}) collective-permute-start(bf16[3,1280]{1,0:T(4,128)(2,1)S(1)} %fusion.20), channel_id=1, source_target_pairs={{0,2},{2,4},{4,6},{6,8},{8,10},{10,12},{12,14},{14,16},{16,18},{18... | collective-permute-start | bytes 23048 | tf_op jit(solution)/shard_map/ppermute | solution.py:17
  147.7 21.6 %copy-start.8 = (f32[128,1024]{1,0:T(8,128)S(1)}, f32[128,1024]{1,0:T(8,128)}, u32[]{:S(2)}) copy-start(f32[128,1024]{1,0:T(8,128)} %get-tuple-element.14) | copy-start | bytes 1572868
  148.9 30.8 %copy-start.18 = (f32[16]{0:T(128)S(1)}, f32[16]{0:T(128)}, u32[]{:S(2)}) copy-start(f32[16]{0:T(128)} %param.26) | copy-start | bytes 196
  148.9 9.4 %collective-permute-start.2 = (bf16[131,1024]{1,0:T(8,128)(2,1)S(1)}, bf16[131,1024]{1,0:T(8,128)(2,1)S(1)}, u32[]{:S(2)}, u32[]{:S(2)}) collective-permute-start(bf16[131,1024]{1,0:T(8,128)(2,1)S(1)} %pad_maximum_fusion.1), channel_id=1, source_target_pairs={{0,2},{2,4},{4,6},{6,8},{8,10},{10,12},{12,14},{14,16},{16,18},{18... | collective-permute-start | bytes 804872 | tf_op jit(solution)/shard_map/ppermute | solution.py:17
  159.6 9.7 %collective-permute-start.3 = (bf16[131,1024]{1,0:T(8,128)(2,1)S(1)}, bf16[131,1024]{1,0:T(8,128)(2,1)S(1)}, u32[]{:S(2)}, u32[]{:S(2)}) collective-permute-start(bf16[131,1024]{1,0:T(8,128)(2,1)S(1)} %pad_maximum_fusion.2), channel_id=1, source_target_pairs={{0,4},{2,6},{4,8},{6,10},{8,12},{10,14},{12,16},{14,18},{16,20},{1... | collective-permute-start | bytes 804872 | tf_op jit(solution)/shard_map/ppermute | solution.py:17
  169.5 7.3 %collective-permute-start.4 = (bf16[131,1024]{1,0:T(8,128)(2,1)S(1)}, bf16[131,1024]{1,0:T(8,128)(2,1)S(1)}, u32[]{:S(2)}, u32[]{:S(2)}) collective-permute-start(bf16[131,1024]{1,0:T(8,128)(2,1)S(1)} %pad_maximum_fusion.3), channel_id=1, source_target_pairs={{0,8},{2,10},{4,12},{6,14},{8,16},{10,18},{12,20},{14,22},{16,24},... | collective-permute-start | bytes 804872 | tf_op jit(solution)/shard_map/ppermute | solution.py:17
  177.0 8.2 %collective-permute-start.5 = (bf16[131,1024]{1,0:T(8,128)(2,1)S(1)}, bf16[131,1024]{1,0:T(8,128)(2,1)S(1)}, u32[]{:S(2)}, u32[]{:S(2)}) collective-permute-start(bf16[131,1024]{1,0:T(8,128)(2,1)S(1)} %pad_maximum_fusion.4), channel_id=1, source_target_pairs={{0,2},{2,4},{4,6},{6,8},{8,10},{10,12},{12,14},{14,16},{16,18},{18... | collective-permute-start | bytes 804872 | tf_op jit(solution)/shard_map/ppermute | solution.py:17
  180.4 17.1 %collective-permute-start.6 = (bf16[128,1024]{1,0:T(8,128)(2,1)S(1)}, bf16[128,1024]{1,0:T(8,128)(2,1)S(1)}, u32[]{:S(2)}, u32[]{:S(2)}) collective-permute-start(bf16[128,1024]{1,0:T(8,128)(2,1)S(1)} %fusion.12), channel_id=1, source_target_pairs={{0,18},{2,20},{4,22},{6,24},{8,26},{10,28},{12,30},{1,19},{3,21},{... | collective-permute-start | bytes 786440 | tf_op jit(solution)/shard_map/ppermute | solution.py:17
  198.4 29.8 %copy-start.13 = (f32[1024]{0:T(1024)S(1)}, f32[1024]{0:T(1024)}, u32[]{:S(2)}) copy-start(f32[1024]{0:T(1024)} %param.27) | copy-start | bytes 12292
  (8 other events, 29.9 us)
Sparse Core Ops, SparseCore 0:
  69.3 15.8 all-gather.1

commit v14 on v13

--- a/solution.py
+++ b/solution.py
@@ -234,7 +234,6 @@
     tail = conv_in[row_count - keep_rows :]
     tail_seg = (segment[row_count - keep_rows :] - segment[row_count - 1]).astype(jnp.bfloat16)
     got_tail, got_seg = shifted((tail, tail_seg), "seq", 1)
-    extended = jnp.concatenate([got_tail, conv_in], 0)
     ext_seg = jnp.concatenate([got_seg.astype(jnp.float32), segment], 0)
     conv_weight = jnp.concatenate([conv_x, conv_bc], 1)
     conv_bias = jnp.concatenate([cbias_x, cbias_bc], 0)
@@ -244,7 +243,9 @@
         total = total + jnp.where(
             same[:, None],
             conv_weight[back_step][None, :]
-            * extended[back_step : back_step + row_count].astype(jnp.float32),
+            * jnp.concatenate(
+                [got_tail[back_step:], conv_in[: row_count - keep_rows + back_step]], 0
+            ).astype(jnp.float32),
             0.0,
         )
     conv_out = jax.nn.silu(total).astype(jnp.bfloat16)

time: 242 us -> 255 us (1.054)
  other arithmetic: 29.6 us -> 45.1 us
    concatenate x1 -> x4, other arithmetic: 0.01 us -> 8.94 us  [shards(): conv_in = jnp.concatenate([x_in, bc_all], 1)]
    convert_element_type x1, other arithmetic: 10.8 us -> 18 us  [shards(): conv_out = jax.nn.silu(total).astype(jnp.bfloat16)]
    concatenate x1 -> x0, other arithmetic: 4 us -> none  [shards(): extended = jnp.concatenate([got_tail, conv_in], 0)]
    unnamed x52 -> x62, local copies, waits for them, and re-layouts: 15.1 us -> 15.3 us
  transfers between devices with their start and end apart: 9 -> 9, of which waited for: 7 -> 7; matrix products, arithmetic and copies ran while one was open for 6% -> 8% of each run, Pallas kernels for 0% -> 0%
where the time goes in v14:
time: 255 us; the launch traced here: 253 us
  blocking collectives  46.7 us (18%)
  other arithmetic  45.1 us (18%)
  waiting for transfers between devices  44.5 us (17%)
  Pallas kernels  36.3 us (14%)
  local copies, waits for them, and re-layouts  28.2 us (11%)
  starting transfers between devices  20.1 us (8%)
  matrix products  17.4 us (7%)
  between operations  14.8 us (6%)
    unnamed x1, blocking collectives  39.3 us
    ppermute x7, waiting for transfers between devices, shifted(): return lax.ppermute(x, axis, pairs)  36.1 us
    pallas_call x1, Pallas kernels, mix_tiles(): pl.pallas_call(mix_tile, grid=(tiles_dev,), in_specs=[pl.BlockSpec((tile_...  21.5 us
    convert_element_type x1, other arithmetic, shards(): conv_out = jax.nn.silu(total).astype(jnp.bfloat16)  18 us
    unnamed x62, local copies, waits for them, and re-layouts  15.3 us
    pallas_call x1, Pallas kernels, contrib_tiles(): pl.pallas_call(contrib_tile, grid=(tiles_dev,), in_specs=[pl.BlockSpec((t...  14.8 us
    dot_general x3, matrix products, shards(): jnp.dot(piece, weight, preferred_element_type=jnp.float32)  14.4 us
    ppermute x7, starting transfers between devices, shifted(): return lax.ppermute(x, axis, pairs)  13.6 us
  transfers between devices with their start and end apart: 9, of which 7 were waited for; matrix products, arithmetic and copies ran while one was open for 8% of the time, Pallas kernels for 0%

profile of v14, /device:TPU:29, one launch (start us, length us, event | category | flops | bytes accessed | tf_op | source)
XLA Modules:
  0.0 253.0 jit_solution(784376946662083776)
XLA Ops:
  9.5 2.5 copy.66
  12.0 6.4 %all-to-all-start = ((bf16[16,128,512]{2,1,0:T(8,128)(2,1)}), bf16[16,128,512]{2,1,0:T(8,128)(2,1)S(1)}, u32[]{:S(2)}, u32[]{:S(2)}) async-start(bf16[16,128,512]{2,1,0:T(8,128)(2,1)} %copy.66), calls=%async_computation | async-start | bytes 4194304 | tf_op jit(solution)/shard_map/all_to_all | solution.py:208
  18.5 5.6 %copy.80 = bf16[128,8,2,1024]{3,1,2,0:T(8,128)(2,1)} copy(bf16[128,8,2,1024]{3,2,1,0:T(2,128)(2,1)} %bitcast.50) | data formatting | bytes 8388608
  25.7 39.3 %all-reduce.1 = s32[256]{0:T(256)S(1)} all-reduce(s32[256]{0:T(256)S(1)} %dynamic-update-slice), channel_id=1, replica_groups=mesh['seq'=16,'head'=2] {'seq'}, use_global_device_ids=true, to_apply=%add.1 | all-reduce | flops 256 | bytes 2048
  66.6 2.5 copy.68
  70.9 2.6 %collective-permute-start = (bf16[3]{0:T(256)(128)(2,1)S(1)}, bf16[3]{0:T(256)(128)(2,1)S(1)}, u32[]{:S(2)}, u32[]{:S(2)}) collective-permute-start(bf16[3]{0:T(256)(128)(2,1)S(1)} %fusion.41), channel_id=1, source_target_pairs={{0,2},{2,4},{4,6},{6,8},{8,10},{10,12},{12,14},{14,16},{16,18},{18... | collective-permute-start | bytes 26 | tf_op jit(solution)/shard_map/ppermute | solution.py:17
  76.8 8.4 %all-gather.2.cloned.1.call-done = bf16[2048,1024]{1,0:T(8,128)(2,1)} async-done(((bf16[2048,512]{1,0:T(8,128)(2,1)}), bf16[2048,1024]{1,0:T(8,128)(2,1)}) %all-gather.2.cloned.1.call-update) | async-done | bytes 4194320 | tf_op jit(solution)/shard_map/all_gather | solution.py:220
  85.2 11.9 %convolution_convert_fusion.gate_ref = bf16[2048,2048]{1,0:T(8,128)(2,1)S(1)} fusion(bf16[2048,1024]{1,0:T(8,128)(2,1)} %all-gather.2.cloned.1.call-done, bf16[1024,2048]{1,0:T(8,128)(2,1)} %bitcast.51), kind=kOutput, calls=%fused_computation.7 | convolution fusion | flops 8594128896 | bytes 16777216 | tf_op jit(solution)/shard_map/dot_general | solution.py:222
  97.8 4.5 %copy-done.6 = bf16[2048,1024]{1,0:T(8,128)(2,1)S(1)} copy-done((bf16[2048,1024]{1,0:T(8,128)(2,1)S(1)}, bf16[2048,1024]{1,0:T(8,128)(2,1)}, u32[]{:S(2)}) %copy-start.6) | copy-done | bytes 4194328
  104.4 2.8 %fusion = bf16[2045,1280]{1,0:T(8,128)(2,1)} fusion(bf16[2048,256]{1,0:T(8,128)(2,1)S(1)} %convolution_convert_fusion.1, bf16[2048,1024]{1,0:T(8,128)(2,1)S(1)} %slice.153), kind=kLoop, calls=%fused_computation.8 | loop fusion | flops 10470400 | bytes 10478080 | tf_op jit(solution)/shard_map/concatenate | solution.py:233
  107.2 2.7 %fusion.1 = bf16[2046,1280]{1,0:T(8,128)(2,1)} fusion(bf16[2048,256]{1,0:T(8,128)(2,1)S(1)} %convolution_convert_fusion.1, bf16[2048,1024]{1,0:T(8,128)(2,1)S(1)} %slice.153), kind=kLoop, calls=%fused_computation.9 | loop fusion | flops 10475520 | bytes 10480640 | tf_op jit(solution)/shard_map/concatenate | solution.py:233
  110.0 2.7 %fusion.2 = bf16[2047,1280]{1,0:T(8,128)(2,1)} fusion(bf16[2048,256]{1,0:T(8,128)(2,1)S(1)} %convolution_convert_fusion.1, bf16[2048,1024]{1,0:T(8,128)(2,1)S(1)} %slice.153), kind=kLoop, calls=%fused_computation.10 | loop fusion | flops 10480640 | bytes 10483200 | tf_op jit(solution)/shard_map/concatenate | solution.py:233
  116.6 3.1 %collective-permute-start.1 = (bf16[3,1280]{1,0:T(4,128)(2,1)}, bf16[3,1280]{1,0:T(4,128)(2,1)S(1)}, u32[]{:S(2)}, u32[]{:S(2)}) collective-permute-start(bf16[3,1280]{1,0:T(4,128)(2,1)} %fusion.23), channel_id=1, source_target_pairs={{0,2},{2,4},{4,6},{6,8},{8,10},{10,12},{12,14},{14,16},{16,18},{18... | collective-permute-start | bytes 23048 | tf_op jit(solution)/shard_map/ppermute | solution.py:17
  119.7 2.1 multiply_multiply_fusion.end_ref
  123.4 18.0 %multiply_convert_fusion.x_ref.b_ref.c_ref = bf16[2048,1280]{1,0:T(8,128)(2,1)S(1)} fusion(bf16[2048,256]{1,0:T(8,128)(2,1)S(1)} %convolution_convert_fusion.1, bf16[2045,1280]{1,0:T(8,128)(2,1)} %fusion, bf16[3,1280]{1,0:T(4,128)(2,1)S(1)} %collective-permute-done.1, bf16[2046,1280]{1,0:T(8,128)(2,1)} %fusion.1, bf16[2,1280]{1,0:T(2,128)(2,1)S(1)} %slice.166, ...), kind=kLoop, calls=%fused_computation.5 | loop fusion | flops 83886080 | bytes 26246144 | tf_op jit(solution)/shard_map/convert_element_type | solution.py:251
  141.4 2.4 copy-done.3
  144.9 14.8 %shard_map.136 = (f32[16,128,1024]{2,1,0:T(8,128)}, f32[128,1024]{1,0:T(8,128)}) custom-call(bf16[2048,1280]{1,0:T(8,128)(2,1)} %copy-done.3, bf16[16,128,128]{2,1,0:T(8,128)(2,1)} %bitcast.53, f32[16,128,16]{2,1,0:T(8,128)} %multiply_multiply_fusion.end_ref, f32[16,1,1024]{2,1,0:T(1,128)} %broadcast_in_dim_reshape.10.pass_ref), custom_call_target="tpu_custom_call" | custom-call | flops 536870912 | bytes 13107200 | tf_op jit(solution)/shard_map/pallas_call | solution.py:102
  162.9 8.5 %collective-permute-done.2 = bf16[131,1024]{1,0:T(8,128)(2,1)S(1)} collective-permute-done((bf16[131,1024]{1,0:T(8,128)(2,1)S(1)}, bf16[131,1024]{1,0:T(8,128)(2,1)S(1)}, u32[]{:S(2)}, u32[]{:S(2)}) %collective-permute-start.2) | collective-permute-done | bytes 268320 | tf_op jit(solution)/shard_map/ppermute | solution.py:17
  174.2 7.2 %collective-permute-done.3 = bf16[131,1024]{1,0:T(8,128)(2,1)S(1)} collective-permute-done((bf16[131,1024]{1,0:T(8,128)(2,1)S(1)}, bf16[131,1024]{1,0:T(8,128)(2,1)S(1)}, u32[]{:S(2)}, u32[]{:S(2)}) %collective-permute-start.3) | collective-permute-done | bytes 268320 | tf_op jit(solution)/shard_map/ppermute | solution.py:17
  184.1 5.4 %collective-permute-done.4 = bf16[131,1024]{1,0:T(8,128)(2,1)S(1)} collective-permute-done((bf16[131,1024]{1,0:T(8,128)(2,1)S(1)}, bf16[131,1024]{1,0:T(8,128)(2,1)S(1)}, u32[]{:S(2)}, u32[]{:S(2)}) %collective-permute-start.4) | collective-permute-done | bytes 268320 | tf_op jit(solution)/shard_map/ppermute | solution.py:17
  197.9 12.7 %collective-permute-done.6 = bf16[128,1024]{1,0:T(8,128)(2,1)S(1)} collective-permute-done((bf16[128,1024]{1,0:T(8,128)(2,1)S(1)}, bf16[128,1024]{1,0:T(8,128)(2,1)S(1)}, u32[]{:S(2)}, u32[]{:S(2)}) %collective-permute-start.6) | collective-permute-done | bytes 262176 | tf_op jit(solution)/shard_map/ppermute | solution.py:17
  211.6 21.5 %shard_map.137 = (f32[2048,1024]{1,0:T(8,128)}, f32[2048,1]{1,0:T(8,128)}) custom-call(bf16[2048,1280]{1,0:T(8,128)(2,1)} %copy-done.3, bf16[2048,1280]{1,0:T(8,128)(2,1)} %copy-done.3, bf16[2048,1280]{1,0:T(8,128)(2,1)} %copy-done.3, f32[16,128,16]{2,1,0:T(8,128)} %bitcast.48, f32[16,16,128]{2,1,0:T(8,128)} %copy-done.8, ...), custom_call_target="tpu_custom_call" | custom-call | flops 3288334336 | bytes 29360128 | tf_op jit(solution)/shard_map/pallas_call | solution.py:138
  233.0 7.4 %psum.7 = f32[2048,1]{1,0:T(8,128)S(1)} all-reduce(f32[2048,1]{1,0:T(8,128)} %get-tuple-element.16), channel_id=1, replica_groups=mesh['seq'=16,'head'=2] {'head'}, use_global_device_ids=true, to_apply=%region_3.4 | all-reduce | flops 2048 | bytes 16384 | tf_op jit(solution)/shard_map/psum | solution.py:300
  240.9 5.3 %multiply_convert_fusion.1 = bf16[2048,1024]{1,0:T(8,128)(2,1)} fusion(f32[2048,1024]{1,0:T(8,128)} %get-tuple-element.15, f32[1024]{0:T(1024)S(1)} %copy-done.18, f32[2048]{0:T(1024)S(1)} %rsqrt_reduce_fusion), kind=kLoop, calls=%fused_computation.6 | loop fusion | flops 6291456 | bytes 12595200 | tf_op jit(solution)/shard_map/convert_element_type | solution.py:301
  (143 shorter events, 37.9 us)
Async XLA Ops:
  12.0 53.2 %all-to-all-start = ((bf16[16,128,512]{2,1,0:T(8,128)(2,1)}), bf16[16,128,512]{2,1,0:T(8,128)(2,1)S(1)}, u32[]{:S(2)}, u32[]{:S(2)}) async-start(bf16[16,128,512]{2,1,0:T(8,128)(2,1)} %copy.66), calls=%async_computation | async-start | bytes 4194304 | tf_op jit(solution)/shard_map/all_to_all | solution.py:208
  18.4 66.8 %all-gather.2.cloned.1.call-start = ((), (), s32[]{:S(2)}) async-start(), calls=%async_computation.1 | async-start | bytes 6291456 | tf_op jit(solution)/shard_map/all_gather | solution.py:220
  65.2 8.4 %copy-start.17 = (f32[4,1024]{1,0:T(4,128)S(1)}, f32[4,1024]{1,0:T(4,128)}, u32[]{:S(2)}) copy-start(f32[4,1024]{1,0:T(4,128)} %param.22) | copy-start | bytes 49156
  65.2 8.4 %copy-start.19 = (f32[4,256]{1,0:T(4,128)S(1)}, f32[4,256]{1,0:T(4,128)}, u32[]{:S(2)}) copy-start(f32[4,256]{1,0:T(4,128)} %param.23) | copy-start | bytes 12292
  65.2 8.4 %copy-start.20 = (f32[1024]{0:T(1024)S(1)}, f32[1024]{0:T(1024)}, u32[]{:S(2)}) copy-start(f32[1024]{0:T(1024)} %param.24) | copy-start | bytes 12292
  65.2 8.4 %copy-start.22 = (f32[256]{0:T(256)S(1)}, f32[256]{0:T(256)}, u32[]{:S(2)}) copy-start(f32[256]{0:T(256)} %param.25) | copy-start | bytes 3076
  65.2 9.9 %copy-start.26 = (f32[16]{0:T(128)S(1)}, f32[16]{0:T(128)}, u32[]{:S(2)}) copy-start(f32[16]{0:T(128)} %param.21) | copy-start | bytes 196
  70.9 5.2 %collective-permute-start = (bf16[3]{0:T(256)(128)(2,1)S(1)}, bf16[3]{0:T(256)(128)(2,1)S(1)}, u32[]{:S(2)}, u32[]{:S(2)}) collective-permute-start(bf16[3]{0:T(256)(128)(2,1)S(1)} %fusion.41), channel_id=1, source_target_pairs={{0,2},{2,4},{4,6},{6,8},{8,10},{10,12},{12,14},{14,16},{16,18},{18... | collective-permute-start | bytes 26 | tf_op jit(solution)/shard_map/ppermute | solution.py:17
  102.4 7.5 %copy-start.2 = (bf16[2048,1024]{1,0:T(8,128)(2,1)}, bf16[2048,1024]{1,0:T(8,128)(2,1)S(1)}, u32[]{:S(2)}) copy-start(bf16[2048,1024]{1,0:T(8,128)(2,1)S(1)} %slice.153) | copy-start | bytes 12582916
  114.3 27.1 %copy-start.8 = (f32[16,16,128]{2,1,0:T(8,128)}, f32[16,16,128]{2,1,0:T(8,128)S(1)}, u32[]{:S(2)}) copy-start(f32[16,16,128]{2,1,0:T(8,128)S(1)} %fusion.19.cumt_ref) | copy-start | bytes 393220
  114.6 26.8 %copy-start.5 = (f32[16,16,128]{1,2,0:T(8,128)}, f32[16,16,128]{1,2,0:T(8,128)S(1)}, u32[]{:S(2)}) copy-start(f32[16,16,128]{1,2,0:T(8,128)S(1)} %copy.73) | copy-start | bytes 393220
  116.6 6.8 %collective-permute-start.1 = (bf16[3,1280]{1,0:T(4,128)(2,1)}, bf16[3,1280]{1,0:T(4,128)(2,1)S(1)}, u32[]{:S(2)}, u32[]{:S(2)}) collective-permute-start(bf16[3,1280]{1,0:T(4,128)(2,1)} %fusion.23), channel_id=1, source_target_pairs={{0,2},{2,4},{4,6},{6,8},{8,10},{10,12},{12,14},{14,16},{16,18},{18... | collective-permute-start | bytes 23048 | tf_op jit(solution)/shard_map/ppermute | solution.py:17
  143.8 19.0 %copy-start.10 = (f32[16,64]{1,0:T(8,128)S(1)}, f32[16,64]{1,0:T(8,128)}, u32[]{:S(2)}) copy-start(f32[16,64]{1,0:T(8,128)} %copy-done.9) | copy-start | bytes 12292
  143.9 27.6 %copy-start.11 = (f32[1,1024]{1,0:T(1,128)S(1)}, f32[1,1024]{1,0:T(1,128)}, u32[]{:S(2)}) copy-start(f32[1,1024]{1,0:T(1,128)} %reshape.224) | copy-start | bytes 12292
  159.7 21.8 %copy-start.7 = (f32[128,1024]{1,0:T(8,128)S(1)}, f32[128,1024]{1,0:T(8,128)}, u32[]{:S(2)}) copy-start(f32[128,1024]{1,0:T(8,128)} %get-tuple-element.14) | copy-start | bytes 1572868
  159.7 23.3 %copy-start.16 = (s32[16]{0:T(128)S(1)}, s32[16]{0:T(128)}, u32[]{:S(2)}) copy-start(s32[16]{0:T(128)} %param.16) | copy-start | bytes 196
  160.9 31.4 %copy-start.23 = (f32[16]{0:T(128)S(1)}, f32[16]{0:T(128)}, u32[]{:S(2)}) copy-start(f32[16]{0:T(128)} %param.26) | copy-start | bytes 196
  160.9 10.5 %collective-permute-start.2 = (bf16[131,1024]{1,0:T(8,128)(2,1)S(1)}, bf16[131,1024]{1,0:T(8,128)(2,1)S(1)}, u32[]{:S(2)}, u32[]{:S(2)}) collective-permute-start(bf16[131,1024]{1,0:T(8,128)(2,1)S(1)} %pad_maximum_fusion.1), channel_id=1, source_target_pairs={{0,2},{2,4},{4,6},{6,8},{8,10},{10,12},{12,14},{14,16},{16,18},{18... | collective-permute-start | bytes 804872 | tf_op jit(solution)/shard_map/ppermute | solution.py:17
  162.9 32.1 %copy-start.14 = (f32[16,16]{1,0:T(8,128)S(1)}, f32[16,16]{1,0:T(8,128)}, u32[]{:S(2)}) copy-start(f32[16,16]{1,0:T(8,128)} %copy-done.13) | copy-start | bytes 3076
  172.7 8.7 %collective-permute-start.3 = (bf16[131,1024]{1,0:T(8,128)(2,1)S(1)}, bf16[131,1024]{1,0:T(8,128)(2,1)S(1)}, u32[]{:S(2)}, u32[]{:S(2)}) collective-permute-start(bf16[131,1024]{1,0:T(8,128)(2,1)S(1)} %pad_maximum_fusion.2), channel_id=1, source_target_pairs={{0,4},{2,6},{4,8},{6,10},{8,12},{10,14},{12,16},{14,18},{16,20},{1... | collective-permute-start | bytes 804872 | tf_op jit(solution)/shard_map/ppermute | solution.py:17
  181.7 7.8 %collective-permute-start.4 = (bf16[131,1024]{1,0:T(8,128)(2,1)S(1)}, bf16[131,1024]{1,0:T(8,128)(2,1)S(1)}, u32[]{:S(2)}, u32[]{:S(2)}) collective-permute-start(bf16[131,1024]{1,0:T(8,128)(2,1)S(1)} %pad_maximum_fusion.3), channel_id=1, source_target_pairs={{0,8},{2,10},{4,12},{6,14},{8,16},{10,18},{12,20},{14,22},{16,24},... | collective-permute-start | bytes 804872 | tf_op jit(solution)/shard_map/ppermute | solution.py:17
  189.7 8.2 %collective-permute-start.5 = (bf16[131,1024]{1,0:T(8,128)(2,1)S(1)}, bf16[131,1024]{1,0:T(8,128)(2,1)S(1)}, u32[]{:S(2)}, u32[]{:S(2)}) collective-permute-start(bf16[131,1024]{1,0:T(8,128)(2,1)S(1)} %pad_maximum_fusion.4), channel_id=1, source_target_pairs={{0,2},{2,4},{4,6},{6,8},{8,10},{10,12},{12,14},{14,16},{16,18},{18... | collective-permute-start | bytes 804872 | tf_op jit(solution)/shard_map/ppermute | solution.py:17
  193.0 17.6 %collective-permute-start.6 = (bf16[128,1024]{1,0:T(8,128)(2,1)S(1)}, bf16[128,1024]{1,0:T(8,128)(2,1)S(1)}, u32[]{:S(2)}, u32[]{:S(2)}) collective-permute-start(bf16[128,1024]{1,0:T(8,128)(2,1)S(1)} %fusion.15), channel_id=1, source_target_pairs={{0,18},{2,20},{4,22},{6,24},{8,26},{10,28},{12,30},{1,19},{3,21},{... | collective-permute-start | bytes 786440 | tf_op jit(solution)/shard_map/ppermute | solution.py:17
  211.6 29.3 %copy-start.18 = (f32[1024]{0:T(1024)S(1)}, f32[1024]{0:T(1024)}, u32[]{:S(2)}) copy-start(f32[1024]{0:T(1024)} %param.27) | copy-start | bytes 12292
  (13 other events, 50.2 us)
Sparse Core Ops, SparseCore 0:
  69.3 15.8 all-gather.1

commit v15 on v13

--- a/solution.py
+++ b/solution.py
@@ -296,7 +296,7 @@
         conv_out, zx, cumul, cumul_t, dt_t, later, before_tile, widen(prefix)[:, None, :],
         entering, d_full,
     )
-    sums = lax.psum(row_sq, "head")
+    sums = lax.psum(row_sq.reshape(tiles_dev, tile_len), "head").reshape(row_count, 1)
     return (gated * lax.rsqrt(sums / INNER + EPSILON) * norm_gain[None, :]).astype(jnp.bfloat16)
 
 

time: 242 us -> 239 us (0.988)
  blocking collectives: 47.5 us -> 43.5 us
    psum x1, blocking collectives: 7.97 us -> 3.98 us  [shards(): lax.psum(row_sq.reshape(tiles_dev, tile_len), 'head').reshape(row_count, 1)]
where the time goes in v15:
time: 239 us; the launch traced here: 238 us
  waiting for transfers between devices  45.8 us (19%)
  blocking collectives  43.5 us (18%)
  Pallas kernels  36.3 us (15%)
  other arithmetic  30.9 us (13%)
  local copies, waits for them, and re-layouts  26.8 us (11%)
  starting transfers between devices  20.3 us (8%)
  matrix products  19.6 us (8%)
  between operations  14.6 us (6%)
    unnamed x1, blocking collectives  39.5 us
    ppermute x7, waiting for transfers between devices, shifted(): return lax.ppermute(x, axis, pairs)  36.5 us
    pallas_call x1, Pallas kernels, mix_tiles(): pl.pallas_call(mix_tile, grid=(tiles_dev,), in_specs=[pl.BlockSpec((tile_...  21.5 us
    dot_general x3, matrix products, shards(): jnp.dot(piece, weight, preferred_element_type=jnp.float32)  16.6 us
    unnamed x52, local copies, waits for them, and re-layouts  15.1 us
    pallas_call x1, Pallas kernels, contrib_tiles(): pl.pallas_call(contrib_tile, grid=(tiles_dev,), in_specs=[pl.BlockSpec((t...  14.8 us
    ppermute x7, starting transfers between devices, shifted(): return lax.ppermute(x, axis, pairs)  13.8 us
    convert_element_type x1, other arithmetic, shards(): conv_out = jax.nn.silu(total).astype(jnp.bfloat16)  10.8 us
  transfers between devices with their start and end apart: 9, of which 7 were waited for; matrix products, arithmetic and copies ran while one was open for 6% of the time, Pallas kernels for 0%

profile of v15, /device:TPU:29, one launch (start us, length us, event | category | flops | bytes accessed | tf_op | source)
XLA Modules:
  0.0 237.7 jit_solution(15282145081579324175)
XLA Ops:
  9.5 2.5 %copy.66 = bf16[16,128,512]{2,1,0:T(8,128)(2,1)} copy(bf16[16,128,512]{2,0,1:T(8,128)(2,1)S(1)} %fusion.4) | data formatting | bytes 4194304 | tf_op jit(solution)/shard_map/convert_element_type | solution.py:207
  12.0 6.4 %all-to-all-start = ((bf16[16,128,512]{2,1,0:T(8,128)(2,1)}), bf16[16,128,512]{2,1,0:T(8,128)(2,1)S(1)}, u32[]{:S(2)}, u32[]{:S(2)}) async-start(bf16[16,128,512]{2,1,0:T(8,128)(2,1)} %copy.66), calls=%async_computation | async-start | bytes 4194304 | tf_op jit(solution)/shard_map/all_to_all | solution.py:208
  18.5 5.6 %copy.80 = bf16[128,8,2,1024]{3,1,2,0:T(8,128)(2,1)} copy(bf16[128,8,2,1024]{3,2,1,0:T(2,128)(2,1)} %bitcast.53) | data formatting | bytes 8388608
  25.5 39.5 %all-reduce.1 = s32[256]{0:T(256)S(1)} all-reduce(s32[256]{0:T(256)S(1)} %dynamic-update-slice), channel_id=1, replica_groups=mesh['seq'=16,'head'=2] {'seq'}, use_global_device_ids=true, to_apply=%add.1 | all-reduce | flops 256 | bytes 2048
  66.6 2.5 %copy.68 = bf16[16,128,512]{2,1,0:T(8,128)(2,1)} copy(bf16[16,128,512]{2,0,1:T(8,128)(2,1)S(1)} %fusion.7) | data formatting | bytes 4194304 | tf_op jit(solution)/shard_map/convert_element_type | solution.py:215
  70.7 2.6 %collective-permute-start = (bf16[3]{0:T(256)(128)(2,1)S(1)}, bf16[3]{0:T(256)(128)(2,1)S(1)}, u32[]{:S(2)}, u32[]{:S(2)}) collective-permute-start(bf16[3]{0:T(256)(128)(2,1)S(1)} %fusion.38), channel_id=1, source_target_pairs={{0,2},{2,4},{4,6},{6,8},{8,10},{10,12},{12,14},{14,16},{16,18},{18... | collective-permute-start | bytes 26 | tf_op jit(solution)/shard_map/ppermute | solution.py:17
  73.8 2.0 collective-permute-done
  75.9 9.2 %all-gather.2.cloned.1.call-done = bf16[2048,1024]{1,0:T(8,128)(2,1)} async-done(((bf16[2048,512]{1,0:T(8,128)(2,1)}), bf16[2048,1024]{1,0:T(8,128)(2,1)}) %all-gather.2.cloned.1.call-update) | async-done | bytes 4194320 | tf_op jit(solution)/shard_map/all_gather | solution.py:220
  85.2 3.4 %compare_select_fusion = f32[2048,16]{0,1:T(8,128)S(1)} fusion(bf16[2048,1024]{1,0:T(8,128)(2,1)} %all-gather.2.cloned.1.call-done, bf16[1024,16]{0,1:T(8,128)(2,1)S(1)} %copy-done.10, f32[16]{0:T(128)S(1)} %copy-done.16), kind=kOutput, calls=%fused_computation.26 | convolution fusion | flops 67338240 | bytes 4358208 | tf_op jit(solution)/shard_map/dot_general | solution.py:222
  89.9 11.9 %convolution_convert_fusion.gate_ref = bf16[2048,2048]{1,0:T(8,128)(2,1)S(1)} fusion(bf16[2048,1024]{1,0:T(8,128)(2,1)} %all-gather.2.cloned.1.call-done, bf16[1024,2048]{1,0:T(8,128)(2,1)} %bitcast.54), kind=kOutput, calls=%fused_computation.2 | convolution fusion | flops 8594128896 | bytes 16777216 | tf_op jit(solution)/shard_map/dot_general | solution.py:222
  102.6 4.5 %copy-done.7 = bf16[2048,1024]{1,0:T(8,128)(2,1)S(1)} copy-done((bf16[2048,1024]{1,0:T(8,128)(2,1)S(1)}, bf16[2048,1024]{1,0:T(8,128)(2,1)}, u32[]{:S(2)}) %copy-start.7) | copy-done | bytes 4194328
  109.2 3.1 %collective-permute-start.1 = (bf16[3,1280]{1,0:T(4,128)(2,1)S(1)}, bf16[3,1280]{1,0:T(4,128)(2,1)S(1)}, u32[]{:S(2)}, u32[]{:S(2)}) collective-permute-start(bf16[3,1280]{1,0:T(4,128)(2,1)S(1)} %fusion.20), channel_id=1, source_target_pairs={{0,2},{2,4},{4,6},{6,8},{8,10},{10,12},{12,14},{14,16},{16,18},{18... | collective-permute-start | bytes 23048 | tf_op jit(solution)/shard_map/ppermute | solution.py:17
  114.6 4.0 %maximum_maximum_fusion = bf16[2051,1280]{1,0:T(8,128)(2,1)S(1)} fusion(bf16[2048,256]{1,0:T(8,128)(2,1)S(1)} %convolution_convert_fusion.1, bf16[2048,1024]{1,0:T(8,128)(2,1)} %copy-done.3, bf16[3,1280]{1,0:T(4,128)(2,1)S(1)} %collective-permute-done.1), kind=kLoop, calls=%fused_computation.5 | loop fusion | flops 15751680 | bytes 10501120 | tf_op jit(solution)/shard_map/concatenate | solution.py:237
  118.6 10.8 %multiply_convert_fusion.x_ref.b_ref.c_ref = bf16[2048,1280]{1,0:T(8,128)(2,1)S(1)} fusion(bf16[2048,256]{1,0:T(8,128)(2,1)S(1)} %convolution_convert_fusion.1, bf16[2051,1280]{1,0:T(8,128)(2,1)S(1)} %maximum_maximum_fusion, f32[1280]{0:T(1024)S(1)} %get-tuple-element.18, f32[1280]{0:T(1024)S(1)} %get-tuple-element.19, f32[1280]{0:T(1024)S(1)} %get-tuple-element.20, ...), kind=kLoop, calls=%fused_computation | loop fusion | flops 60293120 | bytes 26246144 | tf_op jit(solution)/shard_map/convert_element_type | solution.py:250
  129.4 2.4 %copy-done.2 = bf16[2048,1280]{1,0:T(8,128)(2,1)} copy-done((bf16[2048,1280]{1,0:T(8,128)(2,1)}, bf16[2048,1280]{1,0:T(8,128)(2,1)S(1)}, u32[]{:S(2)}) %copy-start.2) | copy-done | bytes 5242904
  132.9 14.8 %shard_map.136 = (f32[16,128,1024]{2,1,0:T(8,128)}, f32[128,1024]{1,0:T(8,128)}) custom-call(bf16[2048,1280]{1,0:T(8,128)(2,1)} %copy-done.2, bf16[16,128,128]{2,1,0:T(8,128)(2,1)} %bitcast.56, f32[16,128,16]{2,1,0:T(8,128)} %multiply_multiply_fusion.end_ref, f32[16,1,1024]{2,1,0:T(1,128)} %broadcast_in_dim_reshape.10.pass_ref), custom_call_target="tpu_custom_call" | custom-call | flops 536870912 | bytes 13107200 | tf_op jit(solution)/shard_map/pallas_call | solution.py:102
  148.9 2.3 collective-permute-start.2
  151.3 7.0 %collective-permute-done.2 = bf16[131,1024]{1,0:T(8,128)(2,1)S(1)} collective-permute-done((bf16[131,1024]{1,0:T(8,128)(2,1)S(1)}, bf16[131,1024]{1,0:T(8,128)(2,1)S(1)}, u32[]{:S(2)}, u32[]{:S(2)}) %collective-permute-start.2) | collective-permute-done | bytes 268320 | tf_op jit(solution)/shard_map/ppermute | solution.py:17
  160.9 8.4 %collective-permute-done.3 = bf16[131,1024]{1,0:T(8,128)(2,1)S(1)} collective-permute-done((bf16[131,1024]{1,0:T(8,128)(2,1)S(1)}, bf16[131,1024]{1,0:T(8,128)(2,1)S(1)}, u32[]{:S(2)}, u32[]{:S(2)}) %collective-permute-start.3) | collective-permute-done | bytes 268320 | tf_op jit(solution)/shard_map/ppermute | solution.py:17
  172.0 4.9 %collective-permute-done.4 = bf16[131,1024]{1,0:T(8,128)(2,1)S(1)} collective-permute-done((bf16[131,1024]{1,0:T(8,128)(2,1)S(1)}, bf16[131,1024]{1,0:T(8,128)(2,1)S(1)}, u32[]{:S(2)}, u32[]{:S(2)}) %collective-permute-start.4) | collective-permute-done | bytes 268320 | tf_op jit(solution)/shard_map/ppermute | solution.py:17
  185.3 12.2 %collective-permute-done.6 = bf16[128,1024]{1,0:T(8,128)(2,1)S(1)} collective-permute-done((bf16[128,1024]{1,0:T(8,128)(2,1)S(1)}, bf16[128,1024]{1,0:T(8,128)(2,1)S(1)}, u32[]{:S(2)}, u32[]{:S(2)}) %collective-permute-start.6) | collective-permute-done | bytes 262176 | tf_op jit(solution)/shard_map/ppermute | solution.py:17
  198.4 21.5 %shard_map.137 = (f32[2048,1024]{1,0:T(8,128)}, f32[2048,1]{1,0:T(8,128)}) custom-call(bf16[2048,1280]{1,0:T(8,128)(2,1)} %copy-done.2, bf16[2048,1280]{1,0:T(8,128)(2,1)} %copy-done.2, bf16[2048,1280]{1,0:T(8,128)(2,1)} %copy-done.2, f32[16,128,16]{2,1,0:T(8,128)} %bitcast.51, f32[16,16,128]{2,1,0:T(8,128)} %copy-done.9, ...), custom_call_target="tpu_custom_call" | custom-call | flops 3288334336 | bytes 29360128 | tf_op jit(solution)/shard_map/pallas_call | solution.py:138
  221.5 4.0 %psum.7 = f32[16,128]{1,0:T(8,128)S(1)} all-reduce(f32[16,128]{1,0:T(8,128)S(1)} %bitcast.63), channel_id=1, replica_groups=mesh['seq'=16,'head'=2] {'head'}, use_global_device_ids=true, to_apply=%region_3.4 | all-reduce | flops 2048 | bytes 16384 | tf_op jit(solution)/shard_map/psum | solution.py:299
  225.5 5.3 %multiply_convert_fusion.1 = bf16[2048,1024]{1,0:T(8,128)(2,1)} fusion(f32[2048,1024]{1,0:T(8,128)} %get-tuple-element.15, f32[1024]{0:T(1024)S(1)} %copy-done.13, f32[2048]{0:T(1024)S(1)} %rsqrt_bitcast_fusion), kind=kLoop, calls=%fused_computation.1 | loop fusion | flops 6291456 | bytes 12595200 | tf_op jit(solution)/shard_map/convert_element_type | solution.py:300
  (130 shorter events, 32.0 us)
Async XLA Ops:
  12.0 53.3 %all-to-all-start = ((bf16[16,128,512]{2,1,0:T(8,128)(2,1)}), bf16[16,128,512]{2,1,0:T(8,128)(2,1)S(1)}, u32[]{:S(2)}, u32[]{:S(2)}) async-start(bf16[16,128,512]{2,1,0:T(8,128)(2,1)} %copy.66), calls=%async_computation | async-start | bytes 4194304 | tf_op jit(solution)/shard_map/all_to_all | solution.py:208
  18.4 5.7 %copy-start.22 = (u32[32]{0:T(128)S(1)}, u32[32]{0:T(128)}, u32[]{:S(2)}) copy-start(u32[32]{0:T(128)} %constant.74) | copy-start | bytes 388
  18.4 6.8 %copy-start.20 = (s32[16]{0:T(128)S(1)}, s32[16]{0:T(128)}, u32[]{:S(2)}) copy-start(s32[16]{0:T(128)} %param.15) | copy-start | bytes 196
  18.4 66.7 %all-gather.2.cloned.1.call-start = ((), (), s32[]{:S(2)}) async-start(), calls=%async_computation.1 | async-start | bytes 6291456 | tf_op jit(solution)/shard_map/all_gather | solution.py:220
  65.2 8.1 %copy-start.12 = (f32[4,1024]{1,0:T(4,128)S(1)}, f32[4,1024]{1,0:T(4,128)}, u32[]{:S(2)}) copy-start(f32[4,1024]{1,0:T(4,128)} %param.22) | copy-start | bytes 49156
  65.2 8.1 %copy-start.14 = (f32[4,256]{1,0:T(4,128)S(1)}, f32[4,256]{1,0:T(4,128)}, u32[]{:S(2)}) copy-start(f32[4,256]{1,0:T(4,128)} %param.23) | copy-start | bytes 12292
  65.2 8.1 %copy-start.15 = (f32[1024]{0:T(1024)S(1)}, f32[1024]{0:T(1024)}, u32[]{:S(2)}) copy-start(f32[1024]{0:T(1024)} %param.24) | copy-start | bytes 12292
  65.2 8.1 %copy-start.17 = (f32[256]{0:T(256)S(1)}, f32[256]{0:T(256)}, u32[]{:S(2)}) copy-start(f32[256]{0:T(256)} %param.25) | copy-start | bytes 3076
  65.2 8.5 %copy-start.21 = (f32[16]{0:T(128)S(1)}, f32[16]{0:T(128)}, u32[]{:S(2)}) copy-start(f32[16]{0:T(128)} %param.21) | copy-start | bytes 196
  65.2 19.9 %copy-start.10 = (bf16[1024,16]{0,1:T(8,128)(2,1)S(1)}, bf16[1024,16]{0,1:T(8,128)(2,1)}, u32[]{:S(2)}) copy-start(bf16[1024,16]{0,1:T(8,128)(2,1)} %param.19) | copy-start | bytes 98308
  65.2 19.9 %copy-start.16 = (f32[16]{0:T(128)S(1)}, f32[16]{0:T(128)}, u32[]{:S(2)}) copy-start(f32[16]{0:T(128)} %param.20) | copy-start | bytes 196
  70.7 5.2 %collective-permute-start = (bf16[3]{0:T(256)(128)(2,1)S(1)}, bf16[3]{0:T(256)(128)(2,1)S(1)}, u32[]{:S(2)}, u32[]{:S(2)}) collective-permute-start(bf16[3]{0:T(256)(128)(2,1)S(1)} %fusion.38), channel_id=1, source_target_pairs={{0,2},{2,4},{4,6},{6,8},{8,10},{10,12},{12,14},{14,16},{16,18},{18... | collective-permute-start | bytes 26 | tf_op jit(solution)/shard_map/ppermute | solution.py:17
  88.9 12.9 %copy-start.9 = (f32[16,16,128]{2,1,0:T(8,128)}, f32[16,16,128]{2,1,0:T(8,128)S(1)}, u32[]{:S(2)}) copy-start(f32[16,16,128]{2,1,0:T(8,128)S(1)} %fusion.16.cumt_ref) | copy-start | bytes 393220
  89.3 23.1 %copy-start.6 = (f32[16,16,128]{1,2,0:T(8,128)}, f32[16,16,128]{1,2,0:T(8,128)S(1)}, u32[]{:S(2)}) copy-start(f32[16,16,128]{1,2,0:T(8,128)S(1)} %copy.73) | copy-start | bytes 393220
  101.9 6.6 %copy-start.5 = (bf16[2048,2048]{1,0:T(8,128)(2,1)}, bf16[2048,2048]{1,0:T(8,128)(2,1)S(1)}, u32[]{:S(2)}) copy-start(bf16[2048,2048]{1,0:T(8,128)(2,1)S(1)} %convolution_convert_fusion.gate_ref) | copy-start | bytes 25165828
  109.2 5.3 %collective-permute-start.1 = (bf16[3,1280]{1,0:T(4,128)(2,1)S(1)}, bf16[3,1280]{1,0:T(4,128)(2,1)S(1)}, u32[]{:S(2)}, u32[]{:S(2)}) collective-permute-start(bf16[3,1280]{1,0:T(4,128)(2,1)S(1)} %fusion.20), channel_id=1, source_target_pairs={{0,2},{2,4},{4,6},{6,8},{8,10},{10,12},{12,14},{14,16},{16,18},{18... | collective-permute-start | bytes 23048 | tf_op jit(solution)/shard_map/ppermute | solution.py:17
  147.7 21.6 %copy-start.8 = (f32[128,1024]{1,0:T(8,128)S(1)}, f32[128,1024]{1,0:T(8,128)}, u32[]{:S(2)}) copy-start(f32[128,1024]{1,0:T(8,128)} %get-tuple-element.14) | copy-start | bytes 1572868
  148.9 30.8 %copy-start.18 = (f32[16]{0:T(128)S(1)}, f32[16]{0:T(128)}, u32[]{:S(2)}) copy-start(f32[16]{0:T(128)} %param.26) | copy-start | bytes 196
  148.9 9.4 %collective-permute-start.2 = (bf16[131,1024]{1,0:T(8,128)(2,1)S(1)}, bf16[131,1024]{1,0:T(8,128)(2,1)S(1)}, u32[]{:S(2)}, u32[]{:S(2)}) collective-permute-start(bf16[131,1024]{1,0:T(8,128)(2,1)S(1)} %pad_maximum_fusion.1), channel_id=1, source_target_pairs={{0,2},{2,4},{4,6},{6,8},{8,10},{10,12},{12,14},{14,16},{16,18},{18... | collective-permute-start | bytes 804872 | tf_op jit(solution)/shard_map/ppermute | solution.py:17
  159.6 9.7 %collective-permute-start.3 = (bf16[131,1024]{1,0:T(8,128)(2,1)S(1)}, bf16[131,1024]{1,0:T(8,128)(2,1)S(1)}, u32[]{:S(2)}, u32[]{:S(2)}) collective-permute-start(bf16[131,1024]{1,0:T(8,128)(2,1)S(1)} %pad_maximum_fusion.2), channel_id=1, source_target_pairs={{0,4},{2,6},{4,8},{6,10},{8,12},{10,14},{12,16},{14,18},{16,20},{1... | collective-permute-start | bytes 804872 | tf_op jit(solution)/shard_map/ppermute | solution.py:17
  169.5 7.3 %collective-permute-start.4 = (bf16[131,1024]{1,0:T(8,128)(2,1)S(1)}, bf16[131,1024]{1,0:T(8,128)(2,1)S(1)}, u32[]{:S(2)}, u32[]{:S(2)}) collective-permute-start(bf16[131,1024]{1,0:T(8,128)(2,1)S(1)} %pad_maximum_fusion.3), channel_id=1, source_target_pairs={{0,8},{2,10},{4,12},{6,14},{8,16},{10,18},{12,20},{14,22},{16,24},... | collective-permute-start | bytes 804872 | tf_op jit(solution)/shard_map/ppermute | solution.py:17
  177.0 8.2 %collective-permute-start.5 = (bf16[131,1024]{1,0:T(8,128)(2,1)S(1)}, bf16[131,1024]{1,0:T(8,128)(2,1)S(1)}, u32[]{:S(2)}, u32[]{:S(2)}) collective-permute-start(bf16[131,1024]{1,0:T(8,128)(2,1)S(1)} %pad_maximum_fusion.4), channel_id=1, source_target_pairs={{0,2},{2,4},{4,6},{6,8},{8,10},{10,12},{12,14},{14,16},{16,18},{18... | collective-permute-start | bytes 804872 | tf_op jit(solution)/shard_map/ppermute | solution.py:17
  180.4 17.1 %collective-permute-start.6 = (bf16[128,1024]{1,0:T(8,128)(2,1)S(1)}, bf16[128,1024]{1,0:T(8,128)(2,1)S(1)}, u32[]{:S(2)}, u32[]{:S(2)}) collective-permute-start(bf16[128,1024]{1,0:T(8,128)(2,1)S(1)} %fusion.12), channel_id=1, source_target_pairs={{0,18},{2,20},{4,22},{6,24},{8,26},{10,28},{12,30},{1,19},{3,21},{... | collective-permute-start | bytes 786440 | tf_op jit(solution)/shard_map/ppermute | solution.py:17
  198.4 27.1 %copy-start.13 = (f32[1024]{0:T(1024)S(1)}, f32[1024]{0:T(1024)}, u32[]{:S(2)}) copy-start(f32[1024]{0:T(1024)} %param.27) | copy-start | bytes 12292
  (8 other events, 29.9 us)
Sparse Core Ops, SparseCore 0:
  69.3 15.8 all-gather.1

commit v16 on v15

--- a/solution.py
+++ b/solution.py
@@ -233,7 +233,8 @@
     conv_in = jnp.concatenate([x_in, bc_all], 1)
     tail = conv_in[row_count - keep_rows :]
     tail_seg = (segment[row_count - keep_rows :] - segment[row_count - 1]).astype(jnp.bfloat16)
-    got_tail, got_seg = shifted((tail, tail_seg), "seq", 1)
+    got_both = shifted(jnp.concatenate([tail, tail_seg[:, None]], 1), "seq", 1)
+    got_tail, got_seg = got_both[:, : tail.shape[1]], got_both[:, tail.shape[1]]
     extended = jnp.concatenate([got_tail, conv_in], 0)
     ext_seg = jnp.concatenate([got_seg.astype(jnp.float32), segment], 0)
     conv_weight = jnp.concatenate([conv_x, conv_bc], 1)

time: 239 us -> 239 us (level)
    all_gather x1, waiting for transfers between devices: 9.23 us -> 13.7 us  [shards(): piece = lax.all_gather(own_rows, 'head', axis=1, tiled=True)]
    ppermute x7 -> x6, waiting for transfers between devices: 36.5 us -> 33.9 us  [shifted(): return lax.ppermute(x, axis, pairs)]
    ppermute x7 -> x6, starting transfers between devices: 13.8 us -> 12 us  [shifted(): return lax.ppermute(x, axis, pairs)]
  transfers between devices with their start and end apart: 9 -> 8, of which waited for: 7 -> 6; matrix products, arithmetic and copies ran while one was open for 6% -> 6% of each run, Pallas kernels for 0% -> 0%
where the time goes in v16:
time: 239 us; the launch traced here: 238 us
  waiting for transfers between devices  47.7 us (20%)
  blocking collectives  43.1 us (18%)
  Pallas kernels  36.3 us (15%)
  other arithmetic  31.1 us (13%)
  local copies, waits for them, and re-layouts  27.1 us (11%)
  matrix products  19.6 us (8%)
  starting transfers between devices  18.4 us (8%)
  between operations  14.7 us (6%)
    unnamed x1, blocking collectives  39.3 us
    ppermute x6, waiting for transfers between devices, shifted(): return lax.ppermute(x, axis, pairs)  33.9 us
    pallas_call x1, Pallas kernels, mix_tiles(): pl.pallas_call(mix_tile, grid=(tiles_dev,), in_specs=[pl.BlockSpec((tile_...  21.5 us
    dot_general x3, matrix products, shards(): jnp.dot(piece, weight, preferred_element_type=jnp.float32)  16.6 us
    unnamed x52, local copies, waits for them, and re-layouts  15.2 us
    pallas_call x1, Pallas kernels, contrib_tiles(): pl.pallas_call(contrib_tile, grid=(tiles_dev,), in_specs=[pl.BlockSpec((t...  14.8 us
    all_gather x1, waiting for transfers between devices, shards(): piece = lax.all_gather(own_rows, 'head', axis=1, tiled=True)  13.7 us
    ppermute x6, starting transfers between devices, shifted(): return lax.ppermute(x, axis, pairs)  12 us
  transfers between devices with their start and end apart: 8, of which 6 were waited for; matrix products, arithmetic and copies ran while one was open for 6% of the time, Pallas kernels for 0%

profile of v16, /device:TPU:29, one launch (start us, length us, event | category | flops | bytes accessed | tf_op | source)
XLA Modules:
  0.0 237.9 jit_solution(7857741201703028783)
XLA Ops:
  9.5 2.5 %copy.71 = bf16[16,128,512]{2,1,0:T(8,128)(2,1)} copy(bf16[16,128,512]{2,0,1:T(8,128)(2,1)S(1)} %fusion.4) | data formatting | bytes 4194304 | tf_op jit(solution)/shard_map/convert_element_type | solution.py:207
  12.0 6.4 %all-to-all-start = ((bf16[16,128,512]{2,1,0:T(8,128)(2,1)}), bf16[16,128,512]{2,1,0:T(8,128)(2,1)S(1)}, u32[]{:S(2)}, u32[]{:S(2)}) async-start(bf16[16,128,512]{2,1,0:T(8,128)(2,1)} %copy.71), calls=%async_computation | async-start | bytes 4194304 | tf_op jit(solution)/shard_map/all_to_all | solution.py:208
  18.5 5.6 %copy.86 = bf16[128,8,2,1024]{3,1,2,0:T(8,128)(2,1)} copy(bf16[128,8,2,1024]{3,2,1,0:T(2,128)(2,1)} %bitcast.55) | data formatting | bytes 8388608
  25.7 39.3 %all-reduce.1 = s32[256]{0:T(256)S(1)} all-reduce(s32[256]{0:T(256)S(1)} %dynamic-update-slice), channel_id=1, replica_groups=mesh['seq'=16,'head'=2] {'seq'}, use_global_device_ids=true, to_apply=%add.1 | all-reduce | flops 256 | bytes 2048
  66.6 2.5 %copy.73 = bf16[16,128,512]{2,1,0:T(8,128)(2,1)} copy(bf16[16,128,512]{2,0,1:T(8,128)(2,1)S(1)} %fusion.7) | data formatting | bytes 4194304 | tf_op jit(solution)/shard_map/convert_element_type | solution.py:215
  71.5 13.7 %all-gather.2.cloned.1.call-done = bf16[2048,1024]{1,0:T(8,128)(2,1)} async-done(((bf16[2048,512]{1,0:T(8,128)(2,1)}), bf16[2048,1024]{1,0:T(8,128)(2,1)}) %all-gather.2.cloned.1.call-update) | async-done | bytes 4194320 | tf_op jit(solution)/shard_map/all_gather | solution.py:220
  85.2 3.4 %compare_select_fusion = f32[2048,16]{0,1:T(8,128)S(1)} fusion(bf16[2048,1024]{1,0:T(8,128)(2,1)} %all-gather.2.cloned.1.call-done, bf16[1024,16]{0,1:T(8,128)(2,1)S(1)} %copy-done.10, f32[16]{0:T(128)S(1)} %copy-done.16), kind=kOutput, calls=%fused_computation.26 | convolution fusion | flops 67338240 | bytes 4358208 | tf_op jit(solution)/shard_map/dot_general | solution.py:222
  90.0 11.9 %convolution_convert_fusion.gate_ref = bf16[2048,2048]{1,0:T(8,128)(2,1)S(1)} fusion(bf16[2048,1024]{1,0:T(8,128)(2,1)} %all-gather.2.cloned.1.call-done, bf16[1024,2048]{1,0:T(8,128)(2,1)} %bitcast.56), kind=kOutput, calls=%fused_computation.2 | convolution fusion | flops 8594128896 | bytes 16777216 | tf_op jit(solution)/shard_map/dot_general | solution.py:222
  102.6 4.5 %copy-done.7 = bf16[2048,1024]{1,0:T(8,128)(2,1)S(1)} copy-done((bf16[2048,1024]{1,0:T(8,128)(2,1)S(1)}, bf16[2048,1024]{1,0:T(8,128)(2,1)}, u32[]{:S(2)}) %copy-start.7) | copy-done | bytes 4194328
  109.3 3.3 %collective-permute-start = (bf16[3,1281]{1,0:T(4,128)(2,1)S(1)}, bf16[3,1281]{1,0:T(4,128)(2,1)S(1)}, u32[]{:S(2)}, u32[]{:S(2)}) collective-permute-start(bf16[3,1281]{1,0:T(4,128)(2,1)S(1)} %pad_maximum_fusion.5), channel_id=1, source_target_pairs={{0,2},{2,4},{4,6},{6,8},{8,10},{10,12},{12,14},{14,16},{16,18},{18... | collective-permute-start | bytes 23066 | tf_op jit(solution)/shard_map/ppermute | solution.py:17
  115.0 4.0 %maximum_maximum_fusion = bf16[2051,1280]{1,0:T(8,128)(2,1)S(1)} fusion(bf16[2048,256]{1,0:T(8,128)(2,1)S(1)} %convolution_convert_fusion.1, bf16[2048,1024]{1,0:T(8,128)(2,1)} %copy-done.3, bf16[3,1280]{1,0:T(4,128)(2,1)S(1)} %slice.162), kind=kLoop, calls=%fused_computation.5 | loop fusion | flops 15751680 | bytes 10501120 | tf_op jit(solution)/shard_map/concatenate | solution.py:238
  119.0 10.9 %multiply_convert_fusion.x_ref.b_ref.c_ref = bf16[2048,1280]{1,0:T(8,128)(2,1)S(1)} fusion(bf16[2048,256]{1,0:T(8,128)(2,1)S(1)} %convolution_convert_fusion.1, bf16[2051,1280]{1,0:T(8,128)(2,1)S(1)} %maximum_maximum_fusion, f32[1280]{0:T(1024)S(1)} %get-tuple-element.18, f32[1280]{0:T(1024)S(1)} %get-tuple-element.19, f32[1280]{0:T(1024)S(1)} %get-tuple-element.20, ...), kind=kLoop, calls=%fused_computation | loop fusion | flops 60293120 | bytes 26246144 | tf_op jit(solution)/shard_map/convert_element_type | solution.py:251
  129.9 2.4 copy-done.2
  133.4 14.8 %shard_map.136 = (f32[16,128,1024]{2,1,0:T(8,128)}, f32[128,1024]{1,0:T(8,128)}) custom-call(bf16[2048,1280]{1,0:T(8,128)(2,1)} %copy-done.2, bf16[16,128,128]{2,1,0:T(8,128)(2,1)} %bitcast.58, f32[16,128,16]{2,1,0:T(8,128)} %multiply_multiply_fusion.end_ref, f32[16,1,1024]{2,1,0:T(1,128)} %broadcast_in_dim_reshape.10.pass_ref), custom_call_target="tpu_custom_call" | custom-call | flops 536870912 | bytes 13107200 | tf_op jit(solution)/shard_map/pallas_call | solution.py:102
  149.4 2.0 collective-permute-start.1
  151.5 7.7 %collective-permute-done.1 = bf16[131,1024]{1,0:T(8,128)(2,1)S(1)} collective-permute-done((bf16[131,1024]{1,0:T(8,128)(2,1)S(1)}, bf16[131,1024]{1,0:T(8,128)(2,1)S(1)}, u32[]{:S(2)}, u32[]{:S(2)}) %collective-permute-start.1) | collective-permute-done | bytes 268320 | tf_op jit(solution)/shard_map/ppermute | solution.py:17
  161.7 7.0 %collective-permute-done.2 = bf16[131,1024]{1,0:T(8,128)(2,1)S(1)} collective-permute-done((bf16[131,1024]{1,0:T(8,128)(2,1)S(1)}, bf16[131,1024]{1,0:T(8,128)(2,1)S(1)}, u32[]{:S(2)}, u32[]{:S(2)}) %collective-permute-start.2) | collective-permute-done | bytes 268320 | tf_op jit(solution)/shard_map/ppermute | solution.py:17
  171.4 4.9 %collective-permute-done.3 = bf16[131,1024]{1,0:T(8,128)(2,1)S(1)} collective-permute-done((bf16[131,1024]{1,0:T(8,128)(2,1)S(1)}, bf16[131,1024]{1,0:T(8,128)(2,1)S(1)}, u32[]{:S(2)}, u32[]{:S(2)}) %collective-permute-start.3) | collective-permute-done | bytes 268320 | tf_op jit(solution)/shard_map/ppermute | solution.py:17
  176.5 2.8 %collective-permute-start.4 = (bf16[131,1024]{1,0:T(8,128)(2,1)S(1)}, bf16[131,1024]{1,0:T(8,128)(2,1)S(1)}, u32[]{:S(2)}, u32[]{:S(2)}) collective-permute-start(bf16[131,1024]{1,0:T(8,128)(2,1)S(1)} %pad_maximum_fusion.4), channel_id=1, source_target_pairs={{0,2},{2,4},{4,6},{6,8},{8,10},{10,12},{12,14},{14,16},{16,18},{18... | collective-permute-start | bytes 804872 | tf_op jit(solution)/shard_map/ppermute | solution.py:17
  184.8 13.2 %collective-permute-done.5 = bf16[128,1024]{1,0:T(8,128)(2,1)S(1)} collective-permute-done((bf16[128,1024]{1,0:T(8,128)(2,1)S(1)}, bf16[128,1024]{1,0:T(8,128)(2,1)S(1)}, u32[]{:S(2)}, u32[]{:S(2)}) %collective-permute-start.5) | collective-permute-done | bytes 262176 | tf_op jit(solution)/shard_map/ppermute | solution.py:17
  198.9 21.5 %shard_map.137 = (f32[2048,1024]{1,0:T(8,128)}, f32[2048,1]{1,0:T(8,128)}) custom-call(bf16[2048,1280]{1,0:T(8,128)(2,1)} %copy-done.2, bf16[2048,1280]{1,0:T(8,128)(2,1)} %copy-done.2, bf16[2048,1280]{1,0:T(8,128)(2,1)} %copy-done.2, f32[16,128,16]{2,1,0:T(8,128)} %bitcast.53, f32[16,16,128]{2,1,0:T(8,128)} %copy-done.9, ...), custom_call_target="tpu_custom_call" | custom-call | flops 3288334336 | bytes 29360128 | tf_op jit(solution)/shard_map/pallas_call | solution.py:138
  220.4 1.6 reduce.7
  221.9 3.8 %psum.7 = f32[16,128]{1,0:T(8,128)S(1)} all-reduce(f32[16,128]{1,0:T(8,128)S(1)} %bitcast.65), channel_id=1, replica_groups=mesh['seq'=16,'head'=2] {'head'}, use_global_device_ids=true, to_apply=%region_3.4 | all-reduce | flops 2048 | bytes 16384 | tf_op jit(solution)/shard_map/psum | solution.py:300
  225.7 5.3 %multiply_convert_fusion.1 = bf16[2048,1024]{1,0:T(8,128)(2,1)} fusion(f32[2048,1024]{1,0:T(8,128)} %get-tuple-element.15, f32[1024]{0:T(1024)S(1)} %copy-done.13, f32[2048]{0:T(1024)S(1)} %rsqrt_bitcast_fusion), kind=kLoop, calls=%fused_computation.1 | loop fusion | flops 6291456 | bytes 12595200 | tf_op jit(solution)/shard_map/convert_element_type | solution.py:301
  (131 shorter events, 28.2 us)
Async XLA Ops:
  12.0 53.3 %all-to-all-start = ((bf16[16,128,512]{2,1,0:T(8,128)(2,1)}), bf16[16,128,512]{2,1,0:T(8,128)(2,1)S(1)}, u32[]{:S(2)}, u32[]{:S(2)}) async-start(bf16[16,128,512]{2,1,0:T(8,128)(2,1)} %copy.71), calls=%async_computation | async-start | bytes 4194304 | tf_op jit(solution)/shard_map/all_to_all | solution.py:208
  18.4 5.7 %copy-start.22 = (u32[32]{0:T(128)S(1)}, u32[32]{0:T(128)}, u32[]{:S(2)}) copy-start(u32[32]{0:T(128)} %constant.74) | copy-start | bytes 388
  18.4 7.0 %copy-start.20 = (s32[16]{0:T(128)S(1)}, s32[16]{0:T(128)}, u32[]{:S(2)}) copy-start(s32[16]{0:T(128)} %param.15) | copy-start | bytes 196
  18.4 66.8 %all-gather.2.cloned.1.call-start = ((), (), s32[]{:S(2)}) async-start(), calls=%async_computation.1 | async-start | bytes 6291456 | tf_op jit(solution)/shard_map/all_gather | solution.py:220
  65.2 5.8 %copy-start.12 = (f32[4,1024]{1,0:T(4,128)S(1)}, f32[4,1024]{1,0:T(4,128)}, u32[]{:S(2)}) copy-start(f32[4,1024]{1,0:T(4,128)} %param.22) | copy-start | bytes 49156
  65.2 5.8 %copy-start.14 = (f32[4,256]{1,0:T(4,128)S(1)}, f32[4,256]{1,0:T(4,128)}, u32[]{:S(2)}) copy-start(f32[4,256]{1,0:T(4,128)} %param.23) | copy-start | bytes 12292
  65.2 5.8 %copy-start.15 = (f32[1024]{0:T(1024)S(1)}, f32[1024]{0:T(1024)}, u32[]{:S(2)}) copy-start(f32[1024]{0:T(1024)} %param.24) | copy-start | bytes 12292
  65.2 5.8 %copy-start.17 = (f32[256]{0:T(256)S(1)}, f32[256]{0:T(256)}, u32[]{:S(2)}) copy-start(f32[256]{0:T(256)} %param.25) | copy-start | bytes 3076
  65.2 6.1 %copy-start.21 = (f32[16]{0:T(128)S(1)}, f32[16]{0:T(128)}, u32[]{:S(2)}) copy-start(f32[16]{0:T(128)} %param.21) | copy-start | bytes 196
  65.2 19.9 %copy-start.10 = (bf16[1024,16]{0,1:T(8,128)(2,1)S(1)}, bf16[1024,16]{0,1:T(8,128)(2,1)}, u32[]{:S(2)}) copy-start(bf16[1024,16]{0,1:T(8,128)(2,1)} %param.19) | copy-start | bytes 98308
  65.3 19.9 %copy-start.16 = (f32[16]{0:T(128)S(1)}, f32[16]{0:T(128)}, u32[]{:S(2)}) copy-start(f32[16]{0:T(128)} %param.20) | copy-start | bytes 196
  89.0 12.9 %copy-start.9 = (f32[16,16,128]{2,1,0:T(8,128)}, f32[16,16,128]{2,1,0:T(8,128)S(1)}, u32[]{:S(2)}) copy-start(f32[16,16,128]{2,1,0:T(8,128)S(1)} %fusion.16.cumt_ref) | copy-start | bytes 393220
  89.3 23.3 %copy-start.6 = (f32[16,16,128]{1,2,0:T(8,128)}, f32[16,16,128]{1,2,0:T(8,128)S(1)}, u32[]{:S(2)}) copy-start(f32[16,16,128]{1,2,0:T(8,128)S(1)} %copy.79) | copy-start | bytes 393220
  101.9 6.6 %copy-start.5 = (bf16[2048,2048]{1,0:T(8,128)(2,1)}, bf16[2048,2048]{1,0:T(8,128)(2,1)S(1)}, u32[]{:S(2)}) copy-start(bf16[2048,2048]{1,0:T(8,128)(2,1)S(1)} %convolution_convert_fusion.gate_ref) | copy-start | bytes 25165828
  109.3 5.5 %collective-permute-start = (bf16[3,1281]{1,0:T(4,128)(2,1)S(1)}, bf16[3,1281]{1,0:T(4,128)(2,1)S(1)}, u32[]{:S(2)}, u32[]{:S(2)}) collective-permute-start(bf16[3,1281]{1,0:T(4,128)(2,1)S(1)} %pad_maximum_fusion.5), channel_id=1, source_target_pairs={{0,2},{2,4},{4,6},{6,8},{8,10},{10,12},{12,14},{14,16},{16,18},{18... | collective-permute-start | bytes 23066 | tf_op jit(solution)/shard_map/ppermute | solution.py:17
  148.2 20.6 %copy-start.8 = (f32[128,1024]{1,0:T(8,128)S(1)}, f32[128,1024]{1,0:T(8,128)}, u32[]{:S(2)}) copy-start(f32[128,1024]{1,0:T(8,128)} %get-tuple-element.14) | copy-start | bytes 1572868
  149.4 30.6 %copy-start.18 = (f32[16]{0:T(128)S(1)}, f32[16]{0:T(128)}, u32[]{:S(2)}) copy-start(f32[16]{0:T(128)} %param.26) | copy-start | bytes 196
  149.4 9.8 %collective-permute-start.1 = (bf16[131,1024]{1,0:T(8,128)(2,1)S(1)}, bf16[131,1024]{1,0:T(8,128)(2,1)S(1)}, u32[]{:S(2)}, u32[]{:S(2)}) collective-permute-start(bf16[131,1024]{1,0:T(8,128)(2,1)S(1)} %pad_maximum_fusion.1), channel_id=1, source_target_pairs={{0,2},{2,4},{4,6},{6,8},{8,10},{10,12},{12,14},{14,16},{16,18},{18... | collective-permute-start | bytes 804872 | tf_op jit(solution)/shard_map/ppermute | solution.py:17
  160.4 8.3 %collective-permute-start.2 = (bf16[131,1024]{1,0:T(8,128)(2,1)S(1)}, bf16[131,1024]{1,0:T(8,128)(2,1)S(1)}, u32[]{:S(2)}, u32[]{:S(2)}) collective-permute-start(bf16[131,1024]{1,0:T(8,128)(2,1)S(1)} %pad_maximum_fusion.2), channel_id=1, source_target_pairs={{0,4},{2,6},{4,8},{6,10},{8,12},{10,14},{12,16},{14,18},{16,20},{1... | collective-permute-start | bytes 804872 | tf_op jit(solution)/shard_map/ppermute | solution.py:17
  169.0 7.3 %collective-permute-start.3 = (bf16[131,1024]{1,0:T(8,128)(2,1)S(1)}, bf16[131,1024]{1,0:T(8,128)(2,1)S(1)}, u32[]{:S(2)}, u32[]{:S(2)}) collective-permute-start(bf16[131,1024]{1,0:T(8,128)(2,1)S(1)} %pad_maximum_fusion.3), channel_id=1, source_target_pairs={{0,8},{2,10},{4,12},{6,14},{8,16},{10,18},{12,20},{14,22},{16,24},... | collective-permute-start | bytes 804872 | tf_op jit(solution)/shard_map/ppermute | solution.py:17
  176.5 8.3 %collective-permute-start.4 = (bf16[131,1024]{1,0:T(8,128)(2,1)S(1)}, bf16[131,1024]{1,0:T(8,128)(2,1)S(1)}, u32[]{:S(2)}, u32[]{:S(2)}) collective-permute-start(bf16[131,1024]{1,0:T(8,128)(2,1)S(1)} %pad_maximum_fusion.4), channel_id=1, source_target_pairs={{0,2},{2,4},{4,6},{6,8},{8,10},{10,12},{12,14},{14,16},{16,18},{18... | collective-permute-start | bytes 804872 | tf_op jit(solution)/shard_map/ppermute | solution.py:17
  180.7 17.3 %collective-permute-start.5 = (bf16[128,1024]{1,0:T(8,128)(2,1)S(1)}, bf16[128,1024]{1,0:T(8,128)(2,1)S(1)}, u32[]{:S(2)}, u32[]{:S(2)}) collective-permute-start(bf16[128,1024]{1,0:T(8,128)(2,1)S(1)} %fusion.12), channel_id=1, source_target_pairs={{0,18},{2,20},{4,22},{6,24},{8,26},{10,28},{12,30},{1,19},{3,21},{... | collective-permute-start | bytes 786440 | tf_op jit(solution)/shard_map/ppermute | solution.py:17
  198.9 26.8 %copy-start.13 = (f32[1024]{0:T(1024)S(1)}, f32[1024]{0:T(1024)}, u32[]{:S(2)}) copy-start(f32[1024]{0:T(1024)} %param.27) | copy-start | bytes 12292
  225.7 5.4 %copy-start.1 = (bf16[16,128,512]{2,1,0:T(8,128)(2,1)S(1)}, bf16[16,128,512]{2,1,0:T(8,128)(2,1)}, u32[]{:S(2)}) copy-start(bf16[16,128,512]{2,1,0:T(8,128)(2,1)} %param.14) | copy-start | bytes 6291460
  (7 other events, 24.6 us)
Sparse Core Ops, SparseCore 0:
  69.3 15.8 all-gather.1

commit v17 on v16

--- a/solution.py
+++ b/solution.py
@@ -217,10 +217,24 @@
     )
     own_rows = arrived.reshape(row_count, columns)
     weight_set = (zx_cols, w_bc, w_dt)
-    piece = lax.all_gather(own_rows, "head", axis=1, tiled=True)
-    acc_zx, acc_bc, acc_dt = tuple(
-        (jnp.dot(piece, weight, preferred_element_type=jnp.float32) for weight in weight_set)
-    )
+    if lax.axis_size("head") == 2:
+        partner_rows = lax.ppermute(own_rows, "head", [(0, 1), (1, 0)])
+        mine_at = lax.axis_index("head") * columns
+        other_at = columns - mine_at
+
+        def project(weight):
+            own_part = lax.dynamic_slice_in_dim(weight, mine_at, columns, 0)
+            other_part = lax.dynamic_slice_in_dim(weight, other_at, columns, 0)
+            return jnp.dot(own_rows, own_part, preferred_element_type=jnp.float32) + jnp.dot(
+                partner_rows, other_part, preferred_element_type=jnp.float32
+            )
+
+        acc_zx, acc_bc, acc_dt = tuple(project(weight) for weight in weight_set)
+    else:
+        piece = lax.all_gather(own_rows, "head", axis=1, tiled=True)
+        acc_zx, acc_bc, acc_dt = tuple(
+            (jnp.dot(piece, weight, preferred_element_type=jnp.float32) for weight in weight_set)
+        )
     zx = acc_zx.astype(jnp.bfloat16)
     x_in = zx[:, inner_here:]
     bc_all = acc_bc.astype(jnp.bfloat16)

time: 239 us -> 229 us (0.958)
  matrix products: 19.6 us -> 33.3 us
  between operations: 14.7 us -> 1.24 us
  waiting for transfers between devices: 47.7 us -> 36.3 us
  other arithmetic: 31.1 us -> 35 us
  local copies, waits for them, and re-layouts: 27.1 us -> 23.8 us
    dot_general x3 -> x6, matrix products: 16.6 us -> 30.4 us  [the longest x3 20.9 us: project(): jnp.dot(partner_rows, other_part, preferred_element_type=jnp.float32)]
    all_gather x1 -> x0, waiting for transfers between devices: 13.7 us -> none  [shards(): piece = lax.all_gather(own_rows, 'head', axis=1, tiled=True)]
    unnamed x52 -> x64, local copies, waits for them, and re-layouts: 15.2 us -> 9.97 us
  transfers between devices with their start and end apart: 8 -> 8, of which waited for: 6 -> 5; matrix products, arithmetic and copies ran while one was open for 6% -> 14% of each run, Pallas kernels for 0% -> 0%
where the time goes in v17:
time: 229 us; the launch traced here: 228 us
  blocking collectives  43 us (19%)
  waiting for transfers between devices  36.3 us (16%)
  Pallas kernels  36.2 us (16%)
  other arithmetic  35 us (15%)
  matrix products  33.3 us (15%)
  local copies, waits for them, and re-layouts  23.8 us (10%)
  starting transfers between devices  19 us (8%)
    unnamed x1, blocking collectives  39.5 us
    ppermute x6, waiting for transfers between devices, shifted(): return lax.ppermute(x, axis, pairs)  36.2 us
    pallas_call x1, Pallas kernels, mix_tiles(): pl.pallas_call(mix_tile, grid=(tiles_dev,), in_specs=[pl.BlockSpec((tile_...  21.4 us
    dot_general x3, matrix products, project(): jnp.dot(partner_rows, other_part, preferred_element_type=jnp.float32)  20.9 us
    pallas_call x1, Pallas kernels, contrib_tiles(): pl.pallas_call(contrib_tile, grid=(tiles_dev,), in_specs=[pl.BlockSpec((t...  14.8 us
    convert_element_type x1, other arithmetic, shards(): conv_out = jax.nn.silu(total).astype(jnp.bfloat16)  10.8 us
    ppermute x6, starting transfers between devices, shifted(): return lax.ppermute(x, axis, pairs)  10.7 us
    unnamed x64, local copies, waits for them, and re-layouts  9.97 us
  transfers between devices with their start and end apart: 8, of which 5 were waited for; matrix products, arithmetic and copies ran while one was open for 14% of the time, Pallas kernels for 0%

profile of v17, /device:TPU:29, one launch (start us, length us, event | category | flops | bytes accessed | tf_op | source)
XLA Modules:
  0.0 227.9 jit_solution(2348691928500266823)
XLA Ops:
  3.0 2.5 %copy.81 = bf16[16,128,512]{2,1,0:T(8,128)(2,1)} copy(bf16[16,128,512]{2,0,1:T(8,128)(2,1)S(1)} %fusion.9) | data formatting | bytes 4194304 | tf_op jit(solution)/shard_map/convert_element_type | solution.py:207
  5.5 6.4 %all-to-all-start = ((bf16[16,128,512]{2,1,0:T(8,128)(2,1)}), bf16[16,128,512]{2,1,0:T(8,128)(2,1)S(1)}, u32[]{:S(2)}, u32[]{:S(2)}) async-start(bf16[16,128,512]{2,1,0:T(8,128)(2,1)} %copy.81), calls=%async_computation | async-start | bytes 4194304 | tf_op jit(solution)/shard_map/all_to_all | solution.py:208
  11.9 5.7 %copy.100 = bf16[128,8,2,1024]{3,1,2,0:T(8,128)(2,1)} copy(bf16[128,8,2,1024]{3,2,1,0:T(2,128)(2,1)} %bitcast.58) | data formatting | bytes 8388608
  19.0 39.5 %all-reduce.1 = s32[256]{0:T(256)S(1)} all-reduce(s32[256]{0:T(256)S(1)} %dynamic-update-slice), channel_id=1, replica_groups=mesh['seq'=16,'head'=2] {'seq'}, use_global_device_ids=true, to_apply=%add.1 | all-reduce | flops 256 | bytes 2048
  68.6 8.2 %fusion.7 = f32[2048,2048]{1,0:T(8,128)} fusion(bf16[2048,512]{1,0:T(8,128)(2,1)S(1)} %bitcast.55, bf16[1024,2048]{1,0:T(8,128)(2,1)S(1)} %bitcast.60, s32[]{:T(128)S(6)} %select_n.90), kind=kOutput, calls=%fused_computation.16 | convolution fusion | flops 4294967296 | bytes 20971524 | tf_op jit(solution)/shard_map/dot_general | solution.py:228
  76.8 14.8 %add_convert_fusion.gate_ref = bf16[2048,2048]{1,0:T(8,128)(2,1)} fusion(f32[2048,2048]{1,0:T(8,128)} %fusion.7, bf16[2048,512]{1,0:T(8,128)(2,1)} %collective-permute-done, bf16[1024,2048]{1,0:T(8,128)(2,1)} %bitcast.59, s32[]{:T(128)S(6)} %select_n.91), kind=kOutput, calls=%fused_computation | convolution fusion | flops 4303355904 | bytes 29360132 | tf_op jit(solution)/shard_map/dot_general | solution.py:228
  91.6 2.6 %slice.153 = bf16[2048,1024]{1,0:T(8,128)(2,1)S(1)} slice(bf16[2048,2048]{1,0:T(8,128)(2,1)} %add_convert_fusion.gate_ref), slice={[0:2048], [1024:2048]} | slice | bytes 8388608 | tf_op jit(solution)/shard_map/slice | solution.py:239
  94.2 3.8 %fusion = bf16[2048,256]{1,0:T(8,128)(2,1)S(1)} fusion(f32[2048,256]{1,0:T(8,128)S(1)} %fusion.21, bf16[2048,512]{1,0:T(8,128)(2,1)} %collective-permute-done, bf16[1024,256]{1,0:T(8,128)(2,1)S(1)} %copy-done.9, s32[]{:T(128)S(6)} %select_n.91), kind=kOutput, calls=%fused_computation.8 | convolution fusion | flops 537919488 | bytes 5505028 | tf_op jit(solution)/shard_map/dot_general | solution.py:228
  98.7 2.7 %collective-permute-start.1 = (bf16[3,1281]{1,0:T(4,128)(2,1)}, bf16[3,1281]{1,0:T(4,128)(2,1)}, u32[]{:S(2)}, u32[]{:S(2)}) collective-permute-start(bf16[3,1281]{1,0:T(4,128)(2,1)} %pad_maximum_fusion.5), channel_id=1, source_target_pairs={{0,2},{2,4},{4,6},{6,8},{8,10},{10,12},{12,14},{14,16},{16,18},{18... | collective-permute-start | bytes 23066 | tf_op jit(solution)/shard_map/ppermute | solution.py:17
  101.4 2.3 compare_select_fusion
  105.7 2.1 multiply_multiply_fusion.end_ref
  109.4 4.0 %maximum_maximum_fusion = bf16[2051,1280]{1,0:T(8,128)(2,1)S(1)} fusion(bf16[2048,256]{1,0:T(8,128)(2,1)S(1)} %fusion, bf16[2048,1024]{1,0:T(8,128)(2,1)} %copy-done.3, bf16[3,1280]{1,0:T(4,128)(2,1)S(1)} %slice.162), kind=kLoop, calls=%fused_computation.5 | loop fusion | flops 15751680 | bytes 10501120 | tf_op jit(solution)/shard_map/concatenate | solution.py:252
  114.4 10.8 %multiply_convert_fusion.x_ref.b_ref.c_ref = bf16[2048,1280]{1,0:T(8,128)(2,1)S(1)} fusion(bf16[2048,256]{1,0:T(8,128)(2,1)S(1)} %fusion, bf16[2051,1280]{1,0:T(8,128)(2,1)S(1)} %maximum_maximum_fusion, f32[1280]{0:T(1024)S(1)} %copy-done.12, f32[1280]{0:T(1024)S(1)} %copy-done.13, f32[1280]{0:T(1024)S(1)} %copy-done.14, f32[1280]{0:T(1024)S(1)} %copy-done.11, ...), kind=kLoop, calls=%fused_computation.1 | loop fusion | flops 60293120 | bytes 26246144 | tf_op jit(solution)/shard_map/convert_element_type | solution.py:265
  125.2 2.4 %copy-done.2 = bf16[2048,1280]{1,0:T(8,128)(2,1)} copy-done((bf16[2048,1280]{1,0:T(8,128)(2,1)}, bf16[2048,1280]{1,0:T(8,128)(2,1)S(1)}, u32[]{:S(2)}) %copy-start.2) | copy-done | bytes 5242904
  128.7 14.8 %shard_map.136 = (f32[16,128,1024]{2,1,0:T(8,128)}, f32[128,1024]{1,0:T(8,128)}) custom-call(bf16[2048,1280]{1,0:T(8,128)(2,1)} %copy-done.2, bf16[16,128,128]{2,1,0:T(8,128)(2,1)} %bitcast.62, f32[16,128,16]{2,1,0:T(8,128)} %multiply_multiply_fusion.end_ref, f32[16,1,1024]{2,1,0:T(1,128)} %broadcast_in_dim_reshape.10.pass_ref), custom_call_target="tpu_custom_call" | custom-call | flops 536870912 | bytes 13107200 | tf_op jit(solution)/shard_map/pallas_call | solution.py:102
  144.7 1.9 collective-permute-start.2
  146.7 8.7 %collective-permute-done.2 = bf16[131,1024]{1,0:T(8,128)(2,1)S(1)} collective-permute-done((bf16[131,1024]{1,0:T(8,128)(2,1)S(1)}, bf16[131,1024]{1,0:T(8,128)(2,1)S(1)}, u32[]{:S(2)}, u32[]{:S(2)}) %collective-permute-start.2) | collective-permute-done | bytes 268320 | tf_op jit(solution)/shard_map/ppermute | solution.py:17
  158.0 7.6 %collective-permute-done.3 = bf16[131,1024]{1,0:T(8,128)(2,1)S(1)} collective-permute-done((bf16[131,1024]{1,0:T(8,128)(2,1)S(1)}, bf16[131,1024]{1,0:T(8,128)(2,1)S(1)}, u32[]{:S(2)}, u32[]{:S(2)}) %collective-permute-start.3) | collective-permute-done | bytes 268320 | tf_op jit(solution)/shard_map/ppermute | solution.py:17
  168.3 5.6 %collective-permute-done.4 = bf16[131,1024]{1,0:T(8,128)(2,1)S(1)} collective-permute-done((bf16[131,1024]{1,0:T(8,128)(2,1)S(1)}, bf16[131,1024]{1,0:T(8,128)(2,1)S(1)}, u32[]{:S(2)}, u32[]{:S(2)}) %collective-permute-start.4) | collective-permute-done | bytes 268320 | tf_op jit(solution)/shard_map/ppermute | solution.py:17
  174.1 2.3 %collective-permute-start.5 = (bf16[131,1024]{1,0:T(8,128)(2,1)S(1)}, bf16[131,1024]{1,0:T(8,128)(2,1)S(1)}, u32[]{:S(2)}, u32[]{:S(2)}) collective-permute-start(bf16[131,1024]{1,0:T(8,128)(2,1)S(1)} %pad_maximum_fusion.4), channel_id=1, source_target_pairs={{0,2},{2,4},{4,6},{6,8},{8,10},{10,12},{12,14},{14,16},{16,18},{18... | collective-permute-start | bytes 804872 | tf_op jit(solution)/shard_map/ppermute | solution.py:17
  182.3 12.7 %collective-permute-done.6 = bf16[128,1024]{1,0:T(8,128)(2,1)S(1)} collective-permute-done((bf16[128,1024]{1,0:T(8,128)(2,1)S(1)}, bf16[128,1024]{1,0:T(8,128)(2,1)S(1)}, u32[]{:S(2)}, u32[]{:S(2)}) %collective-permute-start.6) | collective-permute-done | bytes 262176 | tf_op jit(solution)/shard_map/ppermute | solution.py:17
  195.9 21.4 %shard_map.137 = (f32[2048,1024]{1,0:T(8,128)}, f32[2048,1]{1,0:T(8,128)}) custom-call(bf16[2048,1280]{1,0:T(8,128)(2,1)} %copy-done.2, bf16[2048,1280]{1,0:T(8,128)(2,1)} %copy-done.2, bf16[2048,1280]{1,0:T(8,128)(2,1)} %copy-done.2, f32[16,128,16]{2,1,0:T(8,128)} %bitcast.57, f32[16,16,128]{2,1,0:T(8,128)} %copy-done.8, ...), custom_call_target="tpu_custom_call" | custom-call | flops 3288334336 | bytes 29360128 | tf_op jit(solution)/shard_map/pallas_call | solution.py:138
  219.0 3.5 %psum.7 = f32[16,128]{1,0:T(8,128)S(1)} all-reduce(f32[16,128]{1,0:T(8,128)S(1)} %bitcast.69), channel_id=1, replica_groups=mesh['seq'=16,'head'=2] {'head'}, use_global_device_ids=true, to_apply=%region_3.4 | all-reduce | flops 2048 | bytes 16384 | tf_op jit(solution)/shard_map/psum | solution.py:314
  222.5 5.3 %multiply_convert_fusion.1 = bf16[2048,1024]{1,0:T(8,128)(2,1)} fusion(f32[2048,1024]{1,0:T(8,128)} %get-tuple-element.15, f32[1024]{0:T(1024)S(1)} %copy-done.20, f32[2048]{0:T(1024)S(1)} %rsqrt_bitcast_fusion), kind=kLoop, calls=%fused_computation.2 | loop fusion | flops 6291456 | bytes 12595200 | tf_op jit(solution)/shard_map/convert_element_type | solution.py:315
  (145 shorter events, 35.1 us)
Async XLA Ops:
  5.5 56.4 %all-to-all-start = ((bf16[16,128,512]{2,1,0:T(8,128)(2,1)}), bf16[16,128,512]{2,1,0:T(8,128)(2,1)S(1)}, u32[]{:S(2)}, u32[]{:S(2)}) async-start(bf16[16,128,512]{2,1,0:T(8,128)(2,1)} %copy.81), calls=%async_computation | async-start | bytes 4194304 | tf_op jit(solution)/shard_map/all_to_all | solution.py:208
  11.9 6.9 %copy-start.26 = (s32[16]{0:T(128)S(1)}, s32[16]{0:T(128)}, u32[]{:S(2)}) copy-start(s32[16]{0:T(128)} %param.15) | copy-start | bytes 196
  11.9 46.6 %copy-start.17 = (s32[16]{0:T(128)S(1)}, s32[16]{0:T(128)}, u32[]{:S(2)}) copy-start(s32[16]{0:T(128)} %param.16) | copy-start | bytes 196
  11.9 48.2 %copy-start.21 = (f32[1024]{0:T(1024)S(1)}, f32[1024]{0:T(1024)}, u32[]{:S(2)}) copy-start(f32[1024]{0:T(1024)} %param.24) | copy-start | bytes 12292
  11.9 48.2 %copy-start.23 = (f32[256]{0:T(256)S(1)}, f32[256]{0:T(256)}, u32[]{:S(2)}) copy-start(f32[256]{0:T(256)} %param.25) | copy-start | bytes 3076
  11.9 48.5 %copy-start.19 = (f32[4,1024]{1,0:T(4,128)S(1)}, f32[4,1024]{1,0:T(4,128)}, u32[]{:S(2)}) copy-start(f32[4,1024]{1,0:T(4,128)} %param.22) | copy-start | bytes 49156
  11.9 48.6 %copy-start.27 = (f32[16]{0:T(128)S(1)}, f32[16]{0:T(128)}, u32[]{:S(2)}) copy-start(f32[16]{0:T(128)} %param.21) | copy-start | bytes 196
  17.6 48.7 %copy-start.22 = (f32[4,256]{1,0:T(4,128)S(1)}, f32[4,256]{1,0:T(4,128)}, u32[]{:S(2)}) copy-start(f32[4,256]{1,0:T(4,128)} %param.23) | copy-start | bytes 12292
  17.6 49.5 %copy-start.10 = (bf16[1024,16]{0,1:T(8,128)(2,1)S(1)}, bf16[1024,16]{0,1:T(8,128)(2,1)}, u32[]{:S(2)}) copy-start(bf16[1024,16]{0,1:T(8,128)(2,1)} %param.19) | copy-start | bytes 98308
  59.4 7.0 %copy-start.15 = (f32[2048]{0:T(1024)}, f32[2048]{0:T(1024)S(1)}, u32[]{:S(2)}) copy-start(f32[2048]{0:T(1024)S(1)} %add_bitcast_fusion) | copy-start | bytes 24580
  64.4 12.4 %collective-permute-start = (bf16[2048,512]{1,0:T(8,128)(2,1)S(1)}, bf16[2048,512]{1,0:T(8,128)(2,1)}, u32[]{:S(2)}, u32[]{:S(2)}) collective-permute-start(bf16[2048,512]{1,0:T(8,128)(2,1)S(1)} %bitcast.52), channel_id=1, source_target_pairs={{0,1},{1,0},{2,3},{3,2},{4,5},{5,4},{6,7},{7,6},{8,9},{9,8},{10,11... | collective-permute-start | bytes 6291464 | tf_op jit(solution)/shard_map/ppermute | solution.py:221
  94.2 7.1 %copy-start.24 = (f32[16]{0:T(128)S(1)}, f32[16]{0:T(128)}, u32[]{:S(2)}) copy-start(f32[16]{0:T(128)} %param.20) | copy-start | bytes 196
  98.7 10.0 %collective-permute-start.1 = (bf16[3,1281]{1,0:T(4,128)(2,1)}, bf16[3,1281]{1,0:T(4,128)(2,1)}, u32[]{:S(2)}, u32[]{:S(2)}) collective-permute-start(bf16[3,1281]{1,0:T(4,128)(2,1)} %pad_maximum_fusion.5), channel_id=1, source_target_pairs={{0,2},{2,4},{4,6},{6,8},{8,10},{10,12},{12,14},{14,16},{16,18},{18... | collective-permute-start | bytes 23066 | tf_op jit(solution)/shard_map/ppermute | solution.py:17
  104.0 9.5 %copy-start.8 = (f32[16,16,128]{2,1,0:T(8,128)}, f32[16,16,128]{2,1,0:T(8,128)S(1)}, u32[]{:S(2)}) copy-start(f32[16,16,128]{2,1,0:T(8,128)S(1)} %fusion.24.cumt_ref) | copy-start | bytes 393220
  104.4 9.1 %copy-start.5 = (f32[16,16,128]{1,2,0:T(8,128)}, f32[16,16,128]{1,2,0:T(8,128)S(1)}, u32[]{:S(2)}) copy-start(f32[16,16,128]{1,2,0:T(8,128)S(1)} %copy.91) | copy-start | bytes 393220
  143.5 22.1 %copy-start.6 = (f32[128,1024]{1,0:T(8,128)S(1)}, f32[128,1024]{1,0:T(8,128)}, u32[]{:S(2)}) copy-start(f32[128,1024]{1,0:T(8,128)} %get-tuple-element.14) | copy-start | bytes 1572868
  143.5 23.7 %copy-start.18 = (s32[16]{0:T(128)S(1)}, s32[16]{0:T(128)}, u32[]{:S(2)}) copy-start(s32[16]{0:T(128)} %param.16) | copy-start | bytes 196
  144.7 32.4 %copy-start.25 = (f32[16]{0:T(128)S(1)}, f32[16]{0:T(128)}, u32[]{:S(2)}) copy-start(f32[16]{0:T(128)} %param.26) | copy-start | bytes 196
  144.7 10.7 %collective-permute-start.2 = (bf16[131,1024]{1,0:T(8,128)(2,1)S(1)}, bf16[131,1024]{1,0:T(8,128)(2,1)S(1)}, u32[]{:S(2)}, u32[]{:S(2)}) collective-permute-start(bf16[131,1024]{1,0:T(8,128)(2,1)S(1)} %pad_maximum_fusion.1), channel_id=1, source_target_pairs={{0,2},{2,4},{4,6},{6,8},{8,10},{10,12},{12,14},{14,16},{16,18},{18... | collective-permute-start | bytes 804872 | tf_op jit(solution)/shard_map/ppermute | solution.py:17
  156.7 8.9 %collective-permute-start.3 = (bf16[131,1024]{1,0:T(8,128)(2,1)S(1)}, bf16[131,1024]{1,0:T(8,128)(2,1)S(1)}, u32[]{:S(2)}, u32[]{:S(2)}) collective-permute-start(bf16[131,1024]{1,0:T(8,128)(2,1)S(1)} %pad_maximum_fusion.2), channel_id=1, source_target_pairs={{0,4},{2,6},{4,8},{6,10},{8,12},{10,14},{12,16},{14,18},{16,20},{1... | collective-permute-start | bytes 804872 | tf_op jit(solution)/shard_map/ppermute | solution.py:17
  165.9 8.0 %collective-permute-start.4 = (bf16[131,1024]{1,0:T(8,128)(2,1)S(1)}, bf16[131,1024]{1,0:T(8,128)(2,1)S(1)}, u32[]{:S(2)}, u32[]{:S(2)}) collective-permute-start(bf16[131,1024]{1,0:T(8,128)(2,1)S(1)} %pad_maximum_fusion.3), channel_id=1, source_target_pairs={{0,8},{2,10},{4,12},{6,14},{8,16},{10,18},{12,20},{14,22},{16,24},... | collective-permute-start | bytes 804872 | tf_op jit(solution)/shard_map/ppermute | solution.py:17
  174.1 8.2 %collective-permute-start.5 = (bf16[131,1024]{1,0:T(8,128)(2,1)S(1)}, bf16[131,1024]{1,0:T(8,128)(2,1)S(1)}, u32[]{:S(2)}, u32[]{:S(2)}) collective-permute-start(bf16[131,1024]{1,0:T(8,128)(2,1)S(1)} %pad_maximum_fusion.4), channel_id=1, source_target_pairs={{0,2},{2,4},{4,6},{6,8},{8,10},{10,12},{12,14},{14,16},{16,18},{18... | collective-permute-start | bytes 804872 | tf_op jit(solution)/shard_map/ppermute | solution.py:17
  177.8 17.2 %collective-permute-start.6 = (bf16[128,1024]{1,0:T(8,128)(2,1)S(1)}, bf16[128,1024]{1,0:T(8,128)(2,1)S(1)}, u32[]{:S(2)}, u32[]{:S(2)}) collective-permute-start(bf16[128,1024]{1,0:T(8,128)(2,1)S(1)} %fusion.17), channel_id=1, source_target_pairs={{0,18},{2,20},{4,22},{6,24},{8,26},{10,28},{12,30},{1,19},{3,21},{... | collective-permute-start | bytes 786440 | tf_op jit(solution)/shard_map/ppermute | solution.py:17
  195.9 26.6 %copy-start.20 = (f32[1024]{0:T(1024)S(1)}, f32[1024]{0:T(1024)}, u32[]{:S(2)}) copy-start(f32[1024]{0:T(1024)} %param.27) | copy-start | bytes 12292
  (13 other events, 56.9 us)

commit v18 on v17

--- a/solution.py
+++ b/solution.py
@@ -75,41 +75,47 @@
 
 def contrib_tile(x_ref, bt_ref, end_ref, pass_ref, before_ref, total_ref):
     f32 = jnp.float32
-    tile_len = x_ref.shape[0]
+    group = bt_ref.shape[0]
+    tile_len = bt_ref.shape[2]
     pairs = x_ref.shape[1] // 128
 
     @pl.when(pl.program_id(0) == 0)
     def _():
         total_ref[...] = jnp.zeros_like(total_ref)
 
-    b_t = bt_ref[0]
-    to_end = end_ref[0]
     first_half = lax.broadcasted_iota(jnp.int32, (tile_len, 128), 1) < 64
-    for pair in range(pairs):
-        cols = pl.ds(pair * 128, 128)
-        scale = jnp.where(
-            first_half, to_end[:, 2 * pair : 2 * pair + 1], to_end[:, 2 * pair + 1 : 2 * pair + 2]
-        )
-        scaled = (x_ref[:, cols].astype(f32) * scale).astype(jnp.bfloat16)
-        contrib = jnp.dot(b_t, scaled, preferred_element_type=f32)
-        state = total_ref[:, cols]
-        before_ref[0, :, cols] = state
-        total_ref[:, cols] = pass_ref[0, :, cols] * state + contrib
+    for sub in range(group):
+        b_t = bt_ref[sub]
+        to_end = end_ref[sub]
+        rows = pl.ds(sub * tile_len, tile_len)
+        for pair in range(pairs):
+            cols = pl.ds(pair * 128, 128)
+            scale = jnp.where(
+                first_half,
+                to_end[:, 2 * pair : 2 * pair + 1],
+                to_end[:, 2 * pair + 1 : 2 * pair + 2],
+            )
+            scaled = (x_ref[rows, cols].astype(f32) * scale).astype(jnp.bfloat16)
+            contrib = jnp.dot(b_t, scaled, preferred_element_type=f32)
+            state = total_ref[:, cols]
+            before_ref[sub, :, cols] = state
+            total_ref[:, cols] = pass_ref[sub, :, cols] * state + contrib
 
 
 def contrib_tiles(conv_out, b_t, to_end, passing_wide, inner_here, state_dim):
     tiles_dev, tile_len, heads_here = to_end.shape
+    group = 2 if tiles_dev % 2 == 0 else 1
     return pl.pallas_call(
         contrib_tile,
-        grid=(tiles_dev,),
+        grid=(tiles_dev // group,),
         in_specs=[
-            pl.BlockSpec((tile_len, inner_here), lambda j: (j, 0)),
-            pl.BlockSpec((1, state_dim, tile_len), lambda j: (j, 0, 0)),
-            pl.BlockSpec((1, tile_len, heads_here), lambda j: (j, 0, 0)),
-            pl.BlockSpec((1, 1, inner_here), lambda j: (j, 0, 0)),
+            pl.BlockSpec((group * tile_len, inner_here), lambda j: (j, 0)),
+            pl.BlockSpec((group, state_dim, tile_len), lambda j: (j, 0, 0)),
+            pl.BlockSpec((group, tile_len, heads_here), lambda j: (j, 0, 0)),
+            pl.BlockSpec((group, 1, inner_here), lambda j: (j, 0, 0)),
         ],
         out_specs=[
-            pl.BlockSpec((1, state_dim, inner_here), lambda j: (j, 0, 0)),
+            pl.BlockSpec((group, state_dim, inner_here), lambda j: (j, 0, 0)),
             pl.BlockSpec((state_dim, inner_here), lambda j: (0, 0)),
         ],
         out_shape=[

time: 229 us -> 225 us (0.983)
  Pallas kernels: 36.2 us -> 32.3 us
    pallas_call x1, Pallas kernels: 14.8 us -> 10.9 us  [contrib_tiles(): pl.pallas_call(contrib_tile, grid=(tiles_dev // group,), in_specs=[pl.Blo...]
where the time goes in v18:
time: 225 us; the launch traced here: 224 us
  blocking collectives  43 us (19%)
  waiting for transfers between devices  36.3 us (16%)
  other arithmetic  35 us (16%)
  matrix products  33.3 us (15%)
  Pallas kernels  32.3 us (14%)
  local copies, waits for them, and re-layouts  23.8 us (11%)
  starting transfers between devices  19 us (8%)
    unnamed x1, blocking collectives  39.5 us
    ppermute x6, waiting for transfers between devices, shifted(): return lax.ppermute(x, axis, pairs)  36.3 us
    pallas_call x1, Pallas kernels, mix_tiles(): pl.pallas_call(mix_tile, grid=(tiles_dev,), in_specs=[pl.BlockSpec((tile_...  21.4 us
    dot_general x3, matrix products, project(): jnp.dot(partner_rows, other_part, preferred_element_type=jnp.float32)  20.9 us
    pallas_call x1, Pallas kernels, contrib_tiles(): pl.pallas_call(contrib_tile, grid=(tiles_dev // group,), in_specs=[pl.Blo...  10.9 us
    convert_element_type x1, other arithmetic, shards(): conv_out = jax.nn.silu(total).astype(jnp.bfloat16)  10.8 us
    ppermute x6, starting transfers between devices, shifted(): return lax.ppermute(x, axis, pairs)  10.7 us
    unnamed x64, local copies, waits for them, and re-layouts  9.97 us
  transfers between devices with their start and end apart: 8, of which 5 were waited for; matrix products, arithmetic and copies ran while one was open for 14% of the time, Pallas kernels for 0%

profile of v18, /device:TPU:29, one launch (start us, length us, event | category | flops | bytes accessed | tf_op | source)
XLA Modules:
  0.0 223.9 jit_solution(10704011357298222611)
XLA Ops:
  3.0 2.5 %copy.81 = bf16[16,128,512]{2,1,0:T(8,128)(2,1)} copy(bf16[16,128,512]{2,0,1:T(8,128)(2,1)S(1)} %fusion.9) | data formatting | bytes 4194304 | tf_op jit(solution)/shard_map/convert_element_type | solution.py:213
  5.5 6.4 %all-to-all-start = ((bf16[16,128,512]{2,1,0:T(8,128)(2,1)}), bf16[16,128,512]{2,1,0:T(8,128)(2,1)S(1)}, u32[]{:S(2)}, u32[]{:S(2)}) async-start(bf16[16,128,512]{2,1,0:T(8,128)(2,1)} %copy.81), calls=%async_computation | async-start | bytes 4194304 | tf_op jit(solution)/shard_map/all_to_all | solution.py:214
  11.9 5.7 %copy.100 = bf16[128,8,2,1024]{3,1,2,0:T(8,128)(2,1)} copy(bf16[128,8,2,1024]{3,2,1,0:T(2,128)(2,1)} %bitcast.58) | data formatting | bytes 8388608
  19.0 39.5 %all-reduce.1 = s32[256]{0:T(256)S(1)} all-reduce(s32[256]{0:T(256)S(1)} %dynamic-update-slice), channel_id=1, replica_groups=mesh['seq'=16,'head'=2] {'seq'}, use_global_device_ids=true, to_apply=%add.1 | all-reduce | flops 256 | bytes 2048
  68.6 8.2 %fusion.7 = f32[2048,2048]{1,0:T(8,128)} fusion(bf16[2048,512]{1,0:T(8,128)(2,1)S(1)} %bitcast.55, bf16[1024,2048]{1,0:T(8,128)(2,1)S(1)} %bitcast.60, s32[]{:T(128)S(6)} %select_n.90), kind=kOutput, calls=%fused_computation.16 | convolution fusion | flops 4294967296 | bytes 20971524 | tf_op jit(solution)/shard_map/dot_general | solution.py:234
  76.8 14.8 %add_convert_fusion.gate_ref = bf16[2048,2048]{1,0:T(8,128)(2,1)} fusion(f32[2048,2048]{1,0:T(8,128)} %fusion.7, bf16[2048,512]{1,0:T(8,128)(2,1)} %collective-permute-done, bf16[1024,2048]{1,0:T(8,128)(2,1)} %bitcast.59, s32[]{:T(128)S(6)} %select_n.91), kind=kOutput, calls=%fused_computation | convolution fusion | flops 4303355904 | bytes 29360132 | tf_op jit(solution)/shard_map/dot_general | solution.py:234
  91.6 2.6 %slice.153 = bf16[2048,1024]{1,0:T(8,128)(2,1)S(1)} slice(bf16[2048,2048]{1,0:T(8,128)(2,1)} %add_convert_fusion.gate_ref), slice={[0:2048], [1024:2048]} | slice | bytes 8388608 | tf_op jit(solution)/shard_map/slice | solution.py:245
  94.2 3.8 %fusion = bf16[2048,256]{1,0:T(8,128)(2,1)S(1)} fusion(f32[2048,256]{1,0:T(8,128)S(1)} %fusion.21, bf16[2048,512]{1,0:T(8,128)(2,1)} %collective-permute-done, bf16[1024,256]{1,0:T(8,128)(2,1)S(1)} %copy-done.9, s32[]{:T(128)S(6)} %select_n.91), kind=kOutput, calls=%fused_computation.8 | convolution fusion | flops 537919488 | bytes 5505028 | tf_op jit(solution)/shard_map/dot_general | solution.py:234
  98.7 2.7 %collective-permute-start.1 = (bf16[3,1281]{1,0:T(4,128)(2,1)}, bf16[3,1281]{1,0:T(4,128)(2,1)}, u32[]{:S(2)}, u32[]{:S(2)}) collective-permute-start(bf16[3,1281]{1,0:T(4,128)(2,1)} %pad_maximum_fusion.5), channel_id=1, source_target_pairs={{0,2},{2,4},{4,6},{6,8},{8,10},{10,12},{12,14},{14,16},{16,18},{18... | collective-permute-start | bytes 23066 | tf_op jit(solution)/shard_map/ppermute | solution.py:17
  101.4 2.3 %compare_select_fusion = f32[2048,16]{0,1:T(8,128)S(1)} fusion(f32[2048,16]{0,1:T(8,128)S(1)} %fusion.29, bf16[2048,512]{1,0:T(8,128)(2,1)} %collective-permute-done, f32[16]{0:T(128)S(1)} %copy-done.24, bf16[1024,16]{0,1:T(8,128)(2,1)S(1)} %copy-done.10, s32[]{:T(128)S(6)} %select_n.91), kind=kOutput, calls=%fused_computation.31 | convolution fusion | flops 33816576 | bytes 2376196 | tf_op jit(solution)/shard_map/dot_general | solution.py:234
  105.7 2.1 multiply_multiply_fusion.end_ref
  109.4 4.0 %maximum_maximum_fusion = bf16[2051,1280]{1,0:T(8,128)(2,1)S(1)} fusion(bf16[2048,256]{1,0:T(8,128)(2,1)S(1)} %fusion, bf16[2048,1024]{1,0:T(8,128)(2,1)} %copy-done.3, bf16[3,1280]{1,0:T(4,128)(2,1)S(1)} %slice.162), kind=kLoop, calls=%fused_computation.5 | loop fusion | flops 15751680 | bytes 10501120 | tf_op jit(solution)/shard_map/concatenate | solution.py:258
  114.4 10.8 %multiply_convert_fusion.x_ref.b_ref.c_ref = bf16[2048,1280]{1,0:T(8,128)(2,1)S(1)} fusion(bf16[2048,256]{1,0:T(8,128)(2,1)S(1)} %fusion, bf16[2051,1280]{1,0:T(8,128)(2,1)S(1)} %maximum_maximum_fusion, f32[1280]{0:T(1024)S(1)} %copy-done.12, f32[1280]{0:T(1024)S(1)} %copy-done.13, f32[1280]{0:T(1024)S(1)} %copy-done.14, f32[1280]{0:T(1024)S(1)} %copy-done.11, ...), kind=kLoop, calls=%fused_computation.1 | loop fusion | flops 60293120 | bytes 26246144 | tf_op jit(solution)/shard_map/convert_element_type | solution.py:271
  125.2 2.4 %copy-done.2 = bf16[2048,1280]{1,0:T(8,128)(2,1)} copy-done((bf16[2048,1280]{1,0:T(8,128)(2,1)}, bf16[2048,1280]{1,0:T(8,128)(2,1)S(1)}, u32[]{:S(2)}) %copy-start.2) | copy-done | bytes 5242904
  128.7 10.9 %shard_map.136 = (f32[16,128,1024]{2,1,0:T(8,128)}, f32[128,1024]{1,0:T(8,128)}) custom-call(bf16[2048,1280]{1,0:T(8,128)(2,1)} %copy-done.2, bf16[16,128,128]{2,1,0:T(8,128)(2,1)} %bitcast.62, f32[16,128,16]{2,1,0:T(8,128)} %multiply_multiply_fusion.end_ref, f32[16,1,1024]{2,1,0:T(1,128)} %broadcast_in_dim_reshape.10.pass_ref), custom_call_target="tpu_custom_call" | custom-call | flops 536870912 | bytes 13107200 | tf_op jit(solution)/shard_map/pallas_call | solution.py:108
  140.8 1.9 collective-permute-start.2
  142.8 8.7 %collective-permute-done.2 = bf16[131,1024]{1,0:T(8,128)(2,1)S(1)} collective-permute-done((bf16[131,1024]{1,0:T(8,128)(2,1)S(1)}, bf16[131,1024]{1,0:T(8,128)(2,1)S(1)}, u32[]{:S(2)}, u32[]{:S(2)}) %collective-permute-start.2) | collective-permute-done | bytes 268320 | tf_op jit(solution)/shard_map/ppermute | solution.py:17
  154.1 7.6 %collective-permute-done.3 = bf16[131,1024]{1,0:T(8,128)(2,1)S(1)} collective-permute-done((bf16[131,1024]{1,0:T(8,128)(2,1)S(1)}, bf16[131,1024]{1,0:T(8,128)(2,1)S(1)}, u32[]{:S(2)}, u32[]{:S(2)}) %collective-permute-start.3) | collective-permute-done | bytes 268320 | tf_op jit(solution)/shard_map/ppermute | solution.py:17
  164.4 5.6 %collective-permute-done.4 = bf16[131,1024]{1,0:T(8,128)(2,1)S(1)} collective-permute-done((bf16[131,1024]{1,0:T(8,128)(2,1)S(1)}, bf16[131,1024]{1,0:T(8,128)(2,1)S(1)}, u32[]{:S(2)}, u32[]{:S(2)}) %collective-permute-start.4) | collective-permute-done | bytes 268320 | tf_op jit(solution)/shard_map/ppermute | solution.py:17
  170.2 2.3 %collective-permute-start.5 = (bf16[131,1024]{1,0:T(8,128)(2,1)S(1)}, bf16[131,1024]{1,0:T(8,128)(2,1)S(1)}, u32[]{:S(2)}, u32[]{:S(2)}) collective-permute-start(bf16[131,1024]{1,0:T(8,128)(2,1)S(1)} %pad_maximum_fusion.4), channel_id=1, source_target_pairs={{0,2},{2,4},{4,6},{6,8},{8,10},{10,12},{12,14},{14,16},{16,18},{18... | collective-permute-start | bytes 804872 | tf_op jit(solution)/shard_map/ppermute | solution.py:17
  178.4 12.7 %collective-permute-done.6 = bf16[128,1024]{1,0:T(8,128)(2,1)S(1)} collective-permute-done((bf16[128,1024]{1,0:T(8,128)(2,1)S(1)}, bf16[128,1024]{1,0:T(8,128)(2,1)S(1)}, u32[]{:S(2)}, u32[]{:S(2)}) %collective-permute-start.6) | collective-permute-done | bytes 262176 | tf_op jit(solution)/shard_map/ppermute | solution.py:17
  192.0 21.4 %shard_map.137 = (f32[2048,1024]{1,0:T(8,128)}, f32[2048,1]{1,0:T(8,128)}) custom-call(bf16[2048,1280]{1,0:T(8,128)(2,1)} %copy-done.2, bf16[2048,1280]{1,0:T(8,128)(2,1)} %copy-done.2, bf16[2048,1280]{1,0:T(8,128)(2,1)} %copy-done.2, f32[16,128,16]{2,1,0:T(8,128)} %bitcast.57, f32[16,16,128]{2,1,0:T(8,128)} %copy-done.8, ...), custom_call_target="tpu_custom_call" | custom-call | flops 3288334336 | bytes 29360128 | tf_op jit(solution)/shard_map/pallas_call | solution.py:144
  215.0 3.5 %psum.7 = f32[16,128]{1,0:T(8,128)S(1)} all-reduce(f32[16,128]{1,0:T(8,128)S(1)} %bitcast.69), channel_id=1, replica_groups=mesh['seq'=16,'head'=2] {'head'}, use_global_device_ids=true, to_apply=%region_3.4 | all-reduce | flops 2048 | bytes 16384 | tf_op jit(solution)/shard_map/psum | solution.py:320
  218.6 5.3 %multiply_convert_fusion.1 = bf16[2048,1024]{1,0:T(8,128)(2,1)} fusion(f32[2048,1024]{1,0:T(8,128)} %get-tuple-element.15, f32[1024]{0:T(1024)S(1)} %copy-done.20, f32[2048]{0:T(1024)S(1)} %rsqrt_bitcast_fusion), kind=kLoop, calls=%fused_computation.2 | loop fusion | flops 6291456 | bytes 12595200 | tf_op jit(solution)/shard_map/convert_element_type | solution.py:321
  (145 shorter events, 35.1 us)
Async XLA Ops:
  5.5 56.4 %all-to-all-start = ((bf16[16,128,512]{2,1,0:T(8,128)(2,1)}), bf16[16,128,512]{2,1,0:T(8,128)(2,1)S(1)}, u32[]{:S(2)}, u32[]{:S(2)}) async-start(bf16[16,128,512]{2,1,0:T(8,128)(2,1)} %copy.81), calls=%async_computation | async-start | bytes 4194304 | tf_op jit(solution)/shard_map/all_to_all | solution.py:214
  11.9 6.9 %copy-start.26 = (s32[16]{0:T(128)S(1)}, s32[16]{0:T(128)}, u32[]{:S(2)}) copy-start(s32[16]{0:T(128)} %param.15) | copy-start | bytes 196
  11.9 46.6 %copy-start.17 = (s32[16]{0:T(128)S(1)}, s32[16]{0:T(128)}, u32[]{:S(2)}) copy-start(s32[16]{0:T(128)} %param.16) | copy-start | bytes 196
  11.9 48.2 %copy-start.21 = (f32[1024]{0:T(1024)S(1)}, f32[1024]{0:T(1024)}, u32[]{:S(2)}) copy-start(f32[1024]{0:T(1024)} %param.24) | copy-start | bytes 12292
  11.9 48.2 %copy-start.23 = (f32[256]{0:T(256)S(1)}, f32[256]{0:T(256)}, u32[]{:S(2)}) copy-start(f32[256]{0:T(256)} %param.25) | copy-start | bytes 3076
  11.9 48.5 %copy-start.19 = (f32[4,1024]{1,0:T(4,128)S(1)}, f32[4,1024]{1,0:T(4,128)}, u32[]{:S(2)}) copy-start(f32[4,1024]{1,0:T(4,128)} %param.22) | copy-start | bytes 49156
  11.9 48.6 %copy-start.27 = (f32[16]{0:T(128)S(1)}, f32[16]{0:T(128)}, u32[]{:S(2)}) copy-start(f32[16]{0:T(128)} %param.21) | copy-start | bytes 196
  17.6 48.7 %copy-start.22 = (f32[4,256]{1,0:T(4,128)S(1)}, f32[4,256]{1,0:T(4,128)}, u32[]{:S(2)}) copy-start(f32[4,256]{1,0:T(4,128)} %param.23) | copy-start | bytes 12292
  17.6 49.5 %copy-start.10 = (bf16[1024,16]{0,1:T(8,128)(2,1)S(1)}, bf16[1024,16]{0,1:T(8,128)(2,1)}, u32[]{:S(2)}) copy-start(bf16[1024,16]{0,1:T(8,128)(2,1)} %param.19) | copy-start | bytes 98308
  59.4 7.0 %copy-start.15 = (f32[2048]{0:T(1024)}, f32[2048]{0:T(1024)S(1)}, u32[]{:S(2)}) copy-start(f32[2048]{0:T(1024)S(1)} %add_bitcast_fusion) | copy-start | bytes 24580
  64.4 12.4 %collective-permute-start = (bf16[2048,512]{1,0:T(8,128)(2,1)S(1)}, bf16[2048,512]{1,0:T(8,128)(2,1)}, u32[]{:S(2)}, u32[]{:S(2)}) collective-permute-start(bf16[2048,512]{1,0:T(8,128)(2,1)S(1)} %bitcast.52), channel_id=1, source_target_pairs={{0,1},{1,0},{2,3},{3,2},{4,5},{5,4},{6,7},{7,6},{8,9},{9,8},{10,11... | collective-permute-start | bytes 6291464 | tf_op jit(solution)/shard_map/ppermute | solution.py:227
  94.2 7.1 %copy-start.24 = (f32[16]{0:T(128)S(1)}, f32[16]{0:T(128)}, u32[]{:S(2)}) copy-start(f32[16]{0:T(128)} %param.20) | copy-start | bytes 196
  98.7 10.0 %collective-permute-start.1 = (bf16[3,1281]{1,0:T(4,128)(2,1)}, bf16[3,1281]{1,0:T(4,128)(2,1)}, u32[]{:S(2)}, u32[]{:S(2)}) collective-permute-start(bf16[3,1281]{1,0:T(4,128)(2,1)} %pad_maximum_fusion.5), channel_id=1, source_target_pairs={{0,2},{2,4},{4,6},{6,8},{8,10},{10,12},{12,14},{14,16},{16,18},{18... | collective-permute-start | bytes 23066 | tf_op jit(solution)/shard_map/ppermute | solution.py:17
  104.0 9.5 %copy-start.8 = (f32[16,16,128]{2,1,0:T(8,128)}, f32[16,16,128]{2,1,0:T(8,128)S(1)}, u32[]{:S(2)}) copy-start(f32[16,16,128]{2,1,0:T(8,128)S(1)} %fusion.24.cumt_ref) | copy-start | bytes 393220
  104.4 9.1 %copy-start.5 = (f32[16,16,128]{1,2,0:T(8,128)}, f32[16,16,128]{1,2,0:T(8,128)S(1)}, u32[]{:S(2)}) copy-start(f32[16,16,128]{1,2,0:T(8,128)S(1)} %copy.91) | copy-start | bytes 393220
  139.6 22.2 %copy-start.6 = (f32[128,1024]{1,0:T(8,128)S(1)}, f32[128,1024]{1,0:T(8,128)}, u32[]{:S(2)}) copy-start(f32[128,1024]{1,0:T(8,128)} %get-tuple-element.14) | copy-start | bytes 1572868
  139.6 23.7 %copy-start.18 = (s32[16]{0:T(128)S(1)}, s32[16]{0:T(128)}, u32[]{:S(2)}) copy-start(s32[16]{0:T(128)} %param.16) | copy-start | bytes 196
  140.8 32.3 %copy-start.25 = (f32[16]{0:T(128)S(1)}, f32[16]{0:T(128)}, u32[]{:S(2)}) copy-start(f32[16]{0:T(128)} %param.26) | copy-start | bytes 196
  140.8 10.7 %collective-permute-start.2 = (bf16[131,1024]{1,0:T(8,128)(2,1)S(1)}, bf16[131,1024]{1,0:T(8,128)(2,1)S(1)}, u32[]{:S(2)}, u32[]{:S(2)}) collective-permute-start(bf16[131,1024]{1,0:T(8,128)(2,1)S(1)} %pad_maximum_fusion.1), channel_id=1, source_target_pairs={{0,2},{2,4},{4,6},{6,8},{8,10},{10,12},{12,14},{14,16},{16,18},{18... | collective-permute-start | bytes 804872 | tf_op jit(solution)/shard_map/ppermute | solution.py:17
  152.8 8.9 %collective-permute-start.3 = (bf16[131,1024]{1,0:T(8,128)(2,1)S(1)}, bf16[131,1024]{1,0:T(8,128)(2,1)S(1)}, u32[]{:S(2)}, u32[]{:S(2)}) collective-permute-start(bf16[131,1024]{1,0:T(8,128)(2,1)S(1)} %pad_maximum_fusion.2), channel_id=1, source_target_pairs={{0,4},{2,6},{4,8},{6,10},{8,12},{10,14},{12,16},{14,18},{16,20},{1... | collective-permute-start | bytes 804872 | tf_op jit(solution)/shard_map/ppermute | solution.py:17
  162.0 8.0 %collective-permute-start.4 = (bf16[131,1024]{1,0:T(8,128)(2,1)S(1)}, bf16[131,1024]{1,0:T(8,128)(2,1)S(1)}, u32[]{:S(2)}, u32[]{:S(2)}) collective-permute-start(bf16[131,1024]{1,0:T(8,128)(2,1)S(1)} %pad_maximum_fusion.3), channel_id=1, source_target_pairs={{0,8},{2,10},{4,12},{6,14},{8,16},{10,18},{12,20},{14,22},{16,24},... | collective-permute-start | bytes 804872 | tf_op jit(solution)/shard_map/ppermute | solution.py:17
  170.2 8.2 %collective-permute-start.5 = (bf16[131,1024]{1,0:T(8,128)(2,1)S(1)}, bf16[131,1024]{1,0:T(8,128)(2,1)S(1)}, u32[]{:S(2)}, u32[]{:S(2)}) collective-permute-start(bf16[131,1024]{1,0:T(8,128)(2,1)S(1)} %pad_maximum_fusion.4), channel_id=1, source_target_pairs={{0,2},{2,4},{4,6},{6,8},{8,10},{10,12},{12,14},{14,16},{16,18},{18... | collective-permute-start | bytes 804872 | tf_op jit(solution)/shard_map/ppermute | solution.py:17
  173.9 17.2 %collective-permute-start.6 = (bf16[128,1024]{1,0:T(8,128)(2,1)S(1)}, bf16[128,1024]{1,0:T(8,128)(2,1)S(1)}, u32[]{:S(2)}, u32[]{:S(2)}) collective-permute-start(bf16[128,1024]{1,0:T(8,128)(2,1)S(1)} %fusion.17), channel_id=1, source_target_pairs={{0,18},{2,20},{4,22},{6,24},{8,26},{10,28},{12,30},{1,19},{3,21},{... | collective-permute-start | bytes 786440 | tf_op jit(solution)/shard_map/ppermute | solution.py:17
  192.0 26.6 %copy-start.20 = (f32[1024]{0:T(1024)S(1)}, f32[1024]{0:T(1024)}, u32[]{:S(2)}) copy-start(f32[1024]{0:T(1024)} %param.27) | copy-start | bytes 12292
  (13 other events, 56.9 us)

commit v19 on v18

--- a/solution.py
+++ b/solution.py
@@ -22,55 +22,56 @@
     enter_ref, gate_ref, d_ref, out_ref, sq_ref,
 ):
     f32 = jnp.float32
-    tile_len = x_ref.shape[0]
+    group = cum_ref.shape[0]
+    tile_len = cum_ref.shape[1]
     pairs = x_ref.shape[1] // 128
-    b_mat = b_ref[...]
-    c_mat = c_ref[...]
-    scores = lax.dot_general(
-        c_mat, b_mat, (((1,), (1,)), ((), ())), preferred_element_type=f32
-    )
-    cum = cum_ref[0]
-    cumt = cumt_ref[0]
-    dtt = dtt_ref[0]
-    part_col = partc_ref[0]
-    part_row = partr_ref[0]
     row = lax.broadcasted_iota(jnp.int32, (tile_len, tile_len), 0)
     col = lax.broadcasted_iota(jnp.int32, (tile_len, tile_len), 1)
-    keep = (row >= col) & (part_col == part_row)
-    earlier = 1.0 - part_col
     first_half = lax.broadcasted_iota(jnp.int32, (tile_len, 128), 1) < 64
-    total_sq = jnp.zeros((tile_len, 128), f32)
-    for pair in range(pairs):
-        cols = pl.ds(pair * 128, 128)
-        x_pair = x_ref[:, cols]
-        slabs = []
-        for half in range(2):
-            head = 2 * pair + half
-            diff = cum[:, head : head + 1] - cumt[head : head + 1, :]
-            decay = jnp.where(keep, jnp.exp(jnp.where(keep, diff, 0.0)), 0.0)
-            slabs.append((scores * decay * dtt[head : head + 1, :]).astype(jnp.bfloat16))
-        weights = jnp.concatenate(slabs, axis=1)
-        zero = jnp.zeros_like(x_pair)
-        split_x = jnp.concatenate(
-            [jnp.where(first_half, x_pair, zero), jnp.where(first_half, zero, x_pair)], axis=0
+    for sub in range(group):
+        rows = pl.ds(sub * tile_len, tile_len)
+        c_mat = c_ref[rows, :]
+        scores = lax.dot_general(
+            c_mat, b_ref[rows, :], (((1,), (1,)), ((), ())), preferred_element_type=f32
         )
-        intra = jnp.dot(weights, split_x, preferred_element_type=f32)
-        carried = (
-            before_ref[0, :, cols] + prefix_ref[0, :, cols] * enter_ref[:, cols]
-        ).astype(jnp.bfloat16)
-        projected = jnp.dot(c_mat, carried, preferred_element_type=f32)
-        grow = jnp.where(
-            first_half,
-            jnp.exp(cum[:, 2 * pair : 2 * pair + 1]),
-            jnp.exp(cum[:, 2 * pair + 1 : 2 * pair + 2]),
-        )
-        inter = grow * earlier * projected
-        mixed = intra + inter + d_ref[:, cols] * x_pair.astype(f32)
-        gate = gate_ref[:, cols].astype(f32)
-        gated = mixed * (gate * (0.5 + 0.5 * jnp.tanh(0.5 * gate)))
-        out_ref[:, cols] = gated
-        total_sq = total_sq + gated * gated
-    sq_ref[...] = jnp.sum(total_sq, axis=1, keepdims=True)
+        cum = cum_ref[sub]
+        cumt = cumt_ref[sub]
+        dtt = dtt_ref[sub]
+        part_col = partc_ref[sub]
+        keep = (row >= col) & (part_col == partr_ref[sub])
+        earlier = 1.0 - part_col
+        total_sq = jnp.zeros((tile_len, 128), f32)
+        for pair in range(pairs):
+            cols = pl.ds(pair * 128, 128)
+            x_pair = x_ref[rows, cols]
+            slabs = []
+            for half in range(2):
+                head = 2 * pair + half
+                diff = cum[:, head : head + 1] - cumt[head : head + 1, :]
+                decay = jnp.where(keep, jnp.exp(jnp.where(keep, diff, 0.0)), 0.0)
+                slabs.append((scores * decay * dtt[head : head + 1, :]).astype(jnp.bfloat16))
+            weights = jnp.concatenate(slabs, axis=1)
+            zero = jnp.zeros_like(x_pair)
+            split_x = jnp.concatenate(
+                [jnp.where(first_half, x_pair, zero), jnp.where(first_half, zero, x_pair)], axis=0
+            )
+            intra = jnp.dot(weights, split_x, preferred_element_type=f32)
+            carried = (
+                before_ref[sub, :, cols] + prefix_ref[sub, :, cols] * enter_ref[:, cols]
+            ).astype(jnp.bfloat16)
+            projected = jnp.dot(c_mat, carried, preferred_element_type=f32)
+            grow = jnp.where(
+                first_half,
+                jnp.exp(cum[:, 2 * pair : 2 * pair + 1]),
+                jnp.exp(cum[:, 2 * pair + 1 : 2 * pair + 2]),
+            )
+            inter = grow * earlier * projected
+            mixed = intra + inter + d_ref[:, cols] * x_pair.astype(f32)
+            gate = gate_ref[rows, cols].astype(f32)
+            gated = mixed * (gate * (0.5 + 0.5 * jnp.tanh(0.5 * gate)))
+            out_ref[rows, cols] = gated
+            total_sq = total_sq + gated * gated
+        sq_ref[rows, :] = jnp.sum(total_sq, axis=1, keepdims=True)
 
 
 def contrib_tile(x_ref, bt_ref, end_ref, pass_ref, before_ref, total_ref):
@@ -104,7 +105,7 @@
 
 def contrib_tiles(conv_out, b_t, to_end, passing_wide, inner_here, state_dim):
     tiles_dev, tile_len, heads_here = to_end.shape
-    group = 2 if tiles_dev % 2 == 0 else 1
+    group = 4 if tiles_dev % 4 == 0 else 1
     return pl.pallas_call(
         contrib_tile,
         grid=(tiles_dev // group,),
@@ -140,28 +141,30 @@
     c_block = b_block + state_dim // 128
     part_col = later.reshape(tiles_dev, tile_len, 1)
     part_row = later.reshape(tiles_dev, 1, tile_len)
+    group = 2 if tiles_dev % 2 == 0 else 1
     per_tile = lambda j: (j, 0, 0)
+    span = group * tile_len
     return pl.pallas_call(
         mix_tile,
-        grid=(tiles_dev,),
+        grid=(tiles_dev // group,),
         in_specs=[
-            pl.BlockSpec((tile_len, inner_here), lambda j: (j, 0)),
-            pl.BlockSpec((tile_len, state_dim), lambda j: (j, b_block)),
-            pl.BlockSpec((tile_len, state_dim), lambda j: (j, c_block)),
-            pl.BlockSpec((1, tile_len, heads_here), per_tile),
-            pl.BlockSpec((1, heads_here, tile_len), per_tile),
-            pl.BlockSpec((1, heads_here, tile_len), per_tile),
-            pl.BlockSpec((1, tile_len, 1), per_tile),
-            pl.BlockSpec((1, 1, tile_len), per_tile),
-            pl.BlockSpec((1, state_dim, inner_here), per_tile),
-            pl.BlockSpec((1, 1, inner_here), per_tile),
+            pl.BlockSpec((span, inner_here), lambda j: (j, 0)),
+            pl.BlockSpec((span, state_dim), lambda j: (j, b_block)),
+            pl.BlockSpec((span, state_dim), lambda j: (j, c_block)),
+            pl.BlockSpec((group, tile_len, heads_here), per_tile),
+            pl.BlockSpec((group, heads_here, tile_len), per_tile),
+            pl.BlockSpec((group, heads_here, tile_len), per_tile),
+            pl.BlockSpec((group, tile_len, 1), per_tile),
+            pl.BlockSpec((group, 1, tile_len), per_tile),
+            pl.BlockSpec((group, state_dim, inner_here), per_tile),
+            pl.BlockSpec((group, 1, inner_here), per_tile),
             pl.BlockSpec((state_dim, inner_here), lambda j: (0, 0)),
-            pl.BlockSpec((tile_len, inner_here), lambda j: (j, 0)),
+            pl.BlockSpec((span, inner_here), lambda j: (j, 0)),
             pl.BlockSpec((1, inner_here), lambda j: (0, 0)),
         ],
         out_specs=[
-            pl.BlockSpec((tile_len, inner_here), lambda j: (j, 0)),
-            pl.BlockSpec((tile_len, 1), lambda j: (j, 0)),
+            pl.BlockSpec((span, inner_here), lambda j: (j, 0)),
+            pl.BlockSpec((span, 1), lambda j: (j, 0)),
         ],
         out_shape=[
             jax.ShapeDtypeStruct((rows, inner_here), jnp.float32),

time: 225 us -> 221 us (0.982)
  Pallas kernels: 32.3 us -> 28.5 us
    pallas_call x1, Pallas kernels: 21.4 us -> 19 us  [mix_tiles(): pl.pallas_call(mix_tile, grid=(tiles_dev // group,), in_specs=[pl.BlockSp...]
where the time goes in v19:
time: 221 us; the launch traced here: 220 us
  blocking collectives  43 us (19%)
  waiting for transfers between devices  36.3 us (16%)
  other arithmetic  35 us (16%)
  matrix products  33.3 us (15%)
  Pallas kernels  28.5 us (13%)
  local copies, waits for them, and re-layouts  23.8 us (11%)
  starting transfers between devices  19 us (9%)
    unnamed x1, blocking collectives  39.5 us
    ppermute x6, waiting for transfers between devices, shifted(): return lax.ppermute(x, axis, pairs)  36.3 us
    dot_general x3, matrix products, project(): jnp.dot(partner_rows, other_part, preferred_element_type=jnp.float32)  20.9 us
    pallas_call x1, Pallas kernels, mix_tiles(): pl.pallas_call(mix_tile, grid=(tiles_dev // group,), in_specs=[pl.BlockSp...  19 us
    convert_element_type x1, other arithmetic, shards(): conv_out = jax.nn.silu(total).astype(jnp.bfloat16)  10.8 us
    ppermute x6, starting transfers between devices, shifted(): return lax.ppermute(x, axis, pairs)  10.7 us
    unnamed x64, local copies, waits for them, and re-layouts  9.97 us
    pallas_call x1, Pallas kernels, contrib_tiles(): pl.pallas_call(contrib_tile, grid=(tiles_dev // group,), in_specs=[pl.Blo...  9.55 us
  transfers between devices with their start and end apart: 8, of which 5 were waited for; matrix products, arithmetic and copies ran while one was open for 14% of the time, Pallas kernels for 0%

profile of v19, /device:TPU:29, one launch (start us, length us, event | category | flops | bytes accessed | tf_op | source)
XLA Modules:
  0.0 220.1 jit_solution(9649793595041875954)
XLA Ops:
  3.0 2.5 %copy.81 = bf16[16,128,512]{2,1,0:T(8,128)(2,1)} copy(bf16[16,128,512]{2,0,1:T(8,128)(2,1)S(1)} %fusion.9) | data formatting | bytes 4194304 | tf_op jit(solution)/shard_map/convert_element_type | solution.py:216
  5.5 6.4 %all-to-all-start = ((bf16[16,128,512]{2,1,0:T(8,128)(2,1)}), bf16[16,128,512]{2,1,0:T(8,128)(2,1)S(1)}, u32[]{:S(2)}, u32[]{:S(2)}) async-start(bf16[16,128,512]{2,1,0:T(8,128)(2,1)} %copy.81), calls=%async_computation | async-start | bytes 4194304 | tf_op jit(solution)/shard_map/all_to_all | solution.py:217
  11.9 5.7 %copy.100 = bf16[128,8,2,1024]{3,1,2,0:T(8,128)(2,1)} copy(bf16[128,8,2,1024]{3,2,1,0:T(2,128)(2,1)} %bitcast.58) | data formatting | bytes 8388608
  19.0 39.5 %all-reduce.1 = s32[256]{0:T(256)S(1)} all-reduce(s32[256]{0:T(256)S(1)} %dynamic-update-slice), channel_id=1, replica_groups=mesh['seq'=16,'head'=2] {'seq'}, use_global_device_ids=true, to_apply=%add.1 | all-reduce | flops 256 | bytes 2048
  68.6 8.2 %fusion.7 = f32[2048,2048]{1,0:T(8,128)} fusion(bf16[2048,512]{1,0:T(8,128)(2,1)S(1)} %bitcast.55, bf16[1024,2048]{1,0:T(8,128)(2,1)S(1)} %bitcast.60, s32[]{:T(128)S(6)} %select_n.90), kind=kOutput, calls=%fused_computation.16 | convolution fusion | flops 4294967296 | bytes 20971524 | tf_op jit(solution)/shard_map/dot_general | solution.py:237
  76.8 14.8 %add_convert_fusion.gate_ref = bf16[2048,2048]{1,0:T(8,128)(2,1)} fusion(f32[2048,2048]{1,0:T(8,128)} %fusion.7, bf16[2048,512]{1,0:T(8,128)(2,1)} %collective-permute-done, bf16[1024,2048]{1,0:T(8,128)(2,1)} %bitcast.59, s32[]{:T(128)S(6)} %select_n.91), kind=kOutput, calls=%fused_computation | convolution fusion | flops 4303355904 | bytes 29360132 | tf_op jit(solution)/shard_map/dot_general | solution.py:237
  91.6 2.6 %slice.153 = bf16[2048,1024]{1,0:T(8,128)(2,1)S(1)} slice(bf16[2048,2048]{1,0:T(8,128)(2,1)} %add_convert_fusion.gate_ref), slice={[0:2048], [1024:2048]} | slice | bytes 8388608 | tf_op jit(solution)/shard_map/slice | solution.py:248
  94.2 3.8 %fusion = bf16[2048,256]{1,0:T(8,128)(2,1)S(1)} fusion(f32[2048,256]{1,0:T(8,128)S(1)} %fusion.21, bf16[2048,512]{1,0:T(8,128)(2,1)} %collective-permute-done, bf16[1024,256]{1,0:T(8,128)(2,1)S(1)} %copy-done.9, s32[]{:T(128)S(6)} %select_n.91), kind=kOutput, calls=%fused_computation.8 | convolution fusion | flops 537919488 | bytes 5505028 | tf_op jit(solution)/shard_map/dot_general | solution.py:237
  98.7 2.7 %collective-permute-start.1 = (bf16[3,1281]{1,0:T(4,128)(2,1)}, bf16[3,1281]{1,0:T(4,128)(2,1)}, u32[]{:S(2)}, u32[]{:S(2)}) collective-permute-start(bf16[3,1281]{1,0:T(4,128)(2,1)} %pad_maximum_fusion.5), channel_id=1, source_target_pairs={{0,2},{2,4},{4,6},{6,8},{8,10},{10,12},{12,14},{14,16},{16,18},{18... | collective-permute-start | bytes 23066 | tf_op jit(solution)/shard_map/ppermute | solution.py:17
  101.4 2.3 %compare_select_fusion = f32[2048,16]{0,1:T(8,128)S(1)} fusion(f32[2048,16]{0,1:T(8,128)S(1)} %fusion.29, bf16[2048,512]{1,0:T(8,128)(2,1)} %collective-permute-done, f32[16]{0:T(128)S(1)} %copy-done.24, bf16[1024,16]{0,1:T(8,128)(2,1)S(1)} %copy-done.10, s32[]{:T(128)S(6)} %select_n.91), kind=kOutput, calls=%fused_computation.31 | convolution fusion | flops 33816576 | bytes 2376196 | tf_op jit(solution)/shard_map/dot_general | solution.py:237
  105.7 2.1 multiply_multiply_fusion.end_ref
  109.4 4.0 %maximum_maximum_fusion = bf16[2051,1280]{1,0:T(8,128)(2,1)S(1)} fusion(bf16[2048,256]{1,0:T(8,128)(2,1)S(1)} %fusion, bf16[2048,1024]{1,0:T(8,128)(2,1)} %copy-done.3, bf16[3,1280]{1,0:T(4,128)(2,1)S(1)} %slice.162), kind=kLoop, calls=%fused_computation.5 | loop fusion | flops 15751680 | bytes 10501120 | tf_op jit(solution)/shard_map/concatenate | solution.py:261
  114.4 10.8 %multiply_convert_fusion.x_ref.b_ref.c_ref = bf16[2048,1280]{1,0:T(8,128)(2,1)S(1)} fusion(bf16[2048,256]{1,0:T(8,128)(2,1)S(1)} %fusion, bf16[2051,1280]{1,0:T(8,128)(2,1)S(1)} %maximum_maximum_fusion, f32[1280]{0:T(1024)S(1)} %copy-done.12, f32[1280]{0:T(1024)S(1)} %copy-done.13, f32[1280]{0:T(1024)S(1)} %copy-done.14, f32[1280]{0:T(1024)S(1)} %copy-done.11, ...), kind=kLoop, calls=%fused_computation.1 | loop fusion | flops 60293120 | bytes 26246144 | tf_op jit(solution)/shard_map/convert_element_type | solution.py:274
  125.2 2.4 %copy-done.2 = bf16[2048,1280]{1,0:T(8,128)(2,1)} copy-done((bf16[2048,1280]{1,0:T(8,128)(2,1)}, bf16[2048,1280]{1,0:T(8,128)(2,1)S(1)}, u32[]{:S(2)}) %copy-start.2) | copy-done | bytes 5242904
  128.7 9.6 %shard_map.136 = (f32[16,128,1024]{2,1,0:T(8,128)}, f32[128,1024]{1,0:T(8,128)}) custom-call(bf16[2048,1280]{1,0:T(8,128)(2,1)} %copy-done.2, bf16[16,128,128]{2,1,0:T(8,128)(2,1)} %bitcast.62, f32[16,128,16]{2,1,0:T(8,128)} %multiply_multiply_fusion.end_ref, f32[16,1,1024]{2,1,0:T(1,128)} %broadcast_in_dim_reshape.10.pass_ref), custom_call_target="tpu_custom_call" | custom-call | flops 536870912 | bytes 13107200 | tf_op jit(solution)/shard_map/pallas_call | solution.py:109
  139.5 1.9 collective-permute-start.2
  141.5 8.7 %collective-permute-done.2 = bf16[131,1024]{1,0:T(8,128)(2,1)S(1)} collective-permute-done((bf16[131,1024]{1,0:T(8,128)(2,1)S(1)}, bf16[131,1024]{1,0:T(8,128)(2,1)S(1)}, u32[]{:S(2)}, u32[]{:S(2)}) %collective-permute-start.2) | collective-permute-done | bytes 268320 | tf_op jit(solution)/shard_map/ppermute | solution.py:17
  152.7 7.6 %collective-permute-done.3 = bf16[131,1024]{1,0:T(8,128)(2,1)S(1)} collective-permute-done((bf16[131,1024]{1,0:T(8,128)(2,1)S(1)}, bf16[131,1024]{1,0:T(8,128)(2,1)S(1)}, u32[]{:S(2)}, u32[]{:S(2)}) %collective-permute-start.3) | collective-permute-done | bytes 268320 | tf_op jit(solution)/shard_map/ppermute | solution.py:17
  163.1 5.6 %collective-permute-done.4 = bf16[131,1024]{1,0:T(8,128)(2,1)S(1)} collective-permute-done((bf16[131,1024]{1,0:T(8,128)(2,1)S(1)}, bf16[131,1024]{1,0:T(8,128)(2,1)S(1)}, u32[]{:S(2)}, u32[]{:S(2)}) %collective-permute-start.4) | collective-permute-done | bytes 268320 | tf_op jit(solution)/shard_map/ppermute | solution.py:17
  168.8 2.3 %collective-permute-start.5 = (bf16[131,1024]{1,0:T(8,128)(2,1)S(1)}, bf16[131,1024]{1,0:T(8,128)(2,1)S(1)}, u32[]{:S(2)}, u32[]{:S(2)}) collective-permute-start(bf16[131,1024]{1,0:T(8,128)(2,1)S(1)} %pad_maximum_fusion.4), channel_id=1, source_target_pairs={{0,2},{2,4},{4,6},{6,8},{8,10},{10,12},{12,14},{14,16},{16,18},{18... | collective-permute-start | bytes 804872 | tf_op jit(solution)/shard_map/ppermute | solution.py:17
  177.1 12.7 %collective-permute-done.6 = bf16[128,1024]{1,0:T(8,128)(2,1)S(1)} collective-permute-done((bf16[128,1024]{1,0:T(8,128)(2,1)S(1)}, bf16[128,1024]{1,0:T(8,128)(2,1)S(1)}, u32[]{:S(2)}, u32[]{:S(2)}) %collective-permute-start.6) | collective-permute-done | bytes 262176 | tf_op jit(solution)/shard_map/ppermute | solution.py:17
  190.7 19.0 %shard_map.137 = (f32[2048,1024]{1,0:T(8,128)}, f32[2048,1]{1,0:T(8,128)}) custom-call(bf16[2048,1280]{1,0:T(8,128)(2,1)} %copy-done.2, bf16[2048,1280]{1,0:T(8,128)(2,1)} %copy-done.2, bf16[2048,1280]{1,0:T(8,128)(2,1)} %copy-done.2, f32[16,128,16]{2,1,0:T(8,128)} %bitcast.57, f32[16,16,128]{2,1,0:T(8,128)} %copy-done.8, ...), custom_call_target="tpu_custom_call" | custom-call | flops 3288334336 | bytes 29360128 | tf_op jit(solution)/shard_map/pallas_call | solution.py:147
  211.2 3.5 %psum.7 = f32[16,128]{1,0:T(8,128)S(1)} all-reduce(f32[16,128]{1,0:T(8,128)S(1)} %bitcast.69), channel_id=1, replica_groups=mesh['seq'=16,'head'=2] {'head'}, use_global_device_ids=true, to_apply=%region_3.4 | all-reduce | flops 2048 | bytes 16384 | tf_op jit(solution)/shard_map/psum | solution.py:323
  214.8 5.3 %multiply_convert_fusion.1 = bf16[2048,1024]{1,0:T(8,128)(2,1)} fusion(f32[2048,1024]{1,0:T(8,128)} %get-tuple-element.15, f32[1024]{0:T(1024)S(1)} %copy-done.20, f32[2048]{0:T(1024)S(1)} %rsqrt_bitcast_fusion), kind=kLoop, calls=%fused_computation.2 | loop fusion | flops 6291456 | bytes 12595200 | tf_op jit(solution)/shard_map/convert_element_type | solution.py:324
  (145 shorter events, 35.1 us)
Async XLA Ops:
  5.5 56.4 %all-to-all-start = ((bf16[16,128,512]{2,1,0:T(8,128)(2,1)}), bf16[16,128,512]{2,1,0:T(8,128)(2,1)S(1)}, u32[]{:S(2)}, u32[]{:S(2)}) async-start(bf16[16,128,512]{2,1,0:T(8,128)(2,1)} %copy.81), calls=%async_computation | async-start | bytes 4194304 | tf_op jit(solution)/shard_map/all_to_all | solution.py:217
  11.9 6.9 %copy-start.26 = (s32[16]{0:T(128)S(1)}, s32[16]{0:T(128)}, u32[]{:S(2)}) copy-start(s32[16]{0:T(128)} %param.15) | copy-start | bytes 196
  11.9 46.6 %copy-start.17 = (s32[16]{0:T(128)S(1)}, s32[16]{0:T(128)}, u32[]{:S(2)}) copy-start(s32[16]{0:T(128)} %param.16) | copy-start | bytes 196
  11.9 48.2 %copy-start.21 = (f32[1024]{0:T(1024)S(1)}, f32[1024]{0:T(1024)}, u32[]{:S(2)}) copy-start(f32[1024]{0:T(1024)} %param.24) | copy-start | bytes 12292
  11.9 48.2 %copy-start.23 = (f32[256]{0:T(256)S(1)}, f32[256]{0:T(256)}, u32[]{:S(2)}) copy-start(f32[256]{0:T(256)} %param.25) | copy-start | bytes 3076
  11.9 48.5 %copy-start.19 = (f32[4,1024]{1,0:T(4,128)S(1)}, f32[4,1024]{1,0:T(4,128)}, u32[]{:S(2)}) copy-start(f32[4,1024]{1,0:T(4,128)} %param.22) | copy-start | bytes 49156
  11.9 48.6 %copy-start.27 = (f32[16]{0:T(128)S(1)}, f32[16]{0:T(128)}, u32[]{:S(2)}) copy-start(f32[16]{0:T(128)} %param.21) | copy-start | bytes 196
  17.6 48.7 %copy-start.22 = (f32[4,256]{1,0:T(4,128)S(1)}, f32[4,256]{1,0:T(4,128)}, u32[]{:S(2)}) copy-start(f32[4,256]{1,0:T(4,128)} %param.23) | copy-start | bytes 12292
  17.6 49.5 %copy-start.10 = (bf16[1024,16]{0,1:T(8,128)(2,1)S(1)}, bf16[1024,16]{0,1:T(8,128)(2,1)}, u32[]{:S(2)}) copy-start(bf16[1024,16]{0,1:T(8,128)(2,1)} %param.19) | copy-start | bytes 98308
  59.4 7.0 %copy-start.15 = (f32[2048]{0:T(1024)}, f32[2048]{0:T(1024)S(1)}, u32[]{:S(2)}) copy-start(f32[2048]{0:T(1024)S(1)} %add_bitcast_fusion) | copy-start | bytes 24580
  64.4 12.4 %collective-permute-start = (bf16[2048,512]{1,0:T(8,128)(2,1)S(1)}, bf16[2048,512]{1,0:T(8,128)(2,1)}, u32[]{:S(2)}, u32[]{:S(2)}) collective-permute-start(bf16[2048,512]{1,0:T(8,128)(2,1)S(1)} %bitcast.52), channel_id=1, source_target_pairs={{0,1},{1,0},{2,3},{3,2},{4,5},{5,4},{6,7},{7,6},{8,9},{9,8},{10,11... | collective-permute-start | bytes 6291464 | tf_op jit(solution)/shard_map/ppermute | solution.py:230
  94.2 7.1 %copy-start.24 = (f32[16]{0:T(128)S(1)}, f32[16]{0:T(128)}, u32[]{:S(2)}) copy-start(f32[16]{0:T(128)} %param.20) | copy-start | bytes 196
  98.7 10.0 %collective-permute-start.1 = (bf16[3,1281]{1,0:T(4,128)(2,1)}, bf16[3,1281]{1,0:T(4,128)(2,1)}, u32[]{:S(2)}, u32[]{:S(2)}) collective-permute-start(bf16[3,1281]{1,0:T(4,128)(2,1)} %pad_maximum_fusion.5), channel_id=1, source_target_pairs={{0,2},{2,4},{4,6},{6,8},{8,10},{10,12},{12,14},{14,16},{16,18},{18... | collective-permute-start | bytes 23066 | tf_op jit(solution)/shard_map/ppermute | solution.py:17
  104.0 9.5 %copy-start.8 = (f32[16,16,128]{2,1,0:T(8,128)}, f32[16,16,128]{2,1,0:T(8,128)S(1)}, u32[]{:S(2)}) copy-start(f32[16,16,128]{2,1,0:T(8,128)S(1)} %fusion.24.cumt_ref) | copy-start | bytes 393220
  104.4 9.1 %copy-start.5 = (f32[16,16,128]{1,2,0:T(8,128)}, f32[16,16,128]{1,2,0:T(8,128)S(1)}, u32[]{:S(2)}) copy-start(f32[16,16,128]{1,2,0:T(8,128)S(1)} %copy.91) | copy-start | bytes 393220
  138.2 22.2 %copy-start.6 = (f32[128,1024]{1,0:T(8,128)S(1)}, f32[128,1024]{1,0:T(8,128)}, u32[]{:S(2)}) copy-start(f32[128,1024]{1,0:T(8,128)} %get-tuple-element.14) | copy-start | bytes 1572868
  138.3 23.7 %copy-start.18 = (s32[16]{0:T(128)S(1)}, s32[16]{0:T(128)}, u32[]{:S(2)}) copy-start(s32[16]{0:T(128)} %param.16) | copy-start | bytes 196
  139.4 32.4 %copy-start.25 = (f32[16]{0:T(128)S(1)}, f32[16]{0:T(128)}, u32[]{:S(2)}) copy-start(f32[16]{0:T(128)} %param.26) | copy-start | bytes 196
  139.5 10.7 %collective-permute-start.2 = (bf16[131,1024]{1,0:T(8,128)(2,1)S(1)}, bf16[131,1024]{1,0:T(8,128)(2,1)S(1)}, u32[]{:S(2)}, u32[]{:S(2)}) collective-permute-start(bf16[131,1024]{1,0:T(8,128)(2,1)S(1)} %pad_maximum_fusion.1), channel_id=1, source_target_pairs={{0,2},{2,4},{4,6},{6,8},{8,10},{10,12},{12,14},{14,16},{16,18},{18... | collective-permute-start | bytes 804872 | tf_op jit(solution)/shard_map/ppermute | solution.py:17
  151.4 8.9 %collective-permute-start.3 = (bf16[131,1024]{1,0:T(8,128)(2,1)S(1)}, bf16[131,1024]{1,0:T(8,128)(2,1)S(1)}, u32[]{:S(2)}, u32[]{:S(2)}) collective-permute-start(bf16[131,1024]{1,0:T(8,128)(2,1)S(1)} %pad_maximum_fusion.2), channel_id=1, source_target_pairs={{0,4},{2,6},{4,8},{6,10},{8,12},{10,14},{12,16},{14,18},{16,20},{1... | collective-permute-start | bytes 804872 | tf_op jit(solution)/shard_map/ppermute | solution.py:17
  160.6 8.0 %collective-permute-start.4 = (bf16[131,1024]{1,0:T(8,128)(2,1)S(1)}, bf16[131,1024]{1,0:T(8,128)(2,1)S(1)}, u32[]{:S(2)}, u32[]{:S(2)}) collective-permute-start(bf16[131,1024]{1,0:T(8,128)(2,1)S(1)} %pad_maximum_fusion.3), channel_id=1, source_target_pairs={{0,8},{2,10},{4,12},{6,14},{8,16},{10,18},{12,20},{14,22},{16,24},... | collective-permute-start | bytes 804872 | tf_op jit(solution)/shard_map/ppermute | solution.py:17
  168.8 8.2 %collective-permute-start.5 = (bf16[131,1024]{1,0:T(8,128)(2,1)S(1)}, bf16[131,1024]{1,0:T(8,128)(2,1)S(1)}, u32[]{:S(2)}, u32[]{:S(2)}) collective-permute-start(bf16[131,1024]{1,0:T(8,128)(2,1)S(1)} %pad_maximum_fusion.4), channel_id=1, source_target_pairs={{0,2},{2,4},{4,6},{6,8},{8,10},{10,12},{12,14},{14,16},{16,18},{18... | collective-permute-start | bytes 804872 | tf_op jit(solution)/shard_map/ppermute | solution.py:17
  172.5 17.2 %collective-permute-start.6 = (bf16[128,1024]{1,0:T(8,128)(2,1)S(1)}, bf16[128,1024]{1,0:T(8,128)(2,1)S(1)}, u32[]{:S(2)}, u32[]{:S(2)}) collective-permute-start(bf16[128,1024]{1,0:T(8,128)(2,1)S(1)} %fusion.17), channel_id=1, source_target_pairs={{0,18},{2,20},{4,22},{6,24},{8,26},{10,28},{12,30},{1,19},{3,21},{... | collective-permute-start | bytes 786440 | tf_op jit(solution)/shard_map/ppermute | solution.py:17
  190.7 24.1 %copy-start.20 = (f32[1024]{0:T(1024)S(1)}, f32[1024]{0:T(1024)}, u32[]{:S(2)}) copy-start(f32[1024]{0:T(1024)} %param.27) | copy-start | bytes 12292
  (13 other events, 56.9 us)

commit v20 on v19

--- a/solution.py
+++ b/solution.py
@@ -105,7 +105,7 @@
 
 def contrib_tiles(conv_out, b_t, to_end, passing_wide, inner_here, state_dim):
     tiles_dev, tile_len, heads_here = to_end.shape
-    group = 4 if tiles_dev % 4 == 0 else 1
+    group = 8 if tiles_dev % 8 == 0 else 1
     return pl.pallas_call(
         contrib_tile,
         grid=(tiles_dev // group,),
@@ -141,7 +141,7 @@
     c_block = b_block + state_dim // 128
     part_col = later.reshape(tiles_dev, tile_len, 1)
     part_row = later.reshape(tiles_dev, 1, tile_len)
-    group = 2 if tiles_dev % 2 == 0 else 1
+    group = 4 if tiles_dev % 4 == 0 else 1
     per_tile = lambda j: (j, 0, 0)
     span = group * tile_len
     return pl.pallas_call(

time: 221 us -> 223 us (level)
  Pallas kernels: 28.5 us -> 31 us
where the time goes in v20:
time: 223 us
  blocking collectives  43 us (19%)
  waiting for transfers between devices  36 us (16%)
  other arithmetic  35 us (16%)
  matrix products  33.3 us (15%)
  Pallas kernels  31 us (14%)
  local copies, waits for them, and re-layouts  23.8 us (11%)
  starting transfers between devices  19.3 us (9%)
    unnamed x1, blocking collectives  39.5 us
    ppermute x6, waiting for transfers between devices, shifted(): return lax.ppermute(x, axis, pairs)  36 us
    dot_general x3, matrix products, project(): jnp.dot(partner_rows, other_part, preferred_element_type=jnp.float32)  20.9 us
    pallas_call x1, Pallas kernels, mix_tiles(): pl.pallas_call(mix_tile, grid=(tiles_dev // group,), in_specs=[pl.BlockSp...  20.8 us
    ppermute x6, starting transfers between devices, shifted(): return lax.ppermute(x, axis, pairs)  11 us
    convert_element_type x1, other arithmetic, shards(): conv_out = jax.nn.silu(total).astype(jnp.bfloat16)  10.8 us
    pallas_call x1, Pallas kernels, contrib_tiles(): pl.pallas_call(contrib_tile, grid=(tiles_dev // group,), in_specs=[pl.Blo...  10.3 us
    unnamed x64, local copies, waits for them, and re-layouts  9.97 us
  transfers between devices with their start and end apart: 8, of which 5 were waited for; matrix products, arithmetic and copies ran while one was open for 14% of the time, Pallas kernels for 0%

profile of v20, /device:TPU:29, one launch (start us, length us, event | category | flops | bytes accessed | tf_op | source)
XLA Modules:
  0.0 222.6 jit_solution(15527587143337225274)
XLA Ops:
  3.0 2.5 %copy.81 = bf16[16,128,512]{2,1,0:T(8,128)(2,1)} copy(bf16[16,128,512]{2,0,1:T(8,128)(2,1)S(1)} %fusion.9) | data formatting | bytes 4194304 | tf_op jit(solution)/shard_map/convert_element_type | solution.py:216
  5.5 6.4 %all-to-all-start = ((bf16[16,128,512]{2,1,0:T(8,128)(2,1)}), bf16[16,128,512]{2,1,0:T(8,128)(2,1)S(1)}, u32[]{:S(2)}, u32[]{:S(2)}) async-start(bf16[16,128,512]{2,1,0:T(8,128)(2,1)} %copy.81), calls=%async_computation | async-start | bytes 4194304 | tf_op jit(solution)/shard_map/all_to_all | solution.py:217
  11.9 5.7 %copy.100 = bf16[128,8,2,1024]{3,1,2,0:T(8,128)(2,1)} copy(bf16[128,8,2,1024]{3,2,1,0:T(2,128)(2,1)} %bitcast.58) | data formatting | bytes 8388608
  19.0 39.5 %all-reduce.1 = s32[256]{0:T(256)S(1)} all-reduce(s32[256]{0:T(256)S(1)} %dynamic-update-slice), channel_id=1, replica_groups=mesh['seq'=16,'head'=2] {'seq'}, use_global_device_ids=true, to_apply=%add.1 | all-reduce | flops 256 | bytes 2048
  68.6 8.2 %fusion.7 = f32[2048,2048]{1,0:T(8,128)} fusion(bf16[2048,512]{1,0:T(8,128)(2,1)S(1)} %bitcast.55, bf16[1024,2048]{1,0:T(8,128)(2,1)S(1)} %bitcast.60, s32[]{:T(128)S(6)} %select_n.90), kind=kOutput, calls=%fused_computation.16 | convolution fusion | flops 4294967296 | bytes 20971524 | tf_op jit(solution)/shard_map/dot_general | solution.py:237
  76.8 14.8 %add_convert_fusion.gate_ref = bf16[2048,2048]{1,0:T(8,128)(2,1)} fusion(f32[2048,2048]{1,0:T(8,128)} %fusion.7, bf16[2048,512]{1,0:T(8,128)(2,1)} %collective-permute-done, bf16[1024,2048]{1,0:T(8,128)(2,1)} %bitcast.59, s32[]{:T(128)S(6)} %select_n.91), kind=kOutput, calls=%fused_computation | convolution fusion | flops 4303355904 | bytes 29360132 | tf_op jit(solution)/shard_map/dot_general | solution.py:237
  91.6 2.6 %slice.153 = bf16[2048,1024]{1,0:T(8,128)(2,1)S(1)} slice(bf16[2048,2048]{1,0:T(8,128)(2,1)} %add_convert_fusion.gate_ref), slice={[0:2048], [1024:2048]} | slice | bytes 8388608 | tf_op jit(solution)/shard_map/slice | solution.py:248
  94.2 3.8 %fusion = bf16[2048,256]{1,0:T(8,128)(2,1)S(1)} fusion(f32[2048,256]{1,0:T(8,128)S(1)} %fusion.21, bf16[2048,512]{1,0:T(8,128)(2,1)} %collective-permute-done, bf16[1024,256]{1,0:T(8,128)(2,1)S(1)} %copy-done.9, s32[]{:T(128)S(6)} %select_n.91), kind=kOutput, calls=%fused_computation.8 | convolution fusion | flops 537919488 | bytes 5505028 | tf_op jit(solution)/shard_map/dot_general | solution.py:237
  98.7 2.7 %collective-permute-start.1 = (bf16[3,1281]{1,0:T(4,128)(2,1)}, bf16[3,1281]{1,0:T(4,128)(2,1)}, u32[]{:S(2)}, u32[]{:S(2)}) collective-permute-start(bf16[3,1281]{1,0:T(4,128)(2,1)} %pad_maximum_fusion.5), channel_id=1, source_target_pairs={{0,2},{2,4},{4,6},{6,8},{8,10},{10,12},{12,14},{14,16},{16,18},{18... | collective-permute-start | bytes 23066 | tf_op jit(solution)/shard_map/ppermute | solution.py:17
  101.4 2.3 %compare_select_fusion = f32[2048,16]{0,1:T(8,128)S(1)} fusion(f32[2048,16]{0,1:T(8,128)S(1)} %fusion.29, bf16[2048,512]{1,0:T(8,128)(2,1)} %collective-permute-done, f32[16]{0:T(128)S(1)} %copy-done.24, bf16[1024,16]{0,1:T(8,128)(2,1)S(1)} %copy-done.10, s32[]{:T(128)S(6)} %select_n.91), kind=kOutput, calls=%fused_computation.31 | convolution fusion | flops 33816576 | bytes 2376196 | tf_op jit(solution)/shard_map/dot_general | solution.py:237
  105.7 2.1 multiply_multiply_fusion.end_ref
  109.4 4.0 %maximum_maximum_fusion = bf16[2051,1280]{1,0:T(8,128)(2,1)S(1)} fusion(bf16[2048,256]{1,0:T(8,128)(2,1)S(1)} %fusion, bf16[2048,1024]{1,0:T(8,128)(2,1)} %copy-done.3, bf16[3,1280]{1,0:T(4,128)(2,1)S(1)} %slice.162), kind=kLoop, calls=%fused_computation.5 | loop fusion | flops 15751680 | bytes 10501120 | tf_op jit(solution)/shard_map/concatenate | solution.py:261
  114.4 10.8 %multiply_convert_fusion.x_ref.b_ref.c_ref = bf16[2048,1280]{1,0:T(8,128)(2,1)S(1)} fusion(bf16[2048,256]{1,0:T(8,128)(2,1)S(1)} %fusion, bf16[2051,1280]{1,0:T(8,128)(2,1)S(1)} %maximum_maximum_fusion, f32[1280]{0:T(1024)S(1)} %copy-done.12, f32[1280]{0:T(1024)S(1)} %copy-done.13, f32[1280]{0:T(1024)S(1)} %copy-done.14, f32[1280]{0:T(1024)S(1)} %copy-done.11, ...), kind=kLoop, calls=%fused_computation.1 | loop fusion | flops 60293120 | bytes 26246144 | tf_op jit(solution)/shard_map/convert_element_type | solution.py:274
  125.2 2.4 %copy-done.2 = bf16[2048,1280]{1,0:T(8,128)(2,1)} copy-done((bf16[2048,1280]{1,0:T(8,128)(2,1)}, bf16[2048,1280]{1,0:T(8,128)(2,1)S(1)}, u32[]{:S(2)}) %copy-start.2) | copy-done | bytes 5242904
  128.7 10.3 %shard_map.136 = (f32[16,128,1024]{2,1,0:T(8,128)}, f32[128,1024]{1,0:T(8,128)}) custom-call(bf16[2048,1280]{1,0:T(8,128)(2,1)} %copy-done.2, bf16[16,128,128]{2,1,0:T(8,128)(2,1)} %bitcast.62, f32[16,128,16]{2,1,0:T(8,128)} %multiply_multiply_fusion.end_ref, f32[16,1,1024]{2,1,0:T(1,128)} %broadcast_in_dim_reshape.10.pass_ref), custom_call_target="tpu_custom_call" | custom-call | flops 536870912 | bytes 13107200 | tf_op jit(solution)/shard_map/pallas_call | solution.py:109
  140.2 1.9 collective-permute-start.2
  142.2 8.7 %collective-permute-done.2 = bf16[131,1024]{1,0:T(8,128)(2,1)S(1)} collective-permute-done((bf16[131,1024]{1,0:T(8,128)(2,1)S(1)}, bf16[131,1024]{1,0:T(8,128)(2,1)S(1)}, u32[]{:S(2)}, u32[]{:S(2)}) %collective-permute-start.2) | collective-permute-done | bytes 268320 | tf_op jit(solution)/shard_map/ppermute | solution.py:17
  153.4 7.6 %collective-permute-done.3 = bf16[131,1024]{1,0:T(8,128)(2,1)S(1)} collective-permute-done((bf16[131,1024]{1,0:T(8,128)(2,1)S(1)}, bf16[131,1024]{1,0:T(8,128)(2,1)S(1)}, u32[]{:S(2)}, u32[]{:S(2)}) %collective-permute-start.3) | collective-permute-done | bytes 268320 | tf_op jit(solution)/shard_map/ppermute | solution.py:17
  163.8 5.6 %collective-permute-done.4 = bf16[131,1024]{1,0:T(8,128)(2,1)S(1)} collective-permute-done((bf16[131,1024]{1,0:T(8,128)(2,1)S(1)}, bf16[131,1024]{1,0:T(8,128)(2,1)S(1)}, u32[]{:S(2)}, u32[]{:S(2)}) %collective-permute-start.4) | collective-permute-done | bytes 268320 | tf_op jit(solution)/shard_map/ppermute | solution.py:17
  169.5 2.3 %collective-permute-start.5 = (bf16[131,1024]{1,0:T(8,128)(2,1)S(1)}, bf16[131,1024]{1,0:T(8,128)(2,1)S(1)}, u32[]{:S(2)}, u32[]{:S(2)}) collective-permute-start(bf16[131,1024]{1,0:T(8,128)(2,1)S(1)} %pad_maximum_fusion.4), channel_id=1, source_target_pairs={{0,2},{2,4},{4,6},{6,8},{8,10},{10,12},{12,14},{14,16},{16,18},{18... | collective-permute-start | bytes 804872 | tf_op jit(solution)/shard_map/ppermute | solution.py:17
  177.8 12.6 %collective-permute-done.6 = bf16[128,1024]{1,0:T(8,128)(2,1)S(1)} collective-permute-done((bf16[128,1024]{1,0:T(8,128)(2,1)S(1)}, bf16[128,1024]{1,0:T(8,128)(2,1)S(1)}, u32[]{:S(2)}, u32[]{:S(2)}) %collective-permute-start.6) | collective-permute-done | bytes 262176 | tf_op jit(solution)/shard_map/ppermute | solution.py:17
  191.3 20.8 %shard_map.137 = (f32[2048,1024]{1,0:T(8,128)}, f32[2048,1]{1,0:T(8,128)}) custom-call(bf16[2048,1280]{1,0:T(8,128)(2,1)} %copy-done.2, bf16[2048,1280]{1,0:T(8,128)(2,1)} %copy-done.2, bf16[2048,1280]{1,0:T(8,128)(2,1)} %copy-done.2, f32[16,128,16]{2,1,0:T(8,128)} %bitcast.57, f32[16,16,128]{2,1,0:T(8,128)} %copy-done.8, ...), custom_call_target="tpu_custom_call" | custom-call | flops 3288334336 | bytes 29360128 | tf_op jit(solution)/shard_map/pallas_call | solution.py:147
  213.7 3.6 %psum.7 = f32[16,128]{1,0:T(8,128)S(1)} all-reduce(f32[16,128]{1,0:T(8,128)S(1)} %bitcast.69), channel_id=1, replica_groups=mesh['seq'=16,'head'=2] {'head'}, use_global_device_ids=true, to_apply=%region_3.4 | all-reduce | flops 2048 | bytes 16384 | tf_op jit(solution)/shard_map/psum | solution.py:323
  217.3 5.3 %multiply_convert_fusion.1 = bf16[2048,1024]{1,0:T(8,128)(2,1)} fusion(f32[2048,1024]{1,0:T(8,128)} %get-tuple-element.15, f32[1024]{0:T(1024)S(1)} %copy-done.20, f32[2048]{0:T(1024)S(1)} %rsqrt_bitcast_fusion), kind=kLoop, calls=%fused_computation.2 | loop fusion | flops 6291456 | bytes 12595200 | tf_op jit(solution)/shard_map/convert_element_type | solution.py:324
  (145 shorter events, 35.1 us)
Async XLA Ops:
  5.5 56.4 %all-to-all-start = ((bf16[16,128,512]{2,1,0:T(8,128)(2,1)}), bf16[16,128,512]{2,1,0:T(8,128)(2,1)S(1)}, u32[]{:S(2)}, u32[]{:S(2)}) async-start(bf16[16,128,512]{2,1,0:T(8,128)(2,1)} %copy.81), calls=%async_computation | async-start | bytes 4194304 | tf_op jit(solution)/shard_map/all_to_all | solution.py:217
  11.9 6.9 %copy-start.26 = (s32[16]{0:T(128)S(1)}, s32[16]{0:T(128)}, u32[]{:S(2)}) copy-start(s32[16]{0:T(128)} %param.15) | copy-start | bytes 196
  11.9 46.6 %copy-start.17 = (s32[16]{0:T(128)S(1)}, s32[16]{0:T(128)}, u32[]{:S(2)}) copy-start(s32[16]{0:T(128)} %param.16) | copy-start | bytes 196
  11.9 48.2 %copy-start.21 = (f32[1024]{0:T(1024)S(1)}, f32[1024]{0:T(1024)}, u32[]{:S(2)}) copy-start(f32[1024]{0:T(1024)} %param.24) | copy-start | bytes 12292
  11.9 48.2 %copy-start.23 = (f32[256]{0:T(256)S(1)}, f32[256]{0:T(256)}, u32[]{:S(2)}) copy-start(f32[256]{0:T(256)} %param.25) | copy-start | bytes 3076
  11.9 48.5 %copy-start.19 = (f32[4,1024]{1,0:T(4,128)S(1)}, f32[4,1024]{1,0:T(4,128)}, u32[]{:S(2)}) copy-start(f32[4,1024]{1,0:T(4,128)} %param.22) | copy-start | bytes 49156
  11.9 48.6 %copy-start.27 = (f32[16]{0:T(128)S(1)}, f32[16]{0:T(128)}, u32[]{:S(2)}) copy-start(f32[16]{0:T(128)} %param.21) | copy-start | bytes 196
  17.6 48.7 %copy-start.22 = (f32[4,256]{1,0:T(4,128)S(1)}, f32[4,256]{1,0:T(4,128)}, u32[]{:S(2)}) copy-start(f32[4,256]{1,0:T(4,128)} %param.23) | copy-start | bytes 12292
  17.6 49.5 %copy-start.10 = (bf16[1024,16]{0,1:T(8,128)(2,1)S(1)}, bf16[1024,16]{0,1:T(8,128)(2,1)}, u32[]{:S(2)}) copy-start(bf16[1024,16]{0,1:T(8,128)(2,1)} %param.19) | copy-start | bytes 98308
  59.4 7.0 %copy-start.15 = (f32[2048]{0:T(1024)}, f32[2048]{0:T(1024)S(1)}, u32[]{:S(2)}) copy-start(f32[2048]{0:T(1024)S(1)} %add_bitcast_fusion) | copy-start | bytes 24580
  64.4 12.4 %collective-permute-start = (bf16[2048,512]{1,0:T(8,128)(2,1)S(1)}, bf16[2048,512]{1,0:T(8,128)(2,1)}, u32[]{:S(2)}, u32[]{:S(2)}) collective-permute-start(bf16[2048,512]{1,0:T(8,128)(2,1)S(1)} %bitcast.52), channel_id=1, source_target_pairs={{0,1},{1,0},{2,3},{3,2},{4,5},{5,4},{6,7},{7,6},{8,9},{9,8},{10,11... | collective-permute-start | bytes 6291464 | tf_op jit(solution)/shard_map/ppermute | solution.py:230
  94.2 7.1 %copy-start.24 = (f32[16]{0:T(128)S(1)}, f32[16]{0:T(128)}, u32[]{:S(2)}) copy-start(f32[16]{0:T(128)} %param.20) | copy-start | bytes 196
  98.7 10.0 %collective-permute-start.1 = (bf16[3,1281]{1,0:T(4,128)(2,1)}, bf16[3,1281]{1,0:T(4,128)(2,1)}, u32[]{:S(2)}, u32[]{:S(2)}) collective-permute-start(bf16[3,1281]{1,0:T(4,128)(2,1)} %pad_maximum_fusion.5), channel_id=1, source_target_pairs={{0,2},{2,4},{4,6},{6,8},{8,10},{10,12},{12,14},{14,16},{16,18},{18... | collective-permute-start | bytes 23066 | tf_op jit(solution)/shard_map/ppermute | solution.py:17
  104.0 9.5 %copy-start.8 = (f32[16,16,128]{2,1,0:T(8,128)}, f32[16,16,128]{2,1,0:T(8,128)S(1)}, u32[]{:S(2)}) copy-start(f32[16,16,128]{2,1,0:T(8,128)S(1)} %fusion.24.cumt_ref) | copy-start | bytes 393220
  104.4 9.1 %copy-start.5 = (f32[16,16,128]{1,2,0:T(8,128)}, f32[16,16,128]{1,2,0:T(8,128)S(1)}, u32[]{:S(2)}) copy-start(f32[16,16,128]{1,2,0:T(8,128)S(1)} %copy.91) | copy-start | bytes 393220
  138.9 22.2 %copy-start.6 = (f32[128,1024]{1,0:T(8,128)S(1)}, f32[128,1024]{1,0:T(8,128)}, u32[]{:S(2)}) copy-start(f32[128,1024]{1,0:T(8,128)} %get-tuple-element.14) | copy-start | bytes 1572868
  139.0 23.7 %copy-start.18 = (s32[16]{0:T(128)S(1)}, s32[16]{0:T(128)}, u32[]{:S(2)}) copy-start(s32[16]{0:T(128)} %param.16) | copy-start | bytes 196
  140.1 32.3 %copy-start.25 = (f32[16]{0:T(128)S(1)}, f32[16]{0:T(128)}, u32[]{:S(2)}) copy-start(f32[16]{0:T(128)} %param.26) | copy-start | bytes 196
  140.2 10.7 %collective-permute-start.2 = (bf16[131,1024]{1,0:T(8,128)(2,1)S(1)}, bf16[131,1024]{1,0:T(8,128)(2,1)S(1)}, u32[]{:S(2)}, u32[]{:S(2)}) collective-permute-start(bf16[131,1024]{1,0:T(8,128)(2,1)S(1)} %pad_maximum_fusion.1), channel_id=1, source_target_pairs={{0,2},{2,4},{4,6},{6,8},{8,10},{10,12},{12,14},{14,16},{16,18},{18... | collective-permute-start | bytes 804872 | tf_op jit(solution)/shard_map/ppermute | solution.py:17
  152.1 8.9 %collective-permute-start.3 = (bf16[131,1024]{1,0:T(8,128)(2,1)S(1)}, bf16[131,1024]{1,0:T(8,128)(2,1)S(1)}, u32[]{:S(2)}, u32[]{:S(2)}) collective-permute-start(bf16[131,1024]{1,0:T(8,128)(2,1)S(1)} %pad_maximum_fusion.2), channel_id=1, source_target_pairs={{0,4},{2,6},{4,8},{6,10},{8,12},{10,14},{12,16},{14,18},{16,20},{1... | collective-permute-start | bytes 804872 | tf_op jit(solution)/shard_map/ppermute | solution.py:17
  161.3 8.0 %collective-permute-start.4 = (bf16[131,1024]{1,0:T(8,128)(2,1)S(1)}, bf16[131,1024]{1,0:T(8,128)(2,1)S(1)}, u32[]{:S(2)}, u32[]{:S(2)}) collective-permute-start(bf16[131,1024]{1,0:T(8,128)(2,1)S(1)} %pad_maximum_fusion.3), channel_id=1, source_target_pairs={{0,8},{2,10},{4,12},{6,14},{8,16},{10,18},{12,20},{14,22},{16,24},... | collective-permute-start | bytes 804872 | tf_op jit(solution)/shard_map/ppermute | solution.py:17
  169.5 8.2 %collective-permute-start.5 = (bf16[131,1024]{1,0:T(8,128)(2,1)S(1)}, bf16[131,1024]{1,0:T(8,128)(2,1)S(1)}, u32[]{:S(2)}, u32[]{:S(2)}) collective-permute-start(bf16[131,1024]{1,0:T(8,128)(2,1)S(1)} %pad_maximum_fusion.4), channel_id=1, source_target_pairs={{0,2},{2,4},{4,6},{6,8},{8,10},{10,12},{12,14},{14,16},{16,18},{18... | collective-permute-start | bytes 804872 | tf_op jit(solution)/shard_map/ppermute | solution.py:17
  173.2 17.2 %collective-permute-start.6 = (bf16[128,1024]{1,0:T(8,128)(2,1)S(1)}, bf16[128,1024]{1,0:T(8,128)(2,1)S(1)}, u32[]{:S(2)}, u32[]{:S(2)}) collective-permute-start(bf16[128,1024]{1,0:T(8,128)(2,1)S(1)} %fusion.17), channel_id=1, source_target_pairs={{0,18},{2,20},{4,22},{6,24},{8,26},{10,28},{12,30},{1,19},{3,21},{... | collective-permute-start | bytes 786440 | tf_op jit(solution)/shard_map/ppermute | solution.py:17
  191.3 25.9 %copy-start.20 = (f32[1024]{0:T(1024)S(1)}, f32[1024]{0:T(1024)}, u32[]{:S(2)}) copy-start(f32[1024]{0:T(1024)} %param.27) | copy-start | bytes 12292
  (13 other events, 56.9 us)

commit v21 on v19

--- a/solution.py
+++ b/solution.py
@@ -71,7 +71,7 @@
             gated = mixed * (gate * (0.5 + 0.5 * jnp.tanh(0.5 * gate)))
             out_ref[rows, cols] = gated
             total_sq = total_sq + gated * gated
-        sq_ref[rows, :] = jnp.sum(total_sq, axis=1, keepdims=True)
+        sq_ref[sub] = jnp.sum(total_sq, axis=1).reshape(1, tile_len)
 
 
 def contrib_tile(x_ref, bt_ref, end_ref, pass_ref, before_ref, total_ref):
@@ -164,11 +164,11 @@
         ],
         out_specs=[
             pl.BlockSpec((span, inner_here), lambda j: (j, 0)),
-            pl.BlockSpec((span, 1), lambda j: (j, 0)),
+            pl.BlockSpec((group, 1, tile_len), per_tile),
         ],
         out_shape=[
             jax.ShapeDtypeStruct((rows, inner_here), jnp.float32),
-            jax.ShapeDtypeStruct((rows, 1), jnp.float32),
+            jax.ShapeDtypeStruct((tiles_dev, 1, tile_len), jnp.float32),
         ],
         cost_estimate=pl.CostEstimate(
             flops=tiles_dev * (2 * tile_len * tile_len * (state_dim + 4 * inner_here + 2 * inner_here)),

time: 221 us -> 218 us (0.986)
  other arithmetic: 35 us -> 32 us
where the time goes in v21:
time: 218 us; the launch traced here: 217 us
  blocking collectives  43.1 us (20%)
  waiting for transfers between devices  36.2 us (17%)
  matrix products  33.2 us (15%)
  other arithmetic  32 us (15%)
  Pallas kernels  28.5 us (13%)
  local copies, waits for them, and re-layouts  23.8 us (11%)
  starting transfers between devices  19 us (9%)
    unnamed x1, blocking collectives  39.4 us
    ppermute x6, waiting for transfers between devices, shifted(): return lax.ppermute(x, axis, pairs)  36.2 us
    dot_general x3, matrix products, project(): jnp.dot(partner_rows, other_part, preferred_element_type=jnp.float32)  20.9 us
    pallas_call x1, Pallas kernels, mix_tiles(): pl.pallas_call(mix_tile, grid=(tiles_dev // group,), in_specs=[pl.BlockSp...  19 us
    convert_element_type x1, other arithmetic, shards(): conv_out = jax.nn.silu(total).astype(jnp.bfloat16)  10.9 us
    ppermute x6, starting transfers between devices, shifted(): return lax.ppermute(x, axis, pairs)  10.7 us
    unnamed x64, local copies, waits for them, and re-layouts  10 us
    pallas_call x1, Pallas kernels, contrib_tiles(): pl.pallas_call(contrib_tile, grid=(tiles_dev // group,), in_specs=[pl.Blo...  9.55 us
  transfers between devices with their start and end apart: 8, of which 5 were waited for; matrix products, arithmetic and copies ran while one was open for 14% of the time, Pallas kernels for 0%

profile of v21, /device:TPU:29, one launch (start us, length us, event | category | flops | bytes accessed | tf_op | source)
XLA Modules:
  0.0 217.2 jit_solution(15214616105758904366)
XLA Ops:
  3.0 2.5 %copy.81 = bf16[16,128,512]{2,1,0:T(8,128)(2,1)} copy(bf16[16,128,512]{2,0,1:T(8,128)(2,1)S(1)} %fusion.9) | data formatting | bytes 4194304 | tf_op jit(solution)/shard_map/convert_element_type | solution.py:216
  5.5 6.4 %all-to-all-start = ((bf16[16,128,512]{2,1,0:T(8,128)(2,1)}), bf16[16,128,512]{2,1,0:T(8,128)(2,1)S(1)}, u32[]{:S(2)}, u32[]{:S(2)}) async-start(bf16[16,128,512]{2,1,0:T(8,128)(2,1)} %copy.81), calls=%async_computation | async-start | bytes 4194304 | tf_op jit(solution)/shard_map/all_to_all | solution.py:217
  11.9 5.7 %copy.100 = bf16[128,8,2,1024]{3,1,2,0:T(8,128)(2,1)} copy(bf16[128,8,2,1024]{3,2,1,0:T(2,128)(2,1)} %bitcast.58) | data formatting | bytes 8388608
  19.0 39.4 %all-reduce.1 = s32[256]{0:T(256)S(1)} all-reduce(s32[256]{0:T(256)S(1)} %dynamic-update-slice), channel_id=1, replica_groups=mesh['seq'=16,'head'=2] {'seq'}, use_global_device_ids=true, to_apply=%add.1 | all-reduce | flops 256 | bytes 2048
  63.8 1.9 collective-permute-start
  68.1 8.1 %fusion.7 = f32[2048,2048]{1,0:T(8,128)} fusion(bf16[2048,512]{1,0:T(8,128)(2,1)S(1)} %bitcast.55, bf16[1024,2048]{1,0:T(8,128)(2,1)S(1)} %bitcast.60, s32[]{:T(128)S(6)} %select_n.90), kind=kOutput, calls=%fused_computation.16 | convolution fusion | flops 4294967296 | bytes 20971524 | tf_op jit(solution)/shard_map/dot_general | solution.py:237
  76.1 14.8 %add_convert_fusion.gate_ref = bf16[2048,2048]{1,0:T(8,128)(2,1)} fusion(f32[2048,2048]{1,0:T(8,128)} %fusion.7, bf16[2048,512]{1,0:T(8,128)(2,1)} %collective-permute-done, bf16[1024,2048]{1,0:T(8,128)(2,1)} %bitcast.59, s32[]{:T(128)S(6)} %select_n.91), kind=kOutput, calls=%fused_computation | convolution fusion | flops 4303355904 | bytes 29360132 | tf_op jit(solution)/shard_map/dot_general | solution.py:237
  90.9 2.6 %slice.153 = bf16[2048,1024]{1,0:T(8,128)(2,1)S(1)} slice(bf16[2048,2048]{1,0:T(8,128)(2,1)} %add_convert_fusion.gate_ref), slice={[0:2048], [1024:2048]} | slice | bytes 8388608 | tf_op jit(solution)/shard_map/slice | solution.py:248
  93.6 3.8 %fusion = bf16[2048,256]{1,0:T(8,128)(2,1)S(1)} fusion(f32[2048,256]{1,0:T(8,128)S(1)} %fusion.21, bf16[2048,512]{1,0:T(8,128)(2,1)} %collective-permute-done, bf16[1024,256]{1,0:T(8,128)(2,1)S(1)} %copy-done.9, s32[]{:T(128)S(6)} %select_n.91), kind=kOutput, calls=%fused_computation.8 | convolution fusion | flops 537919488 | bytes 5505028 | tf_op jit(solution)/shard_map/dot_general | solution.py:237
  98.0 2.7 %collective-permute-start.1 = (bf16[3,1281]{1,0:T(4,128)(2,1)}, bf16[3,1281]{1,0:T(4,128)(2,1)}, u32[]{:S(2)}, u32[]{:S(2)}) collective-permute-start(bf16[3,1281]{1,0:T(4,128)(2,1)} %pad_maximum_fusion.5), channel_id=1, source_target_pairs={{0,2},{2,4},{4,6},{6,8},{8,10},{10,12},{12,14},{14,16},{16,18},{18... | collective-permute-start | bytes 23066 | tf_op jit(solution)/shard_map/ppermute | solution.py:17
  100.7 2.3 %compare_select_fusion = f32[2048,16]{0,1:T(8,128)S(1)} fusion(f32[2048,16]{0,1:T(8,128)S(1)} %fusion.29, bf16[2048,512]{1,0:T(8,128)(2,1)} %collective-permute-done, f32[16]{0:T(128)S(1)} %copy-done.24, bf16[1024,16]{0,1:T(8,128)(2,1)S(1)} %copy-done.10, s32[]{:T(128)S(6)} %select_n.91), kind=kOutput, calls=%fused_computation.31 | convolution fusion | flops 33816576 | bytes 2376196 | tf_op jit(solution)/shard_map/dot_general | solution.py:237
  108.0 4.0 %maximum_maximum_fusion = bf16[2051,1280]{1,0:T(8,128)(2,1)S(1)} fusion(bf16[2048,256]{1,0:T(8,128)(2,1)S(1)} %fusion, bf16[2048,1024]{1,0:T(8,128)(2,1)} %copy-done.3, bf16[3,1280]{1,0:T(4,128)(2,1)S(1)} %slice.162), kind=kLoop, calls=%fused_computation.5 | loop fusion | flops 15751680 | bytes 10501120 | tf_op jit(solution)/shard_map/concatenate | solution.py:261
  112.9 10.9 %multiply_convert_fusion.x_ref.b_ref.c_ref = bf16[2048,1280]{1,0:T(8,128)(2,1)S(1)} fusion(bf16[2048,256]{1,0:T(8,128)(2,1)S(1)} %fusion, bf16[2051,1280]{1,0:T(8,128)(2,1)S(1)} %maximum_maximum_fusion, f32[1280]{0:T(1024)S(1)} %copy-done.12, f32[1280]{0:T(1024)S(1)} %copy-done.13, f32[1280]{0:T(1024)S(1)} %copy-done.14, f32[1280]{0:T(1024)S(1)} %copy-done.11, ...), kind=kLoop, calls=%fused_computation.1 | loop fusion | flops 60293120 | bytes 26246144 | tf_op jit(solution)/shard_map/convert_element_type | solution.py:274
  123.8 2.4 %copy-done.2 = bf16[2048,1280]{1,0:T(8,128)(2,1)} copy-done((bf16[2048,1280]{1,0:T(8,128)(2,1)}, bf16[2048,1280]{1,0:T(8,128)(2,1)S(1)}, u32[]{:S(2)}) %copy-start.2) | copy-done | bytes 5242904
  127.3 9.5 %shard_map.136 = (f32[16,128,1024]{2,1,0:T(8,128)}, f32[128,1024]{1,0:T(8,128)}) custom-call(bf16[2048,1280]{1,0:T(8,128)(2,1)} %copy-done.2, bf16[16,128,128]{2,1,0:T(8,128)(2,1)} %bitcast.62, f32[16,128,16]{2,1,0:T(8,128)} %multiply_multiply_fusion.end_ref, f32[16,1,1024]{2,1,0:T(1,128)} %broadcast_in_dim_reshape.10.pass_ref), custom_call_target="tpu_custom_call" | custom-call | flops 536870912 | bytes 13107200 | tf_op jit(solution)/shard_map/pallas_call | solution.py:109
  138.0 1.9 collective-permute-start.2
  140.0 8.7 %collective-permute-done.2 = bf16[131,1024]{1,0:T(8,128)(2,1)S(1)} collective-permute-done((bf16[131,1024]{1,0:T(8,128)(2,1)S(1)}, bf16[131,1024]{1,0:T(8,128)(2,1)S(1)}, u32[]{:S(2)}, u32[]{:S(2)}) %collective-permute-start.2) | collective-permute-done | bytes 268320 | tf_op jit(solution)/shard_map/ppermute | solution.py:17
  151.3 7.6 %collective-permute-done.3 = bf16[131,1024]{1,0:T(8,128)(2,1)S(1)} collective-permute-done((bf16[131,1024]{1,0:T(8,128)(2,1)S(1)}, bf16[131,1024]{1,0:T(8,128)(2,1)S(1)}, u32[]{:S(2)}, u32[]{:S(2)}) %collective-permute-start.3) | collective-permute-done | bytes 268320 | tf_op jit(solution)/shard_map/ppermute | solution.py:17
  161.6 5.6 %collective-permute-done.4 = bf16[131,1024]{1,0:T(8,128)(2,1)S(1)} collective-permute-done((bf16[131,1024]{1,0:T(8,128)(2,1)S(1)}, bf16[131,1024]{1,0:T(8,128)(2,1)S(1)}, u32[]{:S(2)}, u32[]{:S(2)}) %collective-permute-start.4) | collective-permute-done | bytes 268320 | tf_op jit(solution)/shard_map/ppermute | solution.py:17
  167.4 2.3 %collective-permute-start.5 = (bf16[131,1024]{1,0:T(8,128)(2,1)S(1)}, bf16[131,1024]{1,0:T(8,128)(2,1)S(1)}, u32[]{:S(2)}, u32[]{:S(2)}) collective-permute-start(bf16[131,1024]{1,0:T(8,128)(2,1)S(1)} %pad_maximum_fusion.4), channel_id=1, source_target_pairs={{0,2},{2,4},{4,6},{6,8},{8,10},{10,12},{12,14},{14,16},{16,18},{18... | collective-permute-start | bytes 804872 | tf_op jit(solution)/shard_map/ppermute | solution.py:17
  175.7 12.6 %collective-permute-done.6 = bf16[128,1024]{1,0:T(8,128)(2,1)S(1)} collective-permute-done((bf16[128,1024]{1,0:T(8,128)(2,1)S(1)}, bf16[128,1024]{1,0:T(8,128)(2,1)S(1)}, u32[]{:S(2)}, u32[]{:S(2)}) %collective-permute-start.6) | collective-permute-done | bytes 262176 | tf_op jit(solution)/shard_map/ppermute | solution.py:17
  189.1 19.0 %shard_map.137 = (f32[2048,1024]{1,0:T(8,128)}, f32[16,1,128]{2,1,0:T(1,128)}) custom-call(bf16[2048,1280]{1,0:T(8,128)(2,1)} %copy-done.2, bf16[2048,1280]{1,0:T(8,128)(2,1)} %copy-done.2, bf16[2048,1280]{1,0:T(8,128)(2,1)} %copy-done.2, f32[16,128,16]{2,1,0:T(8,128)} %bitcast.57, f32[16,16,128]{2,1,0:T(8,128)} %copy-done.8, ...), custom_call_target="tpu_custom_call" | custom-call | flops 3288334336 | bytes 29360128 | tf_op jit(solution)/shard_map/pallas_call | solution.py:147
  208.1 3.7 %psum.7 = f32[16,128]{1,0:T(8,128)S(1)} all-reduce(f32[16,128]{1,0:T(8,128)} %bitcast.71), channel_id=1, replica_groups=mesh['seq'=16,'head'=2] {'head'}, use_global_device_ids=true, to_apply=%region_3.4 | all-reduce | flops 2048 | bytes 16384 | tf_op jit(solution)/shard_map/psum | solution.py:323
  211.8 5.3 %multiply_convert_fusion.1 = bf16[2048,1024]{1,0:T(8,128)(2,1)} fusion(f32[2048,1024]{1,0:T(8,128)} %get-tuple-element.15, f32[1024]{0:T(1024)S(1)} %copy-done.20, f32[2048]{0:T(1024)S(1)} %rsqrt_bitcast_fusion), kind=kLoop, calls=%fused_computation.2 | loop fusion | flops 6291456 | bytes 12595200 | tf_op jit(solution)/shard_map/convert_element_type | solution.py:324
  (144 shorter events, 32.3 us)
Async XLA Ops:
  5.5 55.8 %all-to-all-start = ((bf16[16,128,512]{2,1,0:T(8,128)(2,1)}), bf16[16,128,512]{2,1,0:T(8,128)(2,1)S(1)}, u32[]{:S(2)}, u32[]{:S(2)}) async-start(bf16[16,128,512]{2,1,0:T(8,128)(2,1)} %copy.81), calls=%async_computation | async-start | bytes 4194304 | tf_op jit(solution)/shard_map/all_to_all | solution.py:217
  11.9 6.9 %copy-start.26 = (s32[16]{0:T(128)S(1)}, s32[16]{0:T(128)}, u32[]{:S(2)}) copy-start(s32[16]{0:T(128)} %param.15) | copy-start | bytes 196
  11.9 46.6 %copy-start.17 = (s32[16]{0:T(128)S(1)}, s32[16]{0:T(128)}, u32[]{:S(2)}) copy-start(s32[16]{0:T(128)} %param.16) | copy-start | bytes 196
  11.9 48.1 %copy-start.21 = (f32[1024]{0:T(1024)S(1)}, f32[1024]{0:T(1024)}, u32[]{:S(2)}) copy-start(f32[1024]{0:T(1024)} %param.24) | copy-start | bytes 12292
  11.9 48.1 %copy-start.23 = (f32[256]{0:T(256)S(1)}, f32[256]{0:T(256)}, u32[]{:S(2)}) copy-start(f32[256]{0:T(256)} %param.25) | copy-start | bytes 3076
  11.9 48.4 %copy-start.19 = (f32[4,1024]{1,0:T(4,128)S(1)}, f32[4,1024]{1,0:T(4,128)}, u32[]{:S(2)}) copy-start(f32[4,1024]{1,0:T(4,128)} %param.22) | copy-start | bytes 49156
  11.9 48.5 %copy-start.27 = (f32[16]{0:T(128)S(1)}, f32[16]{0:T(128)}, u32[]{:S(2)}) copy-start(f32[16]{0:T(128)} %param.21) | copy-start | bytes 196
  17.6 48.1 %copy-start.22 = (f32[4,256]{1,0:T(4,128)S(1)}, f32[4,256]{1,0:T(4,128)}, u32[]{:S(2)}) copy-start(f32[4,256]{1,0:T(4,128)} %param.23) | copy-start | bytes 12292
  17.6 48.9 %copy-start.10 = (bf16[1024,16]{0,1:T(8,128)(2,1)S(1)}, bf16[1024,16]{0,1:T(8,128)(2,1)}, u32[]{:S(2)}) copy-start(bf16[1024,16]{0,1:T(8,128)(2,1)} %param.19) | copy-start | bytes 98308
  59.4 6.5 %copy-start.15 = (f32[2048]{0:T(1024)}, f32[2048]{0:T(1024)S(1)}, u32[]{:S(2)}) copy-start(f32[2048]{0:T(1024)S(1)} %add_bitcast_fusion) | copy-start | bytes 24580
  63.8 12.3 %collective-permute-start = (bf16[2048,512]{1,0:T(8,128)(2,1)S(1)}, bf16[2048,512]{1,0:T(8,128)(2,1)}, u32[]{:S(2)}, u32[]{:S(2)}) collective-permute-start(bf16[2048,512]{1,0:T(8,128)(2,1)S(1)} %bitcast.52), channel_id=1, source_target_pairs={{0,1},{1,0},{2,3},{3,2},{4,5},{5,4},{6,7},{7,6},{8,9},{9,8},{10,11... | collective-permute-start | bytes 6291464 | tf_op jit(solution)/shard_map/ppermute | solution.py:230
  93.6 7.1 %copy-start.24 = (f32[16]{0:T(128)S(1)}, f32[16]{0:T(128)}, u32[]{:S(2)}) copy-start(f32[16]{0:T(128)} %param.20) | copy-start | bytes 196
  98.0 9.2 %collective-permute-start.1 = (bf16[3,1281]{1,0:T(4,128)(2,1)}, bf16[3,1281]{1,0:T(4,128)(2,1)}, u32[]{:S(2)}, u32[]{:S(2)}) collective-permute-start(bf16[3,1281]{1,0:T(4,128)(2,1)} %pad_maximum_fusion.5), channel_id=1, source_target_pairs={{0,2},{2,4},{4,6},{6,8},{8,10},{10,12},{12,14},{14,16},{16,18},{18... | collective-permute-start | bytes 23066 | tf_op jit(solution)/shard_map/ppermute | solution.py:17
  103.3 8.7 %copy-start.8 = (f32[16,16,128]{2,1,0:T(8,128)}, f32[16,16,128]{2,1,0:T(8,128)S(1)}, u32[]{:S(2)}) copy-start(f32[16,16,128]{2,1,0:T(8,128)S(1)} %fusion.24.cumt_ref) | copy-start | bytes 393220
  103.7 8.3 %copy-start.5 = (f32[16,16,128]{1,2,0:T(8,128)}, f32[16,16,128]{1,2,0:T(8,128)S(1)}, u32[]{:S(2)}) copy-start(f32[16,16,128]{1,2,0:T(8,128)S(1)} %copy.91) | copy-start | bytes 393220
  136.8 22.2 %copy-start.6 = (f32[128,1024]{1,0:T(8,128)S(1)}, f32[128,1024]{1,0:T(8,128)}, u32[]{:S(2)}) copy-start(f32[128,1024]{1,0:T(8,128)} %get-tuple-element.14) | copy-start | bytes 1572868
  136.8 23.7 %copy-start.18 = (s32[16]{0:T(128)S(1)}, s32[16]{0:T(128)}, u32[]{:S(2)}) copy-start(s32[16]{0:T(128)} %param.16) | copy-start | bytes 196
  138.0 32.3 %copy-start.25 = (f32[16]{0:T(128)S(1)}, f32[16]{0:T(128)}, u32[]{:S(2)}) copy-start(f32[16]{0:T(128)} %param.26) | copy-start | bytes 196
  138.0 10.7 %collective-permute-start.2 = (bf16[131,1024]{1,0:T(8,128)(2,1)S(1)}, bf16[131,1024]{1,0:T(8,128)(2,1)S(1)}, u32[]{:S(2)}, u32[]{:S(2)}) collective-permute-start(bf16[131,1024]{1,0:T(8,128)(2,1)S(1)} %pad_maximum_fusion.1), channel_id=1, source_target_pairs={{0,2},{2,4},{4,6},{6,8},{8,10},{10,12},{12,14},{14,16},{16,18},{18... | collective-permute-start | bytes 804872 | tf_op jit(solution)/shard_map/ppermute | solution.py:17
  150.0 8.9 %collective-permute-start.3 = (bf16[131,1024]{1,0:T(8,128)(2,1)S(1)}, bf16[131,1024]{1,0:T(8,128)(2,1)S(1)}, u32[]{:S(2)}, u32[]{:S(2)}) collective-permute-start(bf16[131,1024]{1,0:T(8,128)(2,1)S(1)} %pad_maximum_fusion.2), channel_id=1, source_target_pairs={{0,4},{2,6},{4,8},{6,10},{8,12},{10,14},{12,16},{14,18},{16,20},{1... | collective-permute-start | bytes 804872 | tf_op jit(solution)/shard_map/ppermute | solution.py:17
  159.2 8.0 %collective-permute-start.4 = (bf16[131,1024]{1,0:T(8,128)(2,1)S(1)}, bf16[131,1024]{1,0:T(8,128)(2,1)S(1)}, u32[]{:S(2)}, u32[]{:S(2)}) collective-permute-start(bf16[131,1024]{1,0:T(8,128)(2,1)S(1)} %pad_maximum_fusion.3), channel_id=1, source_target_pairs={{0,8},{2,10},{4,12},{6,14},{8,16},{10,18},{12,20},{14,22},{16,24},... | collective-permute-start | bytes 804872 | tf_op jit(solution)/shard_map/ppermute | solution.py:17
  167.4 8.2 %collective-permute-start.5 = (bf16[131,1024]{1,0:T(8,128)(2,1)S(1)}, bf16[131,1024]{1,0:T(8,128)(2,1)S(1)}, u32[]{:S(2)}, u32[]{:S(2)}) collective-permute-start(bf16[131,1024]{1,0:T(8,128)(2,1)S(1)} %pad_maximum_fusion.4), channel_id=1, source_target_pairs={{0,2},{2,4},{4,6},{6,8},{8,10},{10,12},{12,14},{14,16},{16,18},{18... | collective-permute-start | bytes 804872 | tf_op jit(solution)/shard_map/ppermute | solution.py:17
  171.1 17.1 %collective-permute-start.6 = (bf16[128,1024]{1,0:T(8,128)(2,1)S(1)}, bf16[128,1024]{1,0:T(8,128)(2,1)S(1)}, u32[]{:S(2)}, u32[]{:S(2)}) collective-permute-start(bf16[128,1024]{1,0:T(8,128)(2,1)S(1)} %fusion.17), channel_id=1, source_target_pairs={{0,18},{2,20},{4,22},{6,24},{8,26},{10,28},{12,30},{1,19},{3,21},{... | collective-permute-start | bytes 786440 | tf_op jit(solution)/shard_map/ppermute | solution.py:17
  189.1 22.7 %copy-start.20 = (f32[1024]{0:T(1024)S(1)}, f32[1024]{0:T(1024)}, u32[]{:S(2)}) copy-start(f32[1024]{0:T(1024)} %param.27) | copy-start | bytes 12292
  (13 other events, 56.8 us)
